TPU v7x, 32 devices: a whole 2x2x4 slice. The times are simulated.
32 devices in a mesh: vol: 2 (over y), wide: 4 (over z), narrow: 4 (over x, core).
Axes of the slice: x: 2, y: 2, z: 4, core: 2. Of those that a mesh axis runs over, the one named last changes fastest.
Arguments:
- tiles: float32 [32, 32, 128, 128], P(('vol', 'narrow'), 'wide'), parts along dimension 0, as said below
- pattern: int32 [32, 32], P(('vol', 'narrow'), 'wide'), parts along dimension 0, may hold values from 0 to 15, as said below
- seed_label: int32 [4096, 1], P(('vol', 'narrow', 'wide')), parts along dimension 0, may hold values from 0 to 255, as said below
Outputs:
- solution: float32 [4096, 128], P(('vol', 'narrow', 'wide')), parts along dimension 0
- residual: float32 [4096, 128], P(('vol', 'narrow', 'wide')), parts along dimension 0
There are 2 independent parts, one for each index of `vol`. A program takes and returns all parts, laid end to end along the dimension named above; each array names one. Nothing has to cross between parts.
Inputs may be any that keep to these rules, and one draw needn't show every extreme that they name: `pattern`: stored tile k of block row r lies in block column c with (c % (16 // 4)) == k // (32 // 4); every block column is named 32 times in all; W is symmetric: the tile at (r, c) is the transpose of the tile at (c, r), and a tile at (r, r) is symmetric. `tiles`: entries lie between 0 and 8, and W built from them is symmetric. `seed_label`: values under 128 are the seed label of a seeded supervoxel, values of 128 or more mark an unseeded one; exactly 128 supervoxels are seeded, and every value occurs.
All inputs are finite; a program needn't handle non-finite values.
Results may differ from a plain program's by a relative error of at most 0.0003.
Values sent between devices are 32-bit elements; how exact they have to be, the bound alone decides.
No kernel may reach another device: no remote copies, remote signals or barrier semaphores. Data moves between devices by JAX's collectives and lax.ppermute only.
A program may use at most 64 MiB of HBM per device.

v0:
```python
import jax
import jax.numpy as jnp
from jax import lax
from jax.sharding import PartitionSpec as P

SEED_CLASSES = 128
ITERS = 3


SEED_WEIGHT = 2.0
PRIOR = 0.5


def local(tiles, pattern, seed_label):
    groups = tiles.shape[0]
    tile = tiles.shape[2]
    own_rows = seed_label.shape[0]
    br_local = own_rows // tile
    local_column = pattern // groups * br_local + pattern % br_local
    row_sums = jnp.sum(tiles, axis=(1, 3))
    degree = lax.psum_scatter(row_sums, "wide", scatter_dimension=0, tiled=True).reshape(own_rows)
    seeded = (seed_label[:, 0] < SEED_CLASSES).astype(jnp.float32)
    diag_column = (degree + SEED_WEIGHT * seeded + PRIOR)[:, None]

    def reduce_dots(values):
        return lax.psum((values[0],), ("wide", "narrow"))

    labels = seed_label[:, 0]
    rhs = SEED_WEIGHT * (
        labels[:, None] == jnp.arange(SEED_CLASSES, dtype=jnp.int32)[None, :]
    ).astype(jnp.float32)
    solution = jnp.zeros_like(rhs)
    residual = rhs
    direction = rhs
    norm_now = reduce_dots((jnp.sum(residual * residual, axis=0),))[0]
    for step in range(ITERS):
        gathered = lax.all_gather(direction, "narrow", axis=0, tiled=True)
        width = gathered.shape[1]
        blocks = gathered.reshape(-1, tile, width)
        number = own_rows * lax.axis_size("wide") // tile
        picked = blocks[local_column]
        result = jnp.einsum("mkab,mkbl->mal", tiles, picked, precision=lax.Precision.HIGHEST)
        image = diag_column * direction - lax.psum_scatter(
            result.reshape(number * tile, width), "wide", scatter_dimension=0, tiled=True
        )
        curvature = reduce_dots((jnp.sum(direction * image, axis=0),))[0]
        alpha = norm_now / curvature
        solution = solution + alpha * direction
        residual = residual - alpha * image
        norm_next = reduce_dots((jnp.sum(residual * residual, axis=0),))[0]
        direction = residual + norm_next / norm_now * direction
        norm_now = norm_next
    return (solution, residual)


def solution(mesh):
    placed = (
        P(("vol", "narrow"), "wide", None, None),
        P(("vol", "narrow"), "wide"),
        P(("vol", "narrow", "wide"), None),
    )
    return jax.shard_map(
        local,
        mesh=mesh,
        in_specs=placed,
        out_specs=(P(("vol", "narrow", "wide"), None), P(("vol", "narrow", "wide"), None)),
        check_vma=False,
    )
```

profile of v0, /device:TPU:0, one launch (start us, length us, event | category | flops | bytes accessed | tf_op | source)
XLA Modules:
  0.0 264.2 jit_solution(9219994174304380900)
XLA Ops:
  7.2 0.0 reduce-scatter.4.cloned.1.call-start
  7.2 0.7 compare_select_fusion
  7.9 0.1 reshape.40
  8.0 0.7 fusion.6
  8.7 7.2 %all_gather.9 = f32[512,128]{1,0:T(8,128)S(1)} all-gather(f32[128,128]{1,0:T(8,128)S(1)} %fusion.6), channel_id=1, replica_groups=mesh['vol'=2,'wide'=4,'narrow'=4] {'narrow'}, dimensions={0}, use_global_device_ids=true | all-gather | bytes 327680 | tf_op jit(solution)/shard_map/all_gather | solution.py:37
  15.9 0.0 copy-start
  15.9 2.0 gather_fusion
  18.0 0.0 copy-done
  18.0 4.6 %fusion.10 = f32[4,128,128,1]{1,2,3,0:T(8,128)} fusion(f32[4,8,128,128]{3,2,1,0:T(8,128)} %bitcast.44, f32[4,8,128,128]{3,2,1,0:T(8,128)S(1)} %copy-done), kind=kOutput, calls=%fused_computation.39 | convolution fusion | flops 805306368 | bytes 4456448 | tf_op jit(solution)/shard_map/mkab,mkbl->mal/dot_general | solution.py:42
  22.6 0.0 copy-start.3
  22.6 0.0 copy-start.2
  22.6 0.0 reduce-scatter.4.cloned.1.call-update
  22.6 0.0 reduce-scatter.6.cloned.1.call-start
  22.7 0.2 reduce_sum.64
  22.8 0.4 copy-done.3
  23.2 0.6 dynamic-slice
  23.8 12.1 %all-reduce = f32[4,128]{1,0:T(4,128)S(1)} all-reduce(f32[4,128]{1,0:T(4,128)S(1)} %reduce_sum.64), channel_id=2, replica_groups=mesh['vol'=2,'wide'=4,'narrow'=4] {'wide'}, use_global_device_ids=true, to_apply=%region_3.4.clone | all-reduce | flops 512 | bytes 4096
  35.9 0.0 copy-done.2
  35.9 0.7 add_bitcast_fusion
  36.5 7.1 %reduce-scatter.4.cloned.1.call-done = f32[128,128]{1,0:T(8,128)} async-done(((f32[512,128]{1,0:T(8,128)}), f32[128,128]{1,0:T(8,128)}) %reduce-scatter.4.cloned.1.call-update) | async-done | bytes 65552 | tf_op jit(solution)/shard_map/reduce_scatter | solution.py:43
  43.7 1.0 fusion.2
  44.6 29.5 %all-reduce.1 = (f32[128]{0:T(128)S(1)}, f32[128]{0:T(128)S(1)}) all-reduce(f32[128]{0:T(128)S(1)} %get-tuple-element.3, f32[128]{0:T(128)S(1)} %get-tuple-element.2), channel_id=1, replica_groups=mesh['vol'=2,'wide'=4,'narrow'=4] {'wide','narrow'}, use_global_device_ids=true, to_apply=%region_1.2 | all-reduce | flops 256 | bytes 2048 | tf_op jit(solution)/shard_map/psum | solution.py:26
  74.1 1.0 multiply_reduce_fusion.3
  75.1 29.5 %psum.44 = f32[128]{0:T(128)S(1)} all-reduce(f32[128]{0:T(128)S(1)} %multiply_reduce_fusion.3), channel_id=1, replica_groups=mesh['vol'=2,'wide'=4,'narrow'=4] {'wide','narrow'}, use_global_device_ids=true, to_apply=%region_8.9 | all-reduce | flops 128 | bytes 1024 | tf_op jit(solution)/shard_map/psum | solution.py:26
  104.6 0.9 fusion.5
  105.5 5.8 %all_gather.10 = f32[512,128]{1,0:T(8,128)S(1)} all-gather(f32[128,128]{1,0:T(8,128)S(1)} %fusion.5), channel_id=1, replica_groups=mesh['vol'=2,'wide'=4,'narrow'=4] {'narrow'}, dimensions={0}, use_global_device_ids=true | all-gather | bytes 327680 | tf_op jit(solution)/shard_map/all_gather | solution.py:37
  111.3 2.0 gather_fusion.1
  113.3 0.0 copy-start.1
  113.3 4.6 %fusion.11 = f32[4,128,128,1]{1,2,3,0:T(8,128)} fusion(f32[4,8,128,128]{3,2,1,0:T(8,128)} %bitcast.45, f32[4,8,128,128]{3,2,1,0:T(8,128)S(1)} %copy-done), kind=kOutput, calls=%fused_computation.40 | convolution fusion | flops 805306368 | bytes 4456448 | tf_op jit(solution)/shard_map/mkab,mkbl->mal/dot_general | solution.py:42
  118.0 0.0 reduce-scatter.6.cloned.1.call-update
  118.0 0.0 reduce-scatter.8.cloned.1.call-start
  118.0 17.1 %reduce-scatter.6.cloned.1.call-done = f32[128,128]{1,0:T(8,128)} async-done(((f32[512,128]{1,0:T(8,128)}), f32[128,128]{1,0:T(8,128)}) %reduce-scatter.6.cloned.1.call-update) | async-done | bytes 65552 | tf_op jit(solution)/shard_map/reduce_scatter | solution.py:43
  135.2 0.0 copy-done.1
  135.2 1.0 multiply_reduce_fusion.2
  136.1 29.5 %psum.45 = f32[128]{0:T(128)S(1)} all-reduce(f32[128]{0:T(128)S(1)} %multiply_reduce_fusion.2), channel_id=1, replica_groups=mesh['vol'=2,'wide'=4,'narrow'=4] {'wide','narrow'}, use_global_device_ids=true, to_apply=%region_11.12 | all-reduce | flops 128 | bytes 1024 | tf_op jit(solution)/shard_map/psum | solution.py:26
  165.6 1.0 multiply_reduce_fusion.1
  166.6 29.5 %psum.46 = f32[128]{0:T(128)S(1)} all-reduce(f32[128]{0:T(128)S(1)} %get-tuple-element.6), channel_id=1, replica_groups=mesh['vol'=2,'wide'=4,'narrow'=4] {'wide','narrow'}, use_global_device_ids=true, to_apply=%region_13.14 | all-reduce | flops 128 | bytes 1024 | tf_op jit(solution)/shard_map/psum | solution.py:26
  196.1 0.1 multiply_add_fusion
  196.2 5.8 %all_gather.11 = f32[512,128]{1,0:T(8,128)S(1)} all-gather(f32[128,128]{1,0:T(8,128)S(1)} %multiply_add_fusion), channel_id=1, replica_groups=mesh['vol'=2,'wide'=4,'narrow'=4] {'narrow'}, dimensions={0}, use_global_device_ids=true | all-gather | bytes 327680 | tf_op jit(solution)/shard_map/all_gather | solution.py:37
  202.0 2.0 gather_fusion.2
  204.0 4.6 %fusion.12 = f32[4,128,128,1]{1,2,3,0:T(8,128)} fusion(f32[4,8,128,128]{3,2,1,0:T(8,128)} %bitcast.43, f32[4,8,128,128]{3,2,1,0:T(8,128)S(1)} %copy-done), kind=kOutput, calls=%fused_computation.41 | convolution fusion | flops 805306368 | bytes 4456448 | tf_op jit(solution)/shard_map/mkab,mkbl->mal/dot_general | solution.py:42
  208.6 0.0 reduce-scatter.8.cloned.1.call-update
  208.7 17.0 %reduce-scatter.8.cloned.1.call-done = f32[128,128]{1,0:T(8,128)} async-done(((f32[512,128]{1,0:T(8,128)}), f32[128,128]{1,0:T(8,128)}) %reduce-scatter.8.cloned.1.call-update) | async-done | bytes 65552 | tf_op jit(solution)/shard_map/reduce_scatter | solution.py:43
  225.7 0.9 multiply_reduce_fusion
  226.6 29.5 %psum.47 = f32[128]{0:T(128)S(1)} all-reduce(f32[128]{0:T(128)S(1)} %multiply_reduce_fusion), channel_id=1, replica_groups=mesh['vol'=2,'wide'=4,'narrow'=4] {'wide','narrow'}, use_global_device_ids=true, to_apply=%region_16.17 | all-reduce | flops 128 | bytes 1024 | tf_op jit(solution)/shard_map/psum | solution.py:26
  256.1 1.6 multiply_subtract_fusion
  (6 shorter events, 0.0 us)
Async XLA Ops:
  7.2 36.5 %reduce-scatter.4.cloned.1.call-start = ((), (), s32[]{:S(2)}) async-start(), calls=%async_computation.3 | async-start | bytes 327680 | tf_op jit(solution)/shard_map/reduce_scatter | solution.py:43
  15.9 2.0 copy-start
  22.6 0.7 copy-start.3
  22.6 13.3 %copy-start.2 = (s32[128,1]{0,1:T(1,128)S(1)}, s32[128,1]{0,1:T(1,128)}, u32[]{:S(2)}) copy-start(s32[128,1]{0,1:T(1,128)} %param.5) | copy-start | bytes 1540
  22.6 112.6 %reduce-scatter.6.cloned.1.call-start = ((), (), s32[]{:S(2)}) async-start(), calls=%async_computation.4 | async-start | bytes 327680 | tf_op jit(solution)/shard_map/reduce_scatter | solution.py:43
  113.3 21.8 %copy-start.1 = (f32[128,128]{1,0:T(8,128)S(1)}, f32[128,128]{1,0:T(8,128)}, u32[]{:S(2)}) copy-start(f32[128,128]{1,0:T(8,128)} %reduce-scatter.4.cloned.1.call-done) | copy-start | bytes 196612
  118.0 107.7 %reduce-scatter.8.cloned.1.call-start = ((), (), s32[]{:S(2)}) async-start(), calls=%async_computation.5 | async-start | bytes 327680 | tf_op jit(solution)/shard_map/reduce_scatter | solution.py:43
Sparse Core Ops, SparseCore 0:
  22.7 20.8 reduce-scatter.3
  118.1 17.0 reduce-scatter.5
  208.8 16.8 reduce-scatter.7
where the time goes:
time: 265 us; the launch traced here: 264 us
  blocking collectives  178 us (67%)
  waiting for transfers between devices  41.3 us (16%)
  matrix products  13.8 us (5%)
  between operations  13.8 us (5%)
  other arithmetic  9.74 us (4%)
  local copies, waits for them, and re-layouts  7.16 us (3%)
    psum x5, blocking collectives, reduce_dots(): return lax.psum((values[0],), ('wide', 'narrow'))  147 us
    reduce_scatter x3, waiting for transfers between devices, local(): lax.psum_scatter(result.reshape(number * tile, width), 'wide', scatter_di...  41.2 us
    all_gather x3, blocking collectives, local(): gathered = lax.all_gather(direction, 'narrow', axis=0, tiled=True)  18.8 us
    dot_general x3, matrix products, local(): jnp.einsum('mkab,mkbl->mal', tiles, picked, precision=lax.Precision.HIGHEST)  13.8 us
    unnamed x1, blocking collectives  12.1 us
    gather x3, local copies, waits for them, and re-layouts, local(): picked = blocks[local_column]  6.09 us
  transfers between devices with their start and end apart: 3, of which 3 were waited for; matrix products, arithmetic and copies ran while one was open for 1% of the time, Pallas kernels for 0%

commit v1 on v0

v1 whole, which is shorter than its diff:
```python
import jax
import jax.numpy as jnp
from jax import lax
from jax.sharding import PartitionSpec as P

SEED_CLASSES = 128
ITERS = 3


SEED_WEIGHT = 2.0
PRIOR = 0.5


def sum_over(values, axes, count):
    spread = jnp.broadcast_to(values[None], (count,) + values.shape)
    return jnp.sum(lax.all_to_all(spread, axes, 0, 0, tiled=True), axis=0)


def scatter_sum(blocks, axis, count):
    if count > 4:
        return jnp.sum(lax.all_to_all(blocks, axis, 0, 0, tiled=True), axis=0)
    me = lax.axis_index(axis)
    total = lax.dynamic_index_in_dim(blocks, me, 0, keepdims=False)
    for shift in range(1, count):
        sent = lax.dynamic_index_in_dim(blocks, (me + shift) % count, 0, keepdims=False)
        pairs = [(i, (i + shift) % count) for i in range(count)]
        total = total + lax.ppermute(sent, axis, pairs)
    return total


def local(tiles, pattern, seed_label):
    groups = tiles.shape[0]
    tile = tiles.shape[2]
    own_rows = seed_label.shape[0]
    br_local = own_rows // tile
    n_wide = lax.axis_size("wide")
    n_all = n_wide * lax.axis_size("narrow")
    local_column = pattern // groups * br_local + pattern % br_local
    row_sums = jnp.sum(tiles, axis=(1, 3))
    degree = scatter_sum(row_sums.reshape(n_wide, own_rows), "wide", n_wide).reshape(own_rows)
    seeded = (seed_label[:, 0] < SEED_CLASSES).astype(jnp.float32)
    diag_column = (degree + SEED_WEIGHT * seeded + PRIOR)[:, None]

    def reduce_dots(values):
        return sum_over(values, ("wide", "narrow"), n_all)

    labels = seed_label[:, 0]
    rhs = SEED_WEIGHT * (
        labels[:, None] == jnp.arange(SEED_CLASSES, dtype=jnp.int32)[None, :]
    ).astype(jnp.float32)
    solution = jnp.zeros_like(rhs)
    residual = rhs
    direction = rhs
    norm_now = reduce_dots(jnp.sum(residual * residual, axis=0))
    for step in range(ITERS):
        gathered = lax.all_gather(direction, "narrow", axis=0, tiled=True)
        width = gathered.shape[1]
        blocks = gathered.reshape(-1, tile, width)
        picked = blocks[local_column]
        result = jnp.einsum("mkab,mkbl->mal", tiles, picked, precision=lax.Precision.HIGHEST)
        image = diag_column * direction - scatter_sum(
            result.reshape(n_wide, own_rows, width), "wide", n_wide
        )
        curvature = reduce_dots(jnp.sum(direction * image, axis=0))
        alpha = norm_now / curvature
        solution = solution + alpha * direction
        residual = residual - alpha * image
        norm_next = reduce_dots(jnp.sum(residual * residual, axis=0))
        direction = residual + norm_next / norm_now * direction
        norm_now = norm_next
    return (solution, residual)


def solution(mesh):
    placed = (
        P(("vol", "narrow"), "wide", None, None),
        P(("vol", "narrow"), "wide"),
        P(("vol", "narrow", "wide"), None),
    )
    return jax.shard_map(
        local,
        mesh=mesh,
        in_specs=placed,
        out_specs=(P(("vol", "narrow", "wide"), None), P(("vol", "narrow", "wide"), None)),
        check_vma=False,
    )
```

time: 265 us -> 134 us (0.51)
  blocking collectives: 178 us -> 64.3 us
  starting transfers between devices: 0.12 us -> 21.5 us
  waiting for transfers between devices: 41.3 us -> 24.5 us
  between operations: 13.8 us -> 0.8 us
  other arithmetic: 9.74 us -> 3.49 us
    psum x5 -> x0, blocking collectives: 147 us -> none  [reduce_dots(): return lax.psum((values[0],), ('wide', 'narrow'))]
    all_to_all x0 -> x5, blocking collectives: none -> 47 us  [sum_over(): return jnp.sum(lax.all_to_all(spread, axes, 0, 0, tiled=True), axis=0)]
    reduce_scatter x3 -> x0, waiting for transfers between devices: 41.2 us -> none  [local(): lax.psum_scatter(result.reshape(number * tile, width), 'wide', scatter_di...]
    ppermute x0 -> x12, waiting for transfers between devices: none -> 18.3 us  [scatter_sum(): total = total + lax.ppermute(sent, axis, pairs)]
    ppermute x0 -> x12, starting transfers between devices: none -> 18 us  [scatter_sum(): total = total + lax.ppermute(sent, axis, pairs)]
    unnamed x1 -> x0, blocking collectives: 12.1 us -> none
    all_to_all x0 -> x1, waiting for transfers between devices: none -> 6.27 us  [sum_over(): return jnp.sum(lax.all_to_all(spread, axes, 0, 0, tiled=True), axis=0)]
    reduce_sum x5 -> x11, other arithmetic: 4.78 us -> 0.66 us  [the longest x3 0.34 us: local(): curvature = reduce_dots(jnp.sum(direction * image, axis=0))]
  transfers between devices with their start and end apart: 3 -> 13, of which waited for: 3 -> 8; matrix products, arithmetic and copies ran while one was open for 1% -> 5% of each run, Pallas kernels for 0% -> 0%
where the time goes in v1:
time: 134 us; the launch traced here: 133 us
  blocking collectives  64.3 us (48%)
  waiting for transfers between devices  24.5 us (18%)
  starting transfers between devices  21.5 us (16%)
  matrix products  11.6 us (9%)
  local copies, waits for them, and re-layouts  6.92 us (5%)
  other arithmetic  3.49 us (3%)
    all_to_all x5, blocking collectives, sum_over(): return jnp.sum(lax.all_to_all(spread, axes, 0, 0, tiled=True), axis=0)  47 us
    ppermute x12, waiting for transfers between devices, scatter_sum(): total = total + lax.ppermute(sent, axis, pairs)  18.3 us
    ppermute x12, starting transfers between devices, scatter_sum(): total = total + lax.ppermute(sent, axis, pairs)  18 us
    all_gather x3, blocking collectives, local(): gathered = lax.all_gather(direction, 'narrow', axis=0, tiled=True)  17.4 us
    dot_general x3, matrix products, local(): jnp.einsum('mkab,mkbl->mal', tiles, picked, precision=lax.Precision.HIGHEST)  11.6 us
    all_to_all x1, waiting for transfers between devices, sum_over(): return jnp.sum(lax.all_to_all(spread, axes, 0, 0, tiled=True), axis=0)  6.27 us
    gather x3, local copies, waits for them, and re-layouts, local(): picked = blocks[local_column]  6.09 us
    all_to_all x1, starting transfers between devices, sum_over(): return jnp.sum(lax.all_to_all(spread, axes, 0, 0, tiled=True), axis=0)  3.47 us
  transfers between devices with their start and end apart: 13, of which 8 were waited for; matrix products, arithmetic and copies ran while one was open for 5% of the time, Pallas kernels for 0%

profile of v1, /device:TPU:0, one launch (start us, length us, event | category | flops | bytes accessed | tf_op | source)
XLA Modules:
  0.0 133.2 jit_solution(8746872193761540273)
XLA Ops:
  0.6 0.0 copy-start.2
  0.6 0.0 copy-start.1
  0.7 1.8 %reduce_sum.119 = f32[4,128]{1,0:T(4,128)S(1)} reduce(f32[4,8,128,128]{3,2,1,0:T(8,128)} %param.3, f32[]{:T(128)} %constant.110.clone.1), dimensions={1,3}, to_apply=%region_2.3 | reduce | flops 523776 | bytes 2099204 | tf_op jit(solution)/shard_map/reduce_sum | solution.py:39
  2.5 3.1 %collective-permute-start = (f32[128]{0:T(128)S(1)}, f32[128]{0:T(128)S(1)}, u32[]{:S(2)}, u32[]{:S(2)}) collective-permute-start(f32[128]{0:T(128)S(1)} %get-tuple-element.20), channel_id=1, source_target_pairs={{0,4},{4,8},{8,12},{12,0},{1,5},{5,9},{9,13},{13,1},{2,6},{6,10},{... | collective-permute-start | bytes 1544 | tf_op jit(solution)/shard_map/ppermute | solution.py:27
  5.6 2.1 %collective-permute-start.2 = (f32[128]{0:T(128)S(1)}, f32[128]{0:T(128)S(1)}, u32[]{:S(2)}, u32[]{:S(2)}) collective-permute-start(f32[128]{0:T(128)S(1)} %get-tuple-element.21), channel_id=1, source_target_pairs={{0,12},{4,0},{8,4},{12,8},{1,13},{5,1},{9,5},{13,9},{2,14},{6,2},{... | collective-permute-start | bytes 1544 | tf_op jit(solution)/shard_map/ppermute | solution.py:27
  7.6 0.9 collective-permute-start.1
  8.6 0.0 copy-done.2
  8.6 0.1 reshape.80
  8.7 0.0 copy-done.1
  8.7 0.1 fusion.14
  8.8 5.8 %all_gather.9 = f32[512,128]{1,0:T(8,128)S(1)} all-gather(f32[128,128]{1,0:T(8,128)S(1)} %fusion.14), channel_id=1, replica_groups=mesh['vol'=2,'wide'=4,'narrow'=4] {'narrow'}, dimensions={0}, use_global_device_ids=true | all-gather | bytes 327680 | tf_op jit(solution)/shard_map/all_gather | solution.py:56
  14.6 0.0 copy-start
  14.6 2.0 %gather_fusion = f32[32,128,128]{2,1,0:T(8,128)} fusion(f32[4,128,128]{2,1,0:T(8,128)S(1)} %bitcast.116, s32[1024]{0:T(1024)S(1)} %pad_clamp_fusion), kind=kCustom, calls=%fused_computation | custom fusion | bytes 4194432 | tf_op jit(solution)/shard_map/gather | solution.py:59
  16.6 0.0 copy-done
  16.6 3.9 %convolution_bitcast_fusion.2 = f32[4,128,128]{1,2,0:T(8,128)S(1)} fusion(f32[4,8,128,128]{3,2,1,0:T(8,128)} %bitcast.120, f32[4,8,128,128]{3,2,1,0:T(8,128)S(1)} %copy-done), kind=kOutput, calls=%fused_computation.5 | convolution fusion | flops 805306368 | bytes 4456448 | tf_op jit(solution)/shard_map/mkab,mkbl->mal/dot_general | solution.py:60
  20.5 1.6 %collective-permute-start.3 = (f32[128,128]{1,0:T(8,128)S(1)}, f32[128,128]{1,0:T(8,128)S(1)}, u32[]{:S(2)}, u32[]{:S(2)}) collective-permute-start(f32[128,128]{1,0:T(8,128)S(1)} %get-tuple-element.17), channel_id=1, source_target_pairs={{0,4},{4,8},{8,12},{12,0},{1,5},{5,9},{9,13},{13,1},{2,6},{6,10},{... | collective-permute-start | bytes 196616 | tf_op jit(solution)/shard_map/ppermute | solution.py:27
  22.2 2.2 %collective-permute-start.5 = (f32[128,128]{1,0:T(8,128)S(1)}, f32[128,128]{1,0:T(8,128)S(1)}, u32[]{:S(2)}, u32[]{:S(2)}) collective-permute-start(f32[128,128]{1,0:T(8,128)S(1)} %get-tuple-element.18), channel_id=1, source_target_pairs={{0,12},{4,0},{8,4},{12,8},{1,13},{5,1},{9,5},{13,9},{2,14},{6,2},{... | collective-permute-start | bytes 196616 | tf_op jit(solution)/shard_map/ppermute | solution.py:27
  24.4 0.0 collective-permute-done
  24.4 0.3 collective-permute-start.4
  24.7 0.0 collective-permute-done.2
  24.7 0.0 collective-permute-done.1
  24.7 2.6 %collective-permute-done.3 = f32[128,128]{1,0:T(8,128)S(1)} collective-permute-done((f32[128,128]{1,0:T(8,128)S(1)}, f32[128,128]{1,0:T(8,128)S(1)}, u32[]{:S(2)}, u32[]{:S(2)}) %collective-permute-start.3) | collective-permute-done | bytes 65568 | tf_op jit(solution)/shard_map/ppermute | solution.py:27
  27.3 0.3 collective-permute-done.5
  27.6 3.3 %collective-permute-done.4 = f32[128,128]{1,0:T(8,128)S(1)} collective-permute-done((f32[128,128]{1,0:T(8,128)S(1)}, f32[128,128]{1,0:T(8,128)S(1)}, u32[]{:S(2)}, u32[]{:S(2)}) %collective-permute-start.4) | collective-permute-done | bytes 65568 | tf_op jit(solution)/shard_map/ppermute | solution.py:27
  30.9 0.1 fusion.2
  31.1 10.0 %all_to_all.36 = f32[16,1,128]{2,1,0:T(1,128)S(1)} all-to-all(f32[16,1,128]{2,1,0:T(1,128)S(1)} %broadcast_in_dim.14), channel_id=1, replica_groups=mesh['vol'=2,'wide'=4,'narrow'=4] {'wide','narrow'}, dimensions={0} | all-to-all | bytes 16384 | tf_op jit(solution)/shard_map/all_to_all | solution.py:16
  41.0 0.6 broadcast_in_dim.16
  41.6 3.5 %all-to-all-start.1 = ((f32[16,1,128]{2,1,0:T(1,128)}), f32[16,1,128]{2,1,0:T(1,128)S(1)}, u32[]{:S(2)}, u32[]{:S(2)}) async-start(f32[16,1,128]{2,1,0:T(1,128)} %broadcast_in_dim.16), calls=%async_computation.1 | async-start | bytes 16384 | tf_op jit(solution)/shard_map/all_to_all | solution.py:16
  45.1 6.3 %all-to-all-done.1 = f32[16,1,128]{2,1,0:T(1,128)S(1)} async-done(((f32[16,1,128]{2,1,0:T(1,128)}), f32[16,1,128]{2,1,0:T(1,128)S(1)}, u32[]{:S(2)}, u32[]{:S(2)}) %all-to-all-start.1) | async-done | bytes 8224 | tf_op jit(solution)/shard_map/all_to_all | solution.py:16
  51.4 0.1 multiply_reduce_fusion.3
  51.6 9.0 %all_to_all.37 = f32[16,1,128]{2,1,0:T(1,128)S(1)} all-to-all(f32[16,1,128]{2,1,0:T(1,128)S(1)} %broadcast_in_dim.17), channel_id=1, replica_groups=mesh['vol'=2,'wide'=4,'narrow'=4] {'wide','narrow'}, dimensions={0} | all-to-all | bytes 16384 | tf_op jit(solution)/shard_map/all_to_all | solution.py:16
  60.6 0.1 fusion.5
  60.7 5.8 %all_gather.10 = f32[512,128]{1,0:T(8,128)S(1)} all-gather(f32[128,128]{1,0:T(8,128)S(1)} %fusion.5), channel_id=1, replica_groups=mesh['vol'=2,'wide'=4,'narrow'=4] {'narrow'}, dimensions={0}, use_global_device_ids=true | all-gather | bytes 327680 | tf_op jit(solution)/shard_map/all_gather | solution.py:56
  66.4 2.0 %gather_fusion.1 = f32[32,128,128]{2,1,0:T(8,128)} fusion(f32[4,128,128]{2,1,0:T(8,128)S(1)} %bitcast.117, s32[1024]{0:T(1024)S(1)} %pad_clamp_fusion), kind=kCustom, calls=%fused_computation.1 | custom fusion | bytes 4194432 | tf_op jit(solution)/shard_map/gather | solution.py:59
  68.5 3.9 %convolution_bitcast_fusion.1 = f32[4,128,128]{1,2,0:T(8,128)S(1)} fusion(f32[4,8,128,128]{3,2,1,0:T(8,128)} %bitcast.121, f32[4,8,128,128]{3,2,1,0:T(8,128)S(1)} %copy-done), kind=kOutput, calls=%fused_computation.4 | convolution fusion | flops 805306368 | bytes 4456448 | tf_op jit(solution)/shard_map/mkab,mkbl->mal/dot_general | solution.py:60
  72.4 0.6 collective-permute-start.6
  72.9 3.3 %collective-permute-start.8 = (f32[128,128]{1,0:T(8,128)S(1)}, f32[128,128]{1,0:T(8,128)S(1)}, u32[]{:S(2)}, u32[]{:S(2)}) collective-permute-start(f32[128,128]{1,0:T(8,128)S(1)} %get-tuple-element.15), channel_id=1, source_target_pairs={{0,12},{4,0},{8,4},{12,8},{1,13},{5,1},{9,5},{13,9},{2,14},{6,2},{... | collective-permute-start | bytes 196616 | tf_op jit(solution)/shard_map/ppermute | solution.py:27
  76.3 0.0 collective-permute-start.7
  76.3 2.9 %collective-permute-done.6 = f32[128,128]{1,0:T(8,128)S(1)} collective-permute-done((f32[128,128]{1,0:T(8,128)S(1)}, f32[128,128]{1,0:T(8,128)S(1)}, u32[]{:S(2)}, u32[]{:S(2)}) %collective-permute-start.6) | collective-permute-done | bytes 65568 | tf_op jit(solution)/shard_map/ppermute | solution.py:27
  79.1 0.0 collective-permute-done.8
  79.1 3.1 %collective-permute-done.7 = f32[128,128]{1,0:T(8,128)S(1)} collective-permute-done((f32[128,128]{1,0:T(8,128)S(1)}, f32[128,128]{1,0:T(8,128)S(1)}, u32[]{:S(2)}, u32[]{:S(2)}) %collective-permute-start.7) | collective-permute-done | bytes 65568 | tf_op jit(solution)/shard_map/ppermute | solution.py:27
  82.3 0.1 multiply_reduce_fusion.2
  82.4 9.5 %all_to_all.38 = f32[16,1,128]{2,1,0:T(1,128)S(1)} all-to-all(f32[16,1,128]{2,1,0:T(1,128)S(1)} %broadcast_in_dim.18), channel_id=1, replica_groups=mesh['vol'=2,'wide'=4,'narrow'=4] {'wide','narrow'}, dimensions={0} | all-to-all | bytes 16384 | tf_op jit(solution)/shard_map/all_to_all | solution.py:16
  92.0 0.1 multiply_reduce_fusion.1
  92.1 9.0 %all_to_all.39 = f32[16,1,128]{2,1,0:T(1,128)S(1)} all-to-all(f32[16,1,128]{2,1,0:T(1,128)S(1)} %broadcast_in_dim.19), channel_id=1, replica_groups=mesh['vol'=2,'wide'=4,'narrow'=4] {'wide','narrow'}, dimensions={0} | all-to-all | bytes 16384 | tf_op jit(solution)/shard_map/all_to_all | solution.py:16
  101.1 0.1 multiply_add_fusion
  101.2 5.8 %all_gather.11 = f32[512,128]{1,0:T(8,128)S(1)} all-gather(f32[128,128]{1,0:T(8,128)S(1)} %multiply_add_fusion), channel_id=1, replica_groups=mesh['vol'=2,'wide'=4,'narrow'=4] {'narrow'}, dimensions={0}, use_global_device_ids=true | all-gather | bytes 327680 | tf_op jit(solution)/shard_map/all_gather | solution.py:56
  107.0 2.0 %gather_fusion.2 = f32[32,128,128]{2,1,0:T(8,128)} fusion(f32[4,128,128]{2,1,0:T(8,128)S(1)} %bitcast.118, s32[1024]{0:T(1024)S(1)} %pad_clamp_fusion), kind=kCustom, calls=%fused_computation.2 | custom fusion | bytes 4194432 | tf_op jit(solution)/shard_map/gather | solution.py:59
  109.0 3.9 %convolution_bitcast_fusion = f32[4,128,128]{1,2,0:T(8,128)S(1)} fusion(f32[4,8,128,128]{3,2,1,0:T(8,128)} %bitcast.119, f32[4,8,128,128]{3,2,1,0:T(8,128)S(1)} %copy-done), kind=kOutput, calls=%fused_computation.3 | convolution fusion | flops 805306368 | bytes 4456448 | tf_op jit(solution)/shard_map/mkab,mkbl->mal/dot_general | solution.py:60
  112.9 0.6 collective-permute-start.9
  113.5 3.3 %collective-permute-start.11 = (f32[128,128]{1,0:T(8,128)S(1)}, f32[128,128]{1,0:T(8,128)S(1)}, u32[]{:S(2)}, u32[]{:S(2)}) collective-permute-start(f32[128,128]{1,0:T(8,128)S(1)} %get-tuple-element.12), channel_id=1, source_target_pairs={{0,12},{4,0},{8,4},{12,8},{1,13},{5,1},{9,5},{13,9},{2,14},{6,2},{... | collective-permute-start | bytes 196616 | tf_op jit(solution)/shard_map/ppermute | solution.py:27
  116.8 0.0 collective-permute-start.10
  116.8 2.9 %collective-permute-done.9 = f32[128,128]{1,0:T(8,128)S(1)} collective-permute-done((f32[128,128]{1,0:T(8,128)S(1)}, f32[128,128]{1,0:T(8,128)S(1)}, u32[]{:S(2)}, u32[]{:S(2)}) %collective-permute-start.9) | collective-permute-done | bytes 65568 | tf_op jit(solution)/shard_map/ppermute | solution.py:27
  119.7 0.0 collective-permute-done.11
  119.7 3.1 %collective-permute-done.10 = f32[128,128]{1,0:T(8,128)S(1)} collective-permute-done((f32[128,128]{1,0:T(8,128)S(1)}, f32[128,128]{1,0:T(8,128)S(1)}, u32[]{:S(2)}, u32[]{:S(2)}) %collective-permute-start.10) | collective-permute-done | bytes 65568 | tf_op jit(solution)/shard_map/ppermute | solution.py:27
  122.8 0.1 multiply_reduce_fusion
  122.9 9.5 %all_to_all.40 = f32[16,1,128]{2,1,0:T(1,128)S(1)} all-to-all(f32[16,1,128]{2,1,0:T(1,128)S(1)} %broadcast_in_dim.20), channel_id=1, replica_groups=mesh['vol'=2,'wide'=4,'narrow'=4] {'wide','narrow'}, dimensions={0} | all-to-all | bytes 16384 | tf_op jit(solution)/shard_map/all_to_all | solution.py:16
  132.5 0.7 multiply_subtract_fusion
  (23 shorter events, 0.3 us)
Async XLA Ops:
  0.6 8.0 %copy-start.2 = (s32[4,8]{1,0:T(4,128)S(1)}, s32[4,8]{1,0:T(4,128)}, u32[]{:S(2)}) copy-start(s32[4,8]{1,0:T(4,128)} %param.4) | copy-start | bytes 388
  0.6 8.1 %copy-start.1 = (s32[128,1]{0,1:T(1,128)S(1)}, s32[128,1]{0,1:T(1,128)}, u32[]{:S(2)}) copy-start(s32[128,1]{0,1:T(1,128)} %param.5) | copy-start | bytes 1540
  2.5 21.9 %collective-permute-start = (f32[128]{0:T(128)S(1)}, f32[128]{0:T(128)S(1)}, u32[]{:S(2)}, u32[]{:S(2)}) collective-permute-start(f32[128]{0:T(128)S(1)} %get-tuple-element.20), channel_id=1, source_target_pairs={{0,4},{4,8},{8,12},{12,0},{1,5},{5,9},{9,13},{13,1},{2,6},{6,10},{... | collective-permute-start | bytes 1544 | tf_op jit(solution)/shard_map/ppermute | solution.py:27
  5.6 19.2 %collective-permute-start.2 = (f32[128]{0:T(128)S(1)}, f32[128]{0:T(128)S(1)}, u32[]{:S(2)}, u32[]{:S(2)}) collective-permute-start(f32[128]{0:T(128)S(1)} %get-tuple-element.21), channel_id=1, source_target_pairs={{0,12},{4,0},{8,4},{12,8},{1,13},{5,1},{9,5},{13,9},{2,14},{6,2},{... | collective-permute-start | bytes 1544 | tf_op jit(solution)/shard_map/ppermute | solution.py:27
  7.6 17.1 %collective-permute-start.1 = (f32[128]{0:T(128)S(1)}, f32[128]{0:T(128)S(1)}, u32[]{:S(2)}, u32[]{:S(2)}) collective-permute-start(f32[128]{0:T(128)S(1)} %get-tuple-element.22), channel_id=1, source_target_pairs={{0,8},{4,12},{8,0},{12,4},{1,9},{5,13},{9,1},{13,5},{2,10},{6,14},... | collective-permute-start | bytes 1544 | tf_op jit(solution)/shard_map/ppermute | solution.py:27
  14.6 2.0 %copy-start = (f32[4,8,128,128]{3,2,1,0:T(8,128)S(1)}, f32[4,8,128,128]{3,2,1,0:T(8,128)}, u32[]{:S(2)}) copy-start(f32[4,8,128,128]{3,2,1,0:T(8,128)} %param.3) | copy-start | bytes 6291460
  20.5 6.8 %collective-permute-start.3 = (f32[128,128]{1,0:T(8,128)S(1)}, f32[128,128]{1,0:T(8,128)S(1)}, u32[]{:S(2)}, u32[]{:S(2)}) collective-permute-start(f32[128,128]{1,0:T(8,128)S(1)} %get-tuple-element.17), channel_id=1, source_target_pairs={{0,4},{4,8},{8,12},{12,0},{1,5},{5,9},{9,13},{13,1},{2,6},{6,10},{... | collective-permute-start | bytes 196616 | tf_op jit(solution)/shard_map/ppermute | solution.py:27
  22.2 5.5 %collective-permute-start.5 = (f32[128,128]{1,0:T(8,128)S(1)}, f32[128,128]{1,0:T(8,128)S(1)}, u32[]{:S(2)}, u32[]{:S(2)}) collective-permute-start(f32[128,128]{1,0:T(8,128)S(1)} %get-tuple-element.18), channel_id=1, source_target_pairs={{0,12},{4,0},{8,4},{12,8},{1,13},{5,1},{9,5},{13,9},{2,14},{6,2},{... | collective-permute-start | bytes 196616 | tf_op jit(solution)/shard_map/ppermute | solution.py:27
  24.4 6.5 %collective-permute-start.4 = (f32[128,128]{1,0:T(8,128)S(1)}, f32[128,128]{1,0:T(8,128)S(1)}, u32[]{:S(2)}, u32[]{:S(2)}) collective-permute-start(f32[128,128]{1,0:T(8,128)S(1)} %get-tuple-element.19), channel_id=1, source_target_pairs={{0,8},{4,12},{8,0},{12,4},{1,9},{5,13},{9,1},{13,5},{2,10},{6,14},... | collective-permute-start | bytes 196616 | tf_op jit(solution)/shard_map/ppermute | solution.py:27
  41.6 9.8 %all-to-all-start.1 = ((f32[16,1,128]{2,1,0:T(1,128)}), f32[16,1,128]{2,1,0:T(1,128)S(1)}, u32[]{:S(2)}, u32[]{:S(2)}) async-start(f32[16,1,128]{2,1,0:T(1,128)} %broadcast_in_dim.16), calls=%async_computation.1 | async-start | bytes 16384 | tf_op jit(solution)/shard_map/all_to_all | solution.py:16
  72.4 6.8 %collective-permute-start.6 = (f32[128,128]{1,0:T(8,128)S(1)}, f32[128,128]{1,0:T(8,128)S(1)}, u32[]{:S(2)}, u32[]{:S(2)}) collective-permute-start(f32[128,128]{1,0:T(8,128)S(1)} %get-tuple-element.14), channel_id=1, source_target_pairs={{0,4},{4,8},{8,12},{12,0},{1,5},{5,9},{9,13},{13,1},{2,6},{6,10},{... | collective-permute-start | bytes 196616 | tf_op jit(solution)/shard_map/ppermute | solution.py:27
  72.9 6.2 %collective-permute-start.8 = (f32[128,128]{1,0:T(8,128)S(1)}, f32[128,128]{1,0:T(8,128)S(1)}, u32[]{:S(2)}, u32[]{:S(2)}) collective-permute-start(f32[128,128]{1,0:T(8,128)S(1)} %get-tuple-element.15), channel_id=1, source_target_pairs={{0,12},{4,0},{8,4},{12,8},{1,13},{5,1},{9,5},{13,9},{2,14},{6,2},{... | collective-permute-start | bytes 196616 | tf_op jit(solution)/shard_map/ppermute | solution.py:27
  76.3 6.0 %collective-permute-start.7 = (f32[128,128]{1,0:T(8,128)S(1)}, f32[128,128]{1,0:T(8,128)S(1)}, u32[]{:S(2)}, u32[]{:S(2)}) collective-permute-start(f32[128,128]{1,0:T(8,128)S(1)} %get-tuple-element.16), channel_id=1, source_target_pairs={{0,8},{4,12},{8,0},{12,4},{1,9},{5,13},{9,1},{13,5},{2,10},{6,14},... | collective-permute-start | bytes 196616 | tf_op jit(solution)/shard_map/ppermute | solution.py:27
  112.9 6.8 %collective-permute-start.9 = (f32[128,128]{1,0:T(8,128)S(1)}, f32[128,128]{1,0:T(8,128)S(1)}, u32[]{:S(2)}, u32[]{:S(2)}) collective-permute-start(f32[128,128]{1,0:T(8,128)S(1)} %get-tuple-element.11), channel_id=1, source_target_pairs={{0,4},{4,8},{8,12},{12,0},{1,5},{5,9},{9,13},{13,1},{2,6},{6,10},{... | collective-permute-start | bytes 196616 | tf_op jit(solution)/shard_map/ppermute | solution.py:27
  113.5 6.2 %collective-permute-start.11 = (f32[128,128]{1,0:T(8,128)S(1)}, f32[128,128]{1,0:T(8,128)S(1)}, u32[]{:S(2)}, u32[]{:S(2)}) collective-permute-start(f32[128,128]{1,0:T(8,128)S(1)} %get-tuple-element.12), channel_id=1, source_target_pairs={{0,12},{4,0},{8,4},{12,8},{1,13},{5,1},{9,5},{13,9},{2,14},{6,2},{... | collective-permute-start | bytes 196616 | tf_op jit(solution)/shard_map/ppermute | solution.py:27
  116.8 6.0 %collective-permute-start.10 = (f32[128,128]{1,0:T(8,128)S(1)}, f32[128,128]{1,0:T(8,128)S(1)}, u32[]{:S(2)}, u32[]{:S(2)}) collective-permute-start(f32[128,128]{1,0:T(8,128)S(1)} %get-tuple-element.13), channel_id=1, source_target_pairs={{0,8},{4,12},{8,0},{12,4},{1,9},{5,13},{9,1},{13,5},{2,10},{6,14},... | collective-permute-start | bytes 196616 | tf_op jit(solution)/shard_map/ppermute | solution.py:27

commit v2 on v1

--- a/solution.py
+++ b/solution.py
@@ -28,18 +28,44 @@
     return total
 
 
+def gather_blocks(values, axis, count):
+    if count > 4:
+        return lax.all_gather(values, axis, axis=0, tiled=False)
+    parts = [values]
+    for shift in range(1, count):
+        pairs = [(i, (i + shift) % count) for i in range(count)]
+        parts.append(lax.ppermute(values, axis, pairs))
+    return jnp.stack(parts)
+
+
 def local(tiles, pattern, seed_label):
     groups = tiles.shape[0]
     tile = tiles.shape[2]
     own_rows = seed_label.shape[0]
     br_local = own_rows // tile
     n_wide = lax.axis_size("wide")
-    n_all = n_wide * lax.axis_size("narrow")
+    n_narrow = lax.axis_size("narrow")
+    n_all = n_wide * n_narrow
+    width = SEED_CLASSES
     local_column = pattern // groups * br_local + pattern % br_local
+    if n_narrow > 4:
+        source = local_column
+    else:
+        source = (lax.axis_index("narrow") - local_column) % n_narrow
+    pick = source[:, :, None] == jnp.arange(n_narrow, dtype=source.dtype)[None, None, :]
+    dense = jnp.sum(
+        jnp.where(pick[:, :, None, :, None], tiles[:, :, :, None, :], 0.0), axis=1
+    ).reshape(groups * tile, n_narrow * own_rows)
+
     row_sums = jnp.sum(tiles, axis=(1, 3))
     degree = scatter_sum(row_sums.reshape(n_wide, own_rows), "wide", n_wide).reshape(own_rows)
     seeded = (seed_label[:, 0] < SEED_CLASSES).astype(jnp.float32)
     diag_column = (degree + SEED_WEIGHT * seeded + PRIOR)[:, None]
+
+    def product(values):
+        gathered = gather_blocks(values, "narrow", n_narrow).reshape(n_narrow * own_rows, width)
+        partial = jnp.dot(dense, gathered, precision=lax.Precision.HIGHEST)
+        return scatter_sum(partial.reshape(n_wide, own_rows, width), "wide", n_wide)
 
     def reduce_dots(values):
         return sum_over(values, ("wide", "narrow"), n_all)
@@ -51,22 +77,26 @@
     solution = jnp.zeros_like(rhs)
     residual = rhs
     direction = rhs
-    norm_now = reduce_dots(jnp.sum(residual * residual, axis=0))
+    weighted = product(direction)
+    image = diag_column * direction - weighted
+    first = reduce_dots(
+        jnp.stack([jnp.sum(residual * residual, axis=0), jnp.sum(direction * image, axis=0)])
+    )
+    norm_now = first[0]
+    curvature = first[1]
     for step in range(ITERS):
-        gathered = lax.all_gather(direction, "narrow", axis=0, tiled=True)
-        width = gathered.shape[1]
-        blocks = gathered.reshape(-1, tile, width)
-        picked = blocks[local_column]
-        result = jnp.einsum("mkab,mkbl->mal", tiles, picked, precision=lax.Precision.HIGHEST)
-        image = diag_column * direction - scatter_sum(
-            result.reshape(n_wide, own_rows, width), "wide", n_wide
-        )
-        curvature = reduce_dots(jnp.sum(direction * image, axis=0))
         alpha = norm_now / curvature
         solution = solution + alpha * direction
         residual = residual - alpha * image
+        if step == ITERS - 1:
+            break
+        weighted_residual = product(residual)
         norm_next = reduce_dots(jnp.sum(residual * residual, axis=0))
-        direction = residual + norm_next / norm_now * direction
+        ratio = norm_next / norm_now
+        direction = residual + ratio * direction
+        weighted = weighted_residual + ratio * weighted
+        image = diag_column * direction - weighted
+        curvature = reduce_dots(jnp.sum(direction * image, axis=0))
         norm_now = norm_next
     return (solution, residual)
 

time: 134 us -> 96.6 us (0.72)
  blocking collectives: 64.3 us -> 48.4 us
  waiting for transfers between devices: 24.5 us -> 14.4 us
  matrix products: 11.6 us -> 2.96 us
  local copies, waits for them, and re-layouts: 6.92 us -> 0.14 us
  starting transfers between devices: 21.5 us -> 24.4 us
  other arithmetic: 3.49 us -> 5.12 us
    all_gather x3 -> x0, blocking collectives: 17.4 us -> none  [local(): gathered = lax.all_gather(direction, 'narrow', axis=0, tiled=True)]
    dot_general x3, matrix products: 11.6 us -> 2.96 us  [product(): partial = jnp.dot(dense, gathered, precision=lax.Precision.HIGHEST)]
    ppermute x12, waiting for transfers between devices: 18.3 us -> 10.1 us  [scatter_sum(): total = total + lax.ppermute(sent, axis, pairs)]
    ppermute x0 -> x9, starting transfers between devices: none -> 7.63 us  [gather_blocks(): parts.append(lax.ppermute(values, axis, pairs))]
    all_to_all x1 -> x0, waiting for transfers between devices: 6.27 us -> none  [sum_over(): return jnp.sum(lax.all_to_all(spread, axes, 0, 0, tiled=True), axis=0)]
    gather x3 -> x0, local copies, waits for them, and re-layouts: 6.09 us -> none  [local(): picked = blocks[local_column]]
    ppermute x0 -> x9, waiting for transfers between devices: none -> 4.36 us  [gather_blocks(): parts.append(lax.ppermute(values, axis, pairs))]
    all_to_all x1 -> x0, starting transfers between devices: 3.47 us -> none  [sum_over(): return jnp.sum(lax.all_to_all(spread, axes, 0, 0, tiled=True), axis=0)]
  transfers between devices with their start and end apart: 13 -> 21, of which waited for: 8 -> 8; matrix products, arithmetic and copies ran while one was open for 5% -> 4% of each run, Pallas kernels for 0% -> 0%
where the time goes in v2:
time: 96.6 us; the launch traced here: 96.3 us
  blocking collectives  48.4 us (50%)
  starting transfers between devices  24.4 us (25%)
  waiting for transfers between devices  14.4 us (15%)
  other arithmetic  5.12 us (5%)
  matrix products  2.96 us (3%)
    all_to_all x5, blocking collectives, sum_over(): return jnp.sum(lax.all_to_all(spread, axes, 0, 0, tiled=True), axis=0)  48.4 us
    ppermute x12, starting transfers between devices, scatter_sum(): total = total + lax.ppermute(sent, axis, pairs)  16.7 us
    ppermute x12, waiting for transfers between devices, scatter_sum(): total = total + lax.ppermute(sent, axis, pairs)  10.1 us
    ppermute x9, starting transfers between devices, gather_blocks(): parts.append(lax.ppermute(values, axis, pairs))  7.63 us
    ppermute x9, waiting for transfers between devices, gather_blocks(): parts.append(lax.ppermute(values, axis, pairs))  4.36 us
    dot_general x3, matrix products, product(): partial = jnp.dot(dense, gathered, precision=lax.Precision.HIGHEST)  2.96 us
  transfers between devices with their start and end apart: 21, of which 8 were waited for; matrix products, arithmetic and copies ran while one was open for 4% of the time, Pallas kernels for 0%

profile of v2, /device:TPU:0, one launch (start us, length us, event | category | flops | bytes accessed | tf_op | source)
XLA Modules:
  0.0 96.3 jit_solution(10477687918765718138)
XLA Ops:
  0.6 0.0 copy-start
  0.6 0.0 copy-start.2
  0.7 0.9 fusion.33
  1.5 0.5 collective-permute-start.3
  2.1 2.0 %collective-permute-start.5 = (f32[128,128]{1,0:T(8,128)S(1)}, f32[128,128]{1,0:T(8,128)S(1)}, u32[]{:S(2)}, u32[]{:S(2)}) collective-permute-start(f32[128,128]{1,0:T(8,128)S(1)} %fusion.33), channel_id=1, source_target_pairs={{0,3},{1,0},{2,1},{3,2},{4,7},{5,4},{6,5},{7,6},{8,11},{9,8},{10,9... | collective-permute-start | bytes 196616 | tf_op jit(solution)/shard_map/ppermute | solution.py:37
  4.0 2.2 %collective-permute-start.4 = (f32[128,128]{1,0:T(8,128)S(1)}, f32[128,128]{1,0:T(8,128)S(1)}, u32[]{:S(2)}, u32[]{:S(2)}) collective-permute-start(f32[128,128]{1,0:T(8,128)S(1)} %fusion.33), channel_id=1, source_target_pairs={{0,2},{1,3},{2,0},{3,1},{4,6},{5,7},{6,4},{7,5},{8,10},{9,11},{10,... | collective-permute-start | bytes 196616 | tf_op jit(solution)/shard_map/ppermute | solution.py:37
  6.3 1.8 %reduce_sum.120 = f32[4,128]{1,0:T(4,128)S(1)} reduce(f32[4,8,128,128]{3,2,1,0:T(8,128)} %param.3, f32[]{:T(128)} %constant.115.clone.1), dimensions={1,3}, to_apply=%region_1.2 | reduce | flops 523776 | bytes 2099204 | tf_op jit(solution)/shard_map/reduce_sum | solution.py:60
  8.1 1.6 %collective-permute-start = (f32[128]{0:T(128)S(1)}, f32[128]{0:T(128)S(1)}, u32[]{:S(2)}, u32[]{:S(2)}) collective-permute-start(f32[128]{0:T(128)S(1)} %get-tuple-element.24), channel_id=1, source_target_pairs={{0,4},{4,8},{8,12},{12,0},{1,5},{5,9},{9,13},{13,1},{2,6},{6,10},{... | collective-permute-start | bytes 1544 | tf_op jit(solution)/shard_map/ppermute | solution.py:27
  9.7 2.2 %collective-permute-start.2 = (f32[128]{0:T(128)S(1)}, f32[128]{0:T(128)S(1)}, u32[]{:S(2)}, u32[]{:S(2)}) collective-permute-start(f32[128]{0:T(128)S(1)} %get-tuple-element.25), channel_id=1, source_target_pairs={{0,12},{4,0},{8,4},{12,8},{1,13},{5,1},{9,5},{13,9},{2,14},{6,2},{... | collective-permute-start | bytes 1544 | tf_op jit(solution)/shard_map/ppermute | solution.py:27
  12.0 0.1 iota_compare_fusion.2
  12.1 0.0 copy-done
  12.1 0.8 select_reduce_fusion
  12.9 0.1 fusion.34
  13.0 0.0 collective-permute-done.3
  13.0 0.9 collective-permute-start.1
  13.8 0.0 collective-permute-done.5
  13.8 0.0 collective-permute-done.4
  13.8 1.0 %convolution_bitcast_fusion.2 = f32[4,128,128]{2,1,0:T(8,128)S(1)} fusion(f32[4,128,4,128]{3,1,2,0:T(8,128)S(1)} %select_reduce_fusion, f32[1,128,128]{2,1,0:T(8,128)S(1)} %bitcast.114, f32[1,128,128]{2,1,0:T(8,128)S(1)} %bitcast.115, f32[1,128,128]{2,1,0:T(8,128)S(1)} %bitcast.113, f32[1,128,128]{2,1,0:T(8,128)S(1)} %fusion.34), kind=kOutput, calls=%fused_computation.3 | convolution fusion | flops 402849792 | bytes 1572864 | tf_op jit(solution)/shard_map/dot_general | solution.py:67
  14.9 1.6 %collective-permute-start.6 = (f32[128,128]{1,0:T(8,128)S(1)}, f32[128,128]{1,0:T(8,128)S(1)}, u32[]{:S(2)}, u32[]{:S(2)}) collective-permute-start(f32[128,128]{1,0:T(8,128)S(1)} %get-tuple-element.19), channel_id=1, source_target_pairs={{0,4},{4,8},{8,12},{12,0},{1,5},{5,9},{9,13},{13,1},{2,6},{6,10},{... | collective-permute-start | bytes 196616 | tf_op jit(solution)/shard_map/ppermute | solution.py:27
  16.5 2.2 %collective-permute-start.8 = (f32[128,128]{1,0:T(8,128)S(1)}, f32[128,128]{1,0:T(8,128)S(1)}, u32[]{:S(2)}, u32[]{:S(2)}) collective-permute-start(f32[128,128]{1,0:T(8,128)S(1)} %get-tuple-element.20), channel_id=1, source_target_pairs={{0,12},{4,0},{8,4},{12,8},{1,13},{5,1},{9,5},{13,9},{2,14},{6,2},{... | collective-permute-start | bytes 196616 | tf_op jit(solution)/shard_map/ppermute | solution.py:27
  18.7 0.0 collective-permute-done
  18.7 0.3 collective-permute-start.7
  19.1 0.0 collective-permute-done.2
  19.1 0.0 collective-permute-done.1
  19.1 2.0 %collective-permute-done.6 = f32[128,128]{1,0:T(8,128)S(1)} collective-permute-done((f32[128,128]{1,0:T(8,128)S(1)}, f32[128,128]{1,0:T(8,128)S(1)}, u32[]{:S(2)}, u32[]{:S(2)}) %collective-permute-start.6) | collective-permute-done | bytes 65568 | tf_op jit(solution)/shard_map/ppermute | solution.py:27
  21.1 0.5 collective-permute-done.8
  21.6 2.3 %collective-permute-done.7 = f32[128,128]{1,0:T(8,128)S(1)} collective-permute-done((f32[128,128]{1,0:T(8,128)S(1)}, f32[128,128]{1,0:T(8,128)S(1)}, u32[]{:S(2)}, u32[]{:S(2)}) %collective-permute-start.7) | collective-permute-done | bytes 65568 | tf_op jit(solution)/shard_map/ppermute | solution.py:27
  23.9 0.1 fusion.18
  24.1 9.6 %all_to_all.29 = f32[16,2,128]{2,1,0:T(2,128)S(1)} all-to-all(f32[16,2,128]{2,1,0:T(2,128)S(1)} %broadcast_in_dim.33), channel_id=1, replica_groups=mesh['vol'=2,'wide'=4,'narrow'=4] {'wide','narrow'}, dimensions={0} | all-to-all | bytes 32768 | tf_op jit(solution)/shard_map/all_to_all | solution.py:16
  33.7 0.1 multiply_reduce_fusion.3
  33.8 0.2 collective-permute-start.11
  34.0 1.2 %collective-permute-start.10 = (f32[128,128]{1,0:T(8,128)S(1)}, f32[128,128]{1,0:T(8,128)S(1)}, u32[]{:S(2)}, u32[]{:S(2)}) collective-permute-start(f32[128,128]{1,0:T(8,128)S(1)} %get-tuple-element.11), channel_id=1, source_target_pairs={{0,2},{1,3},{2,0},{3,1},{4,6},{5,7},{6,4},{7,5},{8,10},{9,11},{10,... | collective-permute-start | bytes 196616 | tf_op jit(solution)/shard_map/ppermute | solution.py:37
  35.2 0.0 collective-permute-start.9
  35.2 9.6 %all_to_all.30 = f32[16,1,128]{2,1,0:T(1,128)S(1)} all-to-all(f32[16,1,128]{2,1,0:T(1,128)S(1)} %broadcast_in_dim.34), channel_id=1, replica_groups=mesh['vol'=2,'wide'=4,'narrow'=4] {'wide','narrow'}, dimensions={0} | all-to-all | bytes 16384 | tf_op jit(solution)/shard_map/all_to_all | solution.py:16
  44.9 0.0 collective-permute-done.11
  44.9 0.0 collective-permute-done.10
  44.9 0.0 collective-permute-done.9
  44.9 1.0 %convolution_bitcast_fusion.1 = f32[4,128,128]{2,1,0:T(8,128)S(1)} fusion(f32[4,128,4,128]{3,1,2,0:T(8,128)S(1)} %select_reduce_fusion, f32[1,128,128]{2,1,0:T(8,128)S(1)} %bitcast.116, f32[1,128,128]{2,1,0:T(8,128)S(1)} %bitcast.117, f32[1,128,128]{2,1,0:T(8,128)S(1)} %bitcast.118, f32[1,128,128]{2,1,0:T(8,128)S(1)} %bitcast.111), kind=kOutput, calls=%fused_computation.2 | convolution fusion | flops 402849792 | bytes 1572864 | tf_op jit(solution)/shard_map/dot_general | solution.py:67
  45.9 0.6 collective-permute-start.12
  46.5 3.3 %collective-permute-start.14 = (f32[128,128]{1,0:T(8,128)S(1)}, f32[128,128]{1,0:T(8,128)S(1)}, u32[]{:S(2)}, u32[]{:S(2)}) collective-permute-start(f32[128,128]{1,0:T(8,128)S(1)} %get-tuple-element.17), channel_id=1, source_target_pairs={{0,12},{4,0},{8,4},{12,8},{1,13},{5,1},{9,5},{13,9},{2,14},{6,2},{... | collective-permute-start | bytes 196616 | tf_op jit(solution)/shard_map/ppermute | solution.py:27
  49.8 0.0 collective-permute-start.13
  49.8 3.0 %collective-permute-done.12 = f32[128,128]{1,0:T(8,128)S(1)} collective-permute-done((f32[128,128]{1,0:T(8,128)S(1)}, f32[128,128]{1,0:T(8,128)S(1)}, u32[]{:S(2)}, u32[]{:S(2)}) %collective-permute-start.12) | collective-permute-done | bytes 65568 | tf_op jit(solution)/shard_map/ppermute | solution.py:27
  52.7 0.0 collective-permute-done.14
  52.7 2.3 %collective-permute-done.13 = f32[128,128]{1,0:T(8,128)S(1)} collective-permute-done((f32[128,128]{1,0:T(8,128)S(1)}, f32[128,128]{1,0:T(8,128)S(1)}, u32[]{:S(2)}, u32[]{:S(2)}) %collective-permute-start.13) | collective-permute-done | bytes 65568 | tf_op jit(solution)/shard_map/ppermute | solution.py:27
  55.0 0.1 multiply_reduce_fusion.2
  55.2 9.7 %all_to_all.31 = f32[16,1,128]{2,1,0:T(1,128)S(1)} all-to-all(f32[16,1,128]{2,1,0:T(1,128)S(1)} %broadcast_in_dim.35), channel_id=1, replica_groups=mesh['vol'=2,'wide'=4,'narrow'=4] {'wide','narrow'}, dimensions={0} | all-to-all | bytes 16384 | tf_op jit(solution)/shard_map/all_to_all | solution.py:16
  64.9 0.1 multiply_reduce_fusion.1
  65.1 0.1 collective-permute-start.17
  65.1 1.4 %collective-permute-start.16 = (f32[128,128]{1,0:T(8,128)S(1)}, f32[128,128]{1,0:T(8,128)S(1)}, u32[]{:S(2)}, u32[]{:S(2)}) collective-permute-start(f32[128,128]{1,0:T(8,128)S(1)} %get-tuple-element.7), channel_id=1, source_target_pairs={{0,2},{1,3},{2,0},{3,1},{4,6},{5,7},{6,4},{7,5},{8,10},{9,11},{10,... | collective-permute-start | bytes 196616 | tf_op jit(solution)/shard_map/ppermute | solution.py:37
  66.5 0.0 collective-permute-start.15
  66.5 1.0 %collective-permute-done.17 = f32[128,128]{1,0:T(8,128)S(1)} collective-permute-done((f32[128,128]{1,0:T(8,128)S(1)}, f32[128,128]{1,0:T(8,128)S(1)}, u32[]{:S(2)}, u32[]{:S(2)}) %collective-permute-start.17) | collective-permute-done | bytes 65568 | tf_op jit(solution)/shard_map/ppermute | solution.py:37
  67.6 3.2 %collective-permute-done.16 = f32[128,128]{1,0:T(8,128)S(1)} collective-permute-done((f32[128,128]{1,0:T(8,128)S(1)}, f32[128,128]{1,0:T(8,128)S(1)}, u32[]{:S(2)}, u32[]{:S(2)}) %collective-permute-start.16) | collective-permute-done | bytes 65568 | tf_op jit(solution)/shard_map/ppermute | solution.py:37
  70.7 0.2 collective-permute-done.15
  70.9 1.0 %convolution_bitcast_fusion = f32[4,128,128]{2,1,0:T(8,128)S(1)} fusion(f32[4,128,4,128]{3,1,2,0:T(8,128)S(1)} %select_reduce_fusion, f32[1,128,128]{2,1,0:T(8,128)S(1)} %bitcast.119, f32[1,128,128]{2,1,0:T(8,128)S(1)} %bitcast.120, f32[1,128,128]{2,1,0:T(8,128)S(1)} %bitcast.121, f32[1,128,128]{2,1,0:T(8,128)S(1)} %bitcast.112), kind=kOutput, calls=%fused_computation.1 | convolution fusion | flops 402849792 | bytes 1572864 | tf_op jit(solution)/shard_map/dot_general | solution.py:67
  71.9 0.6 collective-permute-start.18
  72.5 3.3 %collective-permute-start.20 = (f32[128,128]{1,0:T(8,128)S(1)}, f32[128,128]{1,0:T(8,128)S(1)}, u32[]{:S(2)}, u32[]{:S(2)}) collective-permute-start(f32[128,128]{1,0:T(8,128)S(1)} %get-tuple-element.14), channel_id=1, source_target_pairs={{0,12},{4,0},{8,4},{12,8},{1,13},{5,1},{9,5},{13,9},{2,14},{6,2},{... | collective-permute-start | bytes 196616 | tf_op jit(solution)/shard_map/ppermute | solution.py:27
  75.8 0.0 collective-permute-start.19
  75.8 10.5 %all_to_all.32 = f32[16,1,128]{2,1,0:T(1,128)S(1)} all-to-all(f32[16,1,128]{2,1,0:T(1,128)S(1)} %broadcast_in_dim.36), channel_id=1, replica_groups=mesh['vol'=2,'wide'=4,'narrow'=4] {'wide','narrow'}, dimensions={0} | all-to-all | bytes 16384 | tf_op jit(solution)/shard_map/all_to_all | solution.py:16
  86.4 0.0 collective-permute-done.18
  86.4 0.0 collective-permute-done.20
  86.4 0.0 collective-permute-done.19
  86.4 0.1 multiply_reduce_fusion
  86.5 9.0 %all_to_all.33 = f32[16,1,128]{2,1,0:T(1,128)S(1)} all-to-all(f32[16,1,128]{2,1,0:T(1,128)S(1)} %broadcast_in_dim.37), channel_id=1, replica_groups=mesh['vol'=2,'wide'=4,'narrow'=4] {'wide','narrow'}, dimensions={0} | all-to-all | bytes 16384 | tf_op jit(solution)/shard_map/all_to_all | solution.py:16
  95.5 0.7 multiply_subtract_fusion
  (25 shorter events, 0.3 us)
Async XLA Ops:
  0.6 11.4 %copy-start = (f32[4,8,128,128]{3,2,1,0:T(8,128)S(1)}, f32[4,8,128,128]{3,2,1,0:T(8,128)}, u32[]{:S(2)}) copy-start(f32[4,8,128,128]{3,2,1,0:T(8,128)} %param.3) | copy-start | bytes 6291460
  0.6 11.3 %copy-start.2 = (s32[4,8]{1,0:T(4,128)S(1)}, s32[4,8]{1,0:T(4,128)}, u32[]{:S(2)}) copy-start(s32[4,8]{1,0:T(4,128)} %param.4) | copy-start | bytes 388
  1.5 11.4 %collective-permute-start.3 = (f32[128,128]{1,0:T(8,128)S(1)}, f32[128,128]{1,0:T(8,128)S(1)}, u32[]{:S(2)}, u32[]{:S(2)}) collective-permute-start(f32[128,128]{1,0:T(8,128)S(1)} %fusion.33), channel_id=1, source_target_pairs={{0,1},{1,2},{2,3},{3,0},{4,5},{5,6},{6,7},{7,4},{8,9},{9,10},{10,1... | collective-permute-start | bytes 196616 | tf_op jit(solution)/shard_map/ppermute | solution.py:37
  2.1 11.8 %collective-permute-start.5 = (f32[128,128]{1,0:T(8,128)S(1)}, f32[128,128]{1,0:T(8,128)S(1)}, u32[]{:S(2)}, u32[]{:S(2)}) collective-permute-start(f32[128,128]{1,0:T(8,128)S(1)} %fusion.33), channel_id=1, source_target_pairs={{0,3},{1,0},{2,1},{3,2},{4,7},{5,4},{6,5},{7,6},{8,11},{9,8},{10,9... | collective-permute-start | bytes 196616 | tf_op jit(solution)/shard_map/ppermute | solution.py:37
  4.0 9.8 %collective-permute-start.4 = (f32[128,128]{1,0:T(8,128)S(1)}, f32[128,128]{1,0:T(8,128)S(1)}, u32[]{:S(2)}, u32[]{:S(2)}) collective-permute-start(f32[128,128]{1,0:T(8,128)S(1)} %fusion.33), channel_id=1, source_target_pairs={{0,2},{1,3},{2,0},{3,1},{4,6},{5,7},{6,4},{7,5},{8,10},{9,11},{10,... | collective-permute-start | bytes 196616 | tf_op jit(solution)/shard_map/ppermute | solution.py:37
  8.1 4.8 %copy-start.1 = (s32[128,1]{0,1:T(1,128)S(1)}, s32[128,1]{0,1:T(1,128)}, u32[]{:S(2)}) copy-start(s32[128,1]{0,1:T(1,128)} %param.5) | copy-start | bytes 1540
  8.1 10.7 %collective-permute-start = (f32[128]{0:T(128)S(1)}, f32[128]{0:T(128)S(1)}, u32[]{:S(2)}, u32[]{:S(2)}) collective-permute-start(f32[128]{0:T(128)S(1)} %get-tuple-element.24), channel_id=1, source_target_pairs={{0,4},{4,8},{8,12},{12,0},{1,5},{5,9},{9,13},{13,1},{2,6},{6,10},{... | collective-permute-start | bytes 1544 | tf_op jit(solution)/shard_map/ppermute | solution.py:27
  9.7 9.4 %collective-permute-start.2 = (f32[128]{0:T(128)S(1)}, f32[128]{0:T(128)S(1)}, u32[]{:S(2)}, u32[]{:S(2)}) collective-permute-start(f32[128]{0:T(128)S(1)} %get-tuple-element.25), channel_id=1, source_target_pairs={{0,12},{4,0},{8,4},{12,8},{1,13},{5,1},{9,5},{13,9},{2,14},{6,2},{... | collective-permute-start | bytes 1544 | tf_op jit(solution)/shard_map/ppermute | solution.py:27
  13.0 6.1 %collective-permute-start.1 = (f32[128]{0:T(128)S(1)}, f32[128]{0:T(128)S(1)}, u32[]{:S(2)}, u32[]{:S(2)}) collective-permute-start(f32[128]{0:T(128)S(1)} %get-tuple-element.26), channel_id=1, source_target_pairs={{0,8},{4,12},{8,0},{12,4},{1,9},{5,13},{9,1},{13,5},{2,10},{6,14},... | collective-permute-start | bytes 1544 | tf_op jit(solution)/shard_map/ppermute | solution.py:27
  14.9 6.2 %collective-permute-start.6 = (f32[128,128]{1,0:T(8,128)S(1)}, f32[128,128]{1,0:T(8,128)S(1)}, u32[]{:S(2)}, u32[]{:S(2)}) collective-permute-start(f32[128,128]{1,0:T(8,128)S(1)} %get-tuple-element.19), channel_id=1, source_target_pairs={{0,4},{4,8},{8,12},{12,0},{1,5},{5,9},{9,13},{13,1},{2,6},{6,10},{... | collective-permute-start | bytes 196616 | tf_op jit(solution)/shard_map/ppermute | solution.py:27
  16.5 5.1 %collective-permute-start.8 = (f32[128,128]{1,0:T(8,128)S(1)}, f32[128,128]{1,0:T(8,128)S(1)}, u32[]{:S(2)}, u32[]{:S(2)}) collective-permute-start(f32[128,128]{1,0:T(8,128)S(1)} %get-tuple-element.20), channel_id=1, source_target_pairs={{0,12},{4,0},{8,4},{12,8},{1,13},{5,1},{9,5},{13,9},{2,14},{6,2},{... | collective-permute-start | bytes 196616 | tf_op jit(solution)/shard_map/ppermute | solution.py:27
  18.7 5.2 %collective-permute-start.7 = (f32[128,128]{1,0:T(8,128)S(1)}, f32[128,128]{1,0:T(8,128)S(1)}, u32[]{:S(2)}, u32[]{:S(2)}) collective-permute-start(f32[128,128]{1,0:T(8,128)S(1)} %get-tuple-element.21), channel_id=1, source_target_pairs={{0,8},{4,12},{8,0},{12,4},{1,9},{5,13},{9,1},{13,5},{2,10},{6,14},... | collective-permute-start | bytes 196616 | tf_op jit(solution)/shard_map/ppermute | solution.py:27
  33.8 11.1 %collective-permute-start.11 = (f32[128,128]{1,0:T(8,128)S(1)}, f32[128,128]{1,0:T(8,128)S(1)}, u32[]{:S(2)}, u32[]{:S(2)}) collective-permute-start(f32[128,128]{1,0:T(8,128)S(1)} %get-tuple-element.11), channel_id=1, source_target_pairs={{0,3},{1,0},{2,1},{3,2},{4,7},{5,4},{6,5},{7,6},{8,11},{9,8},{10,9... | collective-permute-start | bytes 196616 | tf_op jit(solution)/shard_map/ppermute | solution.py:37
  34.0 10.9 %collective-permute-start.10 = (f32[128,128]{1,0:T(8,128)S(1)}, f32[128,128]{1,0:T(8,128)S(1)}, u32[]{:S(2)}, u32[]{:S(2)}) collective-permute-start(f32[128,128]{1,0:T(8,128)S(1)} %get-tuple-element.11), channel_id=1, source_target_pairs={{0,2},{1,3},{2,0},{3,1},{4,6},{5,7},{6,4},{7,5},{8,10},{9,11},{10,... | collective-permute-start | bytes 196616 | tf_op jit(solution)/shard_map/ppermute | solution.py:37
  35.2 9.7 %collective-permute-start.9 = (f32[128,128]{1,0:T(8,128)S(1)}, f32[128,128]{1,0:T(8,128)S(1)}, u32[]{:S(2)}, u32[]{:S(2)}) collective-permute-start(f32[128,128]{1,0:T(8,128)S(1)} %get-tuple-element.11), channel_id=1, source_target_pairs={{0,1},{1,2},{2,3},{3,0},{4,5},{5,6},{6,7},{7,4},{8,9},{9,10},{10,1... | collective-permute-start | bytes 196616 | tf_op jit(solution)/shard_map/ppermute | solution.py:37
  45.9 6.8 %collective-permute-start.12 = (f32[128,128]{1,0:T(8,128)S(1)}, f32[128,128]{1,0:T(8,128)S(1)}, u32[]{:S(2)}, u32[]{:S(2)}) collective-permute-start(f32[128,128]{1,0:T(8,128)S(1)} %get-tuple-element.16), channel_id=1, source_target_pairs={{0,4},{4,8},{8,12},{12,0},{1,5},{5,9},{9,13},{13,1},{2,6},{6,10},{... | collective-permute-start | bytes 196616 | tf_op jit(solution)/shard_map/ppermute | solution.py:27
  46.5 6.3 %collective-permute-start.14 = (f32[128,128]{1,0:T(8,128)S(1)}, f32[128,128]{1,0:T(8,128)S(1)}, u32[]{:S(2)}, u32[]{:S(2)}) collective-permute-start(f32[128,128]{1,0:T(8,128)S(1)} %get-tuple-element.17), channel_id=1, source_target_pairs={{0,12},{4,0},{8,4},{12,8},{1,13},{5,1},{9,5},{13,9},{2,14},{6,2},{... | collective-permute-start | bytes 196616 | tf_op jit(solution)/shard_map/ppermute | solution.py:27
  49.8 5.3 %collective-permute-start.13 = (f32[128,128]{1,0:T(8,128)S(1)}, f32[128,128]{1,0:T(8,128)S(1)}, u32[]{:S(2)}, u32[]{:S(2)}) collective-permute-start(f32[128,128]{1,0:T(8,128)S(1)} %get-tuple-element.18), channel_id=1, source_target_pairs={{0,8},{4,12},{8,0},{12,4},{1,9},{5,13},{9,1},{13,5},{2,10},{6,14},... | collective-permute-start | bytes 196616 | tf_op jit(solution)/shard_map/ppermute | solution.py:27
  65.1 2.5 %collective-permute-start.17 = (f32[128,128]{1,0:T(8,128)S(1)}, f32[128,128]{1,0:T(8,128)S(1)}, u32[]{:S(2)}, u32[]{:S(2)}) collective-permute-start(f32[128,128]{1,0:T(8,128)S(1)} %get-tuple-element.7), channel_id=1, source_target_pairs={{0,3},{1,0},{2,1},{3,2},{4,7},{5,4},{6,5},{7,6},{8,11},{9,8},{10,9... | collective-permute-start | bytes 196616 | tf_op jit(solution)/shard_map/ppermute | solution.py:37
  65.1 5.6 %collective-permute-start.16 = (f32[128,128]{1,0:T(8,128)S(1)}, f32[128,128]{1,0:T(8,128)S(1)}, u32[]{:S(2)}, u32[]{:S(2)}) collective-permute-start(f32[128,128]{1,0:T(8,128)S(1)} %get-tuple-element.7), channel_id=1, source_target_pairs={{0,2},{1,3},{2,0},{3,1},{4,6},{5,7},{6,4},{7,5},{8,10},{9,11},{10,... | collective-permute-start | bytes 196616 | tf_op jit(solution)/shard_map/ppermute | solution.py:37
  66.5 4.3 %collective-permute-start.15 = (f32[128,128]{1,0:T(8,128)S(1)}, f32[128,128]{1,0:T(8,128)S(1)}, u32[]{:S(2)}, u32[]{:S(2)}) collective-permute-start(f32[128,128]{1,0:T(8,128)S(1)} %get-tuple-element.7), channel_id=1, source_target_pairs={{0,1},{1,2},{2,3},{3,0},{4,5},{5,6},{6,7},{7,4},{8,9},{9,10},{10,1... | collective-permute-start | bytes 196616 | tf_op jit(solution)/shard_map/ppermute | solution.py:37
  71.9 14.5 %collective-permute-start.18 = (f32[128,128]{1,0:T(8,128)S(1)}, f32[128,128]{1,0:T(8,128)S(1)}, u32[]{:S(2)}, u32[]{:S(2)}) collective-permute-start(f32[128,128]{1,0:T(8,128)S(1)} %get-tuple-element.13), channel_id=1, source_target_pairs={{0,4},{4,8},{8,12},{12,0},{1,5},{5,9},{9,13},{13,1},{2,6},{6,10},{... | collective-permute-start | bytes 196616 | tf_op jit(solution)/shard_map/ppermute | solution.py:27
  72.5 13.9 %collective-permute-start.20 = (f32[128,128]{1,0:T(8,128)S(1)}, f32[128,128]{1,0:T(8,128)S(1)}, u32[]{:S(2)}, u32[]{:S(2)}) collective-permute-start(f32[128,128]{1,0:T(8,128)S(1)} %get-tuple-element.14), channel_id=1, source_target_pairs={{0,12},{4,0},{8,4},{12,8},{1,13},{5,1},{9,5},{13,9},{2,14},{6,2},{... | collective-permute-start | bytes 196616 | tf_op jit(solution)/shard_map/ppermute | solution.py:27
  75.8 10.6 %collective-permute-start.19 = (f32[128,128]{1,0:T(8,128)S(1)}, f32[128,128]{1,0:T(8,128)S(1)}, u32[]{:S(2)}, u32[]{:S(2)}) collective-permute-start(f32[128,128]{1,0:T(8,128)S(1)} %get-tuple-element.15), channel_id=1, source_target_pairs={{0,8},{4,12},{8,0},{12,4},{1,9},{5,13},{9,1},{13,5},{2,10},{6,14},... | collective-permute-start | bytes 196616 | tf_op jit(solution)/shard_map/ppermute | solution.py:27

commit v3 on v2

--- a/solution.py
+++ b/solution.py
@@ -38,6 +38,12 @@
     return jnp.stack(parts)
 
 
+def source(axis, count, entry):
+    if count > 4:
+        return entry
+    return (lax.axis_index(axis) - entry) % count
+
+
 def local(tiles, pattern, seed_label):
     groups = tiles.shape[0]
     tile = tiles.shape[2]
@@ -48,11 +54,8 @@
     n_all = n_wide * n_narrow
     width = SEED_CLASSES
     local_column = pattern // groups * br_local + pattern % br_local
-    if n_narrow > 4:
-        source = local_column
-    else:
-        source = (lax.axis_index("narrow") - local_column) % n_narrow
-    pick = source[:, :, None] == jnp.arange(n_narrow, dtype=source.dtype)[None, None, :]
+    entries = jnp.arange(n_narrow, dtype=local_column.dtype)
+    pick = local_column[:, :, None] == source("narrow", n_narrow, entries)[None, None, :]
     dense = jnp.sum(
         jnp.where(pick[:, :, None, :, None], tiles[:, :, :, None, :], 0.0), axis=1
     ).reshape(groups * tile, n_narrow * own_rows)
@@ -64,8 +67,16 @@
 
     def product(values):
         gathered = gather_blocks(values, "narrow", n_narrow).reshape(n_narrow * own_rows, width)
+        rows = gather_blocks(values, "wide", n_wide)
         partial = jnp.dot(dense, gathered, precision=lax.Precision.HIGHEST)
-        return scatter_sum(partial.reshape(n_wide, own_rows, width), "wide", n_wide)
+        partial = partial.reshape(n_wide, own_rows, width)
+        quad = jnp.zeros((width,), jnp.float32)
+        for entry in range(n_wide):
+            block = lax.dynamic_index_in_dim(
+                partial, source("wide", n_wide, entry), 0, keepdims=False
+            )
+            quad = quad + jnp.sum(rows[entry] * block, axis=0)
+        return scatter_sum(partial, "wide", n_wide), quad
 
     def reduce_dots(values):
         return sum_over(values, ("wide", "narrow"), n_all)
@@ -77,10 +88,15 @@
     solution = jnp.zeros_like(rhs)
     residual = rhs
     direction = rhs
-    weighted = product(direction)
+    weighted, quad = product(direction)
     image = diag_column * direction - weighted
     first = reduce_dots(
-        jnp.stack([jnp.sum(residual * residual, axis=0), jnp.sum(direction * image, axis=0)])
+        jnp.stack(
+            [
+                jnp.sum(residual * residual, axis=0),
+                jnp.sum(diag_column * direction * direction, axis=0) - quad,
+            ]
+        )
     )
     norm_now = first[0]
     curvature = first[1]
@@ -90,13 +106,23 @@
         residual = residual - alpha * image
         if step == ITERS - 1:
             break
-        weighted_residual = product(residual)
-        norm_next = reduce_dots(jnp.sum(residual * residual, axis=0))
+        weighted_residual, quad = product(residual)
+        sums = reduce_dots(
+            jnp.stack(
+                [
+                    jnp.sum(residual * residual, axis=0),
+                    jnp.sum(diag_column * residual * residual, axis=0) - quad,
+                    jnp.sum(residual * image, axis=0),
+                    jnp.sum(direction * image, axis=0),
+                ]
+            )
+        )
+        norm_next = sums[0]
         ratio = norm_next / norm_now
+        curvature = sums[1] + ratio * (2.0 * sums[2] + ratio * sums[3])
         direction = residual + ratio * direction
         weighted = weighted_residual + ratio * weighted
         image = diag_column * direction - weighted
-        curvature = reduce_dots(jnp.sum(direction * image, axis=0))
         norm_now = norm_next
     return (solution, residual)
 

time: 96.6 us -> 95.3 us (0.987)
  blocking collectives: 48.4 us -> 0 us
  starting transfers between devices: 24.4 us -> 47.5 us
  waiting for transfers between devices: 14.4 us -> 36.5 us
  local copies, waits for them, and re-layouts: 0.14 us -> 1.95 us
    all_to_all x5 -> x0, blocking collectives: 48.4 us -> none  [sum_over(): return jnp.sum(lax.all_to_all(spread, axes, 0, 0, tiled=True), axis=0)]
    ppermute x9 -> x18, waiting for transfers between devices: 4.36 us -> 16.9 us  [gather_blocks(): parts.append(lax.ppermute(values, axis, pairs))]
    all_to_all x0 -> x3, starting transfers between devices: none -> 11.2 us  [sum_over(): return jnp.sum(lax.all_to_all(spread, axes, 0, 0, tiled=True), axis=0)]
    ppermute x9 -> x18, starting transfers between devices: 7.63 us -> 17.1 us  [gather_blocks(): parts.append(lax.ppermute(values, axis, pairs))]
    all_to_all x0 -> x3, waiting for transfers between devices: none -> 5.5 us  [sum_over(): return jnp.sum(lax.all_to_all(spread, axes, 0, 0, tiled=True), axis=0)]
    ppermute x12, waiting for transfers between devices: 10.1 us -> 14.1 us  [scatter_sum(): total = total + lax.ppermute(sent, axis, pairs)]
    ppermute x12, starting transfers between devices: 16.7 us -> 19.2 us  [scatter_sum(): total = total + lax.ppermute(sent, axis, pairs)]
    broadcast_in_dim x5 -> x3, local copies, waits for them, and re-layouts: 0.04 us -> 1.85 us  [sum_over(): spread = jnp.broadcast_to(values[None], (count,) + values.shape)]
  transfers between devices with their start and end apart: 21 -> 33, of which waited for: 8 -> 18; matrix products, arithmetic and copies ran while one was open for 4% -> 6% of each run, Pallas kernels for 0% -> 0%
where the time goes in v3:
time: 95.3 us; the launch traced here: 95 us
  starting transfers between devices  47.5 us (50%)
  waiting for transfers between devices  36.5 us (38%)
  other arithmetic  5.15 us (5%)
  matrix products  2.96 us (3%)
  local copies, waits for them, and re-layouts  1.95 us (2%)
  between operations  1 us (1%)
    ppermute x12, starting transfers between devices, scatter_sum(): total = total + lax.ppermute(sent, axis, pairs)  19.2 us
    ppermute x18, starting transfers between devices, gather_blocks(): parts.append(lax.ppermute(values, axis, pairs))  17.1 us
    ppermute x18, waiting for transfers between devices, gather_blocks(): parts.append(lax.ppermute(values, axis, pairs))  16.9 us
    ppermute x12, waiting for transfers between devices, scatter_sum(): total = total + lax.ppermute(sent, axis, pairs)  14.1 us
    all_to_all x3, starting transfers between devices, sum_over(): return jnp.sum(lax.all_to_all(spread, axes, 0, 0, tiled=True), axis=0)  11.2 us
    all_to_all x3, waiting for transfers between devices, sum_over(): return jnp.sum(lax.all_to_all(spread, axes, 0, 0, tiled=True), axis=0)  5.5 us
    dot_general x3, matrix products, product(): partial = jnp.dot(dense, gathered, precision=lax.Precision.HIGHEST)  2.96 us
  transfers between devices with their start and end apart: 33, of which 18 were waited for; matrix products, arithmetic and copies ran while one was open for 6% of the time, Pallas kernels for 0%

profile of v3, /device:TPU:0, one launch (start us, length us, event | category | flops | bytes accessed | tf_op | source)
XLA Modules:
  0.0 95.0 jit_solution(9473344937508211535)
XLA Ops:
  0.6 0.0 copy-start
  0.7 0.9 fusion.50
  1.6 3.1 %collective-permute-start.6 = (f32[128,128]{1,0:T(8,128)S(1)}, f32[128,128]{1,0:T(8,128)S(1)}, u32[]{:S(2)}, u32[]{:S(2)}) collective-permute-start(f32[128,128]{1,0:T(8,128)S(1)} %fusion.50), channel_id=1, source_target_pairs={{0,4},{4,8},{8,12},{12,0},{1,5},{5,9},{9,13},{13,1},{2,6},{6,10},{... | collective-permute-start | bytes 196616 | tf_op jit(solution)/shard_map/ppermute | solution.py:37
  4.6 0.7 collective-permute-start.5
  5.3 1.8 %reduce_sum.244 = f32[4,128]{1,0:T(4,128)S(1)} reduce(f32[4,8,128,128]{3,2,1,0:T(8,128)} %param.3, f32[]{:T(128)} %constant.177.clone.1), dimensions={1,3}, to_apply=%region_1.2 | reduce | flops 523776 | bytes 2099204 | tf_op jit(solution)/shard_map/reduce_sum | solution.py:63
  7.1 2.4 %collective-permute-start.2 = (f32[128]{0:T(128)S(1)}, f32[128]{0:T(128)S(1)}, u32[]{:S(2)}, u32[]{:S(2)}) collective-permute-start(f32[128]{0:T(128)S(1)} %get-tuple-element.50), channel_id=1, source_target_pairs={{0,12},{4,0},{8,4},{12,8},{1,13},{5,1},{9,5},{13,9},{2,14},{6,2},{... | collective-permute-start | bytes 1544 | tf_op jit(solution)/shard_map/ppermute | solution.py:27
  9.5 0.7 collective-permute-start.1
  10.2 1.6 %collective-permute-start = (f32[128]{0:T(128)S(1)}, f32[128]{0:T(128)S(1)}, u32[]{:S(2)}, u32[]{:S(2)}) collective-permute-start(f32[128]{0:T(128)S(1)} %get-tuple-element.49), channel_id=1, source_target_pairs={{0,4},{4,8},{8,12},{12,0},{1,5},{5,9},{9,13},{13,1},{2,6},{6,10},{... | collective-permute-start | bytes 1544 | tf_op jit(solution)/shard_map/ppermute | solution.py:27
  11.8 0.1 fusion.51
  12.0 0.1 broadcast_compare_fusion
  12.0 0.8 select_reduce_fusion
  12.9 0.0 collective-permute-done.2
  12.9 0.9 collective-permute-start.4
  13.8 0.2 collective-permute-done.1
  13.9 0.0 collective-permute-start.3
  14.0 1.6 %collective-permute-done = f32[128]{0:T(128)S(1)} collective-permute-done((f32[128]{0:T(128)S(1)}, f32[128]{0:T(128)S(1)}, u32[]{:S(2)}, u32[]{:S(2)}) %collective-permute-start) | collective-permute-done | bytes 544 | tf_op jit(solution)/shard_map/ppermute | solution.py:27
  15.5 0.6 collective-permute-start.8
  16.1 0.7 collective-permute-start.7
  16.8 0.7 collective-permute-done.4
  17.6 0.3 collective-permute-done.3
  17.9 1.0 %convolution_bitcast_fusion.2 = f32[4,128,128]{2,1,0:T(8,128)S(1)} fusion(f32[4,128,4,128]{3,1,2,0:T(8,128)S(1)} %select_reduce_fusion, f32[1,128,128]{2,1,0:T(8,128)S(1)} %bitcast.169, f32[1,128,128]{2,1,0:T(8,128)S(1)} %bitcast.170, f32[1,128,128]{2,1,0:T(8,128)S(1)} %bitcast.172, f32[1,128,128]{2,1,0:T(8,128)S(1)} %fusion.51), kind=kOutput, calls=%fused_computation.3 | convolution fusion | flops 402849792 | bytes 1572864 | tf_op jit(solution)/shard_map/dot_general | solution.py:71
  18.9 0.9 collective-permute-done.8
  19.8 3.0 %collective-permute-done.7 = f32[128,128]{1,0:T(8,128)S(1)} collective-permute-done((f32[128,128]{1,0:T(8,128)S(1)}, f32[128,128]{1,0:T(8,128)S(1)}, u32[]{:S(2)}, u32[]{:S(2)}) %collective-permute-start.7) | collective-permute-done | bytes 65568 | tf_op jit(solution)/shard_map/ppermute | solution.py:37
  22.8 0.1 fusion.49
  22.9 0.6 broadcast_in_dim.29
  23.5 4.2 %all-to-all-start = ((f32[16,2,128]{2,1,0:T(2,128)}), f32[16,2,128]{2,1,0:T(2,128)S(1)}, u32[]{:S(2)}, u32[]{:S(2)}) async-start(f32[16,2,128]{2,1,0:T(2,128)} %broadcast_in_dim.29), calls=%async_computation | async-start | bytes 32768 | tf_op jit(solution)/shard_map/all_to_all | solution.py:16
  27.7 3.8 %collective-permute-start.11 = (f32[128,128]{1,0:T(8,128)S(1)}, f32[128,128]{1,0:T(8,128)S(1)}, u32[]{:S(2)}, u32[]{:S(2)}) collective-permute-start(f32[128,128]{1,0:T(8,128)S(1)} %get-tuple-element.45), channel_id=1, source_target_pairs={{0,12},{4,0},{8,4},{12,8},{1,13},{5,1},{9,5},{13,9},{2,14},{6,2},{... | collective-permute-start | bytes 196616 | tf_op jit(solution)/shard_map/ppermute | solution.py:27
  31.5 1.1 %collective-permute-start.9 = (f32[128,128]{1,0:T(8,128)S(1)}, f32[128,128]{1,0:T(8,128)S(1)}, u32[]{:S(2)}, u32[]{:S(2)}) collective-permute-start(f32[128,128]{1,0:T(8,128)S(1)} %get-tuple-element.44), channel_id=1, source_target_pairs={{0,4},{4,8},{8,12},{12,0},{1,5},{5,9},{9,13},{13,1},{2,6},{6,10},{... | collective-permute-start | bytes 196616 | tf_op jit(solution)/shard_map/ppermute | solution.py:27
  32.6 1.6 %all-to-all-done = f32[16,2,128]{2,1,0:T(2,128)S(1)} async-done(((f32[16,2,128]{2,1,0:T(2,128)}), f32[16,2,128]{2,1,0:T(2,128)S(1)}, u32[]{:S(2)}, u32[]{:S(2)}) %all-to-all-start) | async-done | bytes 16416 | tf_op jit(solution)/shard_map/all_to_all | solution.py:16
  34.3 4.2 %collective-permute-done.10 = f32[128,128]{1,0:T(8,128)S(1)} collective-permute-done((f32[128,128]{1,0:T(8,128)S(1)}, f32[128,128]{1,0:T(8,128)S(1)}, u32[]{:S(2)}, u32[]{:S(2)}) %collective-permute-start.10) | collective-permute-done | bytes 65568 | tf_op jit(solution)/shard_map/ppermute | solution.py:27
  38.4 0.1 select_subtract_fusion
  38.6 1.1 %collective-permute-start.14 = (f32[128,128]{1,0:T(8,128)S(1)}, f32[128,128]{1,0:T(8,128)S(1)}, u32[]{:S(2)}, u32[]{:S(2)}) collective-permute-start(f32[128,128]{1,0:T(8,128)S(1)} %get-tuple-element.36), channel_id=1, source_target_pairs={{0,3},{1,0},{2,1},{3,2},{4,7},{5,4},{6,5},{7,6},{8,11},{9,8},{10,9... | collective-permute-start | bytes 196616 | tf_op jit(solution)/shard_map/ppermute | solution.py:37
  39.7 0.6 collective-permute-start.13
  40.2 0.1 collective-permute-start.12
  40.3 0.0 collective-permute-start.15
  40.3 3.8 %collective-permute-start.17 = (f32[128,128]{1,0:T(8,128)S(1)}, f32[128,128]{1,0:T(8,128)S(1)}, u32[]{:S(2)}, u32[]{:S(2)}) collective-permute-start(f32[128,128]{1,0:T(8,128)S(1)} %get-tuple-element.36), channel_id=1, source_target_pairs={{0,12},{4,0},{8,4},{12,8},{1,13},{5,1},{9,5},{13,9},{2,14},{6,2},{... | collective-permute-start | bytes 196616 | tf_op jit(solution)/shard_map/ppermute | solution.py:37
  44.1 0.5 collective-permute-done.13
  44.6 1.0 %convolution_bitcast_fusion.1 = f32[4,128,128]{2,1,0:T(8,128)S(1)} fusion(f32[4,128,4,128]{3,1,2,0:T(8,128)S(1)} %select_reduce_fusion, f32[1,128,128]{2,1,0:T(8,128)S(1)} %bitcast.173, f32[1,128,128]{2,1,0:T(8,128)S(1)} %bitcast.175, f32[1,128,128]{2,1,0:T(8,128)S(1)} %bitcast.177, f32[1,128,128]{2,1,0:T(8,128)S(1)} %bitcast.167), kind=kOutput, calls=%fused_computation.2 | convolution fusion | flops 402849792 | bytes 1572864 | tf_op jit(solution)/shard_map/dot_general | solution.py:71
  45.6 1.0 %collective-permute-done.15 = f32[128,128]{1,0:T(8,128)S(1)} collective-permute-done((f32[128,128]{1,0:T(8,128)S(1)}, f32[128,128]{1,0:T(8,128)S(1)}, u32[]{:S(2)}, u32[]{:S(2)}) %collective-permute-start.15) | collective-permute-done | bytes 65568 | tf_op jit(solution)/shard_map/ppermute | solution.py:37
  46.7 4.4 %collective-permute-done.16 = f32[128,128]{1,0:T(8,128)S(1)} collective-permute-done((f32[128,128]{1,0:T(8,128)S(1)}, f32[128,128]{1,0:T(8,128)S(1)}, u32[]{:S(2)}, u32[]{:S(2)}) %collective-permute-start.16) | collective-permute-done | bytes 65568 | tf_op jit(solution)/shard_map/ppermute | solution.py:37
  51.1 0.1 fusion.43
  51.2 0.6 broadcast_in_dim.30
  51.9 3.5 %all-to-all-start.1 = ((f32[16,4,128]{2,1,0:T(4,128)}), f32[16,4,128]{2,1,0:T(4,128)S(1)}, u32[]{:S(2)}, u32[]{:S(2)}) async-start(f32[16,4,128]{2,1,0:T(4,128)} %broadcast_in_dim.30), calls=%async_computation.1 | async-start | bytes 65536 | tf_op jit(solution)/shard_map/all_to_all | solution.py:16
  55.4 3.7 %collective-permute-start.20 = (f32[128,128]{1,0:T(8,128)S(1)}, f32[128,128]{1,0:T(8,128)S(1)}, u32[]{:S(2)}, u32[]{:S(2)}) collective-permute-start(f32[128,128]{1,0:T(8,128)S(1)} %get-tuple-element.42), channel_id=1, source_target_pairs={{0,12},{4,0},{8,4},{12,8},{1,13},{5,1},{9,5},{13,9},{2,14},{6,2},{... | collective-permute-start | bytes 196616 | tf_op jit(solution)/shard_map/ppermute | solution.py:27
  59.1 1.1 %collective-permute-start.18 = (f32[128,128]{1,0:T(8,128)S(1)}, f32[128,128]{1,0:T(8,128)S(1)}, u32[]{:S(2)}, u32[]{:S(2)}) collective-permute-start(f32[128,128]{1,0:T(8,128)S(1)} %get-tuple-element.41), channel_id=1, source_target_pairs={{0,4},{4,8},{8,12},{12,0},{1,5},{5,9},{9,13},{13,1},{2,6},{6,10},{... | collective-permute-start | bytes 196616 | tf_op jit(solution)/shard_map/ppermute | solution.py:27
  60.2 1.9 %all-to-all-done.1 = f32[16,4,128]{2,1,0:T(4,128)S(1)} async-done(((f32[16,4,128]{2,1,0:T(4,128)}), f32[16,4,128]{2,1,0:T(4,128)S(1)}, u32[]{:S(2)}, u32[]{:S(2)}) %all-to-all-start.1) | async-done | bytes 32800 | tf_op jit(solution)/shard_map/all_to_all | solution.py:16
  62.2 4.1 %collective-permute-done.19 = f32[128,128]{1,0:T(8,128)S(1)} collective-permute-done((f32[128,128]{1,0:T(8,128)S(1)}, f32[128,128]{1,0:T(8,128)S(1)}, u32[]{:S(2)}, u32[]{:S(2)}) %collective-permute-start.19) | collective-permute-done | bytes 65568 | tf_op jit(solution)/shard_map/ppermute | solution.py:27
  66.3 0.1 multiply_subtract_fusion
  66.4 1.1 %collective-permute-start.23 = (f32[128,128]{1,0:T(8,128)S(1)}, f32[128,128]{1,0:T(8,128)S(1)}, u32[]{:S(2)}, u32[]{:S(2)}) collective-permute-start(f32[128,128]{1,0:T(8,128)S(1)} %get-tuple-element.32), channel_id=1, source_target_pairs={{0,3},{1,0},{2,1},{3,2},{4,7},{5,4},{6,5},{7,6},{8,11},{9,8},{10,9... | collective-permute-start | bytes 196616 | tf_op jit(solution)/shard_map/ppermute | solution.py:37
  67.5 0.5 collective-permute-start.22
  68.0 0.2 collective-permute-start.21
  68.2 3.8 %collective-permute-start.26 = (f32[128,128]{1,0:T(8,128)S(1)}, f32[128,128]{1,0:T(8,128)S(1)}, u32[]{:S(2)}, u32[]{:S(2)}) collective-permute-start(f32[128,128]{1,0:T(8,128)S(1)} %get-tuple-element.32), channel_id=1, source_target_pairs={{0,12},{4,0},{8,4},{12,8},{1,13},{5,1},{9,5},{13,9},{2,14},{6,2},{... | collective-permute-start | bytes 196616 | tf_op jit(solution)/shard_map/ppermute | solution.py:37
  72.0 0.4 collective-permute-done.22
  72.4 1.0 %convolution_bitcast_fusion = f32[4,128,128]{2,1,0:T(8,128)S(1)} fusion(f32[4,128,4,128]{3,1,2,0:T(8,128)S(1)} %select_reduce_fusion, f32[1,128,128]{2,1,0:T(8,128)S(1)} %bitcast.171, f32[1,128,128]{2,1,0:T(8,128)S(1)} %bitcast.174, f32[1,128,128]{2,1,0:T(8,128)S(1)} %bitcast.176, f32[1,128,128]{2,1,0:T(8,128)S(1)} %bitcast.168), kind=kOutput, calls=%fused_computation.1 | convolution fusion | flops 402849792 | bytes 1572864 | tf_op jit(solution)/shard_map/dot_general | solution.py:71
  73.4 1.3 %collective-permute-done.24 = f32[128,128]{1,0:T(8,128)S(1)} collective-permute-done((f32[128,128]{1,0:T(8,128)S(1)}, f32[128,128]{1,0:T(8,128)S(1)}, u32[]{:S(2)}, u32[]{:S(2)}) %collective-permute-start.24) | collective-permute-done | bytes 65568 | tf_op jit(solution)/shard_map/ppermute | solution.py:37
  74.7 4.3 %collective-permute-done.25 = f32[128,128]{1,0:T(8,128)S(1)} collective-permute-done((f32[128,128]{1,0:T(8,128)S(1)}, f32[128,128]{1,0:T(8,128)S(1)}, u32[]{:S(2)}, u32[]{:S(2)}) %collective-permute-start.25) | collective-permute-done | bytes 65568 | tf_op jit(solution)/shard_map/ppermute | solution.py:37
  79.0 0.1 fusion.36
  79.2 0.6 broadcast_in_dim.31
  79.8 3.5 %all-to-all-start.2 = ((f32[16,4,128]{2,1,0:T(4,128)}), f32[16,4,128]{2,1,0:T(4,128)S(1)}, u32[]{:S(2)}, u32[]{:S(2)}) async-start(f32[16,4,128]{2,1,0:T(4,128)} %broadcast_in_dim.31), calls=%async_computation.2 | async-start | bytes 65536 | tf_op jit(solution)/shard_map/all_to_all | solution.py:16
  83.3 3.7 %collective-permute-start.29 = (f32[128,128]{1,0:T(8,128)S(1)}, f32[128,128]{1,0:T(8,128)S(1)}, u32[]{:S(2)}, u32[]{:S(2)}) collective-permute-start(f32[128,128]{1,0:T(8,128)S(1)} %get-tuple-element.39), channel_id=1, source_target_pairs={{0,12},{4,0},{8,4},{12,8},{1,13},{5,1},{9,5},{13,9},{2,14},{6,2},{... | collective-permute-start | bytes 196616 | tf_op jit(solution)/shard_map/ppermute | solution.py:27
  87.1 1.1 %collective-permute-start.27 = (f32[128,128]{1,0:T(8,128)S(1)}, f32[128,128]{1,0:T(8,128)S(1)}, u32[]{:S(2)}, u32[]{:S(2)}) collective-permute-start(f32[128,128]{1,0:T(8,128)S(1)} %get-tuple-element.38), channel_id=1, source_target_pairs={{0,4},{4,8},{8,12},{12,0},{1,5},{5,9},{9,13},{13,1},{2,6},{6,10},{... | collective-permute-start | bytes 196616 | tf_op jit(solution)/shard_map/ppermute | solution.py:27
  88.1 1.9 %all-to-all-done.2 = f32[16,4,128]{2,1,0:T(4,128)S(1)} async-done(((f32[16,4,128]{2,1,0:T(4,128)}), f32[16,4,128]{2,1,0:T(4,128)S(1)}, u32[]{:S(2)}, u32[]{:S(2)}) %all-to-all-start.2) | async-done | bytes 32800 | tf_op jit(solution)/shard_map/all_to_all | solution.py:16
  90.1 4.1 %collective-permute-done.28 = f32[128,128]{1,0:T(8,128)S(1)} collective-permute-done((f32[128,128]{1,0:T(8,128)S(1)}, f32[128,128]{1,0:T(8,128)S(1)}, u32[]{:S(2)}, u32[]{:S(2)}) %collective-permute-start.28) | collective-permute-done | bytes 65568 | tf_op jit(solution)/shard_map/ppermute | solution.py:27
  94.2 0.8 fusion.33
  (44 shorter events, 0.4 us)
Async XLA Ops:
  0.6 11.1 %copy-start.1 = (s32[128,1]{0,1:T(1,128)S(1)}, s32[128,1]{0,1:T(1,128)}, u32[]{:S(2)}) copy-start(s32[128,1]{0,1:T(1,128)} %param.5) | copy-start | bytes 1540
  0.6 11.4 %copy-start = (f32[4,8,128,128]{3,2,1,0:T(8,128)S(1)}, f32[4,8,128,128]{3,2,1,0:T(8,128)}, u32[]{:S(2)}) copy-start(f32[4,8,128,128]{3,2,1,0:T(8,128)} %param.3) | copy-start | bytes 6291460
  0.7 11.3 %copy-start.2 = (s32[4,8]{1,0:T(4,128)S(1)}, s32[4,8]{1,0:T(4,128)}, u32[]{:S(2)}) copy-start(s32[4,8]{1,0:T(4,128)} %param.4) | copy-start | bytes 388
  1.6 17.4 %collective-permute-start.6 = (f32[128,128]{1,0:T(8,128)S(1)}, f32[128,128]{1,0:T(8,128)S(1)}, u32[]{:S(2)}, u32[]{:S(2)}) collective-permute-start(f32[128,128]{1,0:T(8,128)S(1)} %fusion.50), channel_id=1, source_target_pairs={{0,4},{4,8},{8,12},{12,0},{1,5},{5,9},{9,13},{13,1},{2,6},{6,10},{... | collective-permute-start | bytes 196616 | tf_op jit(solution)/shard_map/ppermute | solution.py:37
  4.6 11.5 %collective-permute-start.5 = (f32[128,128]{1,0:T(8,128)S(1)}, f32[128,128]{1,0:T(8,128)S(1)}, u32[]{:S(2)}, u32[]{:S(2)}) collective-permute-start(f32[128,128]{1,0:T(8,128)S(1)} %fusion.50), channel_id=1, source_target_pairs={{0,3},{1,0},{2,1},{3,2},{4,7},{5,4},{6,5},{7,6},{8,11},{9,8},{10,9... | collective-permute-start | bytes 196616 | tf_op jit(solution)/shard_map/ppermute | solution.py:37
  7.1 5.8 %collective-permute-start.2 = (f32[128]{0:T(128)S(1)}, f32[128]{0:T(128)S(1)}, u32[]{:S(2)}, u32[]{:S(2)}) collective-permute-start(f32[128]{0:T(128)S(1)} %get-tuple-element.50), channel_id=1, source_target_pairs={{0,12},{4,0},{8,4},{12,8},{1,13},{5,1},{9,5},{13,9},{2,14},{6,2},{... | collective-permute-start | bytes 1544 | tf_op jit(solution)/shard_map/ppermute | solution.py:27
  9.5 4.4 %collective-permute-start.1 = (f32[128]{0:T(128)S(1)}, f32[128]{0:T(128)S(1)}, u32[]{:S(2)}, u32[]{:S(2)}) collective-permute-start(f32[128]{0:T(128)S(1)} %get-tuple-element.51), channel_id=1, source_target_pairs={{0,8},{4,12},{8,0},{12,4},{1,9},{5,13},{9,1},{13,5},{2,10},{6,14},... | collective-permute-start | bytes 1544 | tf_op jit(solution)/shard_map/ppermute | solution.py:27
  10.2 5.3 %collective-permute-start = (f32[128]{0:T(128)S(1)}, f32[128]{0:T(128)S(1)}, u32[]{:S(2)}, u32[]{:S(2)}) collective-permute-start(f32[128]{0:T(128)S(1)} %get-tuple-element.49), channel_id=1, source_target_pairs={{0,4},{4,8},{8,12},{12,0},{1,5},{5,9},{9,13},{13,1},{2,6},{6,10},{... | collective-permute-start | bytes 1544 | tf_op jit(solution)/shard_map/ppermute | solution.py:27
  12.9 4.7 %collective-permute-start.4 = (f32[128,128]{1,0:T(8,128)S(1)}, f32[128,128]{1,0:T(8,128)S(1)}, u32[]{:S(2)}, u32[]{:S(2)}) collective-permute-start(f32[128,128]{1,0:T(8,128)S(1)} %fusion.50), channel_id=1, source_target_pairs={{0,2},{1,3},{2,0},{3,1},{4,6},{5,7},{6,4},{7,5},{8,10},{9,11},{10,... | collective-permute-start | bytes 196616 | tf_op jit(solution)/shard_map/ppermute | solution.py:37
  13.9 4.0 %collective-permute-start.3 = (f32[128,128]{1,0:T(8,128)S(1)}, f32[128,128]{1,0:T(8,128)S(1)}, u32[]{:S(2)}, u32[]{:S(2)}) collective-permute-start(f32[128,128]{1,0:T(8,128)S(1)} %fusion.50), channel_id=1, source_target_pairs={{0,1},{1,2},{2,3},{3,0},{4,5},{5,6},{6,7},{7,4},{8,9},{9,10},{10,1... | collective-permute-start | bytes 196616 | tf_op jit(solution)/shard_map/ppermute | solution.py:37
  15.5 4.3 %collective-permute-start.8 = (f32[128,128]{1,0:T(8,128)S(1)}, f32[128,128]{1,0:T(8,128)S(1)}, u32[]{:S(2)}, u32[]{:S(2)}) collective-permute-start(f32[128,128]{1,0:T(8,128)S(1)} %fusion.50), channel_id=1, source_target_pairs={{0,12},{4,0},{8,4},{12,8},{1,13},{5,1},{9,5},{13,9},{2,14},{6,2},{... | collective-permute-start | bytes 196616 | tf_op jit(solution)/shard_map/ppermute | solution.py:37
  16.1 6.6 %collective-permute-start.7 = (f32[128,128]{1,0:T(8,128)S(1)}, f32[128,128]{1,0:T(8,128)S(1)}, u32[]{:S(2)}, u32[]{:S(2)}) collective-permute-start(f32[128,128]{1,0:T(8,128)S(1)} %fusion.50), channel_id=1, source_target_pairs={{0,8},{4,12},{8,0},{12,4},{1,9},{5,13},{9,1},{13,5},{2,10},{6,14},... | collective-permute-start | bytes 196616 | tf_op jit(solution)/shard_map/ppermute | solution.py:37
  23.5 10.7 %all-to-all-start = ((f32[16,2,128]{2,1,0:T(2,128)}), f32[16,2,128]{2,1,0:T(2,128)S(1)}, u32[]{:S(2)}, u32[]{:S(2)}) async-start(f32[16,2,128]{2,1,0:T(2,128)} %broadcast_in_dim.29), calls=%async_computation | async-start | bytes 32768 | tf_op jit(solution)/shard_map/all_to_all | solution.py:16
  27.7 6.5 %collective-permute-start.11 = (f32[128,128]{1,0:T(8,128)S(1)}, f32[128,128]{1,0:T(8,128)S(1)}, u32[]{:S(2)}, u32[]{:S(2)}) collective-permute-start(f32[128,128]{1,0:T(8,128)S(1)} %get-tuple-element.45), channel_id=1, source_target_pairs={{0,12},{4,0},{8,4},{12,8},{1,13},{5,1},{9,5},{13,9},{2,14},{6,2},{... | collective-permute-start | bytes 196616 | tf_op jit(solution)/shard_map/ppermute | solution.py:27
  31.5 7.0 %collective-permute-start.10 = (f32[128,128]{1,0:T(8,128)S(1)}, f32[128,128]{1,0:T(8,128)S(1)}, u32[]{:S(2)}, u32[]{:S(2)}) collective-permute-start(f32[128,128]{1,0:T(8,128)S(1)} %get-tuple-element.46), channel_id=1, source_target_pairs={{0,8},{4,12},{8,0},{12,4},{1,9},{5,13},{9,1},{13,5},{2,10},{6,14},... | collective-permute-start | bytes 196616 | tf_op jit(solution)/shard_map/ppermute | solution.py:27
  31.5 7.0 %collective-permute-start.9 = (f32[128,128]{1,0:T(8,128)S(1)}, f32[128,128]{1,0:T(8,128)S(1)}, u32[]{:S(2)}, u32[]{:S(2)}) collective-permute-start(f32[128,128]{1,0:T(8,128)S(1)} %get-tuple-element.44), channel_id=1, source_target_pairs={{0,4},{4,8},{8,12},{12,0},{1,5},{5,9},{9,13},{13,1},{2,6},{6,10},{... | collective-permute-start | bytes 196616 | tf_op jit(solution)/shard_map/ppermute | solution.py:27
  38.6 5.6 %collective-permute-start.14 = (f32[128,128]{1,0:T(8,128)S(1)}, f32[128,128]{1,0:T(8,128)S(1)}, u32[]{:S(2)}, u32[]{:S(2)}) collective-permute-start(f32[128,128]{1,0:T(8,128)S(1)} %get-tuple-element.36), channel_id=1, source_target_pairs={{0,3},{1,0},{2,1},{3,2},{4,7},{5,4},{6,5},{7,6},{8,11},{9,8},{10,9... | collective-permute-start | bytes 196616 | tf_op jit(solution)/shard_map/ppermute | solution.py:37
  39.7 5.0 %collective-permute-start.13 = (f32[128,128]{1,0:T(8,128)S(1)}, f32[128,128]{1,0:T(8,128)S(1)}, u32[]{:S(2)}, u32[]{:S(2)}) collective-permute-start(f32[128,128]{1,0:T(8,128)S(1)} %get-tuple-element.36), channel_id=1, source_target_pairs={{0,2},{1,3},{2,0},{3,1},{4,6},{5,7},{6,4},{7,5},{8,10},{9,11},{10,... | collective-permute-start | bytes 196616 | tf_op jit(solution)/shard_map/ppermute | solution.py:37
  40.2 4.4 %collective-permute-start.12 = (f32[128,128]{1,0:T(8,128)S(1)}, f32[128,128]{1,0:T(8,128)S(1)}, u32[]{:S(2)}, u32[]{:S(2)}) collective-permute-start(f32[128,128]{1,0:T(8,128)S(1)} %get-tuple-element.36), channel_id=1, source_target_pairs={{0,1},{1,2},{2,3},{3,0},{4,5},{5,6},{6,7},{7,4},{8,9},{9,10},{10,1... | collective-permute-start | bytes 196616 | tf_op jit(solution)/shard_map/ppermute | solution.py:37
  40.3 6.4 %collective-permute-start.15 = (f32[128,128]{1,0:T(8,128)S(1)}, f32[128,128]{1,0:T(8,128)S(1)}, u32[]{:S(2)}, u32[]{:S(2)}) collective-permute-start(f32[128,128]{1,0:T(8,128)S(1)} %get-tuple-element.36), channel_id=1, source_target_pairs={{0,4},{4,8},{8,12},{12,0},{1,5},{5,9},{9,13},{13,1},{2,6},{6,10},{... | collective-permute-start | bytes 196616 | tf_op jit(solution)/shard_map/ppermute | solution.py:37
  40.3 6.3 %collective-permute-start.17 = (f32[128,128]{1,0:T(8,128)S(1)}, f32[128,128]{1,0:T(8,128)S(1)}, u32[]{:S(2)}, u32[]{:S(2)}) collective-permute-start(f32[128,128]{1,0:T(8,128)S(1)} %get-tuple-element.36), channel_id=1, source_target_pairs={{0,12},{4,0},{8,4},{12,8},{1,13},{5,1},{9,5},{13,9},{2,14},{6,2},{... | collective-permute-start | bytes 196616 | tf_op jit(solution)/shard_map/ppermute | solution.py:37
  44.1 7.0 %collective-permute-start.16 = (f32[128,128]{1,0:T(8,128)S(1)}, f32[128,128]{1,0:T(8,128)S(1)}, u32[]{:S(2)}, u32[]{:S(2)}) collective-permute-start(f32[128,128]{1,0:T(8,128)S(1)} %get-tuple-element.36), channel_id=1, source_target_pairs={{0,8},{4,12},{8,0},{12,4},{1,9},{5,13},{9,1},{13,5},{2,10},{6,14},... | collective-permute-start | bytes 196616 | tf_op jit(solution)/shard_map/ppermute | solution.py:37
  51.9 10.3 %all-to-all-start.1 = ((f32[16,4,128]{2,1,0:T(4,128)}), f32[16,4,128]{2,1,0:T(4,128)S(1)}, u32[]{:S(2)}, u32[]{:S(2)}) async-start(f32[16,4,128]{2,1,0:T(4,128)} %broadcast_in_dim.30), calls=%async_computation.1 | async-start | bytes 65536 | tf_op jit(solution)/shard_map/all_to_all | solution.py:16
  55.4 6.8 %collective-permute-start.20 = (f32[128,128]{1,0:T(8,128)S(1)}, f32[128,128]{1,0:T(8,128)S(1)}, u32[]{:S(2)}, u32[]{:S(2)}) collective-permute-start(f32[128,128]{1,0:T(8,128)S(1)} %get-tuple-element.42), channel_id=1, source_target_pairs={{0,12},{4,0},{8,4},{12,8},{1,13},{5,1},{9,5},{13,9},{2,14},{6,2},{... | collective-permute-start | bytes 196616 | tf_op jit(solution)/shard_map/ppermute | solution.py:27
  59.1 7.2 %collective-permute-start.19 = (f32[128,128]{1,0:T(8,128)S(1)}, f32[128,128]{1,0:T(8,128)S(1)}, u32[]{:S(2)}, u32[]{:S(2)}) collective-permute-start(f32[128,128]{1,0:T(8,128)S(1)} %get-tuple-element.43), channel_id=1, source_target_pairs={{0,8},{4,12},{8,0},{12,4},{1,9},{5,13},{9,1},{13,5},{2,10},{6,14},... | collective-permute-start | bytes 196616 | tf_op jit(solution)/shard_map/ppermute | solution.py:27
  59.1 7.2 %collective-permute-start.18 = (f32[128,128]{1,0:T(8,128)S(1)}, f32[128,128]{1,0:T(8,128)S(1)}, u32[]{:S(2)}, u32[]{:S(2)}) collective-permute-start(f32[128,128]{1,0:T(8,128)S(1)} %get-tuple-element.41), channel_id=1, source_target_pairs={{0,4},{4,8},{8,12},{12,0},{1,5},{5,9},{9,13},{13,1},{2,6},{6,10},{... | collective-permute-start | bytes 196616 | tf_op jit(solution)/shard_map/ppermute | solution.py:27
  66.4 5.6 %collective-permute-start.23 = (f32[128,128]{1,0:T(8,128)S(1)}, f32[128,128]{1,0:T(8,128)S(1)}, u32[]{:S(2)}, u32[]{:S(2)}) collective-permute-start(f32[128,128]{1,0:T(8,128)S(1)} %get-tuple-element.32), channel_id=1, source_target_pairs={{0,3},{1,0},{2,1},{3,2},{4,7},{5,4},{6,5},{7,6},{8,11},{9,8},{10,9... | collective-permute-start | bytes 196616 | tf_op jit(solution)/shard_map/ppermute | solution.py:37
  67.5 4.9 %collective-permute-start.22 = (f32[128,128]{1,0:T(8,128)S(1)}, f32[128,128]{1,0:T(8,128)S(1)}, u32[]{:S(2)}, u32[]{:S(2)}) collective-permute-start(f32[128,128]{1,0:T(8,128)S(1)} %get-tuple-element.32), channel_id=1, source_target_pairs={{0,2},{1,3},{2,0},{3,1},{4,6},{5,7},{6,4},{7,5},{8,10},{9,11},{10,... | collective-permute-start | bytes 196616 | tf_op jit(solution)/shard_map/ppermute | solution.py:37
  68.0 4.4 %collective-permute-start.21 = (f32[128,128]{1,0:T(8,128)S(1)}, f32[128,128]{1,0:T(8,128)S(1)}, u32[]{:S(2)}, u32[]{:S(2)}) collective-permute-start(f32[128,128]{1,0:T(8,128)S(1)} %get-tuple-element.32), channel_id=1, source_target_pairs={{0,1},{1,2},{2,3},{3,0},{4,5},{5,6},{6,7},{7,4},{8,9},{9,10},{10,1... | collective-permute-start | bytes 196616 | tf_op jit(solution)/shard_map/ppermute | solution.py:37
  68.2 6.5 %collective-permute-start.24 = (f32[128,128]{1,0:T(8,128)S(1)}, f32[128,128]{1,0:T(8,128)S(1)}, u32[]{:S(2)}, u32[]{:S(2)}) collective-permute-start(f32[128,128]{1,0:T(8,128)S(1)} %get-tuple-element.32), channel_id=1, source_target_pairs={{0,4},{4,8},{8,12},{12,0},{1,5},{5,9},{9,13},{13,1},{2,6},{6,10},{... | collective-permute-start | bytes 196616 | tf_op jit(solution)/shard_map/ppermute | solution.py:37
  68.2 6.5 %collective-permute-start.26 = (f32[128,128]{1,0:T(8,128)S(1)}, f32[128,128]{1,0:T(8,128)S(1)}, u32[]{:S(2)}, u32[]{:S(2)}) collective-permute-start(f32[128,128]{1,0:T(8,128)S(1)} %get-tuple-element.32), channel_id=1, source_target_pairs={{0,12},{4,0},{8,4},{12,8},{1,13},{5,1},{9,5},{13,9},{2,14},{6,2},{... | collective-permute-start | bytes 196616 | tf_op jit(solution)/shard_map/ppermute | solution.py:37
  72.0 7.0 %collective-permute-start.25 = (f32[128,128]{1,0:T(8,128)S(1)}, f32[128,128]{1,0:T(8,128)S(1)}, u32[]{:S(2)}, u32[]{:S(2)}) collective-permute-start(f32[128,128]{1,0:T(8,128)S(1)} %get-tuple-element.32), channel_id=1, source_target_pairs={{0,8},{4,12},{8,0},{12,4},{1,9},{5,13},{9,1},{13,5},{2,10},{6,14},... | collective-permute-start | bytes 196616 | tf_op jit(solution)/shard_map/ppermute | solution.py:37
  79.8 10.3 %all-to-all-start.2 = ((f32[16,4,128]{2,1,0:T(4,128)}), f32[16,4,128]{2,1,0:T(4,128)S(1)}, u32[]{:S(2)}, u32[]{:S(2)}) async-start(f32[16,4,128]{2,1,0:T(4,128)} %broadcast_in_dim.31), calls=%async_computation.2 | async-start | bytes 65536 | tf_op jit(solution)/shard_map/all_to_all | solution.py:16
  83.3 6.8 %collective-permute-start.29 = (f32[128,128]{1,0:T(8,128)S(1)}, f32[128,128]{1,0:T(8,128)S(1)}, u32[]{:S(2)}, u32[]{:S(2)}) collective-permute-start(f32[128,128]{1,0:T(8,128)S(1)} %get-tuple-element.39), channel_id=1, source_target_pairs={{0,12},{4,0},{8,4},{12,8},{1,13},{5,1},{9,5},{13,9},{2,14},{6,2},{... | collective-permute-start | bytes 196616 | tf_op jit(solution)/shard_map/ppermute | solution.py:27
  87.0 7.2 %collective-permute-start.28 = (f32[128,128]{1,0:T(8,128)S(1)}, f32[128,128]{1,0:T(8,128)S(1)}, u32[]{:S(2)}, u32[]{:S(2)}) collective-permute-start(f32[128,128]{1,0:T(8,128)S(1)} %get-tuple-element.40), channel_id=1, source_target_pairs={{0,8},{4,12},{8,0},{12,4},{1,9},{5,13},{9,1},{13,5},{2,10},{6,14},... | collective-permute-start | bytes 196616 | tf_op jit(solution)/shard_map/ppermute | solution.py:27
  87.1 7.2 %collective-permute-start.27 = (f32[128,128]{1,0:T(8,128)S(1)}, f32[128,128]{1,0:T(8,128)S(1)}, u32[]{:S(2)}, u32[]{:S(2)}) collective-permute-start(f32[128,128]{1,0:T(8,128)S(1)} %get-tuple-element.38), channel_id=1, source_target_pairs={{0,4},{4,8},{8,12},{12,0},{1,5},{5,9},{9,13},{13,1},{2,6},{6,10},{... | collective-permute-start | bytes 196616 | tf_op jit(solution)/shard_map/ppermute | solution.py:27

commit v4 on v3

--- a/solution.py
+++ b/solution.py
@@ -53,42 +53,54 @@
     n_narrow = lax.axis_size("narrow")
     n_all = n_wide * n_narrow
     width = SEED_CLASSES
+    column_blocks = n_narrow * br_local
     local_column = pattern // groups * br_local + pattern % br_local
-    entries = jnp.arange(n_narrow, dtype=local_column.dtype)
-    pick = local_column[:, :, None] == source("narrow", n_narrow, entries)[None, None, :]
+    pick = local_column[:, :, None] == jnp.arange(column_blocks, dtype=local_column.dtype)
     dense = jnp.sum(
         jnp.where(pick[:, :, None, :, None], tiles[:, :, :, None, :], 0.0), axis=1
-    ).reshape(groups * tile, n_narrow * own_rows)
+    )
+    column_sums = jnp.sum(dense, axis=(0, 1)).reshape(n_narrow, own_rows)
+    degree = scatter_sum(column_sums, "narrow", n_narrow)
+    order = source("wide", n_wide, jnp.arange(n_wide))
+    dense = jnp.take(dense.reshape(n_wide, own_rows, column_blocks * tile), order, axis=0)
+    transposed = dense.reshape(groups * tile, column_blocks * tile).T
 
-    row_sums = jnp.sum(tiles, axis=(1, 3))
-    degree = scatter_sum(row_sums.reshape(n_wide, own_rows), "wide", n_wide).reshape(own_rows)
-    seeded = (seed_label[:, 0] < SEED_CLASSES).astype(jnp.float32)
+    labels = seed_label[:, 0]
+    seeded = (labels < SEED_CLASSES).astype(jnp.float32)
     diag_column = (degree + SEED_WEIGHT * seeded + PRIOR)[:, None]
+    classes = jnp.arange(SEED_CLASSES, dtype=jnp.int32)
 
-    def product(values):
-        gathered = gather_blocks(values, "narrow", n_narrow).reshape(n_narrow * own_rows, width)
-        rows = gather_blocks(values, "wide", n_wide)
-        partial = jnp.dot(dense, gathered, precision=lax.Precision.HIGHEST)
-        partial = partial.reshape(n_wide, own_rows, width)
+    def indicator(values):
+        return SEED_WEIGHT * (values[..., None] == classes).astype(jnp.float32)
+
+    def product(row_values, column_values):
+        partial = jnp.dot(
+            transposed, row_values.reshape(groups * tile, width), precision=lax.Precision.HIGHEST
+        ).reshape(n_narrow, own_rows, width)
         quad = jnp.zeros((width,), jnp.float32)
-        for entry in range(n_wide):
+        for entry in range(n_narrow):
             block = lax.dynamic_index_in_dim(
-                partial, source("wide", n_wide, entry), 0, keepdims=False
+                partial, source("narrow", n_narrow, entry), 0, keepdims=False
             )
-            quad = quad + jnp.sum(rows[entry] * block, axis=0)
-        return scatter_sum(partial, "wide", n_wide), quad
+            quad = quad + jnp.sum(column_values[entry] * block, axis=0)
+        return scatter_sum(partial, "narrow", n_narrow), quad
+
+    def product_of(values):
+        return product(
+            gather_blocks(values, "wide", n_wide), gather_blocks(values, "narrow", n_narrow)
+        )
 
     def reduce_dots(values):
         return sum_over(values, ("wide", "narrow"), n_all)
 
-    labels = seed_label[:, 0]
-    rhs = SEED_WEIGHT * (
-        labels[:, None] == jnp.arange(SEED_CLASSES, dtype=jnp.int32)[None, :]
-    ).astype(jnp.float32)
+    rhs = indicator(labels)
     solution = jnp.zeros_like(rhs)
     residual = rhs
     direction = rhs
-    weighted, quad = product(direction)
+    weighted, quad = product(
+        indicator(gather_blocks(labels, "wide", n_wide)),
+        indicator(gather_blocks(labels, "narrow", n_narrow)),
+    )
     image = diag_column * direction - weighted
     first = reduce_dots(
         jnp.stack(
@@ -106,7 +118,7 @@
         residual = residual - alpha * image
         if step == ITERS - 1:
             break
-        weighted_residual, quad = product(residual)
+        weighted_residual, quad = product_of(residual)
         sums = reduce_dots(
             jnp.stack(
                 [

time: 95.3 us -> 80.4 us (0.84)
  waiting for transfers between devices: 36.5 us -> 20.1 us
  local copies, waits for them, and re-layouts: 1.95 us -> 3.17 us
    ppermute x12, waiting for transfers between devices: 14.1 us -> 0.03 us  [scatter_sum(): total = total + lax.ppermute(sent, axis, pairs)]
    ppermute x12, starting transfers between devices: 19.2 us -> 8.43 us  [scatter_sum(): total = total + lax.ppermute(sent, axis, pairs)]
    ppermute x18, waiting for transfers between devices: 16.9 us -> 6.97 us  [gather_blocks(): parts.append(lax.ppermute(values, axis, pairs))]
    all_to_all x3, waiting for transfers between devices: 5.5 us -> 13.1 us  [sum_over(): return jnp.sum(lax.all_to_all(spread, axes, 0, 0, tiled=True), axis=0)]
    ppermute x18, starting transfers between devices: 17.1 us -> 23.2 us  [gather_blocks(): parts.append(lax.ppermute(values, axis, pairs))]
    all_to_all x3, starting transfers between devices: 11.2 us -> 15.4 us  [sum_over(): return jnp.sum(lax.all_to_all(spread, axes, 0, 0, tiled=True), axis=0)]
    reduce_sum x5 -> x4, other arithmetic: 2.93 us -> 3.3 us  [the longest x1 2.94 us: local(): column_sums = jnp.sum(dense, axis=(0, 1)).reshape(n_narrow, own_rows)]
  transfers between devices with their start and end apart: 33 -> 33, of which waited for: 18 -> 12; matrix products, arithmetic and copies ran while one was open for 6% -> 9% of each run, Pallas kernels for 0% -> 0%
where the time goes in v4:
time: 80.4 us; the launch traced here: 80 us
  starting transfers between devices  47 us (58%)
  waiting for transfers between devices  20.1 us (25%)
  other arithmetic  5.65 us (7%)
  local copies, waits for them, and re-layouts  3.17 us (4%)
  matrix products  3.03 us (4%)
  between operations  1.1 us (1%)
    ppermute x18, starting transfers between devices, gather_blocks(): parts.append(lax.ppermute(values, axis, pairs))  23.2 us
    all_to_all x3, starting transfers between devices, sum_over(): return jnp.sum(lax.all_to_all(spread, axes, 0, 0, tiled=True), axis=0)  15.4 us
    all_to_all x3, waiting for transfers between devices, sum_over(): return jnp.sum(lax.all_to_all(spread, axes, 0, 0, tiled=True), axis=0)  13.1 us
    ppermute x12, starting transfers between devices, scatter_sum(): total = total + lax.ppermute(sent, axis, pairs)  8.43 us
    ppermute x18, waiting for transfers between devices, gather_blocks(): parts.append(lax.ppermute(values, axis, pairs))  6.97 us
    dot_general x3, matrix products, product(): jnp.dot(transposed, row_values.reshape(groups * tile, width), precision=l...  3.03 us
    reduce_sum x1, other arithmetic, local(): column_sums = jnp.sum(dense, axis=(0, 1)).reshape(n_narrow, own_rows)  2.94 us
    broadcast_in_dim x3, local copies, waits for them, and re-layouts, sum_over(): spread = jnp.broadcast_to(values[None], (count,) + values.shape)  1.85 us
  transfers between devices with their start and end apart: 33, of which 12 were waited for; matrix products, arithmetic and copies ran while one was open for 9% of the time, Pallas kernels for 0%

profile of v4, /device:TPU:0, one launch (start us, length us, event | category | flops | bytes accessed | tf_op | source)
XLA Modules:
  0.0 80.0 jit_solution(7545192140568131683)
XLA Ops:
  0.6 5.1 %collective-permute-start.8 = (s32[128]{0:T(128)}, s32[128]{0:T(128)S(1)}, u32[]{:S(2)}, u32[]{:S(2)}) collective-permute-start(s32[128]{0:T(128)} %bitcast.179), channel_id=1, source_target_pairs={{0,12},{4,0},{8,4},{12,8},{1,13},{5,1},{9,5},{13,9},{2,14},{6,2},{... | collective-permute-start | bytes 1544 | tf_op jit(solution)/shard_map/ppermute | solution.py:37
  5.7 0.7 add_select_fusion
  6.4 0.1 iota_compare_fusion.4
  6.5 2.9 %select_reduce_fusion.1 = (f32[4,128]{1,0:T(4,128)S(1)}, f32[4,128,4,128]{3,1,2,0:T(8,128)S(1)}) fusion(f32[4,8,128,128]{3,2,1,0:T(8,128)} %param.3, pred[4,8,4]{2,1,0:T(8,128)(4,1)S(1)} %iota_compare_fusion.4), kind=kLoop, calls=%fused_computation.2 | loop fusion | flops 6028800 | bytes 3147904 | tf_op jit(solution)/shard_map/reduce_sum | solution.py:62
  9.5 0.7 collective-permute-start.2
  10.2 0.9 %collective-permute-start.1 = (f32[128]{0:T(128)S(1)}, f32[128]{0:T(128)S(1)}, u32[]{:S(2)}, u32[]{:S(2)}) collective-permute-start(f32[128]{0:T(128)S(1)} %get-tuple-element.57), channel_id=1, source_target_pairs={{0,2},{1,3},{2,0},{3,1},{4,6},{5,7},{6,4},{7,5},{8,10},{9,11},{10,... | collective-permute-start | bytes 1544 | tf_op jit(solution)/shard_map/ppermute | solution.py:27
  11.1 0.2 collective-permute-start
  11.4 0.1 copy_bitcast_fusion
  11.5 0.1 broadcast_bitcast_fusion
  11.6 0.6 gather_fusion
  12.2 0.0 copy-start
  12.2 0.1 bitcast_select_fusion
  12.4 0.3 copy.9
  12.8 0.1 copy-done
  12.9 1.0 %collective-permute-start.6 = (s32[128]{0:T(128)S(1)}, s32[128]{0:T(128)S(1)}, u32[]{:S(2)}, u32[]{:S(2)}) collective-permute-start(s32[128]{0:T(128)S(1)} %bitcast.181), channel_id=1, source_target_pairs={{0,4},{4,8},{8,12},{12,0},{1,5},{5,9},{9,13},{13,1},{2,6},{6,10},{... | collective-permute-start | bytes 1544 | tf_op jit(solution)/shard_map/ppermute | solution.py:37
  13.9 1.3 %collective-permute-start.5 = (s32[128]{0:T(128)S(1)}, s32[128]{0:T(128)S(1)}, u32[]{:S(2)}, u32[]{:S(2)}) collective-permute-start(s32[128]{0:T(128)S(1)} %bitcast.182), channel_id=1, source_target_pairs={{0,3},{1,0},{2,1},{3,2},{4,7},{5,4},{6,5},{7,6},{8,11},{9,8},{10,9... | collective-permute-start | bytes 1544 | tf_op jit(solution)/shard_map/ppermute | solution.py:37
  15.2 0.8 %collective-permute-start.4 = (s32[128]{0:T(128)S(1)}, s32[128]{0:T(128)S(1)}, u32[]{:S(2)}, u32[]{:S(2)}) collective-permute-start(s32[128]{0:T(128)S(1)} %bitcast.183), channel_id=1, source_target_pairs={{0,2},{1,3},{2,0},{3,1},{4,6},{5,7},{6,4},{7,5},{8,10},{9,11},{10,... | collective-permute-start | bytes 1544 | tf_op jit(solution)/shard_map/ppermute | solution.py:37
  16.0 0.1 collective-permute-start.3
  16.1 0.1 fusion.10
  16.2 2.0 %collective-permute-done.6 = s32[128]{0:T(128)S(1)} collective-permute-done((s32[128]{0:T(128)S(1)}, s32[128]{0:T(128)S(1)}, u32[]{:S(2)}, u32[]{:S(2)}) %collective-permute-start.6) | collective-permute-done | bytes 544 | tf_op jit(solution)/shard_map/ppermute | solution.py:37
  18.2 0.5 collective-permute-done.4
  18.7 0.3 collective-permute-done.3
  19.1 0.1 fusion.3
  19.2 1.1 %fusion = f32[4,128,128]{2,1,0:T(8,128)S(1)} fusion(f32[4,128,512]{2,1,0:T(8,128)S(1)} %bitcast.165, s32[512]{0:T(512)S(1)} %get-tuple-element.58), kind=kOutput, calls=%fused_computation.7 | convolution fusion | flops 402784256 | bytes 1312768 | tf_op jit(solution)/shard_map/dot_general | solution.py:77
  20.3 0.1 dynamic-slice_bitcast_fusion.8
  20.4 0.6 broadcast_in_dim.47
  21.0 4.8 %all-to-all-start = ((f32[16,2,128]{2,1,0:T(2,128)}), f32[16,2,128]{2,1,0:T(2,128)S(1)}, u32[]{:S(2)}, u32[]{:S(2)}) async-start(f32[16,2,128]{2,1,0:T(2,128)} %broadcast_in_dim.47), calls=%async_computation | async-start | bytes 32768 | tf_op jit(solution)/shard_map/all_to_all | solution.py:16
  25.8 1.7 %collective-permute-start.11 = (f32[128,128]{1,0:T(8,128)S(1)}, f32[128,128]{1,0:T(8,128)S(1)}, u32[]{:S(2)}, u32[]{:S(2)}) collective-permute-start(f32[128,128]{1,0:T(8,128)S(1)} %get-tuple-element.47), channel_id=1, source_target_pairs={{0,3},{1,0},{2,1},{3,2},{4,7},{5,4},{6,5},{7,6},{8,11},{9,8},{10,9... | collective-permute-start | bytes 196616 | tf_op jit(solution)/shard_map/ppermute | solution.py:27
  27.5 0.4 collective-permute-start.10
  27.9 0.1 collective-permute-start.9
  28.0 4.3 %all-to-all-done = f32[16,2,128]{2,1,0:T(2,128)S(1)} async-done(((f32[16,2,128]{2,1,0:T(2,128)}), f32[16,2,128]{2,1,0:T(2,128)S(1)}, u32[]{:S(2)}, u32[]{:S(2)}) %all-to-all-start) | async-done | bytes 16416 | tf_op jit(solution)/shard_map/all_to_all | solution.py:16
  32.4 0.1 select_subtract_fusion
  32.5 3.4 %collective-permute-start.14 = (f32[128,128]{1,0:T(8,128)S(1)}, f32[128,128]{1,0:T(8,128)S(1)}, u32[]{:S(2)}, u32[]{:S(2)}) collective-permute-start(f32[128,128]{1,0:T(8,128)S(1)} %get-tuple-element.38), channel_id=1, source_target_pairs={{0,12},{4,0},{8,4},{12,8},{1,13},{5,1},{9,5},{13,9},{2,14},{6,2},{... | collective-permute-start | bytes 196616 | tf_op jit(solution)/shard_map/ppermute | solution.py:37
  35.9 1.1 %collective-permute-start.12 = (f32[128,128]{1,0:T(8,128)S(1)}, f32[128,128]{1,0:T(8,128)S(1)}, u32[]{:S(2)}, u32[]{:S(2)}) collective-permute-start(f32[128,128]{1,0:T(8,128)S(1)} %get-tuple-element.38), channel_id=1, source_target_pairs={{0,4},{4,8},{8,12},{12,0},{1,5},{5,9},{9,13},{13,1},{2,6},{6,10},{... | collective-permute-start | bytes 196616 | tf_op jit(solution)/shard_map/ppermute | solution.py:37
  37.0 1.7 %collective-permute-start.17 = (f32[128,128]{1,0:T(8,128)S(1)}, f32[128,128]{1,0:T(8,128)S(1)}, u32[]{:S(2)}, u32[]{:S(2)}) collective-permute-start(f32[128,128]{1,0:T(8,128)S(1)} %get-tuple-element.38), channel_id=1, source_target_pairs={{0,3},{1,0},{2,1},{3,2},{4,7},{5,4},{6,5},{7,6},{8,11},{9,8},{10,9... | collective-permute-start | bytes 196616 | tf_op jit(solution)/shard_map/ppermute | solution.py:37
  38.8 1.2 %collective-permute-start.16 = (f32[128,128]{1,0:T(8,128)S(1)}, f32[128,128]{1,0:T(8,128)S(1)}, u32[]{:S(2)}, u32[]{:S(2)}) collective-permute-start(f32[128,128]{1,0:T(8,128)S(1)} %get-tuple-element.38), channel_id=1, source_target_pairs={{0,2},{1,3},{2,0},{3,1},{4,6},{5,7},{6,4},{7,5},{8,10},{9,11},{10,... | collective-permute-start | bytes 196616 | tf_op jit(solution)/shard_map/ppermute | solution.py:37
  40.0 1.2 %collective-permute-done.13 = f32[128,128]{1,0:T(8,128)S(1)} collective-permute-done((f32[128,128]{1,0:T(8,128)S(1)}, f32[128,128]{1,0:T(8,128)S(1)}, u32[]{:S(2)}, u32[]{:S(2)}) %collective-permute-start.13) | collective-permute-done | bytes 65568 | tf_op jit(solution)/shard_map/ppermute | solution.py:37
  41.2 0.8 collective-permute-done.12
  42.0 1.0 %fusion.65 = f32[4,128,128]{2,1,0:T(8,128)S(1)} fusion(f32[4,128,512]{2,1,0:T(8,128)S(1)} %bitcast.166, f32[512,128,1]{1,0,2:T(8,128)S(1)} %bitcast.172), kind=kOutput, calls=%fused_computation.149 | convolution fusion | flops 402653184 | bytes 1572864 | tf_op jit(solution)/shard_map/dot_general | solution.py:77
  43.0 0.1 collective-permute-done.16
  43.1 0.1 fusion.35
  43.2 0.6 broadcast_in_dim.48
  43.9 5.3 %all-to-all-start.1 = ((f32[16,4,128]{2,1,0:T(4,128)}), f32[16,4,128]{2,1,0:T(4,128)S(1)}, u32[]{:S(2)}, u32[]{:S(2)}) async-start(f32[16,4,128]{2,1,0:T(4,128)} %broadcast_in_dim.48), calls=%async_computation.1 | async-start | bytes 65536 | tf_op jit(solution)/shard_map/all_to_all | solution.py:16
  49.2 1.7 %collective-permute-start.20 = (f32[128,128]{1,0:T(8,128)S(1)}, f32[128,128]{1,0:T(8,128)S(1)}, u32[]{:S(2)}, u32[]{:S(2)}) collective-permute-start(f32[128,128]{1,0:T(8,128)S(1)} %get-tuple-element.44), channel_id=1, source_target_pairs={{0,3},{1,0},{2,1},{3,2},{4,7},{5,4},{6,5},{7,6},{8,11},{9,8},{10,9... | collective-permute-start | bytes 196616 | tf_op jit(solution)/shard_map/ppermute | solution.py:27
  50.9 0.4 collective-permute-start.19
  51.2 0.1 collective-permute-start.18
  51.4 4.4 %all-to-all-done.1 = f32[16,4,128]{2,1,0:T(4,128)S(1)} async-done(((f32[16,4,128]{2,1,0:T(4,128)}), f32[16,4,128]{2,1,0:T(4,128)S(1)}, u32[]{:S(2)}, u32[]{:S(2)}) %all-to-all-start.1) | async-done | bytes 32800 | tf_op jit(solution)/shard_map/all_to_all | solution.py:16
  55.8 0.1 multiply_subtract_fusion
  56.0 3.3 %collective-permute-start.23 = (f32[128,128]{1,0:T(8,128)S(1)}, f32[128,128]{1,0:T(8,128)S(1)}, u32[]{:S(2)}, u32[]{:S(2)}) collective-permute-start(f32[128,128]{1,0:T(8,128)S(1)} %get-tuple-element.34), channel_id=1, source_target_pairs={{0,12},{4,0},{8,4},{12,8},{1,13},{5,1},{9,5},{13,9},{2,14},{6,2},{... | collective-permute-start | bytes 196616 | tf_op jit(solution)/shard_map/ppermute | solution.py:37
  59.3 1.1 %collective-permute-start.21 = (f32[128,128]{1,0:T(8,128)S(1)}, f32[128,128]{1,0:T(8,128)S(1)}, u32[]{:S(2)}, u32[]{:S(2)}) collective-permute-start(f32[128,128]{1,0:T(8,128)S(1)} %get-tuple-element.34), channel_id=1, source_target_pairs={{0,4},{4,8},{8,12},{12,0},{1,5},{5,9},{9,13},{13,1},{2,6},{6,10},{... | collective-permute-start | bytes 196616 | tf_op jit(solution)/shard_map/ppermute | solution.py:37
  60.4 1.7 %collective-permute-start.26 = (f32[128,128]{1,0:T(8,128)S(1)}, f32[128,128]{1,0:T(8,128)S(1)}, u32[]{:S(2)}, u32[]{:S(2)}) collective-permute-start(f32[128,128]{1,0:T(8,128)S(1)} %get-tuple-element.34), channel_id=1, source_target_pairs={{0,3},{1,0},{2,1},{3,2},{4,7},{5,4},{6,5},{7,6},{8,11},{9,8},{10,9... | collective-permute-start | bytes 196616 | tf_op jit(solution)/shard_map/ppermute | solution.py:37
  62.2 1.2 %collective-permute-start.25 = (f32[128,128]{1,0:T(8,128)S(1)}, f32[128,128]{1,0:T(8,128)S(1)}, u32[]{:S(2)}, u32[]{:S(2)}) collective-permute-start(f32[128,128]{1,0:T(8,128)S(1)} %get-tuple-element.34), channel_id=1, source_target_pairs={{0,2},{1,3},{2,0},{3,1},{4,6},{5,7},{6,4},{7,5},{8,10},{9,11},{10,... | collective-permute-start | bytes 196616 | tf_op jit(solution)/shard_map/ppermute | solution.py:37
  63.4 1.2 %collective-permute-done.22 = f32[128,128]{1,0:T(8,128)S(1)} collective-permute-done((f32[128,128]{1,0:T(8,128)S(1)}, f32[128,128]{1,0:T(8,128)S(1)}, u32[]{:S(2)}, u32[]{:S(2)}) %collective-permute-start.22) | collective-permute-done | bytes 65568 | tf_op jit(solution)/shard_map/ppermute | solution.py:37
  64.6 0.8 collective-permute-done.21
  65.4 1.0 %fusion.66 = f32[4,128,128]{2,1,0:T(8,128)S(1)} fusion(f32[4,128,512]{2,1,0:T(8,128)S(1)} %bitcast.167, f32[512,128,1]{1,0,2:T(8,128)S(1)} %bitcast.171), kind=kOutput, calls=%fused_computation.150 | convolution fusion | flops 402653184 | bytes 1572864 | tf_op jit(solution)/shard_map/dot_general | solution.py:77
  66.4 0.1 collective-permute-done.25
  66.5 0.1 fusion.28
  66.7 0.6 broadcast_in_dim.49
  67.3 5.3 %all-to-all-start.2 = ((f32[16,4,128]{2,1,0:T(4,128)}), f32[16,4,128]{2,1,0:T(4,128)S(1)}, u32[]{:S(2)}, u32[]{:S(2)}) async-start(f32[16,4,128]{2,1,0:T(4,128)} %broadcast_in_dim.49), calls=%async_computation.2 | async-start | bytes 65536 | tf_op jit(solution)/shard_map/all_to_all | solution.py:16
  72.6 1.7 %collective-permute-start.29 = (f32[128,128]{1,0:T(8,128)S(1)}, f32[128,128]{1,0:T(8,128)S(1)}, u32[]{:S(2)}, u32[]{:S(2)}) collective-permute-start(f32[128,128]{1,0:T(8,128)S(1)} %get-tuple-element.41), channel_id=1, source_target_pairs={{0,3},{1,0},{2,1},{3,2},{4,7},{5,4},{6,5},{7,6},{8,11},{9,8},{10,9... | collective-permute-start | bytes 196616 | tf_op jit(solution)/shard_map/ppermute | solution.py:27
  74.3 0.4 collective-permute-start.28
  74.6 0.1 collective-permute-start.27
  74.8 4.4 %all-to-all-done.2 = f32[16,4,128]{2,1,0:T(4,128)S(1)} async-done(((f32[16,4,128]{2,1,0:T(4,128)}), f32[16,4,128]{2,1,0:T(4,128)S(1)}, u32[]{:S(2)}, u32[]{:S(2)}) %all-to-all-start.2) | async-done | bytes 32800 | tf_op jit(solution)/shard_map/all_to_all | solution.py:16
  79.2 0.8 fusion.25
  (48 shorter events, 0.4 us)
Async XLA Ops:
  0.6 15.4 %collective-permute-start.8 = (s32[128]{0:T(128)}, s32[128]{0:T(128)S(1)}, u32[]{:S(2)}, u32[]{:S(2)}) collective-permute-start(s32[128]{0:T(128)} %bitcast.179), channel_id=1, source_target_pairs={{0,12},{4,0},{8,4},{12,8},{1,13},{5,1},{9,5},{13,9},{2,14},{6,2},{... | collective-permute-start | bytes 1544 | tf_op jit(solution)/shard_map/ppermute | solution.py:37
  5.7 10.5 %collective-permute-start.7 = (s32[128]{0:T(128)}, s32[128]{0:T(128)S(1)}, u32[]{:S(2)}, u32[]{:S(2)}) collective-permute-start(s32[128]{0:T(128)} %bitcast.180), channel_id=1, source_target_pairs={{0,8},{4,12},{8,0},{12,4},{1,9},{5,13},{9,1},{13,5},{2,10},{6,14},... | collective-permute-start | bytes 1544 | tf_op jit(solution)/shard_map/ppermute | solution.py:37
  9.5 3.3 %collective-permute-start.2 = (f32[128]{0:T(128)S(1)}, f32[128]{0:T(128)S(1)}, u32[]{:S(2)}, u32[]{:S(2)}) collective-permute-start(f32[128]{0:T(128)S(1)} %get-tuple-element.56), channel_id=1, source_target_pairs={{0,3},{1,0},{2,1},{3,2},{4,7},{5,4},{6,5},{7,6},{8,11},{9,8},{10,9... | collective-permute-start | bytes 1544 | tf_op jit(solution)/shard_map/ppermute | solution.py:27
  10.2 3.7 %collective-permute-start.1 = (f32[128]{0:T(128)S(1)}, f32[128]{0:T(128)S(1)}, u32[]{:S(2)}, u32[]{:S(2)}) collective-permute-start(f32[128]{0:T(128)S(1)} %get-tuple-element.57), channel_id=1, source_target_pairs={{0,2},{1,3},{2,0},{3,1},{4,6},{5,7},{6,4},{7,5},{8,10},{9,11},{10,... | collective-permute-start | bytes 1544 | tf_op jit(solution)/shard_map/ppermute | solution.py:27
  11.1 4.1 %collective-permute-start = (f32[128]{0:T(128)S(1)}, f32[128]{0:T(128)S(1)}, u32[]{:S(2)}, u32[]{:S(2)}) collective-permute-start(f32[128]{0:T(128)S(1)} %get-tuple-element.55), channel_id=1, source_target_pairs={{0,1},{1,2},{2,3},{3,0},{4,5},{5,6},{6,7},{7,4},{8,9},{9,10},{10,1... | collective-permute-start | bytes 1544 | tf_op jit(solution)/shard_map/ppermute | solution.py:27
  12.2 0.7 copy-start
  12.9 5.3 %collective-permute-start.6 = (s32[128]{0:T(128)S(1)}, s32[128]{0:T(128)S(1)}, u32[]{:S(2)}, u32[]{:S(2)}) collective-permute-start(s32[128]{0:T(128)S(1)} %bitcast.181), channel_id=1, source_target_pairs={{0,4},{4,8},{8,12},{12,0},{1,5},{5,9},{9,13},{13,1},{2,6},{6,10},{... | collective-permute-start | bytes 1544 | tf_op jit(solution)/shard_map/ppermute | solution.py:37
  13.9 4.3 %collective-permute-start.5 = (s32[128]{0:T(128)S(1)}, s32[128]{0:T(128)S(1)}, u32[]{:S(2)}, u32[]{:S(2)}) collective-permute-start(s32[128]{0:T(128)S(1)} %bitcast.182), channel_id=1, source_target_pairs={{0,3},{1,0},{2,1},{3,2},{4,7},{5,4},{6,5},{7,6},{8,11},{9,8},{10,9... | collective-permute-start | bytes 1544 | tf_op jit(solution)/shard_map/ppermute | solution.py:37
  15.2 3.5 %collective-permute-start.4 = (s32[128]{0:T(128)S(1)}, s32[128]{0:T(128)S(1)}, u32[]{:S(2)}, u32[]{:S(2)}) collective-permute-start(s32[128]{0:T(128)S(1)} %bitcast.183), channel_id=1, source_target_pairs={{0,2},{1,3},{2,0},{3,1},{4,6},{5,7},{6,4},{7,5},{8,10},{9,11},{10,... | collective-permute-start | bytes 1544 | tf_op jit(solution)/shard_map/ppermute | solution.py:37
  16.0 3.0 %collective-permute-start.3 = (s32[128]{0:T(128)S(1)}, s32[128]{0:T(128)S(1)}, u32[]{:S(2)}, u32[]{:S(2)}) collective-permute-start(s32[128]{0:T(128)S(1)} %bitcast.184), channel_id=1, source_target_pairs={{0,1},{1,2},{2,3},{3,0},{4,5},{5,6},{6,7},{7,4},{8,9},{9,10},{10,1... | collective-permute-start | bytes 1544 | tf_op jit(solution)/shard_map/ppermute | solution.py:37
  21.0 11.3 %all-to-all-start = ((f32[16,2,128]{2,1,0:T(2,128)}), f32[16,2,128]{2,1,0:T(2,128)S(1)}, u32[]{:S(2)}, u32[]{:S(2)}) async-start(f32[16,2,128]{2,1,0:T(2,128)} %broadcast_in_dim.47), calls=%async_computation | async-start | bytes 32768 | tf_op jit(solution)/shard_map/all_to_all | solution.py:16
  25.8 6.5 %collective-permute-start.11 = (f32[128,128]{1,0:T(8,128)S(1)}, f32[128,128]{1,0:T(8,128)S(1)}, u32[]{:S(2)}, u32[]{:S(2)}) collective-permute-start(f32[128,128]{1,0:T(8,128)S(1)} %get-tuple-element.47), channel_id=1, source_target_pairs={{0,3},{1,0},{2,1},{3,2},{4,7},{5,4},{6,5},{7,6},{8,11},{9,8},{10,9... | collective-permute-start | bytes 196616 | tf_op jit(solution)/shard_map/ppermute | solution.py:27
  27.5 4.9 %collective-permute-start.10 = (f32[128,128]{1,0:T(8,128)S(1)}, f32[128,128]{1,0:T(8,128)S(1)}, u32[]{:S(2)}, u32[]{:S(2)}) collective-permute-start(f32[128,128]{1,0:T(8,128)S(1)} %get-tuple-element.48), channel_id=1, source_target_pairs={{0,2},{1,3},{2,0},{3,1},{4,6},{5,7},{6,4},{7,5},{8,10},{9,11},{10,... | collective-permute-start | bytes 196616 | tf_op jit(solution)/shard_map/ppermute | solution.py:27
  27.9 4.5 %collective-permute-start.9 = (f32[128,128]{1,0:T(8,128)S(1)}, f32[128,128]{1,0:T(8,128)S(1)}, u32[]{:S(2)}, u32[]{:S(2)}) collective-permute-start(f32[128,128]{1,0:T(8,128)S(1)} %get-tuple-element.46), channel_id=1, source_target_pairs={{0,1},{1,2},{2,3},{3,0},{4,5},{5,6},{6,7},{7,4},{8,9},{9,10},{10,1... | collective-permute-start | bytes 196616 | tf_op jit(solution)/shard_map/ppermute | solution.py:27
  32.5 6.3 %collective-permute-start.14 = (f32[128,128]{1,0:T(8,128)S(1)}, f32[128,128]{1,0:T(8,128)S(1)}, u32[]{:S(2)}, u32[]{:S(2)}) collective-permute-start(f32[128,128]{1,0:T(8,128)S(1)} %get-tuple-element.38), channel_id=1, source_target_pairs={{0,12},{4,0},{8,4},{12,8},{1,13},{5,1},{9,5},{13,9},{2,14},{6,2},{... | collective-permute-start | bytes 196616 | tf_op jit(solution)/shard_map/ppermute | solution.py:37
  35.9 5.3 %collective-permute-start.13 = (f32[128,128]{1,0:T(8,128)S(1)}, f32[128,128]{1,0:T(8,128)S(1)}, u32[]{:S(2)}, u32[]{:S(2)}) collective-permute-start(f32[128,128]{1,0:T(8,128)S(1)} %get-tuple-element.38), channel_id=1, source_target_pairs={{0,8},{4,12},{8,0},{12,4},{1,9},{5,13},{9,1},{13,5},{2,10},{6,14},... | collective-permute-start | bytes 196616 | tf_op jit(solution)/shard_map/ppermute | solution.py:37
  35.9 6.1 %collective-permute-start.12 = (f32[128,128]{1,0:T(8,128)S(1)}, f32[128,128]{1,0:T(8,128)S(1)}, u32[]{:S(2)}, u32[]{:S(2)}) collective-permute-start(f32[128,128]{1,0:T(8,128)S(1)} %get-tuple-element.38), channel_id=1, source_target_pairs={{0,4},{4,8},{8,12},{12,0},{1,5},{5,9},{9,13},{13,1},{2,6},{6,10},{... | collective-permute-start | bytes 196616 | tf_op jit(solution)/shard_map/ppermute | solution.py:37
  37.0 6.0 %collective-permute-start.15 = (f32[128,128]{1,0:T(8,128)S(1)}, f32[128,128]{1,0:T(8,128)S(1)}, u32[]{:S(2)}, u32[]{:S(2)}) collective-permute-start(f32[128,128]{1,0:T(8,128)S(1)} %get-tuple-element.38), channel_id=1, source_target_pairs={{0,1},{1,2},{2,3},{3,0},{4,5},{5,6},{6,7},{7,4},{8,9},{9,10},{10,1... | collective-permute-start | bytes 196616 | tf_op jit(solution)/shard_map/ppermute | solution.py:37
  37.0 6.0 %collective-permute-start.17 = (f32[128,128]{1,0:T(8,128)S(1)}, f32[128,128]{1,0:T(8,128)S(1)}, u32[]{:S(2)}, u32[]{:S(2)}) collective-permute-start(f32[128,128]{1,0:T(8,128)S(1)} %get-tuple-element.38), channel_id=1, source_target_pairs={{0,3},{1,0},{2,1},{3,2},{4,7},{5,4},{6,5},{7,6},{8,11},{9,8},{10,9... | collective-permute-start | bytes 196616 | tf_op jit(solution)/shard_map/ppermute | solution.py:37
  38.8 4.3 %collective-permute-start.16 = (f32[128,128]{1,0:T(8,128)S(1)}, f32[128,128]{1,0:T(8,128)S(1)}, u32[]{:S(2)}, u32[]{:S(2)}) collective-permute-start(f32[128,128]{1,0:T(8,128)S(1)} %get-tuple-element.38), channel_id=1, source_target_pairs={{0,2},{1,3},{2,0},{3,1},{4,6},{5,7},{6,4},{7,5},{8,10},{9,11},{10,... | collective-permute-start | bytes 196616 | tf_op jit(solution)/shard_map/ppermute | solution.py:37
  43.9 11.9 %all-to-all-start.1 = ((f32[16,4,128]{2,1,0:T(4,128)}), f32[16,4,128]{2,1,0:T(4,128)S(1)}, u32[]{:S(2)}, u32[]{:S(2)}) async-start(f32[16,4,128]{2,1,0:T(4,128)} %broadcast_in_dim.48), calls=%async_computation.1 | async-start | bytes 65536 | tf_op jit(solution)/shard_map/all_to_all | solution.py:16
  49.2 6.6 %collective-permute-start.20 = (f32[128,128]{1,0:T(8,128)S(1)}, f32[128,128]{1,0:T(8,128)S(1)}, u32[]{:S(2)}, u32[]{:S(2)}) collective-permute-start(f32[128,128]{1,0:T(8,128)S(1)} %get-tuple-element.44), channel_id=1, source_target_pairs={{0,3},{1,0},{2,1},{3,2},{4,7},{5,4},{6,5},{7,6},{8,11},{9,8},{10,9... | collective-permute-start | bytes 196616 | tf_op jit(solution)/shard_map/ppermute | solution.py:27
  50.9 4.9 %collective-permute-start.19 = (f32[128,128]{1,0:T(8,128)S(1)}, f32[128,128]{1,0:T(8,128)S(1)}, u32[]{:S(2)}, u32[]{:S(2)}) collective-permute-start(f32[128,128]{1,0:T(8,128)S(1)} %get-tuple-element.45), channel_id=1, source_target_pairs={{0,2},{1,3},{2,0},{3,1},{4,6},{5,7},{6,4},{7,5},{8,10},{9,11},{10,... | collective-permute-start | bytes 196616 | tf_op jit(solution)/shard_map/ppermute | solution.py:27
  51.2 4.6 %collective-permute-start.18 = (f32[128,128]{1,0:T(8,128)S(1)}, f32[128,128]{1,0:T(8,128)S(1)}, u32[]{:S(2)}, u32[]{:S(2)}) collective-permute-start(f32[128,128]{1,0:T(8,128)S(1)} %get-tuple-element.43), channel_id=1, source_target_pairs={{0,1},{1,2},{2,3},{3,0},{4,5},{5,6},{6,7},{7,4},{8,9},{9,10},{10,1... | collective-permute-start | bytes 196616 | tf_op jit(solution)/shard_map/ppermute | solution.py:27
  56.0 6.2 %collective-permute-start.23 = (f32[128,128]{1,0:T(8,128)S(1)}, f32[128,128]{1,0:T(8,128)S(1)}, u32[]{:S(2)}, u32[]{:S(2)}) collective-permute-start(f32[128,128]{1,0:T(8,128)S(1)} %get-tuple-element.34), channel_id=1, source_target_pairs={{0,12},{4,0},{8,4},{12,8},{1,13},{5,1},{9,5},{13,9},{2,14},{6,2},{... | collective-permute-start | bytes 196616 | tf_op jit(solution)/shard_map/ppermute | solution.py:37
  59.3 5.3 %collective-permute-start.22 = (f32[128,128]{1,0:T(8,128)S(1)}, f32[128,128]{1,0:T(8,128)S(1)}, u32[]{:S(2)}, u32[]{:S(2)}) collective-permute-start(f32[128,128]{1,0:T(8,128)S(1)} %get-tuple-element.34), channel_id=1, source_target_pairs={{0,8},{4,12},{8,0},{12,4},{1,9},{5,13},{9,1},{13,5},{2,10},{6,14},... | collective-permute-start | bytes 196616 | tf_op jit(solution)/shard_map/ppermute | solution.py:37
  59.3 6.1 %collective-permute-start.21 = (f32[128,128]{1,0:T(8,128)S(1)}, f32[128,128]{1,0:T(8,128)S(1)}, u32[]{:S(2)}, u32[]{:S(2)}) collective-permute-start(f32[128,128]{1,0:T(8,128)S(1)} %get-tuple-element.34), channel_id=1, source_target_pairs={{0,4},{4,8},{8,12},{12,0},{1,5},{5,9},{9,13},{13,1},{2,6},{6,10},{... | collective-permute-start | bytes 196616 | tf_op jit(solution)/shard_map/ppermute | solution.py:37
  60.4 6.0 %collective-permute-start.24 = (f32[128,128]{1,0:T(8,128)S(1)}, f32[128,128]{1,0:T(8,128)S(1)}, u32[]{:S(2)}, u32[]{:S(2)}) collective-permute-start(f32[128,128]{1,0:T(8,128)S(1)} %get-tuple-element.34), channel_id=1, source_target_pairs={{0,1},{1,2},{2,3},{3,0},{4,5},{5,6},{6,7},{7,4},{8,9},{9,10},{10,1... | collective-permute-start | bytes 196616 | tf_op jit(solution)/shard_map/ppermute | solution.py:37
  60.4 6.0 %collective-permute-start.26 = (f32[128,128]{1,0:T(8,128)S(1)}, f32[128,128]{1,0:T(8,128)S(1)}, u32[]{:S(2)}, u32[]{:S(2)}) collective-permute-start(f32[128,128]{1,0:T(8,128)S(1)} %get-tuple-element.34), channel_id=1, source_target_pairs={{0,3},{1,0},{2,1},{3,2},{4,7},{5,4},{6,5},{7,6},{8,11},{9,8},{10,9... | collective-permute-start | bytes 196616 | tf_op jit(solution)/shard_map/ppermute | solution.py:37
  62.2 4.3 %collective-permute-start.25 = (f32[128,128]{1,0:T(8,128)S(1)}, f32[128,128]{1,0:T(8,128)S(1)}, u32[]{:S(2)}, u32[]{:S(2)}) collective-permute-start(f32[128,128]{1,0:T(8,128)S(1)} %get-tuple-element.34), channel_id=1, source_target_pairs={{0,2},{1,3},{2,0},{3,1},{4,6},{5,7},{6,4},{7,5},{8,10},{9,11},{10,... | collective-permute-start | bytes 196616 | tf_op jit(solution)/shard_map/ppermute | solution.py:37
  67.3 11.9 %all-to-all-start.2 = ((f32[16,4,128]{2,1,0:T(4,128)}), f32[16,4,128]{2,1,0:T(4,128)S(1)}, u32[]{:S(2)}, u32[]{:S(2)}) async-start(f32[16,4,128]{2,1,0:T(4,128)} %broadcast_in_dim.49), calls=%async_computation.2 | async-start | bytes 65536 | tf_op jit(solution)/shard_map/all_to_all | solution.py:16
  72.6 6.6 %collective-permute-start.29 = (f32[128,128]{1,0:T(8,128)S(1)}, f32[128,128]{1,0:T(8,128)S(1)}, u32[]{:S(2)}, u32[]{:S(2)}) collective-permute-start(f32[128,128]{1,0:T(8,128)S(1)} %get-tuple-element.41), channel_id=1, source_target_pairs={{0,3},{1,0},{2,1},{3,2},{4,7},{5,4},{6,5},{7,6},{8,11},{9,8},{10,9... | collective-permute-start | bytes 196616 | tf_op jit(solution)/shard_map/ppermute | solution.py:27
  74.3 4.9 %collective-permute-start.28 = (f32[128,128]{1,0:T(8,128)S(1)}, f32[128,128]{1,0:T(8,128)S(1)}, u32[]{:S(2)}, u32[]{:S(2)}) collective-permute-start(f32[128,128]{1,0:T(8,128)S(1)} %get-tuple-element.42), channel_id=1, source_target_pairs={{0,2},{1,3},{2,0},{3,1},{4,6},{5,7},{6,4},{7,5},{8,10},{9,11},{10,... | collective-permute-start | bytes 196616 | tf_op jit(solution)/shard_map/ppermute | solution.py:27
  74.6 4.6 %collective-permute-start.27 = (f32[128,128]{1,0:T(8,128)S(1)}, f32[128,128]{1,0:T(8,128)S(1)}, u32[]{:S(2)}, u32[]{:S(2)}) collective-permute-start(f32[128,128]{1,0:T(8,128)S(1)} %get-tuple-element.40), channel_id=1, source_target_pairs={{0,1},{1,2},{2,3},{3,0},{4,5},{5,6},{6,7},{7,4},{8,9},{9,10},{10,1... | collective-permute-start | bytes 196616 | tf_op jit(solution)/shard_map/ppermute | solution.py:27

commit v5 on v4

--- a/solution.py
+++ b/solution.py
@@ -73,22 +73,11 @@
     def indicator(values):
         return SEED_WEIGHT * (values[..., None] == classes).astype(jnp.float32)
 
-    def product(row_values, column_values):
+    def product(row_values):
         partial = jnp.dot(
             transposed, row_values.reshape(groups * tile, width), precision=lax.Precision.HIGHEST
         ).reshape(n_narrow, own_rows, width)
-        quad = jnp.zeros((width,), jnp.float32)
-        for entry in range(n_narrow):
-            block = lax.dynamic_index_in_dim(
-                partial, source("narrow", n_narrow, entry), 0, keepdims=False
-            )
-            quad = quad + jnp.sum(column_values[entry] * block, axis=0)
-        return scatter_sum(partial, "narrow", n_narrow), quad
-
-    def product_of(values):
-        return product(
-            gather_blocks(values, "wide", n_wide), gather_blocks(values, "narrow", n_narrow)
-        )
+        return scatter_sum(partial, "narrow", n_narrow)
 
     def reduce_dots(values):
         return sum_over(values, ("wide", "narrow"), n_all)
@@ -97,18 +86,11 @@
     solution = jnp.zeros_like(rhs)
     residual = rhs
     direction = rhs
-    weighted, quad = product(
-        indicator(gather_blocks(labels, "wide", n_wide)),
-        indicator(gather_blocks(labels, "narrow", n_narrow)),
-    )
-    image = diag_column * direction - weighted
+    rows_residual = indicator(gather_blocks(labels, "wide", n_wide))
+    image = diag_column * direction - product(rows_residual)
+    rows_image = gather_blocks(image, "wide", n_wide)
     first = reduce_dots(
-        jnp.stack(
-            [
-                jnp.sum(residual * residual, axis=0),
-                jnp.sum(diag_column * direction * direction, axis=0) - quad,
-            ]
-        )
+        jnp.stack([jnp.sum(residual * residual, axis=0), jnp.sum(direction * image, axis=0)])
     )
     norm_now = first[0]
     curvature = first[1]
@@ -118,12 +100,14 @@
         residual = residual - alpha * image
         if step == ITERS - 1:
             break
-        weighted_residual, quad = product_of(residual)
+        rows_residual = rows_residual - alpha * rows_image
+        applied = diag_column * residual - product(rows_residual)
+        rows_applied = gather_blocks(applied, "wide", n_wide)
         sums = reduce_dots(
             jnp.stack(
                 [
                     jnp.sum(residual * residual, axis=0),
-                    jnp.sum(diag_column * residual * residual, axis=0) - quad,
+                    jnp.sum(residual * applied, axis=0),
                     jnp.sum(residual * image, axis=0),
                     jnp.sum(direction * image, axis=0),
                 ]
@@ -133,8 +117,8 @@
         ratio = norm_next / norm_now
         curvature = sums[1] + ratio * (2.0 * sums[2] + ratio * sums[3])
         direction = residual + ratio * direction
-        weighted = weighted_residual + ratio * weighted
-        image = diag_column * direction - weighted
+        image = applied + ratio * image
+        rows_image = rows_applied + ratio * rows_image
         norm_now = norm_next
     return (solution, residual)
 

time: 80.4 us -> 78 us (0.970)
  starting transfers between devices: 47 us -> 31.3 us
  blocking collectives: 0 us -> 9.6 us
  waiting for transfers between devices: 20.1 us -> 24.9 us
    ppermute x12, waiting for transfers between devices: 0.03 us -> 13 us  [scatter_sum(): total = total + lax.ppermute(sent, axis, pairs)]
    all_to_all x0 -> x1, blocking collectives: none -> 9.6 us  [sum_over(): return jnp.sum(lax.all_to_all(spread, axes, 0, 0, tiled=True), axis=0)]
    all_to_all x3 -> x2, waiting for transfers between devices: 13.1 us -> 3.72 us  [sum_over(): return jnp.sum(lax.all_to_all(spread, axes, 0, 0, tiled=True), axis=0)]
    ppermute x18 -> x9, starting transfers between devices: 23.2 us -> 15.7 us  [gather_blocks(): parts.append(lax.ppermute(values, axis, pairs))]
    all_to_all x3 -> x2, starting transfers between devices: 15.4 us -> 8.06 us  [sum_over(): return jnp.sum(lax.all_to_all(spread, axes, 0, 0, tiled=True), axis=0)]
    ppermute x18 -> x9, waiting for transfers between devices: 6.97 us -> 8.22 us  [gather_blocks(): parts.append(lax.ppermute(values, axis, pairs))]
    ppermute x12, starting transfers between devices: 8.43 us -> 7.53 us  [scatter_sum(): total = total + lax.ppermute(sent, axis, pairs)]
  transfers between devices with their start and end apart: 33 -> 23, of which waited for: 12 -> 10; matrix products, arithmetic and copies ran while one was open for 9% -> 8% of each run, Pallas kernels for 0% -> 0%
where the time goes in v5:
time: 78 us; the launch traced here: 77.7 us
  starting transfers between devices  31.3 us (40%)
  waiting for transfers between devices  24.9 us (32%)
  blocking collectives  9.6 us (12%)
  other arithmetic  5.45 us (7%)
  matrix products  3.03 us (4%)
  local copies, waits for them, and re-layouts  2.48 us (3%)
  between operations  0.87 us (1%)
    ppermute x9, starting transfers between devices, gather_blocks(): parts.append(lax.ppermute(values, axis, pairs))  15.7 us
    ppermute x12, waiting for transfers between devices, scatter_sum(): total = total + lax.ppermute(sent, axis, pairs)  13 us
    all_to_all x1, blocking collectives, sum_over(): return jnp.sum(lax.all_to_all(spread, axes, 0, 0, tiled=True), axis=0)  9.6 us
    ppermute x9, waiting for transfers between devices, gather_blocks(): parts.append(lax.ppermute(values, axis, pairs))  8.22 us
    all_to_all x2, starting transfers between devices, sum_over(): return jnp.sum(lax.all_to_all(spread, axes, 0, 0, tiled=True), axis=0)  8.06 us
    ppermute x12, starting transfers between devices, scatter_sum(): total = total + lax.ppermute(sent, axis, pairs)  7.53 us
    all_to_all x2, waiting for transfers between devices, sum_over(): return jnp.sum(lax.all_to_all(spread, axes, 0, 0, tiled=True), axis=0)  3.72 us
    dot_general x3, matrix products, product(): jnp.dot(transposed, row_values.reshape(groups * tile, width), precision=l...  3.03 us
  transfers between devices with their start and end apart: 23, of which 10 were waited for; matrix products, arithmetic and copies ran while one was open for 8% of the time, Pallas kernels for 0%

profile of v5, /device:TPU:0, one launch (start us, length us, event | category | flops | bytes accessed | tf_op | source)
XLA Modules:
  0.0 77.7 jit_solution(17767216178125317209)
XLA Ops:
  0.6 5.1 %collective-permute-start.5 = (s32[128]{0:T(128)}, s32[128]{0:T(128)S(1)}, u32[]{:S(2)}, u32[]{:S(2)}) collective-permute-start(s32[128]{0:T(128)} %bitcast.169), channel_id=1, source_target_pairs={{0,12},{4,0},{8,4},{12,8},{1,13},{5,1},{9,5},{13,9},{2,14},{6,2},{... | collective-permute-start | bytes 1544 | tf_op jit(solution)/shard_map/ppermute | solution.py:37
  5.7 0.0 collective-permute-start.4
  5.7 1.0 %collective-permute-start.3 = (s32[128]{0:T(128)}, s32[128]{0:T(128)S(1)}, u32[]{:S(2)}, u32[]{:S(2)}) collective-permute-start(s32[128]{0:T(128)} %bitcast.171), channel_id=1, source_target_pairs={{0,4},{4,8},{8,12},{12,0},{1,5},{5,9},{9,13},{13,1},{2,6},{6,10},{... | collective-permute-start | bytes 1544 | tf_op jit(solution)/shard_map/ppermute | solution.py:37
  6.7 0.7 add_select_fusion
  7.4 0.1 iota_compare_fusion.4
  7.5 2.9 %select_reduce_fusion.1 = (f32[4,128]{1,0:T(4,128)S(1)}, f32[4,128,4,128]{3,1,2,0:T(8,128)S(1)}) fusion(f32[4,8,128,128]{3,2,1,0:T(8,128)} %param.3, pred[4,8,4]{2,1,0:T(8,128)(4,1)S(1)} %iota_compare_fusion.4), kind=kLoop, calls=%fused_computation.2 | loop fusion | flops 6028800 | bytes 3147904 | tf_op jit(solution)/shard_map/reduce_sum | solution.py:62
  10.5 0.1 collective-permute-start.2
  10.6 1.5 %collective-permute-start.1 = (f32[128]{0:T(128)S(1)}, f32[128]{0:T(128)S(1)}, u32[]{:S(2)}, u32[]{:S(2)}) collective-permute-start(f32[128]{0:T(128)S(1)} %get-tuple-element.39), channel_id=1, source_target_pairs={{0,2},{1,3},{2,0},{3,1},{4,6},{5,7},{6,4},{7,5},{8,10},{9,11},{10,... | collective-permute-start | bytes 1544 | tf_op jit(solution)/shard_map/ppermute | solution.py:27
  12.1 0.1 copy_bitcast_fusion
  12.3 0.1 broadcast_bitcast_fusion
  12.4 0.6 gather_fusion
  13.0 0.0 copy-start
  13.0 0.1 bitcast_select_fusion
  13.1 0.3 copy.9
  13.5 0.0 collective-permute-done.5
  13.5 0.2 collective-permute-start
  13.7 0.0 collective-permute-done.4
  13.7 0.0 collective-permute-done.3
  13.7 1.1 %fusion.2 = f32[4,128,128]{2,1,0:T(8,128)S(1)} fusion(f32[4,128,512]{2,1,0:T(8,128)S(1)} %bitcast.151, s32[512]{0:T(512)S(1)} %get-tuple-element.36), kind=kOutput, calls=%fused_computation.9 | convolution fusion | flops 402784256 | bytes 1312768 | tf_op jit(solution)/shard_map/dot_general | solution.py:77
  14.8 1.6 %collective-permute-start.8 = (f32[128,128]{1,0:T(8,128)S(1)}, f32[128,128]{1,0:T(8,128)S(1)}, u32[]{:S(2)}, u32[]{:S(2)}) collective-permute-start(f32[128,128]{1,0:T(8,128)S(1)} %get-tuple-element.31), channel_id=1, source_target_pairs={{0,3},{1,0},{2,1},{3,2},{4,7},{5,4},{6,5},{7,6},{8,11},{9,8},{10,9... | collective-permute-start | bytes 196616 | tf_op jit(solution)/shard_map/ppermute | solution.py:27
  16.5 0.6 collective-permute-start.7
  17.0 0.0 collective-permute-done.2
  17.0 0.0 collective-permute-start.6
  17.0 0.0 collective-permute-done.1
  17.0 0.0 collective-permute-done
  17.1 1.4 %collective-permute-done.8 = f32[128,128]{1,0:T(8,128)S(1)} collective-permute-done((f32[128,128]{1,0:T(8,128)S(1)}, f32[128,128]{1,0:T(8,128)S(1)}, u32[]{:S(2)}, u32[]{:S(2)}) %collective-permute-start.8) | collective-permute-done | bytes 65568 | tf_op jit(solution)/shard_map/ppermute | solution.py:27
  18.5 3.0 %collective-permute-done.7 = f32[128,128]{1,0:T(8,128)S(1)} collective-permute-done((f32[128,128]{1,0:T(8,128)S(1)}, f32[128,128]{1,0:T(8,128)S(1)}, u32[]{:S(2)}, u32[]{:S(2)}) %collective-permute-start.7) | collective-permute-done | bytes 65568 | tf_op jit(solution)/shard_map/ppermute | solution.py:27
  21.4 0.0 collective-permute-done.6
  21.4 0.1 fusion.8
  21.5 0.6 broadcast_in_dim.47
  22.2 4.6 %all-to-all-start = ((f32[16,2,128]{2,1,0:T(2,128)}), f32[16,2,128]{2,1,0:T(2,128)S(1)}, u32[]{:S(2)}, u32[]{:S(2)}) async-start(f32[16,2,128]{2,1,0:T(2,128)} %broadcast_in_dim.47), calls=%async_computation | async-start | bytes 32768 | tf_op jit(solution)/shard_map/all_to_all | solution.py:16
  26.7 3.7 %collective-permute-start.11 = (f32[128,128]{1,0:T(8,128)S(1)}, f32[128,128]{1,0:T(8,128)S(1)}, u32[]{:S(2)}, u32[]{:S(2)}) collective-permute-start(f32[128,128]{1,0:T(8,128)S(1)} %get-tuple-element.23), channel_id=1, source_target_pairs={{0,12},{4,0},{8,4},{12,8},{1,13},{5,1},{9,5},{13,9},{2,14},{6,2},{... | collective-permute-start | bytes 196616 | tf_op jit(solution)/shard_map/ppermute | solution.py:37
  30.5 0.0 collective-permute-start.10
  30.5 1.1 %collective-permute-start.9 = (f32[128,128]{1,0:T(8,128)S(1)}, f32[128,128]{1,0:T(8,128)S(1)}, u32[]{:S(2)}, u32[]{:S(2)}) collective-permute-start(f32[128,128]{1,0:T(8,128)S(1)} %get-tuple-element.23), channel_id=1, source_target_pairs={{0,4},{4,8},{8,12},{12,0},{1,5},{5,9},{9,13},{13,1},{2,6},{6,10},{... | collective-permute-start | bytes 196616 | tf_op jit(solution)/shard_map/ppermute | solution.py:37
  31.6 1.7 %all-to-all-done = f32[16,2,128]{2,1,0:T(2,128)S(1)} async-done(((f32[16,2,128]{2,1,0:T(2,128)}), f32[16,2,128]{2,1,0:T(2,128)S(1)}, u32[]{:S(2)}, u32[]{:S(2)}) %all-to-all-start) | async-done | bytes 16416 | tf_op jit(solution)/shard_map/all_to_all | solution.py:16
  33.3 0.0 collective-permute-done.11
  33.3 4.1 %collective-permute-done.10 = f32[128,128]{1,0:T(8,128)S(1)} collective-permute-done((f32[128,128]{1,0:T(8,128)S(1)}, f32[128,128]{1,0:T(8,128)S(1)}, u32[]{:S(2)}, u32[]{:S(2)}) %collective-permute-start.10) | collective-permute-done | bytes 65568 | tf_op jit(solution)/shard_map/ppermute | solution.py:37
  37.5 0.0 collective-permute-done.9
  37.5 0.1 multiply_subtract_fusion
  37.6 1.0 %fusion.47 = f32[4,128,128]{2,1,0:T(8,128)S(1)} fusion(f32[4,128,512]{2,1,0:T(8,128)S(1)} %bitcast.152, f32[512,128,1]{1,0,2:T(8,128)S(1)} %bitcast.157), kind=kOutput, calls=%fused_computation.119 | convolution fusion | flops 402653184 | bytes 1572864 | tf_op jit(solution)/shard_map/dot_general | solution.py:77
  38.6 1.2 %collective-permute-start.14 = (f32[128,128]{1,0:T(8,128)S(1)}, f32[128,128]{1,0:T(8,128)S(1)}, u32[]{:S(2)}, u32[]{:S(2)}) collective-permute-start(f32[128,128]{1,0:T(8,128)S(1)} %get-tuple-element.28), channel_id=1, source_target_pairs={{0,3},{1,0},{2,1},{3,2},{4,7},{5,4},{6,5},{7,6},{8,11},{9,8},{10,9... | collective-permute-start | bytes 196616 | tf_op jit(solution)/shard_map/ppermute | solution.py:27
  39.8 0.6 collective-permute-start.13
  40.4 0.0 collective-permute-start.12
  40.4 1.8 %collective-permute-done.14 = f32[128,128]{1,0:T(8,128)S(1)} collective-permute-done((f32[128,128]{1,0:T(8,128)S(1)}, f32[128,128]{1,0:T(8,128)S(1)}, u32[]{:S(2)}, u32[]{:S(2)}) %collective-permute-start.14) | collective-permute-done | bytes 65568 | tf_op jit(solution)/shard_map/ppermute | solution.py:27
  42.2 2.6 %collective-permute-done.13 = f32[128,128]{1,0:T(8,128)S(1)} collective-permute-done((f32[128,128]{1,0:T(8,128)S(1)}, f32[128,128]{1,0:T(8,128)S(1)}, u32[]{:S(2)}, u32[]{:S(2)}) %collective-permute-start.13) | collective-permute-done | bytes 65568 | tf_op jit(solution)/shard_map/ppermute | solution.py:27
  44.8 0.1 multiply_reduce_fusion.6
  44.9 0.6 broadcast_in_dim.48
  45.5 3.5 %all-to-all-start.1 = ((f32[16,4,128]{2,1,0:T(4,128)}), f32[16,4,128]{2,1,0:T(4,128)S(1)}, u32[]{:S(2)}, u32[]{:S(2)}) async-start(f32[16,4,128]{2,1,0:T(4,128)} %broadcast_in_dim.48), calls=%async_computation.1 | async-start | bytes 65536 | tf_op jit(solution)/shard_map/all_to_all | solution.py:16
  49.0 3.7 %collective-permute-start.17 = (f32[128,128]{1,0:T(8,128)S(1)}, f32[128,128]{1,0:T(8,128)S(1)}, u32[]{:S(2)}, u32[]{:S(2)}) collective-permute-start(f32[128,128]{1,0:T(8,128)S(1)} %get-tuple-element.22), channel_id=1, source_target_pairs={{0,12},{4,0},{8,4},{12,8},{1,13},{5,1},{9,5},{13,9},{2,14},{6,2},{... | collective-permute-start | bytes 196616 | tf_op jit(solution)/shard_map/ppermute | solution.py:37
  52.7 0.0 collective-permute-start.16
  52.7 1.1 %collective-permute-start.15 = (f32[128,128]{1,0:T(8,128)S(1)}, f32[128,128]{1,0:T(8,128)S(1)}, u32[]{:S(2)}, u32[]{:S(2)}) collective-permute-start(f32[128,128]{1,0:T(8,128)S(1)} %get-tuple-element.22), channel_id=1, source_target_pairs={{0,4},{4,8},{8,12},{12,0},{1,5},{5,9},{9,13},{13,1},{2,6},{6,10},{... | collective-permute-start | bytes 196616 | tf_op jit(solution)/shard_map/ppermute | solution.py:37
  53.8 2.0 %all-to-all-done.1 = f32[16,4,128]{2,1,0:T(4,128)S(1)} async-done(((f32[16,4,128]{2,1,0:T(4,128)}), f32[16,4,128]{2,1,0:T(4,128)S(1)}, u32[]{:S(2)}, u32[]{:S(2)}) %all-to-all-start.1) | async-done | bytes 32800 | tf_op jit(solution)/shard_map/all_to_all | solution.py:16
  55.9 4.1 %collective-permute-done.16 = f32[128,128]{1,0:T(8,128)S(1)} collective-permute-done((f32[128,128]{1,0:T(8,128)S(1)}, f32[128,128]{1,0:T(8,128)S(1)}, u32[]{:S(2)}, u32[]{:S(2)}) %collective-permute-start.16) | collective-permute-done | bytes 65568 | tf_op jit(solution)/shard_map/ppermute | solution.py:37
  60.0 0.1 fusion.1
  60.1 1.0 %fusion.48 = f32[4,128,128]{2,1,0:T(8,128)S(1)} fusion(f32[4,128,512]{2,1,0:T(8,128)S(1)} %bitcast.153, f32[512,128,1]{1,0,2:T(8,128)S(1)} %bitcast.158), kind=kOutput, calls=%fused_computation.120 | convolution fusion | flops 402653184 | bytes 1572864 | tf_op jit(solution)/shard_map/dot_general | solution.py:77
  61.1 1.0 %collective-permute-start.20 = (f32[128,128]{1,0:T(8,128)S(1)}, f32[128,128]{1,0:T(8,128)S(1)}, u32[]{:S(2)}, u32[]{:S(2)}) collective-permute-start(f32[128,128]{1,0:T(8,128)S(1)} %get-tuple-element.25), channel_id=1, source_target_pairs={{0,3},{1,0},{2,1},{3,2},{4,7},{5,4},{6,5},{7,6},{8,11},{9,8},{10,9... | collective-permute-start | bytes 196616 | tf_op jit(solution)/shard_map/ppermute | solution.py:27
  62.1 0.6 collective-permute-start.19
  62.7 0.2 collective-permute-start.18
  62.9 1.7 %collective-permute-done.20 = f32[128,128]{1,0:T(8,128)S(1)} collective-permute-done((f32[128,128]{1,0:T(8,128)S(1)}, f32[128,128]{1,0:T(8,128)S(1)}, u32[]{:S(2)}, u32[]{:S(2)}) %collective-permute-start.20) | collective-permute-done | bytes 65568 | tf_op jit(solution)/shard_map/ppermute | solution.py:27
  64.6 2.5 %collective-permute-done.19 = f32[128,128]{1,0:T(8,128)S(1)} collective-permute-done((f32[128,128]{1,0:T(8,128)S(1)}, f32[128,128]{1,0:T(8,128)S(1)}, u32[]{:S(2)}, u32[]{:S(2)}) %collective-permute-start.19) | collective-permute-done | bytes 65568 | tf_op jit(solution)/shard_map/ppermute | solution.py:27
  67.1 0.0 collective-permute-done.18
  67.1 0.1 multiply_reduce_fusion.3
  67.3 9.6 %all_to_all.15 = f32[16,4,128]{2,1,0:T(4,128)S(1)} all-to-all(f32[16,4,128]{2,1,0:T(4,128)S(1)} %broadcast_in_dim.49), channel_id=1, replica_groups=mesh['vol'=2,'wide'=4,'narrow'=4] {'wide','narrow'}, dimensions={0} | all-to-all | bytes 65536 | tf_op jit(solution)/shard_map/all_to_all | solution.py:16
  76.9 0.7 multiply_subtract_fusion.1
  (25 shorter events, 0.3 us)
Async XLA Ops:
  0.6 12.9 %collective-permute-start.5 = (s32[128]{0:T(128)}, s32[128]{0:T(128)S(1)}, u32[]{:S(2)}, u32[]{:S(2)}) collective-permute-start(s32[128]{0:T(128)} %bitcast.169), channel_id=1, source_target_pairs={{0,12},{4,0},{8,4},{12,8},{1,13},{5,1},{9,5},{13,9},{2,14},{6,2},{... | collective-permute-start | bytes 1544 | tf_op jit(solution)/shard_map/ppermute | solution.py:37
  5.7 8.0 %collective-permute-start.4 = (s32[128]{0:T(128)}, s32[128]{0:T(128)S(1)}, u32[]{:S(2)}, u32[]{:S(2)}) collective-permute-start(s32[128]{0:T(128)} %bitcast.170), channel_id=1, source_target_pairs={{0,8},{4,12},{8,0},{12,4},{1,9},{5,13},{9,1},{13,5},{2,10},{6,14},... | collective-permute-start | bytes 1544 | tf_op jit(solution)/shard_map/ppermute | solution.py:37
  5.7 8.0 %collective-permute-start.3 = (s32[128]{0:T(128)}, s32[128]{0:T(128)S(1)}, u32[]{:S(2)}, u32[]{:S(2)}) collective-permute-start(s32[128]{0:T(128)} %bitcast.171), channel_id=1, source_target_pairs={{0,4},{4,8},{8,12},{12,0},{1,5},{5,9},{9,13},{13,1},{2,6},{6,10},{... | collective-permute-start | bytes 1544 | tf_op jit(solution)/shard_map/ppermute | solution.py:37
  10.5 6.5 %collective-permute-start.2 = (f32[128]{0:T(128)S(1)}, f32[128]{0:T(128)S(1)}, u32[]{:S(2)}, u32[]{:S(2)}) collective-permute-start(f32[128]{0:T(128)S(1)} %get-tuple-element.38), channel_id=1, source_target_pairs={{0,3},{1,0},{2,1},{3,2},{4,7},{5,4},{6,5},{7,6},{8,11},{9,8},{10,9... | collective-permute-start | bytes 1544 | tf_op jit(solution)/shard_map/ppermute | solution.py:27
  10.6 6.4 %collective-permute-start.1 = (f32[128]{0:T(128)S(1)}, f32[128]{0:T(128)S(1)}, u32[]{:S(2)}, u32[]{:S(2)}) collective-permute-start(f32[128]{0:T(128)S(1)} %get-tuple-element.39), channel_id=1, source_target_pairs={{0,2},{1,3},{2,0},{3,1},{4,6},{5,7},{6,4},{7,5},{8,10},{9,11},{10,... | collective-permute-start | bytes 1544 | tf_op jit(solution)/shard_map/ppermute | solution.py:27
  13.0 0.7 copy-start
  13.5 3.5 %collective-permute-start = (f32[128]{0:T(128)S(1)}, f32[128]{0:T(128)S(1)}, u32[]{:S(2)}, u32[]{:S(2)}) collective-permute-start(f32[128]{0:T(128)S(1)} %get-tuple-element.37), channel_id=1, source_target_pairs={{0,1},{1,2},{2,3},{3,0},{4,5},{5,6},{6,7},{7,4},{8,9},{9,10},{10,1... | collective-permute-start | bytes 1544 | tf_op jit(solution)/shard_map/ppermute | solution.py:27
  14.8 3.6 %collective-permute-start.8 = (f32[128,128]{1,0:T(8,128)S(1)}, f32[128,128]{1,0:T(8,128)S(1)}, u32[]{:S(2)}, u32[]{:S(2)}) collective-permute-start(f32[128,128]{1,0:T(8,128)S(1)} %get-tuple-element.31), channel_id=1, source_target_pairs={{0,3},{1,0},{2,1},{3,2},{4,7},{5,4},{6,5},{7,6},{8,11},{9,8},{10,9... | collective-permute-start | bytes 196616 | tf_op jit(solution)/shard_map/ppermute | solution.py:27
  16.5 4.9 %collective-permute-start.7 = (f32[128,128]{1,0:T(8,128)S(1)}, f32[128,128]{1,0:T(8,128)S(1)}, u32[]{:S(2)}, u32[]{:S(2)}) collective-permute-start(f32[128,128]{1,0:T(8,128)S(1)} %get-tuple-element.32), channel_id=1, source_target_pairs={{0,2},{1,3},{2,0},{3,1},{4,6},{5,7},{6,4},{7,5},{8,10},{9,11},{10,... | collective-permute-start | bytes 196616 | tf_op jit(solution)/shard_map/ppermute | solution.py:27
  17.0 4.4 %collective-permute-start.6 = (f32[128,128]{1,0:T(8,128)S(1)}, f32[128,128]{1,0:T(8,128)S(1)}, u32[]{:S(2)}, u32[]{:S(2)}) collective-permute-start(f32[128,128]{1,0:T(8,128)S(1)} %get-tuple-element.30), channel_id=1, source_target_pairs={{0,1},{1,2},{2,3},{3,0},{4,5},{5,6},{6,7},{7,4},{8,9},{9,10},{10,1... | collective-permute-start | bytes 196616 | tf_op jit(solution)/shard_map/ppermute | solution.py:27
  22.2 11.1 %all-to-all-start = ((f32[16,2,128]{2,1,0:T(2,128)}), f32[16,2,128]{2,1,0:T(2,128)S(1)}, u32[]{:S(2)}, u32[]{:S(2)}) async-start(f32[16,2,128]{2,1,0:T(2,128)} %broadcast_in_dim.47), calls=%async_computation | async-start | bytes 32768 | tf_op jit(solution)/shard_map/all_to_all | solution.py:16
  26.7 6.6 %collective-permute-start.11 = (f32[128,128]{1,0:T(8,128)S(1)}, f32[128,128]{1,0:T(8,128)S(1)}, u32[]{:S(2)}, u32[]{:S(2)}) collective-permute-start(f32[128,128]{1,0:T(8,128)S(1)} %get-tuple-element.23), channel_id=1, source_target_pairs={{0,12},{4,0},{8,4},{12,8},{1,13},{5,1},{9,5},{13,9},{2,14},{6,2},{... | collective-permute-start | bytes 196616 | tf_op jit(solution)/shard_map/ppermute | solution.py:37
  30.5 7.0 %collective-permute-start.10 = (f32[128,128]{1,0:T(8,128)S(1)}, f32[128,128]{1,0:T(8,128)S(1)}, u32[]{:S(2)}, u32[]{:S(2)}) collective-permute-start(f32[128,128]{1,0:T(8,128)S(1)} %get-tuple-element.23), channel_id=1, source_target_pairs={{0,8},{4,12},{8,0},{12,4},{1,9},{5,13},{9,1},{13,5},{2,10},{6,14},... | collective-permute-start | bytes 196616 | tf_op jit(solution)/shard_map/ppermute | solution.py:37
  30.5 7.0 %collective-permute-start.9 = (f32[128,128]{1,0:T(8,128)S(1)}, f32[128,128]{1,0:T(8,128)S(1)}, u32[]{:S(2)}, u32[]{:S(2)}) collective-permute-start(f32[128,128]{1,0:T(8,128)S(1)} %get-tuple-element.23), channel_id=1, source_target_pairs={{0,4},{4,8},{8,12},{12,0},{1,5},{5,9},{9,13},{13,1},{2,6},{6,10},{... | collective-permute-start | bytes 196616 | tf_op jit(solution)/shard_map/ppermute | solution.py:37
  38.6 3.5 %collective-permute-start.14 = (f32[128,128]{1,0:T(8,128)S(1)}, f32[128,128]{1,0:T(8,128)S(1)}, u32[]{:S(2)}, u32[]{:S(2)}) collective-permute-start(f32[128,128]{1,0:T(8,128)S(1)} %get-tuple-element.28), channel_id=1, source_target_pairs={{0,3},{1,0},{2,1},{3,2},{4,7},{5,4},{6,5},{7,6},{8,11},{9,8},{10,9... | collective-permute-start | bytes 196616 | tf_op jit(solution)/shard_map/ppermute | solution.py:27
  39.8 5.0 %collective-permute-start.13 = (f32[128,128]{1,0:T(8,128)S(1)}, f32[128,128]{1,0:T(8,128)S(1)}, u32[]{:S(2)}, u32[]{:S(2)}) collective-permute-start(f32[128,128]{1,0:T(8,128)S(1)} %get-tuple-element.29), channel_id=1, source_target_pairs={{0,2},{1,3},{2,0},{3,1},{4,6},{5,7},{6,4},{7,5},{8,10},{9,11},{10,... | collective-permute-start | bytes 196616 | tf_op jit(solution)/shard_map/ppermute | solution.py:27
  40.4 4.4 %collective-permute-start.12 = (f32[128,128]{1,0:T(8,128)S(1)}, f32[128,128]{1,0:T(8,128)S(1)}, u32[]{:S(2)}, u32[]{:S(2)}) collective-permute-start(f32[128,128]{1,0:T(8,128)S(1)} %get-tuple-element.27), channel_id=1, source_target_pairs={{0,1},{1,2},{2,3},{3,0},{4,5},{5,6},{6,7},{7,4},{8,9},{9,10},{10,1... | collective-permute-start | bytes 196616 | tf_op jit(solution)/shard_map/ppermute | solution.py:27
  45.5 10.3 %all-to-all-start.1 = ((f32[16,4,128]{2,1,0:T(4,128)}), f32[16,4,128]{2,1,0:T(4,128)S(1)}, u32[]{:S(2)}, u32[]{:S(2)}) async-start(f32[16,4,128]{2,1,0:T(4,128)} %broadcast_in_dim.48), calls=%async_computation.1 | async-start | bytes 65536 | tf_op jit(solution)/shard_map/all_to_all | solution.py:16
  49.0 6.8 %collective-permute-start.17 = (f32[128,128]{1,0:T(8,128)S(1)}, f32[128,128]{1,0:T(8,128)S(1)}, u32[]{:S(2)}, u32[]{:S(2)}) collective-permute-start(f32[128,128]{1,0:T(8,128)S(1)} %get-tuple-element.22), channel_id=1, source_target_pairs={{0,12},{4,0},{8,4},{12,8},{1,13},{5,1},{9,5},{13,9},{2,14},{6,2},{... | collective-permute-start | bytes 196616 | tf_op jit(solution)/shard_map/ppermute | solution.py:37
  52.7 7.2 %collective-permute-start.16 = (f32[128,128]{1,0:T(8,128)S(1)}, f32[128,128]{1,0:T(8,128)S(1)}, u32[]{:S(2)}, u32[]{:S(2)}) collective-permute-start(f32[128,128]{1,0:T(8,128)S(1)} %get-tuple-element.22), channel_id=1, source_target_pairs={{0,8},{4,12},{8,0},{12,4},{1,9},{5,13},{9,1},{13,5},{2,10},{6,14},... | collective-permute-start | bytes 196616 | tf_op jit(solution)/shard_map/ppermute | solution.py:37
  52.7 7.2 %collective-permute-start.15 = (f32[128,128]{1,0:T(8,128)S(1)}, f32[128,128]{1,0:T(8,128)S(1)}, u32[]{:S(2)}, u32[]{:S(2)}) collective-permute-start(f32[128,128]{1,0:T(8,128)S(1)} %get-tuple-element.22), channel_id=1, source_target_pairs={{0,4},{4,8},{8,12},{12,0},{1,5},{5,9},{9,13},{13,1},{2,6},{6,10},{... | collective-permute-start | bytes 196616 | tf_op jit(solution)/shard_map/ppermute | solution.py:37
  61.1 3.5 %collective-permute-start.20 = (f32[128,128]{1,0:T(8,128)S(1)}, f32[128,128]{1,0:T(8,128)S(1)}, u32[]{:S(2)}, u32[]{:S(2)}) collective-permute-start(f32[128,128]{1,0:T(8,128)S(1)} %get-tuple-element.25), channel_id=1, source_target_pairs={{0,3},{1,0},{2,1},{3,2},{4,7},{5,4},{6,5},{7,6},{8,11},{9,8},{10,9... | collective-permute-start | bytes 196616 | tf_op jit(solution)/shard_map/ppermute | solution.py:27
  62.1 5.0 %collective-permute-start.19 = (f32[128,128]{1,0:T(8,128)S(1)}, f32[128,128]{1,0:T(8,128)S(1)}, u32[]{:S(2)}, u32[]{:S(2)}) collective-permute-start(f32[128,128]{1,0:T(8,128)S(1)} %get-tuple-element.26), channel_id=1, source_target_pairs={{0,2},{1,3},{2,0},{3,1},{4,6},{5,7},{6,4},{7,5},{8,10},{9,11},{10,... | collective-permute-start | bytes 196616 | tf_op jit(solution)/shard_map/ppermute | solution.py:27
  62.7 4.4 %collective-permute-start.18 = (f32[128,128]{1,0:T(8,128)S(1)}, f32[128,128]{1,0:T(8,128)S(1)}, u32[]{:S(2)}, u32[]{:S(2)}) collective-permute-start(f32[128,128]{1,0:T(8,128)S(1)} %get-tuple-element.24), channel_id=1, source_target_pairs={{0,1},{1,2},{2,3},{3,0},{4,5},{5,6},{6,7},{7,4},{8,9},{9,10},{10,1... | collective-permute-start | bytes 196616 | tf_op jit(solution)/shard_map/ppermute | solution.py:27

commit v6 on v5

--- a/solution.py
+++ b/solution.py
@@ -38,6 +38,33 @@
     return jnp.stack(parts)
 
 
+def scatter_with(blocks, extra, axis, count):
+    rows = blocks.shape[1]
+    if count > 4:
+        payload = jnp.concatenate(
+            [blocks, jnp.broadcast_to(extra[None], (count,) + extra.shape)], axis=1
+        )
+        got = lax.all_to_all(payload, axis, 0, 0, tiled=True)
+        return jnp.sum(got[:, :rows], axis=0), got[:, rows:]
+    me = lax.axis_index(axis)
+    total = lax.dynamic_index_in_dim(blocks, me, 0, keepdims=False)
+    extras = [extra]
+    for shift in range(1, count):
+        sent = lax.dynamic_index_in_dim(blocks, (me + shift) % count, 0, keepdims=False)
+        pairs = [(i, (i + shift) % count) for i in range(count)]
+        got = lax.ppermute(jnp.concatenate([sent, extra], axis=0), axis, pairs)
+        total = total + got[:rows]
+        extras.append(got[rows:])
+    return total, jnp.stack(extras)
+
+
+def canonical_sum(extras, axis, count):
+    if count > 4:
+        return jnp.sum(extras, axis=0)
+    order = (lax.axis_index(axis) - jnp.arange(count)) % count
+    return jnp.sum(jnp.take(extras, order, axis=0), axis=0)
+
+
 def source(axis, count, entry):
     if count > 4:
         return entry
@@ -73,24 +100,44 @@
     def indicator(values):
         return SEED_WEIGHT * (values[..., None] == classes).astype(jnp.float32)
 
-    def product(row_values):
+    def product(row_values, column_values):
         partial = jnp.dot(
             transposed, row_values.reshape(groups * tile, width), precision=lax.Precision.HIGHEST
         ).reshape(n_narrow, own_rows, width)
-        return scatter_sum(partial, "narrow", n_narrow)
+        quad = jnp.zeros((width,), jnp.float32)
+        for entry in range(n_narrow):
+            block = lax.dynamic_index_in_dim(
+                partial, source("narrow", n_narrow, entry), 0, keepdims=False
+            )
+            quad = quad + jnp.sum(column_values[entry] * block, axis=0)
+        return partial, quad
 
-    def reduce_dots(values):
-        return sum_over(values, ("wide", "narrow"), n_all)
+    def exchange(partial, partial_sums, applied_of, last):
+        weighted, extras = scatter_with(partial, partial_sums, "narrow", n_narrow)
+        narrow_sums = canonical_sum(extras, "narrow", n_narrow)
+        applied = applied_of(weighted)
+        if last:
+            sums = canonical_sum(gather_blocks(narrow_sums, "wide", n_wide), "wide", n_wide)
+            return applied, None, None, sums
+        got = gather_blocks(jnp.concatenate([applied, narrow_sums], axis=0), "wide", n_wide)
+        sums = canonical_sum(got[:, own_rows:], "wide", n_wide)
+        return applied, got[:, :own_rows], gather_blocks(applied, "narrow", n_narrow), sums
 
     rhs = indicator(labels)
     solution = jnp.zeros_like(rhs)
     residual = rhs
     direction = rhs
     rows_residual = indicator(gather_blocks(labels, "wide", n_wide))
-    image = diag_column * direction - product(rows_residual)
-    rows_image = gather_blocks(image, "wide", n_wide)
-    first = reduce_dots(
-        jnp.stack([jnp.sum(residual * residual, axis=0), jnp.sum(direction * image, axis=0)])
+    columns_residual = indicator(gather_blocks(labels, "narrow", n_narrow))
+    partial, quad = product(rows_residual, columns_residual)
+    partial_sums = jnp.stack(
+        [
+            jnp.sum(residual * residual, axis=0),
+            jnp.sum(diag_column * direction * direction, axis=0) - quad,
+        ]
+    )
+    image, rows_image, columns_image, first = exchange(
+        partial, partial_sums, lambda weighted: diag_column * direction - weighted, ITERS == 1
     )
     norm_now = first[0]
     curvature = first[1]
@@ -101,24 +148,30 @@
         if step == ITERS - 1:
             break
         rows_residual = rows_residual - alpha * rows_image
-        applied = diag_column * residual - product(rows_residual)
-        rows_applied = gather_blocks(applied, "wide", n_wide)
-        sums = reduce_dots(
-            jnp.stack(
-                [
-                    jnp.sum(residual * residual, axis=0),
-                    jnp.sum(residual * applied, axis=0),
-                    jnp.sum(residual * image, axis=0),
-                    jnp.sum(direction * image, axis=0),
-                ]
-            )
+        columns_residual = columns_residual - alpha * columns_image
+        partial, quad = product(rows_residual, columns_residual)
+        partial_sums = jnp.stack(
+            [
+                jnp.sum(residual * residual, axis=0),
+                jnp.sum(diag_column * residual * residual, axis=0) - quad,
+                jnp.sum(residual * image, axis=0),
+                jnp.sum(direction * image, axis=0),
+            ]
+        )
+        applied, rows_applied, columns_applied, sums = exchange(
+            partial,
+            partial_sums,
+            lambda weighted: diag_column * residual - weighted,
+            step == ITERS - 2,
         )
         norm_next = sums[0]
         ratio = norm_next / norm_now
         curvature = sums[1] + ratio * (2.0 * sums[2] + ratio * sums[3])
         direction = residual + ratio * direction
         image = applied + ratio * image
-        rows_image = rows_applied + ratio * rows_image
+        if step < ITERS - 2:
+            rows_image = rows_applied + ratio * rows_image
+            columns_image = columns_applied + ratio * columns_image
         norm_now = norm_next
     return (solution, residual)
 

time: 78 us -> 72.2 us (0.926)
  blocking collectives: 9.6 us -> 0 us
  waiting for transfers between devices: 24.9 us -> 28.2 us
  starting transfers between devices: 31.3 us -> 28.1 us
  local copies, waits for them, and re-layouts: 2.48 us -> 4.77 us
  other arithmetic: 5.45 us -> 6.86 us
    ppermute x0 -> x9, waiting for transfers between devices: none -> 12.7 us  [scatter_with(): got = lax.ppermute(jnp.concatenate([sent, extra], axis=0), axis, pairs)]
    ppermute x12 -> x3, waiting for transfers between devices: 13 us -> 1.85 us  [scatter_sum(): total = total + lax.ppermute(sent, axis, pairs)]
    all_to_all x1 -> x0, blocking collectives: 9.6 us -> none  [sum_over(): return jnp.sum(lax.all_to_all(spread, axes, 0, 0, tiled=True), axis=0)]
    all_to_all x2 -> x0, starting transfers between devices: 8.06 us -> none  [sum_over(): return jnp.sum(lax.all_to_all(spread, axes, 0, 0, tiled=True), axis=0)]
    ppermute x9 -> x21, waiting for transfers between devices: 8.22 us -> 13.6 us  [gather_blocks(): parts.append(lax.ppermute(values, axis, pairs))]
    ppermute x9 -> x21, starting transfers between devices: 15.7 us -> 20.9 us  [gather_blocks(): parts.append(lax.ppermute(values, axis, pairs))]
    ppermute x12 -> x3, starting transfers between devices: 7.53 us -> 2.76 us  [scatter_sum(): total = total + lax.ppermute(sent, axis, pairs)]
    ppermute x0 -> x9, starting transfers between devices: none -> 4.42 us  [scatter_with(): got = lax.ppermute(jnp.concatenate([sent, extra], axis=0), axis, pairs)]
  transfers between devices with their start and end apart: 23 -> 33, of which waited for: 10 -> 17; matrix products, arithmetic and copies ran while one was open for 8% -> 11% of each run, Pallas kernels for 0% -> 0%
where the time goes in v6:
time: 72.2 us; the launch traced here: 72.1 us
  waiting for transfers between devices  28.2 us (39%)
  starting transfers between devices  28.1 us (39%)
  other arithmetic  6.86 us (10%)
  local copies, waits for them, and re-layouts  4.77 us (7%)
  matrix products  3.03 us (4%)
  between operations  1.13 us (2%)
    ppermute x21, starting transfers between devices, gather_blocks(): parts.append(lax.ppermute(values, axis, pairs))  20.9 us
    ppermute x21, waiting for transfers between devices, gather_blocks(): parts.append(lax.ppermute(values, axis, pairs))  13.6 us
    ppermute x9, waiting for transfers between devices, scatter_with(): got = lax.ppermute(jnp.concatenate([sent, extra], axis=0), axis, pairs)  12.7 us
    ppermute x9, starting transfers between devices, scatter_with(): got = lax.ppermute(jnp.concatenate([sent, extra], axis=0), axis, pairs)  4.42 us
    gather x6, local copies, waits for them, and re-layouts, canonical_sum(): return jnp.sum(jnp.take(extras, order, axis=0), axis=0)  3.42 us
    dot_general x3, matrix products, product(): jnp.dot(transposed, row_values.reshape(groups * tile, width), precision=l...  3.03 us
    reduce_sum x1, other arithmetic, local(): column_sums = jnp.sum(dense, axis=(0, 1)).reshape(n_narrow, own_rows)  2.97 us
    ppermute x3, starting transfers between devices, scatter_sum(): total = total + lax.ppermute(sent, axis, pairs)  2.76 us
  transfers between devices with their start and end apart: 33, of which 17 were waited for; matrix products, arithmetic and copies ran while one was open for 11% of the time, Pallas kernels for 0%

profile of v6, /device:TPU:0, one launch (start us, length us, event | category | flops | bytes accessed | tf_op | source)
XLA Modules:
  0.0 72.1 jit_solution(6997976380234733527)
XLA Ops:
  0.6 5.1 %collective-permute-start.5 = (s32[128]{0:T(128)}, s32[128]{0:T(128)S(1)}, u32[]{:S(2)}, u32[]{:S(2)}) collective-permute-start(s32[128]{0:T(128)} %bitcast.208), channel_id=1, source_target_pairs={{0,12},{4,0},{8,4},{12,8},{1,13},{5,1},{9,5},{13,9},{2,14},{6,2},{... | collective-permute-start | bytes 1544 | tf_op jit(solution)/shard_map/ppermute | solution.py:37
  5.7 0.7 collective-permute-start.8
  6.4 0.8 %collective-permute-start.7 = (s32[128]{0:T(128)}, s32[128]{0:T(128)S(1)}, u32[]{:S(2)}, u32[]{:S(2)}) collective-permute-start(s32[128]{0:T(128)} %bitcast.211), channel_id=1, source_target_pairs={{0,2},{1,3},{2,0},{3,1},{4,6},{5,7},{6,4},{7,5},{8,10},{9,11},{10,... | collective-permute-start | bytes 1544 | tf_op jit(solution)/shard_map/ppermute | solution.py:37
  7.2 0.2 collective-permute-start.6
  7.6 0.7 add_select_fusion
  8.4 3.0 %select_reduce_fusion.1 = (f32[4,128]{1,0:T(4,128)S(1)}, f32[4,128,4,128]{3,1,2,0:T(8,128)S(1)}) fusion(f32[4,8,128,128]{3,2,1,0:T(8,128)} %param.7, pred[4,8,4]{2,1,0:T(8,128)(4,1)S(1)} %iota_compare_fusion.5), kind=kLoop, calls=%fused_computation.8 | loop fusion | flops 6028800 | bytes 3147904 | tf_op jit(solution)/shard_map/reduce_sum | solution.py:89
  11.4 0.1 copy_bitcast_fusion
  11.6 0.6 gather_fusion
  12.2 0.1 bitcast_select_fusion
  12.4 0.3 copy.7
  12.8 1.6 %collective-permute-start.2 = (f32[128]{0:T(128)S(1)}, f32[128]{0:T(128)S(1)}, u32[]{:S(2)}, u32[]{:S(2)}) collective-permute-start(f32[128]{0:T(128)S(1)} %get-tuple-element.65), channel_id=1, source_target_pairs={{0,3},{1,0},{2,1},{3,2},{4,7},{5,4},{6,5},{7,6},{8,11},{9,8},{10,9... | collective-permute-start | bytes 1544 | tf_op jit(solution)/shard_map/ppermute | solution.py:27
  14.4 1.2 %collective-permute-start.1 = (f32[128]{0:T(128)S(1)}, f32[128]{0:T(128)S(1)}, u32[]{:S(2)}, u32[]{:S(2)}) collective-permute-start(f32[128]{0:T(128)S(1)} %get-tuple-element.66), channel_id=1, source_target_pairs={{0,2},{1,3},{2,0},{3,1},{4,6},{5,7},{6,4},{7,5},{8,10},{9,11},{10,... | collective-permute-start | bytes 1544 | tf_op jit(solution)/shard_map/ppermute | solution.py:27
  15.6 0.1 fusion.8
  15.8 0.9 %collective-permute-start.3 = (s32[128]{0:T(128)S(1)}, s32[128]{0:T(128)S(1)}, u32[]{:S(2)}, u32[]{:S(2)}) collective-permute-start(s32[128]{0:T(128)S(1)} %bitcast.214), channel_id=1, source_target_pairs={{0,4},{4,8},{8,12},{12,0},{1,5},{5,9},{9,13},{13,1},{2,6},{6,10},{... | collective-permute-start | bytes 1544 | tf_op jit(solution)/shard_map/ppermute | solution.py:37
  16.7 1.2 %collective-permute-done.1 = f32[128]{0:T(128)S(1)} collective-permute-done((f32[128]{0:T(128)S(1)}, f32[128]{0:T(128)S(1)}, u32[]{:S(2)}, u32[]{:S(2)}) %collective-permute-start.1) | collective-permute-done | bytes 544 | tf_op jit(solution)/shard_map/ppermute | solution.py:27
  17.9 0.6 collective-permute-done
  18.6 0.1 fusion.18
  18.7 2.5 %collective-permute-done.3 = s32[128]{0:T(128)S(1)} collective-permute-done((s32[128]{0:T(128)S(1)}, s32[128]{0:T(128)S(1)}, u32[]{:S(2)}, u32[]{:S(2)}) %collective-permute-start.3) | collective-permute-done | bytes 544 | tf_op jit(solution)/shard_map/ppermute | solution.py:37
  21.2 1.1 %fusion.5 = f32[4,128,128]{2,1,0:T(8,128)S(1)} fusion(f32[4,128,512]{2,1,0:T(8,128)S(1)} %bitcast.175, s32[512]{0:T(512)S(1)} %get-tuple-element.63), kind=kOutput, calls=%fused_computation.24 | convolution fusion | flops 402784256 | bytes 1312768 | tf_op jit(solution)/shard_map/dot_general | solution.py:104
  22.3 0.6 collective-permute-start.11
  23.0 1.0 %collective-permute-start.10 = (f32[130,128]{1,0:T(8,128)S(1)}, f32[130,128]{1,0:T(8,128)S(1)}, u32[]{:S(2)}, u32[]{:S(2)}) collective-permute-start(f32[130,128]{1,0:T(8,128)S(1)} %get-tuple-element.68), channel_id=1, source_target_pairs={{0,2},{1,3},{2,0},{3,1},{4,6},{5,7},{6,4},{7,5},{8,10},{9,11},{10,... | collective-permute-start | bytes 199688 | tf_op jit(solution)/shard_map/ppermute | solution.py:55
  24.0 1.5 %collective-permute-done.11 = f32[130,128]{1,0:T(8,128)S(1)} collective-permute-done((f32[130,128]{1,0:T(8,128)S(1)}, f32[130,128]{1,0:T(8,128)S(1)}, u32[]{:S(2)}, u32[]{:S(2)}) %collective-permute-start.11) | collective-permute-done | bytes 66592 | tf_op jit(solution)/shard_map/ppermute | solution.py:55
  25.5 3.0 %collective-permute-done.10 = f32[130,128]{1,0:T(8,128)S(1)} collective-permute-done((f32[130,128]{1,0:T(8,128)S(1)}, f32[130,128]{1,0:T(8,128)S(1)}, u32[]{:S(2)}, u32[]{:S(2)}) %collective-permute-start.10) | collective-permute-done | bytes 66592 | tf_op jit(solution)/shard_map/ppermute | solution.py:55
  28.5 0.6 gather_fusion.1
  29.3 0.5 collective-permute-start.14
  29.8 0.6 collective-permute-start.13
  30.4 1.9 %collective-permute-start.12 = (f32[130,128]{1,0:T(8,128)S(1)}, f32[130,128]{1,0:T(8,128)S(1)}, u32[]{:S(2)}, u32[]{:S(2)}) collective-permute-start(f32[130,128]{1,0:T(8,128)S(1)} %get-tuple-element.61), channel_id=1, source_target_pairs={{0,4},{4,8},{8,12},{12,0},{1,5},{5,9},{9,13},{13,1},{2,6},{6,10},{... | collective-permute-start | bytes 199688 | tf_op jit(solution)/shard_map/ppermute | solution.py:37
  32.3 1.0 %collective-permute-start.16 = (f32[128,128]{1,0:T(8,128)S(1)}, f32[128,128]{1,0:T(8,128)S(1)}, u32[]{:S(2)}, u32[]{:S(2)}) collective-permute-start(f32[128,128]{1,0:T(8,128)S(1)} %fusion.12), channel_id=1, source_target_pairs={{0,2},{1,3},{2,0},{3,1},{4,6},{5,7},{6,4},{7,5},{8,10},{9,11},{10,... | collective-permute-start | bytes 196616 | tf_op jit(solution)/shard_map/ppermute | solution.py:37
  33.4 0.3 collective-permute-done.14
  33.7 3.2 %collective-permute-done.13 = f32[130,128]{1,0:T(8,128)S(1)} collective-permute-done((f32[130,128]{1,0:T(8,128)S(1)}, f32[130,128]{1,0:T(8,128)S(1)}, u32[]{:S(2)}, u32[]{:S(2)}) %collective-permute-start.13) | collective-permute-done | bytes 66592 | tf_op jit(solution)/shard_map/ppermute | solution.py:37
  36.9 0.6 gather_fusion.2
  37.7 0.2 multiply_subtract_fusion
  37.9 1.0 %fusion.65 = f32[4,128,128]{2,1,0:T(8,128)S(1)} fusion(f32[4,128,512]{2,1,0:T(8,128)S(1)} %bitcast.176, f32[512,128,1]{1,0,2:T(8,128)S(1)} %bitcast.183), kind=kOutput, calls=%fused_computation.214 | convolution fusion | flops 402653184 | bytes 1572864 | tf_op jit(solution)/shard_map/dot_general | solution.py:104
  38.9 0.1 multiply_reduce_fusion.3
  39.2 1.1 %collective-permute-start.19 = (f32[132,128]{1,0:T(8,128)S(1)}, f32[132,128]{1,0:T(8,128)S(1)}, u32[]{:S(2)}, u32[]{:S(2)}) collective-permute-start(f32[132,128]{1,0:T(8,128)S(1)} %concatenate.47), channel_id=1, source_target_pairs={{0,2},{1,3},{2,0},{3,1},{4,6},{5,7},{6,4},{7,5},{8,10},{9,11},{10,... | collective-permute-start | bytes 202760 | tf_op jit(solution)/shard_map/ppermute | solution.py:55
  40.3 0.3 collective-permute-start.18
  40.6 0.5 collective-permute-done.20
  41.1 3.2 %collective-permute-done.19 = f32[132,128]{1,0:T(8,128)S(1)} collective-permute-done((f32[132,128]{1,0:T(8,128)S(1)}, f32[132,128]{1,0:T(8,128)S(1)}, u32[]{:S(2)}, u32[]{:S(2)}) %collective-permute-start.19) | collective-permute-done | bytes 67616 | tf_op jit(solution)/shard_map/ppermute | solution.py:55
  44.3 0.4 collective-permute-done.18
  44.7 0.6 gather_fusion.3
  45.4 0.1 multiply_subtract_fusion.3
  45.5 2.5 %collective-permute-start.23 = (f32[132,128]{1,0:T(8,128)S(1)}, f32[132,128]{1,0:T(8,128)S(1)}, u32[]{:S(2)}, u32[]{:S(2)}) collective-permute-start(f32[132,128]{1,0:T(8,128)S(1)} %get-tuple-element.59), channel_id=1, source_target_pairs={{0,12},{4,0},{8,4},{12,8},{1,13},{5,1},{9,5},{13,9},{2,14},{6,2},{... | collective-permute-start | bytes 202760 | tf_op jit(solution)/shard_map/ppermute | solution.py:37
  48.0 1.5 %collective-permute-start.21 = (f32[132,128]{1,0:T(8,128)S(1)}, f32[132,128]{1,0:T(8,128)S(1)}, u32[]{:S(2)}, u32[]{:S(2)}) collective-permute-start(f32[132,128]{1,0:T(8,128)S(1)} %get-tuple-element.59), channel_id=1, source_target_pairs={{0,4},{4,8},{8,12},{12,0},{1,5},{5,9},{9,13},{13,1},{2,6},{6,10},{... | collective-permute-start | bytes 202760 | tf_op jit(solution)/shard_map/ppermute | solution.py:37
  49.6 1.0 %collective-permute-start.25 = (f32[128,128]{1,0:T(8,128)S(1)}, f32[128,128]{1,0:T(8,128)S(1)}, u32[]{:S(2)}, u32[]{:S(2)}) collective-permute-start(f32[128,128]{1,0:T(8,128)S(1)} %multiply_subtract_fusion.3), channel_id=1, source_target_pairs={{0,2},{1,3},{2,0},{3,1},{4,6},{5,7},{6,4},{7,5},{8,10},{9,11},{10,... | collective-permute-start | bytes 196616 | tf_op jit(solution)/shard_map/ppermute | solution.py:37
  50.6 0.2 collective-permute-start.24
  50.8 3.8 %collective-permute-done.22 = f32[132,128]{1,0:T(8,128)S(1)} collective-permute-done((f32[132,128]{1,0:T(8,128)S(1)}, f32[132,128]{1,0:T(8,128)S(1)}, u32[]{:S(2)}, u32[]{:S(2)}) %collective-permute-start.22) | collective-permute-done | bytes 67616 | tf_op jit(solution)/shard_map/ppermute | solution.py:37
  54.6 0.6 gather_fusion.4
  55.3 0.1 fusion.2
  55.4 1.0 %fusion.66 = f32[4,128,128]{2,1,0:T(8,128)S(1)} fusion(f32[4,128,512]{2,1,0:T(8,128)S(1)} %bitcast.177, f32[512,128,1]{1,0,2:T(8,128)S(1)} %bitcast.181), kind=kOutput, calls=%fused_computation.215 | convolution fusion | flops 402653184 | bytes 1572864 | tf_op jit(solution)/shard_map/dot_general | solution.py:104
  56.5 0.1 fusion.4
  56.7 0.1 multiply_reduce_fusion.1
  56.9 1.1 %collective-permute-start.28 = (f32[132,128]{1,0:T(8,128)S(1)}, f32[132,128]{1,0:T(8,128)S(1)}, u32[]{:S(2)}, u32[]{:S(2)}) collective-permute-start(f32[132,128]{1,0:T(8,128)S(1)} %concatenate.51), channel_id=1, source_target_pairs={{0,2},{1,3},{2,0},{3,1},{4,6},{5,7},{6,4},{7,5},{8,10},{9,11},{10,... | collective-permute-start | bytes 202760 | tf_op jit(solution)/shard_map/ppermute | solution.py:55
  58.0 0.3 collective-permute-start.27
  58.3 0.6 collective-permute-done.29
  58.9 3.1 %collective-permute-done.28 = f32[132,128]{1,0:T(8,128)S(1)} collective-permute-done((f32[132,128]{1,0:T(8,128)S(1)}, f32[132,128]{1,0:T(8,128)S(1)}, u32[]{:S(2)}, u32[]{:S(2)}) %collective-permute-start.28) | collective-permute-done | bytes 67616 | tf_op jit(solution)/shard_map/ppermute | solution.py:55
  62.0 0.5 collective-permute-done.27
  62.4 0.6 gather_fusion.5
  63.1 1.9 %collective-permute-start.32 = (f32[4,128]{1,0:T(4,128)S(1)}, f32[4,128]{1,0:T(4,128)S(1)}, u32[]{:S(2)}, u32[]{:S(2)}) collective-permute-start(f32[4,128]{1,0:T(4,128)S(1)} %select_reduce_fusion.3), channel_id=1, source_target_pairs={{0,12},{4,0},{8,4},{12,8},{1,13},{5,1},{9,5},{13,9},{2,14},{6,2},{... | collective-permute-start | bytes 6152 | tf_op jit(solution)/shard_map/ppermute | solution.py:37
  65.0 0.2 collective-permute-start.31
  65.2 1.6 %collective-permute-start.30 = (f32[4,128]{1,0:T(4,128)S(1)}, f32[4,128]{1,0:T(4,128)S(1)}, u32[]{:S(2)}, u32[]{:S(2)}) collective-permute-start(f32[4,128]{1,0:T(4,128)S(1)} %select_reduce_fusion.3), channel_id=1, source_target_pairs={{0,4},{4,8},{8,12},{12,0},{1,5},{5,9},{9,13},{13,1},{2,6},{6,10},{... | collective-permute-start | bytes 6152 | tf_op jit(solution)/shard_map/ppermute | solution.py:37
  66.9 2.6 %collective-permute-done.31 = f32[4,128]{1,0:T(4,128)S(1)} collective-permute-done((f32[4,128]{1,0:T(4,128)S(1)}, f32[4,128]{1,0:T(4,128)S(1)}, u32[]{:S(2)}, u32[]{:S(2)}) %collective-permute-start.31) | collective-permute-done | bytes 2080 | tf_op jit(solution)/shard_map/ppermute | solution.py:37
  69.5 1.1 %collective-permute-done.30 = f32[4,128]{1,0:T(4,128)S(1)} collective-permute-done((f32[4,128]{1,0:T(4,128)S(1)}, f32[4,128]{1,0:T(4,128)S(1)}, u32[]{:S(2)}, u32[]{:S(2)}) %collective-permute-start.30) | collective-permute-done | bytes 2080 | tf_op jit(solution)/shard_map/ppermute | solution.py:37
  70.6 0.6 gather_fusion.6
  71.3 0.8 %fusion.17 = (f32[128,128]{1,0:T(8,128)}, f32[128,128]{1,0:T(8,128)}) fusion(f32[132,128]{1,0:T(8,128)S(1)} %collective-permute-done.29, f32[132,128]{1,0:T(8,128)S(1)} %collective-permute-done.28, f32[132,128]{1,0:T(8,128)S(1)} %collective-permute-done.27, f32[128,128]{1,0:T(8,128)S(1)} %get-tuple-element.30, f32[4,128,128]{2,1,0:T(8,128)S(1)} %fusion.66, ...), kind=kLoop, calls=%fused_computation.60 | loop fusion | flops 393216 | bytes 527876 | tf_op jit(solution)/shard_map/sub | solution.py:147
  (87 shorter events, 1.7 us)
Async XLA Ops:
  0.6 18.1 %collective-permute-start.5 = (s32[128]{0:T(128)}, s32[128]{0:T(128)S(1)}, u32[]{:S(2)}, u32[]{:S(2)}) collective-permute-start(s32[128]{0:T(128)} %bitcast.208), channel_id=1, source_target_pairs={{0,12},{4,0},{8,4},{12,8},{1,13},{5,1},{9,5},{13,9},{2,14},{6,2},{... | collective-permute-start | bytes 1544 | tf_op jit(solution)/shard_map/ppermute | solution.py:37
  5.7 13.0 %collective-permute-start.4 = (s32[128]{0:T(128)}, s32[128]{0:T(128)S(1)}, u32[]{:S(2)}, u32[]{:S(2)}) collective-permute-start(s32[128]{0:T(128)} %bitcast.209), channel_id=1, source_target_pairs={{0,8},{4,12},{8,0},{12,4},{1,9},{5,13},{9,1},{13,5},{2,10},{6,14},... | collective-permute-start | bytes 1544 | tf_op jit(solution)/shard_map/ppermute | solution.py:37
  5.7 7.1 %collective-permute-start.8 = (s32[128]{0:T(128)}, s32[128]{0:T(128)S(1)}, u32[]{:S(2)}, u32[]{:S(2)}) collective-permute-start(s32[128]{0:T(128)} %bitcast.210), channel_id=1, source_target_pairs={{0,3},{1,0},{2,1},{3,2},{4,7},{5,4},{6,5},{7,6},{8,11},{9,8},{10,9... | collective-permute-start | bytes 1544 | tf_op jit(solution)/shard_map/ppermute | solution.py:37
  6.4 8.0 %collective-permute-start.7 = (s32[128]{0:T(128)}, s32[128]{0:T(128)S(1)}, u32[]{:S(2)}, u32[]{:S(2)}) collective-permute-start(s32[128]{0:T(128)} %bitcast.211), channel_id=1, source_target_pairs={{0,2},{1,3},{2,0},{3,1},{4,6},{5,7},{6,4},{7,5},{8,10},{9,11},{10,... | collective-permute-start | bytes 1544 | tf_op jit(solution)/shard_map/ppermute | solution.py:37
  7.2 8.4 %collective-permute-start.6 = (s32[128]{0:T(128)}, s32[128]{0:T(128)S(1)}, u32[]{:S(2)}, u32[]{:S(2)}) collective-permute-start(s32[128]{0:T(128)} %bitcast.212), channel_id=1, source_target_pairs={{0,1},{1,2},{2,3},{3,0},{4,5},{5,6},{6,7},{7,4},{8,9},{9,10},{10,1... | collective-permute-start | bytes 1544 | tf_op jit(solution)/shard_map/ppermute | solution.py:37
  12.2 3.3 %copy-start = (s32[128,1]{0,1:T(1,128)S(1)}, s32[128,1]{0,1:T(1,128)}, u32[]{:S(2)}) copy-start(s32[128,1]{0,1:T(1,128)} %param.9) | copy-start | bytes 1540
  12.8 2.9 %collective-permute-start.2 = (f32[128]{0:T(128)S(1)}, f32[128]{0:T(128)S(1)}, u32[]{:S(2)}, u32[]{:S(2)}) collective-permute-start(f32[128]{0:T(128)S(1)} %get-tuple-element.65), channel_id=1, source_target_pairs={{0,3},{1,0},{2,1},{3,2},{4,7},{5,4},{6,5},{7,6},{8,11},{9,8},{10,9... | collective-permute-start | bytes 1544 | tf_op jit(solution)/shard_map/ppermute | solution.py:27
  14.4 3.5 %collective-permute-start.1 = (f32[128]{0:T(128)S(1)}, f32[128]{0:T(128)S(1)}, u32[]{:S(2)}, u32[]{:S(2)}) collective-permute-start(f32[128]{0:T(128)S(1)} %get-tuple-element.66), channel_id=1, source_target_pairs={{0,2},{1,3},{2,0},{3,1},{4,6},{5,7},{6,4},{7,5},{8,10},{9,11},{10,... | collective-permute-start | bytes 1544 | tf_op jit(solution)/shard_map/ppermute | solution.py:27
  15.6 3.0 %collective-permute-start = (f32[128]{0:T(128)S(1)}, f32[128]{0:T(128)S(1)}, u32[]{:S(2)}, u32[]{:S(2)}) collective-permute-start(f32[128]{0:T(128)S(1)} %get-tuple-element.64), channel_id=1, source_target_pairs={{0,1},{1,2},{2,3},{3,0},{4,5},{5,6},{6,7},{7,4},{8,9},{9,10},{10,1... | collective-permute-start | bytes 1544 | tf_op jit(solution)/shard_map/ppermute | solution.py:27
  15.8 5.4 %collective-permute-start.3 = (s32[128]{0:T(128)S(1)}, s32[128]{0:T(128)S(1)}, u32[]{:S(2)}, u32[]{:S(2)}) collective-permute-start(s32[128]{0:T(128)S(1)} %bitcast.214), channel_id=1, source_target_pairs={{0,4},{4,8},{8,12},{12,0},{1,5},{5,9},{9,13},{13,1},{2,6},{6,10},{... | collective-permute-start | bytes 1544 | tf_op jit(solution)/shard_map/ppermute | solution.py:37
  22.3 3.2 %collective-permute-start.11 = (f32[130,128]{1,0:T(8,128)S(1)}, f32[130,128]{1,0:T(8,128)S(1)}, u32[]{:S(2)}, u32[]{:S(2)}) collective-permute-start(f32[130,128]{1,0:T(8,128)S(1)} %get-tuple-element.69), channel_id=1, source_target_pairs={{0,3},{1,0},{2,1},{3,2},{4,7},{5,4},{6,5},{7,6},{8,11},{9,8},{10,9... | collective-permute-start | bytes 199688 | tf_op jit(solution)/shard_map/ppermute | solution.py:55
  23.0 5.5 %collective-permute-start.10 = (f32[130,128]{1,0:T(8,128)S(1)}, f32[130,128]{1,0:T(8,128)S(1)}, u32[]{:S(2)}, u32[]{:S(2)}) collective-permute-start(f32[130,128]{1,0:T(8,128)S(1)} %get-tuple-element.68), channel_id=1, source_target_pairs={{0,2},{1,3},{2,0},{3,1},{4,6},{5,7},{6,4},{7,5},{8,10},{9,11},{10,... | collective-permute-start | bytes 199688 | tf_op jit(solution)/shard_map/ppermute | solution.py:55
  24.0 4.5 %collective-permute-start.9 = (f32[130,128]{1,0:T(8,128)S(1)}, f32[130,128]{1,0:T(8,128)S(1)}, u32[]{:S(2)}, u32[]{:S(2)}) collective-permute-start(f32[130,128]{1,0:T(8,128)S(1)} %get-tuple-element.67), channel_id=1, source_target_pairs={{0,1},{1,2},{2,3},{3,0},{4,5},{5,6},{6,7},{7,4},{8,9},{9,10},{10,1... | collective-permute-start | bytes 199688 | tf_op jit(solution)/shard_map/ppermute | solution.py:55
  29.3 4.4 %collective-permute-start.14 = (f32[130,128]{1,0:T(8,128)S(1)}, f32[130,128]{1,0:T(8,128)S(1)}, u32[]{:S(2)}, u32[]{:S(2)}) collective-permute-start(f32[130,128]{1,0:T(8,128)S(1)} %get-tuple-element.61), channel_id=1, source_target_pairs={{0,12},{4,0},{8,4},{12,8},{1,13},{5,1},{9,5},{13,9},{2,14},{6,2},{... | collective-permute-start | bytes 199688 | tf_op jit(solution)/shard_map/ppermute | solution.py:37
  29.8 7.1 %collective-permute-start.13 = (f32[130,128]{1,0:T(8,128)S(1)}, f32[130,128]{1,0:T(8,128)S(1)}, u32[]{:S(2)}, u32[]{:S(2)}) collective-permute-start(f32[130,128]{1,0:T(8,128)S(1)} %get-tuple-element.61), channel_id=1, source_target_pairs={{0,8},{4,12},{8,0},{12,4},{1,9},{5,13},{9,1},{13,5},{2,10},{6,14},... | collective-permute-start | bytes 199688 | tf_op jit(solution)/shard_map/ppermute | solution.py:37
  30.4 6.5 %collective-permute-start.12 = (f32[130,128]{1,0:T(8,128)S(1)}, f32[130,128]{1,0:T(8,128)S(1)}, u32[]{:S(2)}, u32[]{:S(2)}) collective-permute-start(f32[130,128]{1,0:T(8,128)S(1)} %get-tuple-element.61), channel_id=1, source_target_pairs={{0,4},{4,8},{8,12},{12,0},{1,5},{5,9},{9,13},{13,1},{2,6},{6,10},{... | collective-permute-start | bytes 199688 | tf_op jit(solution)/shard_map/ppermute | solution.py:37
  32.3 5.2 %collective-permute-start.17 = (f32[128,128]{1,0:T(8,128)S(1)}, f32[128,128]{1,0:T(8,128)S(1)}, u32[]{:S(2)}, u32[]{:S(2)}) collective-permute-start(f32[128,128]{1,0:T(8,128)S(1)} %fusion.12), channel_id=1, source_target_pairs={{0,3},{1,0},{2,1},{3,2},{4,7},{5,4},{6,5},{7,6},{8,11},{9,8},{10,9... | collective-permute-start | bytes 196616 | tf_op jit(solution)/shard_map/ppermute | solution.py:37
  32.3 5.3 %collective-permute-start.16 = (f32[128,128]{1,0:T(8,128)S(1)}, f32[128,128]{1,0:T(8,128)S(1)}, u32[]{:S(2)}, u32[]{:S(2)}) collective-permute-start(f32[128,128]{1,0:T(8,128)S(1)} %fusion.12), channel_id=1, source_target_pairs={{0,2},{1,3},{2,0},{3,1},{4,6},{5,7},{6,4},{7,5},{8,10},{9,11},{10,... | collective-permute-start | bytes 196616 | tf_op jit(solution)/shard_map/ppermute | solution.py:37
  33.7 4.0 %collective-permute-start.15 = (f32[128,128]{1,0:T(8,128)S(1)}, f32[128,128]{1,0:T(8,128)S(1)}, u32[]{:S(2)}, u32[]{:S(2)}) collective-permute-start(f32[128,128]{1,0:T(8,128)S(1)} %fusion.12), channel_id=1, source_target_pairs={{0,1},{1,2},{2,3},{3,0},{4,5},{5,6},{6,7},{7,4},{8,9},{9,10},{10,1... | collective-permute-start | bytes 196616 | tf_op jit(solution)/shard_map/ppermute | solution.py:37
  39.1 2.0 %collective-permute-start.20 = (f32[132,128]{1,0:T(8,128)S(1)}, f32[132,128]{1,0:T(8,128)S(1)}, u32[]{:S(2)}, u32[]{:S(2)}) collective-permute-start(f32[132,128]{1,0:T(8,128)S(1)} %concatenate.48), channel_id=1, source_target_pairs={{0,3},{1,0},{2,1},{3,2},{4,7},{5,4},{6,5},{7,6},{8,11},{9,8},{10,9... | collective-permute-start | bytes 202760 | tf_op jit(solution)/shard_map/ppermute | solution.py:55
  39.2 5.1 %collective-permute-start.19 = (f32[132,128]{1,0:T(8,128)S(1)}, f32[132,128]{1,0:T(8,128)S(1)}, u32[]{:S(2)}, u32[]{:S(2)}) collective-permute-start(f32[132,128]{1,0:T(8,128)S(1)} %concatenate.47), channel_id=1, source_target_pairs={{0,2},{1,3},{2,0},{3,1},{4,6},{5,7},{6,4},{7,5},{8,10},{9,11},{10,... | collective-permute-start | bytes 202760 | tf_op jit(solution)/shard_map/ppermute | solution.py:55
  40.3 4.4 %collective-permute-start.18 = (f32[132,128]{1,0:T(8,128)S(1)}, f32[132,128]{1,0:T(8,128)S(1)}, u32[]{:S(2)}, u32[]{:S(2)}) collective-permute-start(f32[132,128]{1,0:T(8,128)S(1)} %concatenate.46), channel_id=1, source_target_pairs={{0,1},{1,2},{2,3},{3,0},{4,5},{5,6},{6,7},{7,4},{8,9},{9,10},{10,1... | collective-permute-start | bytes 202760 | tf_op jit(solution)/shard_map/ppermute | solution.py:55
  45.5 5.1 %collective-permute-start.23 = (f32[132,128]{1,0:T(8,128)S(1)}, f32[132,128]{1,0:T(8,128)S(1)}, u32[]{:S(2)}, u32[]{:S(2)}) collective-permute-start(f32[132,128]{1,0:T(8,128)S(1)} %get-tuple-element.59), channel_id=1, source_target_pairs={{0,12},{4,0},{8,4},{12,8},{1,13},{5,1},{9,5},{13,9},{2,14},{6,2},{... | collective-permute-start | bytes 202760 | tf_op jit(solution)/shard_map/ppermute | solution.py:37
  48.0 6.6 %collective-permute-start.22 = (f32[132,128]{1,0:T(8,128)S(1)}, f32[132,128]{1,0:T(8,128)S(1)}, u32[]{:S(2)}, u32[]{:S(2)}) collective-permute-start(f32[132,128]{1,0:T(8,128)S(1)} %get-tuple-element.59), channel_id=1, source_target_pairs={{0,8},{4,12},{8,0},{12,4},{1,9},{5,13},{9,1},{13,5},{2,10},{6,14},... | collective-permute-start | bytes 202760 | tf_op jit(solution)/shard_map/ppermute | solution.py:37
  48.0 6.6 %collective-permute-start.21 = (f32[132,128]{1,0:T(8,128)S(1)}, f32[132,128]{1,0:T(8,128)S(1)}, u32[]{:S(2)}, u32[]{:S(2)}) collective-permute-start(f32[132,128]{1,0:T(8,128)S(1)} %get-tuple-element.59), channel_id=1, source_target_pairs={{0,4},{4,8},{8,12},{12,0},{1,5},{5,9},{9,13},{13,1},{2,6},{6,10},{... | collective-permute-start | bytes 202760 | tf_op jit(solution)/shard_map/ppermute | solution.py:37
  49.5 6.9 %collective-permute-start.26 = (f32[128,128]{1,0:T(8,128)S(1)}, f32[128,128]{1,0:T(8,128)S(1)}, u32[]{:S(2)}, u32[]{:S(2)}) collective-permute-start(f32[128,128]{1,0:T(8,128)S(1)} %multiply_subtract_fusion.3), channel_id=1, source_target_pairs={{0,3},{1,0},{2,1},{3,2},{4,7},{5,4},{6,5},{7,6},{8,11},{9,8},{10,9... | collective-permute-start | bytes 196616 | tf_op jit(solution)/shard_map/ppermute | solution.py:37
  49.6 6.9 %collective-permute-start.25 = (f32[128,128]{1,0:T(8,128)S(1)}, f32[128,128]{1,0:T(8,128)S(1)}, u32[]{:S(2)}, u32[]{:S(2)}) collective-permute-start(f32[128,128]{1,0:T(8,128)S(1)} %multiply_subtract_fusion.3), channel_id=1, source_target_pairs={{0,2},{1,3},{2,0},{3,1},{4,6},{5,7},{6,4},{7,5},{8,10},{9,11},{10,... | collective-permute-start | bytes 196616 | tf_op jit(solution)/shard_map/ppermute | solution.py:37
  50.6 5.9 %collective-permute-start.24 = (f32[128,128]{1,0:T(8,128)S(1)}, f32[128,128]{1,0:T(8,128)S(1)}, u32[]{:S(2)}, u32[]{:S(2)}) collective-permute-start(f32[128,128]{1,0:T(8,128)S(1)} %multiply_subtract_fusion.3), channel_id=1, source_target_pairs={{0,1},{1,2},{2,3},{3,0},{4,5},{5,6},{6,7},{7,4},{8,9},{9,10},{10,1... | collective-permute-start | bytes 196616 | tf_op jit(solution)/shard_map/ppermute | solution.py:37
  56.9 2.1 %collective-permute-start.29 = (f32[132,128]{1,0:T(8,128)S(1)}, f32[132,128]{1,0:T(8,128)S(1)}, u32[]{:S(2)}, u32[]{:S(2)}) collective-permute-start(f32[132,128]{1,0:T(8,128)S(1)} %concatenate.52), channel_id=1, source_target_pairs={{0,3},{1,0},{2,1},{3,2},{4,7},{5,4},{6,5},{7,6},{8,11},{9,8},{10,9... | collective-permute-start | bytes 202760 | tf_op jit(solution)/shard_map/ppermute | solution.py:55
  56.9 5.0 %collective-permute-start.28 = (f32[132,128]{1,0:T(8,128)S(1)}, f32[132,128]{1,0:T(8,128)S(1)}, u32[]{:S(2)}, u32[]{:S(2)}) collective-permute-start(f32[132,128]{1,0:T(8,128)S(1)} %concatenate.51), channel_id=1, source_target_pairs={{0,2},{1,3},{2,0},{3,1},{4,6},{5,7},{6,4},{7,5},{8,10},{9,11},{10,... | collective-permute-start | bytes 202760 | tf_op jit(solution)/shard_map/ppermute | solution.py:55
  58.0 4.4 %collective-permute-start.27 = (f32[132,128]{1,0:T(8,128)S(1)}, f32[132,128]{1,0:T(8,128)S(1)}, u32[]{:S(2)}, u32[]{:S(2)}) collective-permute-start(f32[132,128]{1,0:T(8,128)S(1)} %concatenate.50), channel_id=1, source_target_pairs={{0,1},{1,2},{2,3},{3,0},{4,5},{5,6},{6,7},{7,4},{8,9},{9,10},{10,1... | collective-permute-start | bytes 202760 | tf_op jit(solution)/shard_map/ppermute | solution.py:55
  63.1 3.8 %collective-permute-start.32 = (f32[4,128]{1,0:T(4,128)S(1)}, f32[4,128]{1,0:T(4,128)S(1)}, u32[]{:S(2)}, u32[]{:S(2)}) collective-permute-start(f32[4,128]{1,0:T(4,128)S(1)} %select_reduce_fusion.3), channel_id=1, source_target_pairs={{0,12},{4,0},{8,4},{12,8},{1,13},{5,1},{9,5},{13,9},{2,14},{6,2},{... | collective-permute-start | bytes 6152 | tf_op jit(solution)/shard_map/ppermute | solution.py:37
  65.0 4.5 %collective-permute-start.31 = (f32[4,128]{1,0:T(4,128)S(1)}, f32[4,128]{1,0:T(4,128)S(1)}, u32[]{:S(2)}, u32[]{:S(2)}) collective-permute-start(f32[4,128]{1,0:T(4,128)S(1)} %select_reduce_fusion.3), channel_id=1, source_target_pairs={{0,8},{4,12},{8,0},{12,4},{1,9},{5,13},{9,1},{13,5},{2,10},{6,14},... | collective-permute-start | bytes 6152 | tf_op jit(solution)/shard_map/ppermute | solution.py:37
  65.2 5.4 %collective-permute-start.30 = (f32[4,128]{1,0:T(4,128)S(1)}, f32[4,128]{1,0:T(4,128)S(1)}, u32[]{:S(2)}, u32[]{:S(2)}) collective-permute-start(f32[4,128]{1,0:T(4,128)S(1)} %select_reduce_fusion.3), channel_id=1, source_target_pairs={{0,4},{4,8},{8,12},{12,0},{1,5},{5,9},{9,13},{13,1},{2,6},{6,10},{... | collective-permute-start | bytes 6152 | tf_op jit(solution)/shard_map/ppermute | solution.py:37

commit v7 on v6

--- a/solution.py
+++ b/solution.py
@@ -61,8 +61,15 @@
 def canonical_sum(extras, axis, count):
     if count > 4:
         return jnp.sum(extras, axis=0)
-    order = (lax.axis_index(axis) - jnp.arange(count)) % count
-    return jnp.sum(jnp.take(extras, order, axis=0), axis=0)
+    me = lax.axis_index(axis)
+    total = None
+    for device in range(count):
+        wanted = (me - device) % count
+        term = extras[count - 1]
+        for entry in range(count - 2, -1, -1):
+            term = jnp.where(wanted == entry, extras[entry], term)
+        total = term if total is None else total + term
+    return total
 
 
 def source(axis, count, entry):
@@ -87,14 +94,13 @@
         jnp.where(pick[:, :, None, :, None], tiles[:, :, :, None, :], 0.0), axis=1
     )
     column_sums = jnp.sum(dense, axis=(0, 1)).reshape(n_narrow, own_rows)
-    degree = scatter_sum(column_sums, "narrow", n_narrow)
     order = source("wide", n_wide, jnp.arange(n_wide))
     dense = jnp.take(dense.reshape(n_wide, own_rows, column_blocks * tile), order, axis=0)
     transposed = dense.reshape(groups * tile, column_blocks * tile).T
 
     labels = seed_label[:, 0]
     seeded = (labels < SEED_CLASSES).astype(jnp.float32)
-    diag_column = (degree + SEED_WEIGHT * seeded + PRIOR)[:, None]
+    fixed_column = (SEED_WEIGHT * seeded + PRIOR)[:, None]
     classes = jnp.arange(SEED_CLASSES, dtype=jnp.int32)
 
     def indicator(values):
@@ -112,16 +118,17 @@
             quad = quad + jnp.sum(column_values[entry] * block, axis=0)
         return partial, quad
 
-    def exchange(partial, partial_sums, applied_of, last):
+    def narrow_step(partial, partial_sums):
         weighted, extras = scatter_with(partial, partial_sums, "narrow", n_narrow)
-        narrow_sums = canonical_sum(extras, "narrow", n_narrow)
-        applied = applied_of(weighted)
+        return weighted, canonical_sum(extras, "narrow", n_narrow)
+
+    def wide_step(applied, narrow_sums, last):
         if last:
             sums = canonical_sum(gather_blocks(narrow_sums, "wide", n_wide), "wide", n_wide)
-            return applied, None, None, sums
+            return None, None, sums
         got = gather_blocks(jnp.concatenate([applied, narrow_sums], axis=0), "wide", n_wide)
         sums = canonical_sum(got[:, own_rows:], "wide", n_wide)
-        return applied, got[:, :own_rows], gather_blocks(applied, "narrow", n_narrow), sums
+        return got[:, :own_rows], gather_blocks(applied, "narrow", n_narrow), sums
 
     rhs = indicator(labels)
     solution = jnp.zeros_like(rhs)
@@ -130,15 +137,25 @@
     rows_residual = indicator(gather_blocks(labels, "wide", n_wide))
     columns_residual = indicator(gather_blocks(labels, "narrow", n_narrow))
     partial, quad = product(rows_residual, columns_residual)
+    degree_part = jnp.zeros((width,), jnp.float32)
+    for entry in range(n_narrow):
+        sums_block = lax.dynamic_index_in_dim(
+            column_sums, source("narrow", n_narrow, entry), 0, keepdims=False
+        )
+        degree_part = degree_part + jnp.sum(
+            sums_block[:, None] * columns_residual[entry] * columns_residual[entry], axis=0
+        )
     partial_sums = jnp.stack(
         [
             jnp.sum(residual * residual, axis=0),
-            jnp.sum(diag_column * direction * direction, axis=0) - quad,
+            degree_part + jnp.sum(fixed_column * direction * direction, axis=0) - quad,
         ]
     )
-    image, rows_image, columns_image, first = exchange(
-        partial, partial_sums, lambda weighted: diag_column * direction - weighted, ITERS == 1
-    )
+    carried = jnp.concatenate([partial, column_sums[:, None, :]], axis=1)
+    weighted, narrow_sums = narrow_step(carried, partial_sums)
+    diag_column = weighted[own_rows][:, None] + fixed_column
+    image = diag_column * direction - weighted[:own_rows]
+    rows_image, columns_image, first = wide_step(image, narrow_sums, ITERS == 1)
     norm_now = first[0]
     curvature = first[1]
     for step in range(ITERS):
@@ -158,12 +175,9 @@
                 jnp.sum(direction * image, axis=0),
             ]
         )
-        applied, rows_applied, columns_applied, sums = exchange(
-            partial,
-            partial_sums,
-            lambda weighted: diag_column * residual - weighted,
-            step == ITERS - 2,
-        )
+        weighted, narrow_sums = narrow_step(partial, partial_sums)
+        applied = diag_column * residual - weighted
+        rows_applied, columns_applied, sums = wide_step(applied, narrow_sums, step == ITERS - 2)
         norm_next = sums[0]
         ratio = norm_next / norm_now
         curvature = sums[1] + ratio * (2.0 * sums[2] + ratio * sums[3])

time: 72.2 us -> 67.2 us (0.931)
  waiting for transfers between devices: 28.2 us -> 24.6 us
  local copies, waits for them, and re-layouts: 4.77 us -> 1.33 us
  starting transfers between devices: 28.1 us -> 29.7 us
    gather x6 -> x0, local copies, waits for them, and re-layouts: 3.42 us -> none  [canonical_sum(): return jnp.sum(jnp.take(extras, order, axis=0), axis=0)]
    ppermute x9, starting transfers between devices: 4.42 us -> 7.2 us  [scatter_with(): got = lax.ppermute(jnp.concatenate([sent, extra], axis=0), axis, pairs)]
    ppermute x3 -> x0, starting transfers between devices: 2.76 us -> none  [scatter_sum(): total = total + lax.ppermute(sent, axis, pairs)]
    ppermute x9, waiting for transfers between devices: 12.7 us -> 10.7 us  [scatter_with(): got = lax.ppermute(jnp.concatenate([sent, extra], axis=0), axis, pairs)]
    ppermute x3 -> x0, waiting for transfers between devices: 1.85 us -> none  [scatter_sum(): total = total + lax.ppermute(sent, axis, pairs)]
    ppermute x21, starting transfers between devices: 20.9 us -> 22.5 us  [gather_blocks(): parts.append(lax.ppermute(values, axis, pairs))]
  transfers between devices with their start and end apart: 33 -> 30, of which waited for: 17 -> 16; matrix products, arithmetic and copies ran while one was open for 11% -> 11% of each run, Pallas kernels for 0% -> 0%
where the time goes in v7:
time: 67.2 us; the launch traced here: 67 us
  starting transfers between devices  29.7 us (44%)
  waiting for transfers between devices  24.6 us (37%)
  other arithmetic  7.26 us (11%)
  matrix products  3.03 us (5%)
  local copies, waits for them, and re-layouts  1.33 us (2%)
  between operations  1.11 us (2%)
    ppermute x21, starting transfers between devices, gather_blocks(): parts.append(lax.ppermute(values, axis, pairs))  22.5 us
    ppermute x21, waiting for transfers between devices, gather_blocks(): parts.append(lax.ppermute(values, axis, pairs))  13.9 us
    ppermute x9, waiting for transfers between devices, scatter_with(): got = lax.ppermute(jnp.concatenate([sent, extra], axis=0), axis, pairs)  10.7 us
    ppermute x9, starting transfers between devices, scatter_with(): got = lax.ppermute(jnp.concatenate([sent, extra], axis=0), axis, pairs)  7.2 us
    dot_general x3, matrix products, product(): jnp.dot(transposed, row_values.reshape(groups * tile, width), precision=l...  3.03 us
    reduce_sum x1, other arithmetic, local(): column_sums = jnp.sum(dense, axis=(0, 1)).reshape(n_narrow, own_rows)  2.97 us
  transfers between devices with their start and end apart: 30, of which 16 were waited for; matrix products, arithmetic and copies ran while one was open for 11% of the time, Pallas kernels for 0%

profile of v7, /device:TPU:0, one launch (start us, length us, event | category | flops | bytes accessed | tf_op | source)
XLA Modules:
  0.0 67.0 jit_solution(12431413428870609240)
XLA Ops:
  0.6 2.4 %collective-permute-start.5 = (s32[128]{0:T(128)}, s32[128]{0:T(128)S(1)}, u32[]{:S(2)}, u32[]{:S(2)}) collective-permute-start(s32[128]{0:T(128)} %bitcast.261), channel_id=1, source_target_pairs={{0,3},{1,0},{2,1},{3,2},{4,7},{5,4},{6,5},{7,6},{8,11},{9,8},{10,9... | collective-permute-start | bytes 1544 | tf_op jit(solution)/shard_map/ppermute | solution.py:37
  3.1 0.6 collective-permute-start.4
  3.7 0.2 collective-permute-start.3
  3.9 3.6 %collective-permute-start.2 = (s32[128]{0:T(128)}, s32[128]{0:T(128)S(1)}, u32[]{:S(2)}, u32[]{:S(2)}) collective-permute-start(s32[128]{0:T(128)} %bitcast.264), channel_id=1, source_target_pairs={{0,12},{4,0},{8,4},{12,8},{1,13},{5,1},{9,5},{13,9},{2,14},{6,2},{... | collective-permute-start | bytes 1544 | tf_op jit(solution)/shard_map/ppermute | solution.py:37
  7.6 0.7 fusion.78
  8.2 0.7 %add_select_fusion = s32[4,8]{1,0:T(4,128)S(1)} fusion(s32[4,8]{1,0:T(4,128)} %param.4), kind=kLoop, calls=%fused_computation.143 | loop fusion | flops 480 | bytes 256 | tf_op jit(solution)/shard_map/jit(floor_divide)/jit(_where)/select_n | solution.py:91
  8.9 0.1 iota_compare_fusion.5
  9.0 3.0 %select_reduce_fusion = (f32[4,128]{1,0:T(4,128)S(1)}, f32[4,128,4,128]{3,1,2,0:T(8,128)S(1)}) fusion(f32[4,8,128,128]{3,2,1,0:T(8,128)} %param.3, pred[4,8,4]{2,1,0:T(8,128)(4,1)S(1)} %iota_compare_fusion.5), kind=kLoop, calls=%fused_computation.1 | loop fusion | flops 6028800 | bytes 3147904 | tf_op jit(solution)/shard_map/reduce_sum | solution.py:96
  12.0 0.1 copy_bitcast_fusion
  12.1 0.1 broadcast_bitcast_fusion
  12.2 0.1 fusion.32
  12.3 0.6 gather_fusion
  12.9 0.1 bitcast_select_fusion
  13.1 0.3 copy.7
  13.5 1.1 %collective-permute-start = (s32[128]{0:T(128)S(1)}, s32[128]{0:T(128)S(1)}, u32[]{:S(2)}, u32[]{:S(2)}) collective-permute-start(s32[128]{0:T(128)S(1)} %bitcast.267), channel_id=1, source_target_pairs={{0,4},{4,8},{8,12},{12,0},{1,5},{5,9},{9,13},{13,1},{2,6},{6,10},{... | collective-permute-start | bytes 1544 | tf_op jit(solution)/shard_map/ppermute | solution.py:37
  14.6 0.1 fusion.8
  14.8 4.1 %collective-permute-done = s32[128]{0:T(128)S(1)} collective-permute-done((s32[128]{0:T(128)S(1)}, s32[128]{0:T(128)S(1)}, u32[]{:S(2)}, u32[]{:S(2)}) %collective-permute-start) | collective-permute-done | bytes 544 | tf_op jit(solution)/shard_map/ppermute | solution.py:37
  18.9 1.1 %fusion.5 = f32[4,128,128]{2,1,0:T(8,128)S(1)} fusion(f32[4,128,512]{2,1,0:T(8,128)S(1)} %bitcast.230, s32[512]{0:T(512)S(1)} %get-tuple-element.61), kind=kOutput, calls=%fused_computation.22 | convolution fusion | flops 402784256 | bytes 1312768 | tf_op jit(solution)/shard_map/dot_general | solution.py:110
  20.0 0.2 fusion.29
  20.3 1.7 %collective-permute-start.8 = (f32[131,128]{1,0:T(8,128)S(1)}, f32[131,128]{1,0:T(8,128)S(1)}, u32[]{:S(2)}, u32[]{:S(2)}) collective-permute-start(f32[131,128]{1,0:T(8,128)S(1)} %get-tuple-element.68), channel_id=1, source_target_pairs={{0,3},{1,0},{2,1},{3,2},{4,7},{5,4},{6,5},{7,6},{8,11},{9,8},{10,9... | collective-permute-start | bytes 201224 | tf_op jit(solution)/shard_map/ppermute | solution.py:55
  22.0 1.2 %collective-permute-start.7 = (f32[131,128]{1,0:T(8,128)S(1)}, f32[131,128]{1,0:T(8,128)S(1)}, u32[]{:S(2)}, u32[]{:S(2)}) collective-permute-start(f32[131,128]{1,0:T(8,128)S(1)} %get-tuple-element.67), channel_id=1, source_target_pairs={{0,2},{1,3},{2,0},{3,1},{4,6},{5,7},{6,4},{7,5},{8,10},{9,11},{10,... | collective-permute-start | bytes 201224 | tf_op jit(solution)/shard_map/ppermute | solution.py:55
  23.2 0.8 %collective-permute-done.6 = f32[131,128]{1,0:T(8,128)S(1)} collective-permute-done((f32[131,128]{1,0:T(8,128)S(1)}, f32[131,128]{1,0:T(8,128)S(1)}, u32[]{:S(2)}, u32[]{:S(2)}) %collective-permute-start.6) | collective-permute-done | bytes 67104 | tf_op jit(solution)/shard_map/ppermute | solution.py:55
  24.0 0.2 collective-permute-done.8
  24.2 2.2 %collective-permute-done.7 = f32[131,128]{1,0:T(8,128)S(1)} collective-permute-done((f32[131,128]{1,0:T(8,128)S(1)}, f32[131,128]{1,0:T(8,128)S(1)}, u32[]{:S(2)}, u32[]{:S(2)}) %collective-permute-start.7) | collective-permute-done | bytes 67104 | tf_op jit(solution)/shard_map/ppermute | solution.py:55
  26.5 0.1 fusion.34
  26.7 0.1 collective-permute-start.9
  26.7 3.8 %collective-permute-start.11 = (f32[130,128]{1,0:T(8,128)S(1)}, f32[130,128]{1,0:T(8,128)S(1)}, u32[]{:S(2)}, u32[]{:S(2)}) collective-permute-start(f32[130,128]{1,0:T(8,128)S(1)} %get-tuple-element.58), channel_id=1, source_target_pairs={{0,12},{4,0},{8,4},{12,8},{1,13},{5,1},{9,5},{13,9},{2,14},{6,2},{... | collective-permute-start | bytes 199688 | tf_op jit(solution)/shard_map/ppermute | solution.py:37
  30.5 1.1 %collective-permute-start.13 = (f32[128,128]{1,0:T(8,128)S(1)}, f32[128,128]{1,0:T(8,128)S(1)}, u32[]{:S(2)}, u32[]{:S(2)}) collective-permute-start(f32[128,128]{1,0:T(8,128)S(1)} %fusion.34), channel_id=1, source_target_pairs={{0,2},{1,3},{2,0},{3,1},{4,6},{5,7},{6,4},{7,5},{8,10},{9,11},{10,... | collective-permute-start | bytes 196616 | tf_op jit(solution)/shard_map/ppermute | solution.py:37
  31.6 0.1 fusion.89
  31.7 1.5 %collective-permute-done.9 = f32[130,128]{1,0:T(8,128)S(1)} collective-permute-done((f32[130,128]{1,0:T(8,128)S(1)}, f32[130,128]{1,0:T(8,128)S(1)}, u32[]{:S(2)}, u32[]{:S(2)}) %collective-permute-start.9) | collective-permute-done | bytes 66592 | tf_op jit(solution)/shard_map/ppermute | solution.py:37
  33.3 2.6 %collective-permute-done.10 = f32[130,128]{1,0:T(8,128)S(1)} collective-permute-done((f32[130,128]{1,0:T(8,128)S(1)}, f32[130,128]{1,0:T(8,128)S(1)}, u32[]{:S(2)}, u32[]{:S(2)}) %collective-permute-start.10) | collective-permute-done | bytes 66592 | tf_op jit(solution)/shard_map/ppermute | solution.py:37
  35.9 0.1 multiply_reduce_fusion.3
  36.1 0.9 %collective-permute-done.12 = f32[128,128]{1,0:T(8,128)S(1)} collective-permute-done((f32[128,128]{1,0:T(8,128)S(1)}, f32[128,128]{1,0:T(8,128)S(1)}, u32[]{:S(2)}, u32[]{:S(2)}) %collective-permute-start.12) | collective-permute-done | bytes 65568 | tf_op jit(solution)/shard_map/ppermute | solution.py:37
  37.0 0.2 multiply_subtract_fusion.1
  37.2 1.0 %fusion.82 = f32[4,128,128]{2,1,0:T(8,128)S(1)} fusion(f32[4,128,512]{2,1,0:T(8,128)S(1)} %bitcast.231, f32[512,128,1]{1,0,2:T(8,128)S(1)} %bitcast.236), kind=kOutput, calls=%fused_computation.216 | convolution fusion | flops 402653184 | bytes 1572864 | tf_op jit(solution)/shard_map/dot_general | solution.py:110
  38.2 0.1 fusion.45
  38.4 1.8 %collective-permute-start.17 = (f32[132,128]{1,0:T(8,128)S(1)}, f32[132,128]{1,0:T(8,128)S(1)}, u32[]{:S(2)}, u32[]{:S(2)}) collective-permute-start(f32[132,128]{1,0:T(8,128)S(1)} %concatenate.52), channel_id=1, source_target_pairs={{0,3},{1,0},{2,1},{3,2},{4,7},{5,4},{6,5},{7,6},{8,11},{9,8},{10,9... | collective-permute-start | bytes 202760 | tf_op jit(solution)/shard_map/ppermute | solution.py:55
  40.2 1.0 %collective-permute-start.16 = (f32[132,128]{1,0:T(8,128)S(1)}, f32[132,128]{1,0:T(8,128)S(1)}, u32[]{:S(2)}, u32[]{:S(2)}) collective-permute-start(f32[132,128]{1,0:T(8,128)S(1)} %concatenate.51), channel_id=1, source_target_pairs={{0,2},{1,3},{2,0},{3,1},{4,6},{5,7},{6,4},{7,5},{8,10},{9,11},{10,... | collective-permute-start | bytes 202760 | tf_op jit(solution)/shard_map/ppermute | solution.py:55
  41.2 0.8 %collective-permute-done.15 = f32[132,128]{1,0:T(8,128)S(1)} collective-permute-done((f32[132,128]{1,0:T(8,128)S(1)}, f32[132,128]{1,0:T(8,128)S(1)}, u32[]{:S(2)}, u32[]{:S(2)}) %collective-permute-start.15) | collective-permute-done | bytes 67616 | tf_op jit(solution)/shard_map/ppermute | solution.py:55
  42.1 0.2 collective-permute-done.17
  42.2 2.3 %collective-permute-done.16 = f32[132,128]{1,0:T(8,128)S(1)} collective-permute-done((f32[132,128]{1,0:T(8,128)S(1)}, f32[132,128]{1,0:T(8,128)S(1)}, u32[]{:S(2)}, u32[]{:S(2)}) %collective-permute-start.16) | collective-permute-done | bytes 67616 | tf_op jit(solution)/shard_map/ppermute | solution.py:55
  44.6 0.1 multiply_subtract_fusion.3
  44.7 0.8 %collective-permute-start.20 = (f32[132,128]{1,0:T(8,128)S(1)}, f32[132,128]{1,0:T(8,128)S(1)}, u32[]{:S(2)}, u32[]{:S(2)}) collective-permute-start(f32[132,128]{1,0:T(8,128)S(1)} %get-tuple-element.56), channel_id=1, source_target_pairs={{0,12},{4,0},{8,4},{12,8},{1,13},{5,1},{9,5},{13,9},{2,14},{6,2},{... | collective-permute-start | bytes 202760 | tf_op jit(solution)/shard_map/ppermute | solution.py:37
  45.5 1.2 %collective-permute-start.19 = (f32[132,128]{1,0:T(8,128)S(1)}, f32[132,128]{1,0:T(8,128)S(1)}, u32[]{:S(2)}, u32[]{:S(2)}) collective-permute-start(f32[132,128]{1,0:T(8,128)S(1)} %get-tuple-element.56), channel_id=1, source_target_pairs={{0,8},{4,12},{8,0},{12,4},{1,9},{5,13},{9,1},{13,5},{2,10},{6,14},... | collective-permute-start | bytes 202760 | tf_op jit(solution)/shard_map/ppermute | solution.py:37
  46.8 1.9 %collective-permute-start.18 = (f32[132,128]{1,0:T(8,128)S(1)}, f32[132,128]{1,0:T(8,128)S(1)}, u32[]{:S(2)}, u32[]{:S(2)}) collective-permute-start(f32[132,128]{1,0:T(8,128)S(1)} %get-tuple-element.56), channel_id=1, source_target_pairs={{0,4},{4,8},{8,12},{12,0},{1,5},{5,9},{9,13},{13,1},{2,6},{6,10},{... | collective-permute-start | bytes 202760 | tf_op jit(solution)/shard_map/ppermute | solution.py:37
  48.7 0.9 %collective-permute-start.22 = (f32[128,128]{1,0:T(8,128)S(1)}, f32[128,128]{1,0:T(8,128)S(1)}, u32[]{:S(2)}, u32[]{:S(2)}) collective-permute-start(f32[128,128]{1,0:T(8,128)S(1)} %multiply_subtract_fusion.3), channel_id=1, source_target_pairs={{0,2},{1,3},{2,0},{3,1},{4,6},{5,7},{6,4},{7,5},{8,10},{9,11},{10,... | collective-permute-start | bytes 196616 | tf_op jit(solution)/shard_map/ppermute | solution.py:37
  49.7 0.2 collective-permute-start.21
  49.9 3.1 %collective-permute-done.19 = f32[132,128]{1,0:T(8,128)S(1)} collective-permute-done((f32[132,128]{1,0:T(8,128)S(1)}, f32[132,128]{1,0:T(8,128)S(1)}, u32[]{:S(2)}, u32[]{:S(2)}) %collective-permute-start.19) | collective-permute-done | bytes 67616 | tf_op jit(solution)/shard_map/ppermute | solution.py:37
  53.1 0.1 fusion.2
  53.2 1.0 %fusion.83 = f32[4,128,128]{2,1,0:T(8,128)S(1)} fusion(f32[4,128,512]{2,1,0:T(8,128)S(1)} %bitcast.232, f32[512,128,1]{1,0,2:T(8,128)S(1)} %bitcast.234), kind=kOutput, calls=%fused_computation.217 | convolution fusion | flops 402653184 | bytes 1572864 | tf_op jit(solution)/shard_map/dot_general | solution.py:110
  54.3 0.1 fusion.4
  54.4 0.1 dynamic-slice_bitcast_fusion.1
  54.5 0.1 multiply_reduce_fusion.2
  54.7 1.0 %collective-permute-start.25 = (f32[132,128]{1,0:T(8,128)S(1)}, f32[132,128]{1,0:T(8,128)S(1)}, u32[]{:S(2)}, u32[]{:S(2)}) collective-permute-start(f32[132,128]{1,0:T(8,128)S(1)} %concatenate.55), channel_id=1, source_target_pairs={{0,2},{1,3},{2,0},{3,1},{4,6},{5,7},{6,4},{7,5},{8,10},{9,11},{10,... | collective-permute-start | bytes 202760 | tf_op jit(solution)/shard_map/ppermute | solution.py:55
  55.8 0.3 collective-permute-start.24
  56.0 0.7 %collective-permute-done.26 = f32[132,128]{1,0:T(8,128)S(1)} collective-permute-done((f32[132,128]{1,0:T(8,128)S(1)}, f32[132,128]{1,0:T(8,128)S(1)}, u32[]{:S(2)}, u32[]{:S(2)}) %collective-permute-start.26) | collective-permute-done | bytes 67616 | tf_op jit(solution)/shard_map/ppermute | solution.py:55
  56.8 3.0 %collective-permute-done.25 = f32[132,128]{1,0:T(8,128)S(1)} collective-permute-done((f32[132,128]{1,0:T(8,128)S(1)}, f32[132,128]{1,0:T(8,128)S(1)}, u32[]{:S(2)}, u32[]{:S(2)}) %collective-permute-start.25) | collective-permute-done | bytes 67616 | tf_op jit(solution)/shard_map/ppermute | solution.py:55
  59.8 0.4 collective-permute-done.24
  60.2 0.3 collective-permute-start.27
  60.5 2.1 %collective-permute-start.28 = (f32[4,128]{1,0:T(4,128)S(1)}, f32[4,128]{1,0:T(4,128)S(1)}, u32[]{:S(2)}, u32[]{:S(2)}) collective-permute-start(f32[4,128]{1,0:T(4,128)S(1)} %select_add_fusion.1), channel_id=1, source_target_pairs={{0,8},{4,12},{8,0},{12,4},{1,9},{5,13},{9,1},{13,5},{2,10},{6,14},... | collective-permute-start | bytes 6152 | tf_op jit(solution)/shard_map/ppermute | solution.py:37
  62.6 2.1 %collective-permute-start.29 = (f32[4,128]{1,0:T(4,128)S(1)}, f32[4,128]{1,0:T(4,128)S(1)}, u32[]{:S(2)}, u32[]{:S(2)}) collective-permute-start(f32[4,128]{1,0:T(4,128)S(1)} %select_add_fusion.1), channel_id=1, source_target_pairs={{0,12},{4,0},{8,4},{12,8},{1,13},{5,1},{9,5},{13,9},{2,14},{6,2},{... | collective-permute-start | bytes 6152 | tf_op jit(solution)/shard_map/ppermute | solution.py:37
  64.7 0.9 %collective-permute-done.27 = f32[4,128]{1,0:T(4,128)S(1)} collective-permute-done((f32[4,128]{1,0:T(4,128)S(1)}, f32[4,128]{1,0:T(4,128)S(1)}, u32[]{:S(2)}, u32[]{:S(2)}) %collective-permute-start.27) | collective-permute-done | bytes 2080 | tf_op jit(solution)/shard_map/ppermute | solution.py:37
  65.6 0.6 collective-permute-done.29
  66.2 0.8 %fusion.27 = (f32[128,128]{1,0:T(8,128)}, f32[128,128]{1,0:T(8,128)}) fusion(f32[132,128]{1,0:T(8,128)S(1)} %collective-permute-done.26, f32[132,128]{1,0:T(8,128)S(1)} %collective-permute-done.25, f32[132,128]{1,0:T(8,128)S(1)} %collective-permute-done.24, f32[128,128]{1,0:T(8,128)S(1)} %get-tuple-element.38, f32[4,128,128]{2,1,0:T(8,128)S(1)} %fusion.83, ...), kind=kLoop, calls=%fused_computation.77 | loop fusion | flops 425984 | bytes 527876 | tf_op jit(solution)/shard_map/sub | solution.py:164
  (56 shorter events, 0.7 us)
Async XLA Ops:
  0.6 12.9 %collective-permute-start.5 = (s32[128]{0:T(128)}, s32[128]{0:T(128)S(1)}, u32[]{:S(2)}, u32[]{:S(2)}) collective-permute-start(s32[128]{0:T(128)} %bitcast.261), channel_id=1, source_target_pairs={{0,3},{1,0},{2,1},{3,2},{4,7},{5,4},{6,5},{7,6},{8,11},{9,8},{10,9... | collective-permute-start | bytes 1544 | tf_op jit(solution)/shard_map/ppermute | solution.py:37
  3.1 11.5 %collective-permute-start.4 = (s32[128]{0:T(128)}, s32[128]{0:T(128)S(1)}, u32[]{:S(2)}, u32[]{:S(2)}) collective-permute-start(s32[128]{0:T(128)} %bitcast.262), channel_id=1, source_target_pairs={{0,2},{1,3},{2,0},{3,1},{4,6},{5,7},{6,4},{7,5},{8,10},{9,11},{10,... | collective-permute-start | bytes 1544 | tf_op jit(solution)/shard_map/ppermute | solution.py:37
  3.7 10.9 %collective-permute-start.3 = (s32[128]{0:T(128)}, s32[128]{0:T(128)S(1)}, u32[]{:S(2)}, u32[]{:S(2)}) collective-permute-start(s32[128]{0:T(128)} %bitcast.263), channel_id=1, source_target_pairs={{0,1},{1,2},{2,3},{3,0},{4,5},{5,6},{6,7},{7,4},{8,9},{9,10},{10,1... | collective-permute-start | bytes 1544 | tf_op jit(solution)/shard_map/ppermute | solution.py:37
  3.9 10.9 %collective-permute-start.2 = (s32[128]{0:T(128)}, s32[128]{0:T(128)S(1)}, u32[]{:S(2)}, u32[]{:S(2)}) collective-permute-start(s32[128]{0:T(128)} %bitcast.264), channel_id=1, source_target_pairs={{0,12},{4,0},{8,4},{12,8},{1,13},{5,1},{9,5},{13,9},{2,14},{6,2},{... | collective-permute-start | bytes 1544 | tf_op jit(solution)/shard_map/ppermute | solution.py:37
  7.5 7.3 %collective-permute-start.1 = (s32[128]{0:T(128)}, s32[128]{0:T(128)S(1)}, u32[]{:S(2)}, u32[]{:S(2)}) collective-permute-start(s32[128]{0:T(128)} %bitcast.265), channel_id=1, source_target_pairs={{0,8},{4,12},{8,0},{12,4},{1,9},{5,13},{9,1},{13,5},{2,10},{6,14},... | collective-permute-start | bytes 1544 | tf_op jit(solution)/shard_map/ppermute | solution.py:37
  9.0 3.2 %copy-start = (s32[128,1]{0,1:T(1,128)S(1)}, s32[128,1]{0,1:T(1,128)}, u32[]{:S(2)}) copy-start(s32[128,1]{0,1:T(1,128)} %param.5) | copy-start | bytes 1540
  13.5 5.4 %collective-permute-start = (s32[128]{0:T(128)S(1)}, s32[128]{0:T(128)S(1)}, u32[]{:S(2)}, u32[]{:S(2)}) collective-permute-start(s32[128]{0:T(128)S(1)} %bitcast.267), channel_id=1, source_target_pairs={{0,4},{4,8},{8,12},{12,0},{1,5},{5,9},{9,13},{13,1},{2,6},{6,10},{... | collective-permute-start | bytes 1544 | tf_op jit(solution)/shard_map/ppermute | solution.py:37
  20.2 3.8 %collective-permute-start.6 = (f32[131,128]{1,0:T(8,128)S(1)}, f32[131,128]{1,0:T(8,128)S(1)}, u32[]{:S(2)}, u32[]{:S(2)}) collective-permute-start(f32[131,128]{1,0:T(8,128)S(1)} %get-tuple-element.66), channel_id=1, source_target_pairs={{0,1},{1,2},{2,3},{3,0},{4,5},{5,6},{6,7},{7,4},{8,9},{9,10},{10,1... | collective-permute-start | bytes 201224 | tf_op jit(solution)/shard_map/ppermute | solution.py:55
  20.3 4.0 %collective-permute-start.8 = (f32[131,128]{1,0:T(8,128)S(1)}, f32[131,128]{1,0:T(8,128)S(1)}, u32[]{:S(2)}, u32[]{:S(2)}) collective-permute-start(f32[131,128]{1,0:T(8,128)S(1)} %get-tuple-element.68), channel_id=1, source_target_pairs={{0,3},{1,0},{2,1},{3,2},{4,7},{5,4},{6,5},{7,6},{8,11},{9,8},{10,9... | collective-permute-start | bytes 201224 | tf_op jit(solution)/shard_map/ppermute | solution.py:55
  22.0 4.5 %collective-permute-start.7 = (f32[131,128]{1,0:T(8,128)S(1)}, f32[131,128]{1,0:T(8,128)S(1)}, u32[]{:S(2)}, u32[]{:S(2)}) collective-permute-start(f32[131,128]{1,0:T(8,128)S(1)} %get-tuple-element.67), channel_id=1, source_target_pairs={{0,2},{1,3},{2,0},{3,1},{4,6},{5,7},{6,4},{7,5},{8,10},{9,11},{10,... | collective-permute-start | bytes 201224 | tf_op jit(solution)/shard_map/ppermute | solution.py:55
  26.7 6.6 %collective-permute-start.9 = (f32[130,128]{1,0:T(8,128)S(1)}, f32[130,128]{1,0:T(8,128)S(1)}, u32[]{:S(2)}, u32[]{:S(2)}) collective-permute-start(f32[130,128]{1,0:T(8,128)S(1)} %get-tuple-element.58), channel_id=1, source_target_pairs={{0,4},{4,8},{8,12},{12,0},{1,5},{5,9},{9,13},{13,1},{2,6},{6,10},{... | collective-permute-start | bytes 199688 | tf_op jit(solution)/shard_map/ppermute | solution.py:37
  26.7 6.5 %collective-permute-start.11 = (f32[130,128]{1,0:T(8,128)S(1)}, f32[130,128]{1,0:T(8,128)S(1)}, u32[]{:S(2)}, u32[]{:S(2)}) collective-permute-start(f32[130,128]{1,0:T(8,128)S(1)} %get-tuple-element.58), channel_id=1, source_target_pairs={{0,12},{4,0},{8,4},{12,8},{1,13},{5,1},{9,5},{13,9},{2,14},{6,2},{... | collective-permute-start | bytes 199688 | tf_op jit(solution)/shard_map/ppermute | solution.py:37
  30.5 5.3 %collective-permute-start.10 = (f32[130,128]{1,0:T(8,128)S(1)}, f32[130,128]{1,0:T(8,128)S(1)}, u32[]{:S(2)}, u32[]{:S(2)}) collective-permute-start(f32[130,128]{1,0:T(8,128)S(1)} %get-tuple-element.58), channel_id=1, source_target_pairs={{0,8},{4,12},{8,0},{12,4},{1,9},{5,13},{9,1},{13,5},{2,10},{6,14},... | collective-permute-start | bytes 199688 | tf_op jit(solution)/shard_map/ppermute | solution.py:37
  30.5 5.5 %collective-permute-start.14 = (f32[128,128]{1,0:T(8,128)S(1)}, f32[128,128]{1,0:T(8,128)S(1)}, u32[]{:S(2)}, u32[]{:S(2)}) collective-permute-start(f32[128,128]{1,0:T(8,128)S(1)} %fusion.34), channel_id=1, source_target_pairs={{0,3},{1,0},{2,1},{3,2},{4,7},{5,4},{6,5},{7,6},{8,11},{9,8},{10,9... | collective-permute-start | bytes 196616 | tf_op jit(solution)/shard_map/ppermute | solution.py:37
  30.5 5.5 %collective-permute-start.13 = (f32[128,128]{1,0:T(8,128)S(1)}, f32[128,128]{1,0:T(8,128)S(1)}, u32[]{:S(2)}, u32[]{:S(2)}) collective-permute-start(f32[128,128]{1,0:T(8,128)S(1)} %fusion.34), channel_id=1, source_target_pairs={{0,2},{1,3},{2,0},{3,1},{4,6},{5,7},{6,4},{7,5},{8,10},{9,11},{10,... | collective-permute-start | bytes 196616 | tf_op jit(solution)/shard_map/ppermute | solution.py:37
  33.3 3.7 %collective-permute-start.12 = (f32[128,128]{1,0:T(8,128)S(1)}, f32[128,128]{1,0:T(8,128)S(1)}, u32[]{:S(2)}, u32[]{:S(2)}) collective-permute-start(f32[128,128]{1,0:T(8,128)S(1)} %fusion.34), channel_id=1, source_target_pairs={{0,1},{1,2},{2,3},{3,0},{4,5},{5,6},{6,7},{7,4},{8,9},{9,10},{10,1... | collective-permute-start | bytes 196616 | tf_op jit(solution)/shard_map/ppermute | solution.py:37
  38.3 3.8 %collective-permute-start.15 = (f32[132,128]{1,0:T(8,128)S(1)}, f32[132,128]{1,0:T(8,128)S(1)}, u32[]{:S(2)}, u32[]{:S(2)}) collective-permute-start(f32[132,128]{1,0:T(8,128)S(1)} %concatenate.50), channel_id=1, source_target_pairs={{0,1},{1,2},{2,3},{3,0},{4,5},{5,6},{6,7},{7,4},{8,9},{9,10},{10,1... | collective-permute-start | bytes 202760 | tf_op jit(solution)/shard_map/ppermute | solution.py:55
  38.4 3.9 %collective-permute-start.17 = (f32[132,128]{1,0:T(8,128)S(1)}, f32[132,128]{1,0:T(8,128)S(1)}, u32[]{:S(2)}, u32[]{:S(2)}) collective-permute-start(f32[132,128]{1,0:T(8,128)S(1)} %concatenate.52), channel_id=1, source_target_pairs={{0,3},{1,0},{2,1},{3,2},{4,7},{5,4},{6,5},{7,6},{8,11},{9,8},{10,9... | collective-permute-start | bytes 202760 | tf_op jit(solution)/shard_map/ppermute | solution.py:55
  40.2 4.4 %collective-permute-start.16 = (f32[132,128]{1,0:T(8,128)S(1)}, f32[132,128]{1,0:T(8,128)S(1)}, u32[]{:S(2)}, u32[]{:S(2)}) collective-permute-start(f32[132,128]{1,0:T(8,128)S(1)} %concatenate.51), channel_id=1, source_target_pairs={{0,2},{1,3},{2,0},{3,1},{4,6},{5,7},{6,4},{7,5},{8,10},{9,11},{10,... | collective-permute-start | bytes 202760 | tf_op jit(solution)/shard_map/ppermute | solution.py:55
  44.7 5.0 %collective-permute-start.20 = (f32[132,128]{1,0:T(8,128)S(1)}, f32[132,128]{1,0:T(8,128)S(1)}, u32[]{:S(2)}, u32[]{:S(2)}) collective-permute-start(f32[132,128]{1,0:T(8,128)S(1)} %get-tuple-element.56), channel_id=1, source_target_pairs={{0,12},{4,0},{8,4},{12,8},{1,13},{5,1},{9,5},{13,9},{2,14},{6,2},{... | collective-permute-start | bytes 202760 | tf_op jit(solution)/shard_map/ppermute | solution.py:37
  45.5 7.5 %collective-permute-start.19 = (f32[132,128]{1,0:T(8,128)S(1)}, f32[132,128]{1,0:T(8,128)S(1)}, u32[]{:S(2)}, u32[]{:S(2)}) collective-permute-start(f32[132,128]{1,0:T(8,128)S(1)} %get-tuple-element.56), channel_id=1, source_target_pairs={{0,8},{4,12},{8,0},{12,4},{1,9},{5,13},{9,1},{13,5},{2,10},{6,14},... | collective-permute-start | bytes 202760 | tf_op jit(solution)/shard_map/ppermute | solution.py:37
  46.8 6.3 %collective-permute-start.18 = (f32[132,128]{1,0:T(8,128)S(1)}, f32[132,128]{1,0:T(8,128)S(1)}, u32[]{:S(2)}, u32[]{:S(2)}) collective-permute-start(f32[132,128]{1,0:T(8,128)S(1)} %get-tuple-element.56), channel_id=1, source_target_pairs={{0,4},{4,8},{8,12},{12,0},{1,5},{5,9},{9,13},{13,1},{2,6},{6,10},{... | collective-permute-start | bytes 202760 | tf_op jit(solution)/shard_map/ppermute | solution.py:37
  48.7 5.5 %collective-permute-start.23 = (f32[128,128]{1,0:T(8,128)S(1)}, f32[128,128]{1,0:T(8,128)S(1)}, u32[]{:S(2)}, u32[]{:S(2)}) collective-permute-start(f32[128,128]{1,0:T(8,128)S(1)} %multiply_subtract_fusion.3), channel_id=1, source_target_pairs={{0,3},{1,0},{2,1},{3,2},{4,7},{5,4},{6,5},{7,6},{8,11},{9,8},{10,9... | collective-permute-start | bytes 196616 | tf_op jit(solution)/shard_map/ppermute | solution.py:37
  48.7 5.5 %collective-permute-start.22 = (f32[128,128]{1,0:T(8,128)S(1)}, f32[128,128]{1,0:T(8,128)S(1)}, u32[]{:S(2)}, u32[]{:S(2)}) collective-permute-start(f32[128,128]{1,0:T(8,128)S(1)} %multiply_subtract_fusion.3), channel_id=1, source_target_pairs={{0,2},{1,3},{2,0},{3,1},{4,6},{5,7},{6,4},{7,5},{8,10},{9,11},{10,... | collective-permute-start | bytes 196616 | tf_op jit(solution)/shard_map/ppermute | solution.py:37
  49.7 4.6 %collective-permute-start.21 = (f32[128,128]{1,0:T(8,128)S(1)}, f32[128,128]{1,0:T(8,128)S(1)}, u32[]{:S(2)}, u32[]{:S(2)}) collective-permute-start(f32[128,128]{1,0:T(8,128)S(1)} %multiply_subtract_fusion.3), channel_id=1, source_target_pairs={{0,1},{1,2},{2,3},{3,0},{4,5},{5,6},{6,7},{7,4},{8,9},{9,10},{10,1... | collective-permute-start | bytes 196616 | tf_op jit(solution)/shard_map/ppermute | solution.py:37
  54.6 2.1 %collective-permute-start.26 = (f32[132,128]{1,0:T(8,128)S(1)}, f32[132,128]{1,0:T(8,128)S(1)}, u32[]{:S(2)}, u32[]{:S(2)}) collective-permute-start(f32[132,128]{1,0:T(8,128)S(1)} %concatenate.56), channel_id=1, source_target_pairs={{0,3},{1,0},{2,1},{3,2},{4,7},{5,4},{6,5},{7,6},{8,11},{9,8},{10,9... | collective-permute-start | bytes 202760 | tf_op jit(solution)/shard_map/ppermute | solution.py:55
  54.7 5.0 %collective-permute-start.25 = (f32[132,128]{1,0:T(8,128)S(1)}, f32[132,128]{1,0:T(8,128)S(1)}, u32[]{:S(2)}, u32[]{:S(2)}) collective-permute-start(f32[132,128]{1,0:T(8,128)S(1)} %concatenate.55), channel_id=1, source_target_pairs={{0,2},{1,3},{2,0},{3,1},{4,6},{5,7},{6,4},{7,5},{8,10},{9,11},{10,... | collective-permute-start | bytes 202760 | tf_op jit(solution)/shard_map/ppermute | solution.py:55
  55.8 4.4 %collective-permute-start.24 = (f32[132,128]{1,0:T(8,128)S(1)}, f32[132,128]{1,0:T(8,128)S(1)}, u32[]{:S(2)}, u32[]{:S(2)}) collective-permute-start(f32[132,128]{1,0:T(8,128)S(1)} %concatenate.54), channel_id=1, source_target_pairs={{0,1},{1,2},{2,3},{3,0},{4,5},{5,6},{6,7},{7,4},{8,9},{9,10},{10,1... | collective-permute-start | bytes 202760 | tf_op jit(solution)/shard_map/ppermute | solution.py:55
  60.2 5.4 %collective-permute-start.27 = (f32[4,128]{1,0:T(4,128)S(1)}, f32[4,128]{1,0:T(4,128)S(1)}, u32[]{:S(2)}, u32[]{:S(2)}) collective-permute-start(f32[4,128]{1,0:T(4,128)S(1)} %select_add_fusion.1), channel_id=1, source_target_pairs={{0,4},{4,8},{8,12},{12,0},{1,5},{5,9},{9,13},{13,1},{2,6},{6,10},{... | collective-permute-start | bytes 6152 | tf_op jit(solution)/shard_map/ppermute | solution.py:37
  60.5 5.2 %collective-permute-start.28 = (f32[4,128]{1,0:T(4,128)S(1)}, f32[4,128]{1,0:T(4,128)S(1)}, u32[]{:S(2)}, u32[]{:S(2)}) collective-permute-start(f32[4,128]{1,0:T(4,128)S(1)} %select_add_fusion.1), channel_id=1, source_target_pairs={{0,8},{4,12},{8,0},{12,4},{1,9},{5,13},{9,1},{13,5},{2,10},{6,14},... | collective-permute-start | bytes 6152 | tf_op jit(solution)/shard_map/ppermute | solution.py:37
  62.6 3.6 %collective-permute-start.29 = (f32[4,128]{1,0:T(4,128)S(1)}, f32[4,128]{1,0:T(4,128)S(1)}, u32[]{:S(2)}, u32[]{:S(2)}) collective-permute-start(f32[4,128]{1,0:T(4,128)S(1)} %select_add_fusion.1), channel_id=1, source_target_pairs={{0,12},{4,0},{8,4},{12,8},{1,13},{5,1},{9,5},{13,9},{2,14},{6,2},{... | collective-permute-start | bytes 6152 | tf_op jit(solution)/shard_map/ppermute | solution.py:37

commit v8 on v7

--- a/solution.py
+++ b/solution.py
@@ -29,7 +29,7 @@
 
 
 def gather_blocks(values, axis, count):
-    if count > 4:
+    if count > 4 or axis == "narrow":
         return lax.all_gather(values, axis, axis=0, tiled=False)
     parts = [values]
     for shift in range(1, count):
@@ -73,7 +73,7 @@
 
 
 def source(axis, count, entry):
-    if count > 4:
+    if count > 4 or axis == "narrow":
         return entry
     return (lax.axis_index(axis) - entry) % count
 

time: 67.2 us -> 69.5 us (1.034)
  blocking collectives: 0 us -> 16.7 us
  waiting for transfers between devices: 24.6 us -> 14 us
  starting transfers between devices: 29.7 us -> 26.2 us
    all_gather x0 -> x3, blocking collectives: none -> 16.7 us  [gather_blocks(): return lax.all_gather(values, axis, axis=0, tiled=False)]
    ppermute x21 -> x12, waiting for transfers between devices: 13.9 us -> 1.38 us  [gather_blocks(): parts.append(lax.ppermute(values, axis, pairs))]
    ppermute x21 -> x12, starting transfers between devices: 22.5 us -> 20 us  [gather_blocks(): parts.append(lax.ppermute(values, axis, pairs))]
    ppermute x9, waiting for transfers between devices: 10.7 us -> 12.6 us  [scatter_with(): got = lax.ppermute(jnp.concatenate([sent, extra], axis=0), axis, pairs)]
    ppermute x9, starting transfers between devices: 7.2 us -> 6.21 us  [scatter_with(): got = lax.ppermute(jnp.concatenate([sent, extra], axis=0), axis, pairs)]
  transfers between devices with their start and end apart: 30 -> 21, of which waited for: 16 -> 11; matrix products, arithmetic and copies ran while one was open for 11% -> 9% of each run, Pallas kernels for 0% -> 0%
where the time goes in v8:
time: 69.5 us; the launch traced here: 69.2 us
  starting transfers between devices  26.2 us (38%)
  blocking collectives  16.7 us (24%)
  waiting for transfers between devices  14 us (20%)
  other arithmetic  7.06 us (10%)
  matrix products  3.03 us (4%)
  local copies, waits for them, and re-layouts  1.32 us (2%)
  between operations  0.97 us (1%)
    ppermute x12, starting transfers between devices, gather_blocks(): parts.append(lax.ppermute(values, axis, pairs))  20 us
    all_gather x3, blocking collectives, gather_blocks(): return lax.all_gather(values, axis, axis=0, tiled=False)  16.7 us
    ppermute x9, waiting for transfers between devices, scatter_with(): got = lax.ppermute(jnp.concatenate([sent, extra], axis=0), axis, pairs)  12.6 us
    ppermute x9, starting transfers between devices, scatter_with(): got = lax.ppermute(jnp.concatenate([sent, extra], axis=0), axis, pairs)  6.21 us
    dot_general x3, matrix products, product(): jnp.dot(transposed, row_values.reshape(groups * tile, width), precision=l...  3.03 us
    reduce_sum x1, other arithmetic, local(): column_sums = jnp.sum(dense, axis=(0, 1)).reshape(n_narrow, own_rows)  2.97 us
  transfers between devices with their start and end apart: 21, of which 11 were waited for; matrix products, arithmetic and copies ran while one was open for 9% of the time, Pallas kernels for 0%

profile of v8, /device:TPU:0, one launch (start us, length us, event | category | flops | bytes accessed | tf_op | source)
XLA Modules:
  0.0 69.2 jit_solution(8570006934061006853)
XLA Ops:
  0.6 5.1 %collective-permute-start.2 = (s32[128]{0:T(128)}, s32[128]{0:T(128)S(1)}, u32[]{:S(2)}, u32[]{:S(2)}) collective-permute-start(s32[128]{0:T(128)} %bitcast.256), channel_id=1, source_target_pairs={{0,12},{4,0},{8,4},{12,8},{1,13},{5,1},{9,5},{13,9},{2,14},{6,2},{... | collective-permute-start | bytes 1544 | tf_op jit(solution)/shard_map/ppermute | solution.py:37
  5.7 1.0 %collective-permute-start = (s32[128]{0:T(128)}, s32[128]{0:T(128)S(1)}, u32[]{:S(2)}, u32[]{:S(2)}) collective-permute-start(s32[128]{0:T(128)} %bitcast.258), channel_id=1, source_target_pairs={{0,4},{4,8},{8,12},{12,0},{1,5},{5,9},{9,13},{13,1},{2,6},{6,10},{... | collective-permute-start | bytes 1544 | tf_op jit(solution)/shard_map/ppermute | solution.py:37
  6.8 5.2 %all-gather = s32[512,1]{0,1:T(1,128)S(1)} all-gather(s32[128,1]{0,1:T(1,128)} %param.5), channel_id=2, replica_groups=mesh['vol'=2,'wide'=4,'narrow'=4] {'narrow'}, dimensions={0}, use_global_device_ids=true | all-gather | bytes 2560 | tf_op jit(solution)/shard_map/all_gather | solution.py:33
  12.0 0.7 fusion.72
  12.6 0.7 add_select_fusion
  13.3 0.1 iota_compare_fusion.5
  13.4 3.0 %select_reduce_fusion = (f32[4,128]{1,0:T(4,128)S(1)}, f32[4,128,4,128]{3,1,2,0:T(8,128)S(1)}) fusion(f32[4,8,128,128]{3,2,1,0:T(8,128)} %param.3, pred[4,8,4]{2,1,0:T(8,128)(4,1)S(1)} %iota_compare_fusion.5), kind=kLoop, calls=%fused_computation.1 | loop fusion | flops 6028800 | bytes 3147904 | tf_op jit(solution)/shard_map/reduce_sum | solution.py:96
  16.4 0.1 copy_bitcast_fusion
  16.5 0.1 broadcast_bitcast_fusion
  16.6 0.1 fusion.6
  16.7 0.1 fusion.30
  16.9 0.6 gather_fusion
  17.5 0.1 bitcast_select_fusion
  17.6 0.3 copy.7
  18.0 0.0 collective-permute-done.2
  18.0 0.0 collective-permute-done.1
  18.1 1.1 %fusion.3 = f32[4,128,128]{2,1,0:T(8,128)S(1)} fusion(f32[4,128,512]{2,1,0:T(8,128)S(1)} %bitcast.229, s32[512]{0:T(512)S(1)} %get-tuple-element.61), kind=kOutput, calls=%fused_computation.18 | convolution fusion | flops 402784256 | bytes 1312768 | tf_op jit(solution)/shard_map/dot_general | solution.py:110
  19.1 0.2 fusion.27
  19.4 1.4 %collective-permute-start.5 = (f32[131,128]{1,0:T(8,128)S(1)}, f32[131,128]{1,0:T(8,128)S(1)}, u32[]{:S(2)}, u32[]{:S(2)}) collective-permute-start(f32[131,128]{1,0:T(8,128)S(1)} %get-tuple-element.70), channel_id=1, source_target_pairs={{0,3},{1,0},{2,1},{3,2},{4,7},{5,4},{6,5},{7,6},{8,11},{9,8},{10,9... | collective-permute-start | bytes 201224 | tf_op jit(solution)/shard_map/ppermute | solution.py:55
  20.8 0.5 collective-permute-start.4
  21.3 1.7 %collective-permute-done.5 = f32[131,128]{1,0:T(8,128)S(1)} collective-permute-done((f32[131,128]{1,0:T(8,128)S(1)}, f32[131,128]{1,0:T(8,128)S(1)}, u32[]{:S(2)}, u32[]{:S(2)}) %collective-permute-start.5) | collective-permute-done | bytes 67104 | tf_op jit(solution)/shard_map/ppermute | solution.py:55
  23.0 2.8 %collective-permute-done.4 = f32[131,128]{1,0:T(8,128)S(1)} collective-permute-done((f32[131,128]{1,0:T(8,128)S(1)}, f32[131,128]{1,0:T(8,128)S(1)}, u32[]{:S(2)}, u32[]{:S(2)}) %collective-permute-start.4) | collective-permute-done | bytes 67104 | tf_op jit(solution)/shard_map/ppermute | solution.py:55
  25.9 0.1 fusion.32
  26.0 2.5 %collective-permute-start.6 = (f32[130,128]{1,0:T(8,128)S(1)}, f32[130,128]{1,0:T(8,128)S(1)}, u32[]{:S(2)}, u32[]{:S(2)}) collective-permute-start(f32[130,128]{1,0:T(8,128)S(1)} %get-tuple-element.58), channel_id=1, source_target_pairs={{0,4},{4,8},{8,12},{12,0},{1,5},{5,9},{9,13},{13,1},{2,6},{6,10},{... | collective-permute-start | bytes 199688 | tf_op jit(solution)/shard_map/ppermute | solution.py:37
  28.5 1.3 %collective-permute-start.8 = (f32[130,128]{1,0:T(8,128)S(1)}, f32[130,128]{1,0:T(8,128)S(1)}, u32[]{:S(2)}, u32[]{:S(2)}) collective-permute-start(f32[130,128]{1,0:T(8,128)S(1)} %get-tuple-element.58), channel_id=1, source_target_pairs={{0,12},{4,0},{8,4},{12,8},{1,13},{5,1},{9,5},{13,9},{2,14},{6,2},{... | collective-permute-start | bytes 199688 | tf_op jit(solution)/shard_map/ppermute | solution.py:37
  29.9 0.2 collective-permute-start.7
  30.1 5.8 %all-gather.1 = f32[512,128]{1,0:T(8,128)S(1)} all-gather(f32[128,128]{1,0:T(8,128)S(1)} %fusion.32), channel_id=3, replica_groups=mesh['vol'=2,'wide'=4,'narrow'=4] {'narrow'}, dimensions={0}, use_global_device_ids=true | all-gather | bytes 327680 | tf_op jit(solution)/shard_map/all_gather | solution.py:33
  35.8 0.0 collective-permute-done.6
  35.8 0.0 collective-permute-done.8
  35.8 0.1 collective-permute-done.7
  35.9 0.2 multiply_subtract_fusion.1
  36.1 1.0 %fusion.76 = f32[4,128,128]{2,1,0:T(8,128)S(1)} fusion(f32[4,128,512]{2,1,0:T(8,128)S(1)} %bitcast.230, f32[512,128,1]{1,0,2:T(8,128)S(1)} %bitcast.237), kind=kOutput, calls=%fused_computation.208 | convolution fusion | flops 402653184 | bytes 1572864 | tf_op jit(solution)/shard_map/dot_general | solution.py:110
  37.1 0.1 multiply_reduce_fusion.3
  37.3 0.1 fusion.43
  37.4 1.1 %collective-permute-start.11 = (f32[132,128]{1,0:T(8,128)S(1)}, f32[132,128]{1,0:T(8,128)S(1)}, u32[]{:S(2)}, u32[]{:S(2)}) collective-permute-start(f32[132,128]{1,0:T(8,128)S(1)} %concatenate.52), channel_id=1, source_target_pairs={{0,3},{1,0},{2,1},{3,2},{4,7},{5,4},{6,5},{7,6},{8,11},{9,8},{10,9... | collective-permute-start | bytes 202760 | tf_op jit(solution)/shard_map/ppermute | solution.py:55
  38.5 0.9 %collective-permute-start.10 = (f32[132,128]{1,0:T(8,128)S(1)}, f32[132,128]{1,0:T(8,128)S(1)}, u32[]{:S(2)}, u32[]{:S(2)}) collective-permute-start(f32[132,128]{1,0:T(8,128)S(1)} %concatenate.51), channel_id=1, source_target_pairs={{0,2},{1,3},{2,0},{3,1},{4,6},{5,7},{6,4},{7,5},{8,10},{9,11},{10,... | collective-permute-start | bytes 202760 | tf_op jit(solution)/shard_map/ppermute | solution.py:55
  39.5 0.0 collective-permute-start.9
  39.5 1.2 %collective-permute-done.11 = f32[132,128]{1,0:T(8,128)S(1)} collective-permute-done((f32[132,128]{1,0:T(8,128)S(1)}, f32[132,128]{1,0:T(8,128)S(1)}, u32[]{:S(2)}, u32[]{:S(2)}) %collective-permute-start.11) | collective-permute-done | bytes 67616 | tf_op jit(solution)/shard_map/ppermute | solution.py:55
  40.7 2.6 %collective-permute-done.10 = f32[132,128]{1,0:T(8,128)S(1)} collective-permute-done((f32[132,128]{1,0:T(8,128)S(1)}, f32[132,128]{1,0:T(8,128)S(1)}, u32[]{:S(2)}, u32[]{:S(2)}) %collective-permute-start.10) | collective-permute-done | bytes 67616 | tf_op jit(solution)/shard_map/ppermute | solution.py:55
  43.3 0.3 collective-permute-done.9
  43.6 0.1 multiply_subtract_fusion.4
  43.8 1.5 %collective-permute-start.12 = (f32[132,128]{1,0:T(8,128)S(1)}, f32[132,128]{1,0:T(8,128)S(1)}, u32[]{:S(2)}, u32[]{:S(2)}) collective-permute-start(f32[132,128]{1,0:T(8,128)S(1)} %get-tuple-element.56), channel_id=1, source_target_pairs={{0,4},{4,8},{8,12},{12,0},{1,5},{5,9},{9,13},{13,1},{2,6},{6,10},{... | collective-permute-start | bytes 202760 | tf_op jit(solution)/shard_map/ppermute | solution.py:37
  45.2 2.4 %collective-permute-start.14 = (f32[132,128]{1,0:T(8,128)S(1)}, f32[132,128]{1,0:T(8,128)S(1)}, u32[]{:S(2)}, u32[]{:S(2)}) collective-permute-start(f32[132,128]{1,0:T(8,128)S(1)} %get-tuple-element.56), channel_id=1, source_target_pairs={{0,12},{4,0},{8,4},{12,8},{1,13},{5,1},{9,5},{13,9},{2,14},{6,2},{... | collective-permute-start | bytes 202760 | tf_op jit(solution)/shard_map/ppermute | solution.py:37
  47.7 1.0 %collective-permute-start.13 = (f32[132,128]{1,0:T(8,128)S(1)}, f32[132,128]{1,0:T(8,128)S(1)}, u32[]{:S(2)}, u32[]{:S(2)}) collective-permute-start(f32[132,128]{1,0:T(8,128)S(1)} %get-tuple-element.56), channel_id=1, source_target_pairs={{0,8},{4,12},{8,0},{12,4},{1,9},{5,13},{9,1},{13,5},{2,10},{6,14},... | collective-permute-start | bytes 202760 | tf_op jit(solution)/shard_map/ppermute | solution.py:37
  48.6 5.8 %all-gather.2 = f32[512,128]{1,0:T(8,128)S(1)} all-gather(f32[128,128]{1,0:T(8,128)S(1)} %multiply_subtract_fusion.4), channel_id=4, replica_groups=mesh['vol'=2,'wide'=4,'narrow'=4] {'narrow'}, dimensions={0}, use_global_device_ids=true | all-gather | bytes 327680 | tf_op jit(solution)/shard_map/all_gather | solution.py:33
  54.4 0.0 collective-permute-done.14
  54.4 0.0 collective-permute-done.13
  54.5 0.2 multiply_subtract_fusion
  54.7 1.0 %fusion.77 = f32[4,128,128]{2,1,0:T(8,128)S(1)} fusion(f32[4,128,512]{2,1,0:T(8,128)S(1)} %bitcast.231, f32[512,128,1]{1,0,2:T(8,128)S(1)} %bitcast.236), kind=kOutput, calls=%fused_computation.209 | convolution fusion | flops 402653184 | bytes 1572864 | tf_op jit(solution)/shard_map/dot_general | solution.py:110
  55.7 0.1 dynamic-slice_bitcast_fusion.1
  55.7 0.1 multiply_reduce_fusion.2
  55.9 1.1 %collective-permute-start.17 = (f32[132,128]{1,0:T(8,128)S(1)}, f32[132,128]{1,0:T(8,128)S(1)}, u32[]{:S(2)}, u32[]{:S(2)}) collective-permute-start(f32[132,128]{1,0:T(8,128)S(1)} %concatenate.56), channel_id=1, source_target_pairs={{0,3},{1,0},{2,1},{3,2},{4,7},{5,4},{6,5},{7,6},{8,11},{9,8},{10,9... | collective-permute-start | bytes 202760 | tf_op jit(solution)/shard_map/ppermute | solution.py:55
  57.0 1.0 %collective-permute-start.16 = (f32[132,128]{1,0:T(8,128)S(1)}, f32[132,128]{1,0:T(8,128)S(1)}, u32[]{:S(2)}, u32[]{:S(2)}) collective-permute-start(f32[132,128]{1,0:T(8,128)S(1)} %concatenate.55), channel_id=1, source_target_pairs={{0,2},{1,3},{2,0},{3,1},{4,6},{5,7},{6,4},{7,5},{8,10},{9,11},{10,... | collective-permute-start | bytes 202760 | tf_op jit(solution)/shard_map/ppermute | solution.py:55
  58.1 0.0 collective-permute-start.15
  58.1 1.1 %collective-permute-done.17 = f32[132,128]{1,0:T(8,128)S(1)} collective-permute-done((f32[132,128]{1,0:T(8,128)S(1)}, f32[132,128]{1,0:T(8,128)S(1)}, u32[]{:S(2)}, u32[]{:S(2)}) %collective-permute-start.17) | collective-permute-done | bytes 67616 | tf_op jit(solution)/shard_map/ppermute | solution.py:55
  59.2 2.4 %collective-permute-done.16 = f32[132,128]{1,0:T(8,128)S(1)} collective-permute-done((f32[132,128]{1,0:T(8,128)S(1)}, f32[132,128]{1,0:T(8,128)S(1)}, u32[]{:S(2)}, u32[]{:S(2)}) %collective-permute-start.16) | collective-permute-done | bytes 67616 | tf_op jit(solution)/shard_map/ppermute | solution.py:55
  61.6 0.5 collective-permute-done.15
  62.2 0.7 %collective-permute-start.18 = (f32[4,128]{1,0:T(4,128)S(1)}, f32[4,128]{1,0:T(4,128)S(1)}, u32[]{:S(2)}, u32[]{:S(2)}) collective-permute-start(f32[4,128]{1,0:T(4,128)S(1)} %select_add_fusion.1), channel_id=1, source_target_pairs={{0,4},{4,8},{8,12},{12,0},{1,5},{5,9},{9,13},{13,1},{2,6},{6,10},{... | collective-permute-start | bytes 6152 | tf_op jit(solution)/shard_map/ppermute | solution.py:37
  62.9 1.4 %collective-permute-start.19 = (f32[4,128]{1,0:T(4,128)S(1)}, f32[4,128]{1,0:T(4,128)S(1)}, u32[]{:S(2)}, u32[]{:S(2)}) collective-permute-start(f32[4,128]{1,0:T(4,128)S(1)} %select_add_fusion.1), channel_id=1, source_target_pairs={{0,8},{4,12},{8,0},{12,4},{1,9},{5,13},{9,1},{13,5},{2,10},{6,14},... | collective-permute-start | bytes 6152 | tf_op jit(solution)/shard_map/ppermute | solution.py:37
  64.3 2.8 %collective-permute-start.20 = (f32[4,128]{1,0:T(4,128)S(1)}, f32[4,128]{1,0:T(4,128)S(1)}, u32[]{:S(2)}, u32[]{:S(2)}) collective-permute-start(f32[4,128]{1,0:T(4,128)S(1)} %select_add_fusion.1), channel_id=1, source_target_pairs={{0,12},{4,0},{8,4},{12,8},{1,13},{5,1},{9,5},{13,9},{2,14},{6,2},{... | collective-permute-start | bytes 6152 | tf_op jit(solution)/shard_map/ppermute | solution.py:37
  67.1 0.5 collective-permute-done.18
  67.6 0.0 collective-permute-done.19
  67.6 0.8 %collective-permute-done.20 = f32[4,128]{1,0:T(4,128)S(1)} collective-permute-done((f32[4,128]{1,0:T(4,128)S(1)}, f32[4,128]{1,0:T(4,128)S(1)}, u32[]{:S(2)}, u32[]{:S(2)}) %collective-permute-start.20) | collective-permute-done | bytes 2080 | tf_op jit(solution)/shard_map/ppermute | solution.py:37
  68.5 0.8 %fusion.25 = (f32[128,128]{1,0:T(8,128)}, f32[128,128]{1,0:T(8,128)}) fusion(f32[132,128]{1,0:T(8,128)S(1)} %collective-permute-done.17, f32[132,128]{1,0:T(8,128)S(1)} %collective-permute-done.16, f32[132,128]{1,0:T(8,128)S(1)} %collective-permute-done.15, f32[128,128]{1,0:T(8,128)S(1)} %get-tuple-element.38, f32[4,128,128]{2,1,0:T(8,128)S(1)} %fusion.77, ...), kind=kLoop, calls=%fused_computation.74 | loop fusion | flops 425984 | bytes 527876 | tf_op jit(solution)/shard_map/sub | solution.py:164
  (38 shorter events, 0.5 us)
Async XLA Ops:
  0.6 17.4 %collective-permute-start.2 = (s32[128]{0:T(128)}, s32[128]{0:T(128)S(1)}, u32[]{:S(2)}, u32[]{:S(2)}) collective-permute-start(s32[128]{0:T(128)} %bitcast.256), channel_id=1, source_target_pairs={{0,12},{4,0},{8,4},{12,8},{1,13},{5,1},{9,5},{13,9},{2,14},{6,2},{... | collective-permute-start | bytes 1544 | tf_op jit(solution)/shard_map/ppermute | solution.py:37
  5.7 12.3 %collective-permute-start.1 = (s32[128]{0:T(128)}, s32[128]{0:T(128)S(1)}, u32[]{:S(2)}, u32[]{:S(2)}) collective-permute-start(s32[128]{0:T(128)} %bitcast.257), channel_id=1, source_target_pairs={{0,8},{4,12},{8,0},{12,4},{1,9},{5,13},{9,1},{13,5},{2,10},{6,14},... | collective-permute-start | bytes 1544 | tf_op jit(solution)/shard_map/ppermute | solution.py:37
  5.7 12.3 %collective-permute-start = (s32[128]{0:T(128)}, s32[128]{0:T(128)S(1)}, u32[]{:S(2)}, u32[]{:S(2)}) collective-permute-start(s32[128]{0:T(128)} %bitcast.258), channel_id=1, source_target_pairs={{0,4},{4,8},{8,12},{12,0},{1,5},{5,9},{9,13},{13,1},{2,6},{6,10},{... | collective-permute-start | bytes 1544 | tf_op jit(solution)/shard_map/ppermute | solution.py:37
  13.4 3.4 %copy-start = (s32[128,1]{0,1:T(1,128)S(1)}, s32[128,1]{0,1:T(1,128)}, u32[]{:S(2)}) copy-start(s32[128,1]{0,1:T(1,128)} %param.5) | copy-start | bytes 1540
  19.4 3.7 %collective-permute-start.5 = (f32[131,128]{1,0:T(8,128)S(1)}, f32[131,128]{1,0:T(8,128)S(1)}, u32[]{:S(2)}, u32[]{:S(2)}) collective-permute-start(f32[131,128]{1,0:T(8,128)S(1)} %get-tuple-element.70), channel_id=1, source_target_pairs={{0,3},{1,0},{2,1},{3,2},{4,7},{5,4},{6,5},{7,6},{8,11},{9,8},{10,9... | collective-permute-start | bytes 201224 | tf_op jit(solution)/shard_map/ppermute | solution.py:55
  20.8 5.0 %collective-permute-start.4 = (f32[131,128]{1,0:T(8,128)S(1)}, f32[131,128]{1,0:T(8,128)S(1)}, u32[]{:S(2)}, u32[]{:S(2)}) collective-permute-start(f32[131,128]{1,0:T(8,128)S(1)} %get-tuple-element.69), channel_id=1, source_target_pairs={{0,2},{1,3},{2,0},{3,1},{4,6},{5,7},{6,4},{7,5},{8,10},{9,11},{10,... | collective-permute-start | bytes 201224 | tf_op jit(solution)/shard_map/ppermute | solution.py:55
  21.3 4.5 %collective-permute-start.3 = (f32[131,128]{1,0:T(8,128)S(1)}, f32[131,128]{1,0:T(8,128)S(1)}, u32[]{:S(2)}, u32[]{:S(2)}) collective-permute-start(f32[131,128]{1,0:T(8,128)S(1)} %get-tuple-element.68), channel_id=1, source_target_pairs={{0,1},{1,2},{2,3},{3,0},{4,5},{5,6},{6,7},{7,4},{8,9},{9,10},{10,1... | collective-permute-start | bytes 201224 | tf_op jit(solution)/shard_map/ppermute | solution.py:55
  26.0 9.8 %collective-permute-start.6 = (f32[130,128]{1,0:T(8,128)S(1)}, f32[130,128]{1,0:T(8,128)S(1)}, u32[]{:S(2)}, u32[]{:S(2)}) collective-permute-start(f32[130,128]{1,0:T(8,128)S(1)} %get-tuple-element.58), channel_id=1, source_target_pairs={{0,4},{4,8},{8,12},{12,0},{1,5},{5,9},{9,13},{13,1},{2,6},{6,10},{... | collective-permute-start | bytes 199688 | tf_op jit(solution)/shard_map/ppermute | solution.py:37
  28.5 7.3 %collective-permute-start.8 = (f32[130,128]{1,0:T(8,128)S(1)}, f32[130,128]{1,0:T(8,128)S(1)}, u32[]{:S(2)}, u32[]{:S(2)}) collective-permute-start(f32[130,128]{1,0:T(8,128)S(1)} %get-tuple-element.58), channel_id=1, source_target_pairs={{0,12},{4,0},{8,4},{12,8},{1,13},{5,1},{9,5},{13,9},{2,14},{6,2},{... | collective-permute-start | bytes 199688 | tf_op jit(solution)/shard_map/ppermute | solution.py:37
  29.9 6.0 %collective-permute-start.7 = (f32[130,128]{1,0:T(8,128)S(1)}, f32[130,128]{1,0:T(8,128)S(1)}, u32[]{:S(2)}, u32[]{:S(2)}) collective-permute-start(f32[130,128]{1,0:T(8,128)S(1)} %get-tuple-element.58), channel_id=1, source_target_pairs={{0,8},{4,12},{8,0},{12,4},{1,9},{5,13},{9,1},{13,5},{2,10},{6,14},... | collective-permute-start | bytes 199688 | tf_op jit(solution)/shard_map/ppermute | solution.py:37
  37.4 3.4 %collective-permute-start.11 = (f32[132,128]{1,0:T(8,128)S(1)}, f32[132,128]{1,0:T(8,128)S(1)}, u32[]{:S(2)}, u32[]{:S(2)}) collective-permute-start(f32[132,128]{1,0:T(8,128)S(1)} %concatenate.52), channel_id=1, source_target_pairs={{0,3},{1,0},{2,1},{3,2},{4,7},{5,4},{6,5},{7,6},{8,11},{9,8},{10,9... | collective-permute-start | bytes 202760 | tf_op jit(solution)/shard_map/ppermute | solution.py:55
  38.5 4.8 %collective-permute-start.10 = (f32[132,128]{1,0:T(8,128)S(1)}, f32[132,128]{1,0:T(8,128)S(1)}, u32[]{:S(2)}, u32[]{:S(2)}) collective-permute-start(f32[132,128]{1,0:T(8,128)S(1)} %concatenate.51), channel_id=1, source_target_pairs={{0,2},{1,3},{2,0},{3,1},{4,6},{5,7},{6,4},{7,5},{8,10},{9,11},{10,... | collective-permute-start | bytes 202760 | tf_op jit(solution)/shard_map/ppermute | solution.py:55
  39.5 4.2 %collective-permute-start.9 = (f32[132,128]{1,0:T(8,128)S(1)}, f32[132,128]{1,0:T(8,128)S(1)}, u32[]{:S(2)}, u32[]{:S(2)}) collective-permute-start(f32[132,128]{1,0:T(8,128)S(1)} %concatenate.50), channel_id=1, source_target_pairs={{0,1},{1,2},{2,3},{3,0},{4,5},{5,6},{6,7},{7,4},{8,9},{9,10},{10,1... | collective-permute-start | bytes 202760 | tf_op jit(solution)/shard_map/ppermute | solution.py:55
  43.8 10.6 %collective-permute-start.12 = (f32[132,128]{1,0:T(8,128)S(1)}, f32[132,128]{1,0:T(8,128)S(1)}, u32[]{:S(2)}, u32[]{:S(2)}) collective-permute-start(f32[132,128]{1,0:T(8,128)S(1)} %get-tuple-element.56), channel_id=1, source_target_pairs={{0,4},{4,8},{8,12},{12,0},{1,5},{5,9},{9,13},{13,1},{2,6},{6,10},{... | collective-permute-start | bytes 202760 | tf_op jit(solution)/shard_map/ppermute | solution.py:37
  45.2 9.2 %collective-permute-start.14 = (f32[132,128]{1,0:T(8,128)S(1)}, f32[132,128]{1,0:T(8,128)S(1)}, u32[]{:S(2)}, u32[]{:S(2)}) collective-permute-start(f32[132,128]{1,0:T(8,128)S(1)} %get-tuple-element.56), channel_id=1, source_target_pairs={{0,12},{4,0},{8,4},{12,8},{1,13},{5,1},{9,5},{13,9},{2,14},{6,2},{... | collective-permute-start | bytes 202760 | tf_op jit(solution)/shard_map/ppermute | solution.py:37
  47.7 6.7 %collective-permute-start.13 = (f32[132,128]{1,0:T(8,128)S(1)}, f32[132,128]{1,0:T(8,128)S(1)}, u32[]{:S(2)}, u32[]{:S(2)}) collective-permute-start(f32[132,128]{1,0:T(8,128)S(1)} %get-tuple-element.56), channel_id=1, source_target_pairs={{0,8},{4,12},{8,0},{12,4},{1,9},{5,13},{9,1},{13,5},{2,10},{6,14},... | collective-permute-start | bytes 202760 | tf_op jit(solution)/shard_map/ppermute | solution.py:37
  55.9 3.3 %collective-permute-start.17 = (f32[132,128]{1,0:T(8,128)S(1)}, f32[132,128]{1,0:T(8,128)S(1)}, u32[]{:S(2)}, u32[]{:S(2)}) collective-permute-start(f32[132,128]{1,0:T(8,128)S(1)} %concatenate.56), channel_id=1, source_target_pairs={{0,3},{1,0},{2,1},{3,2},{4,7},{5,4},{6,5},{7,6},{8,11},{9,8},{10,9... | collective-permute-start | bytes 202760 | tf_op jit(solution)/shard_map/ppermute | solution.py:55
  57.0 4.6 %collective-permute-start.16 = (f32[132,128]{1,0:T(8,128)S(1)}, f32[132,128]{1,0:T(8,128)S(1)}, u32[]{:S(2)}, u32[]{:S(2)}) collective-permute-start(f32[132,128]{1,0:T(8,128)S(1)} %concatenate.55), channel_id=1, source_target_pairs={{0,2},{1,3},{2,0},{3,1},{4,6},{5,7},{6,4},{7,5},{8,10},{9,11},{10,... | collective-permute-start | bytes 202760 | tf_op jit(solution)/shard_map/ppermute | solution.py:55
  58.1 4.1 %collective-permute-start.15 = (f32[132,128]{1,0:T(8,128)S(1)}, f32[132,128]{1,0:T(8,128)S(1)}, u32[]{:S(2)}, u32[]{:S(2)}) collective-permute-start(f32[132,128]{1,0:T(8,128)S(1)} %concatenate.54), channel_id=1, source_target_pairs={{0,1},{1,2},{2,3},{3,0},{4,5},{5,6},{6,7},{7,4},{8,9},{9,10},{10,1... | collective-permute-start | bytes 202760 | tf_op jit(solution)/shard_map/ppermute | solution.py:55
  62.2 5.4 %collective-permute-start.18 = (f32[4,128]{1,0:T(4,128)S(1)}, f32[4,128]{1,0:T(4,128)S(1)}, u32[]{:S(2)}, u32[]{:S(2)}) collective-permute-start(f32[4,128]{1,0:T(4,128)S(1)} %select_add_fusion.1), channel_id=1, source_target_pairs={{0,4},{4,8},{8,12},{12,0},{1,5},{5,9},{9,13},{13,1},{2,6},{6,10},{... | collective-permute-start | bytes 6152 | tf_op jit(solution)/shard_map/ppermute | solution.py:37
  62.9 4.7 %collective-permute-start.19 = (f32[4,128]{1,0:T(4,128)S(1)}, f32[4,128]{1,0:T(4,128)S(1)}, u32[]{:S(2)}, u32[]{:S(2)}) collective-permute-start(f32[4,128]{1,0:T(4,128)S(1)} %select_add_fusion.1), channel_id=1, source_target_pairs={{0,8},{4,12},{8,0},{12,4},{1,9},{5,13},{9,1},{13,5},{2,10},{6,14},... | collective-permute-start | bytes 6152 | tf_op jit(solution)/shard_map/ppermute | solution.py:37
  64.3 4.2 %collective-permute-start.20 = (f32[4,128]{1,0:T(4,128)S(1)}, f32[4,128]{1,0:T(4,128)S(1)}, u32[]{:S(2)}, u32[]{:S(2)}) collective-permute-start(f32[4,128]{1,0:T(4,128)S(1)} %select_add_fusion.1), channel_id=1, source_target_pairs={{0,12},{4,0},{8,4},{12,8},{1,13},{5,1},{9,5},{13,9},{2,14},{6,2},{... | collective-permute-start | bytes 6152 | tf_op jit(solution)/shard_map/ppermute | solution.py:37

commit v9 on v7

--- a/solution.py
+++ b/solution.py
@@ -31,6 +31,10 @@
 def gather_blocks(values, axis, count):
     if count > 4:
         return lax.all_gather(values, axis, axis=0, tiled=False)
+    if axis == "narrow" and count == 4:
+        partner = lax.ppermute(values, axis, [(i, i ^ 1) for i in range(count)])
+        both = jnp.stack([values, partner])
+        return jnp.concatenate([both, lax.ppermute(both, axis, [(i, i ^ 2) for i in range(count)])])
     parts = [values]
     for shift in range(1, count):
         pairs = [(i, (i + shift) % count) for i in range(count)]
@@ -75,6 +79,8 @@
 def source(axis, count, entry):
     if count > 4:
         return entry
+    if axis == "narrow" and count == 4:
+        return lax.axis_index(axis) ^ entry
     return (lax.axis_index(axis) - entry) % count
 
 

time: 67.2 us -> 64.5 us (0.960)
  waiting for transfers between devices: 24.6 us -> 18.2 us
  starting transfers between devices: 29.7 us -> 33.5 us
    ppermute x0 -> x6, starting transfers between devices: none -> 5.41 us  [the longest x3 4.46 us: gather_blocks(): lax.ppermute(both, axis, [(i, i ^ 2) for i in range(count)])]
    ppermute x21 -> x12, waiting for transfers between devices: 13.9 us -> 9.23 us  [gather_blocks(): parts.append(lax.ppermute(values, axis, pairs))]
    ppermute x9, waiting for transfers between devices: 10.7 us -> 7.81 us  [scatter_with(): got = lax.ppermute(jnp.concatenate([sent, extra], axis=0), axis, pairs)]
    ppermute x21 -> x12, starting transfers between devices: 22.5 us -> 20.1 us  [gather_blocks(): parts.append(lax.ppermute(values, axis, pairs))]
    ppermute x0 -> x6, waiting for transfers between devices: none -> 1.12 us  [the longest x3 1.12 us: gather_blocks(): lax.ppermute(both, axis, [(i, i ^ 2) for i in range(count)])]
    ppermute x9, starting transfers between devices: 7.2 us -> 7.95 us  [scatter_with(): got = lax.ppermute(jnp.concatenate([sent, extra], axis=0), axis, pairs)]
  transfers between devices with their start and end apart: 30 -> 27, of which waited for: 16 -> 17; matrix products, arithmetic and copies ran while one was open for 11% -> 12% of each run, Pallas kernels for 0% -> 0%
where the time goes in v9:
time: 64.5 us; the launch traced here: 64.3 us
  starting transfers between devices  33.5 us (52%)
  waiting for transfers between devices  18.2 us (28%)
  other arithmetic  7.31 us (11%)
  matrix products  3.02 us (5%)
  local copies, waits for them, and re-layouts  1.34 us (2%)
  between operations  1.01 us (2%)
    ppermute x12, starting transfers between devices, gather_blocks(): parts.append(lax.ppermute(values, axis, pairs))  20.1 us
    ppermute x12, waiting for transfers between devices, gather_blocks(): parts.append(lax.ppermute(values, axis, pairs))  9.23 us
    ppermute x9, starting transfers between devices, scatter_with(): got = lax.ppermute(jnp.concatenate([sent, extra], axis=0), axis, pairs)  7.95 us
    ppermute x9, waiting for transfers between devices, scatter_with(): got = lax.ppermute(jnp.concatenate([sent, extra], axis=0), axis, pairs)  7.81 us
    ppermute x3, starting transfers between devices, gather_blocks(): lax.ppermute(both, axis, [(i, i ^ 2) for i in range(count)])  4.46 us
    dot_general x3, matrix products, product(): jnp.dot(transposed, row_values.reshape(groups * tile, width), precision=l...  3.02 us
    reduce_sum x1, other arithmetic, local(): column_sums = jnp.sum(dense, axis=(0, 1)).reshape(n_narrow, own_rows)  2.97 us
  transfers between devices with their start and end apart: 27, of which 17 were waited for; matrix products, arithmetic and copies ran while one was open for 12% of the time, Pallas kernels for 0%

profile of v9, /device:TPU:0, one launch (start us, length us, event | category | flops | bytes accessed | tf_op | source)
XLA Modules:
  0.0 64.3 jit_solution(13825385618763578475)
XLA Ops:
  0.6 3.1 %collective-permute-start = (s32[128]{0:T(128)}, s32[128]{0:T(128)S(1)}, u32[]{:S(2)}, u32[]{:S(2)}) collective-permute-start(s32[128]{0:T(128)} %bitcast.266), channel_id=1, source_target_pairs={{0,4},{4,8},{8,12},{12,0},{1,5},{5,9},{9,13},{13,1},{2,6},{6,10},{... | collective-permute-start | bytes 1544 | tf_op jit(solution)/shard_map/ppermute | solution.py:41
  3.7 2.6 %collective-permute-start.1 = (s32[128]{0:T(128)}, s32[128]{0:T(128)S(1)}, u32[]{:S(2)}, u32[]{:S(2)}) collective-permute-start(s32[128]{0:T(128)} %bitcast.267), channel_id=1, source_target_pairs={{0,8},{4,12},{8,0},{12,4},{1,9},{5,13},{9,1},{13,5},{2,10},{6,14},... | collective-permute-start | bytes 1544 | tf_op jit(solution)/shard_map/ppermute | solution.py:41
  6.3 1.3 %collective-permute-start.2 = (s32[128]{0:T(128)}, s32[128]{0:T(128)S(1)}, u32[]{:S(2)}, u32[]{:S(2)}) collective-permute-start(s32[128]{0:T(128)} %bitcast.268), channel_id=1, source_target_pairs={{0,12},{4,0},{8,4},{12,8},{1,13},{5,1},{9,5},{13,9},{2,14},{6,2},{... | collective-permute-start | bytes 1544 | tf_op jit(solution)/shard_map/ppermute | solution.py:41
  7.7 0.7 %fusion.79 = f32[128]{0:T(128)S(1)} fusion(s32[128,1]{0,1:T(1,128)} %param.5), kind=kLoop, calls=%fused_computation.216 | loop fusion | flops 384 | bytes 1024 | tf_op jit(solution)/shard_map/mul | solution.py:157
  8.4 0.7 %add_select_fusion = s32[4,8]{1,0:T(4,128)S(1)} fusion(s32[4,8]{1,0:T(4,128)} %param.4), kind=kLoop, calls=%fused_computation.147 | loop fusion | flops 480 | bytes 256 | tf_op jit(solution)/shard_map/jit(floor_divide)/jit(_where)/select_n | solution.py:97
  9.1 0.1 iota_compare_fusion.5
  9.1 3.0 %select_reduce_fusion = (f32[4,128]{1,0:T(4,128)S(1)}, f32[4,128,4,128]{3,1,2,0:T(8,128)S(1)}) fusion(f32[4,8,128,128]{3,2,1,0:T(8,128)} %param.3, pred[4,8,4]{2,1,0:T(8,128)(4,1)S(1)} %iota_compare_fusion.5), kind=kLoop, calls=%fused_computation.1 | loop fusion | flops 6028800 | bytes 3147904 | tf_op jit(solution)/shard_map/reduce_sum | solution.py:102
  12.1 0.1 copy_bitcast_fusion
  12.3 0.1 broadcast_bitcast_fusion
  12.3 0.1 fusion.32
  12.5 0.6 gather_fusion
  13.1 0.1 bitcast_select_fusion
  13.3 0.3 copy.7
  13.7 1.6 %collective-permute-start.4 = (s32[2,128]{1,0:T(2,128)S(1)}, s32[2,128]{1,0:T(2,128)S(1)}, u32[]{:S(2)}, u32[]{:S(2)}) collective-permute-start(s32[2,128]{1,0:T(2,128)S(1)} %pad_add_fusion.2), channel_id=1, source_target_pairs={{0,2},{1,3},{2,0},{3,1},{4,6},{5,7},{6,4},{7,5},{8,10},{9,11},{10,... | collective-permute-start | bytes 3080 | tf_op jit(solution)/shard_map/ppermute | solution.py:37
  15.3 1.1 %fusion.5 = f32[4,128,128]{2,1,0:T(8,128)S(1)} fusion(f32[4,128,512]{2,1,0:T(8,128)S(1)} %bitcast.238, s32[512]{0:T(512)S(1)} %get-tuple-element.61), kind=kOutput, calls=%fused_computation.22 | convolution fusion | flops 402784256 | bytes 1312768 | tf_op jit(solution)/shard_map/dot_general | solution.py:116
  16.3 1.0 %collective-permute-done.4 = s32[2,128]{1,0:T(2,128)S(1)} collective-permute-done((s32[2,128]{1,0:T(2,128)S(1)}, s32[2,128]{1,0:T(2,128)S(1)}, u32[]{:S(2)}, u32[]{:S(2)}) %collective-permute-start.4) | collective-permute-done | bytes 1056 | tf_op jit(solution)/shard_map/ppermute | solution.py:37
  17.3 0.1 fusion.8
  17.5 0.2 fusion.29
  17.7 0.1 collective-permute-start.5
  17.7 1.6 %collective-permute-start.6 = (f32[131,128]{1,0:T(8,128)S(1)}, f32[131,128]{1,0:T(8,128)S(1)}, u32[]{:S(2)}, u32[]{:S(2)}) collective-permute-start(f32[131,128]{1,0:T(8,128)S(1)} %get-tuple-element.69), channel_id=1, source_target_pairs={{0,2},{1,3},{2,0},{3,1},{4,6},{5,7},{6,4},{7,5},{8,10},{9,11},{10,... | collective-permute-start | bytes 201224 | tf_op jit(solution)/shard_map/ppermute | solution.py:59
  19.3 1.4 %collective-permute-start.7 = (f32[131,128]{1,0:T(8,128)S(1)}, f32[131,128]{1,0:T(8,128)S(1)}, u32[]{:S(2)}, u32[]{:S(2)}) collective-permute-start(f32[131,128]{1,0:T(8,128)S(1)} %get-tuple-element.70), channel_id=1, source_target_pairs={{0,3},{1,0},{2,1},{3,2},{4,7},{5,4},{6,5},{7,6},{8,11},{9,8},{10,9... | collective-permute-start | bytes 201224 | tf_op jit(solution)/shard_map/ppermute | solution.py:59
  20.7 0.9 %collective-permute-done.5 = f32[131,128]{1,0:T(8,128)S(1)} collective-permute-done((f32[131,128]{1,0:T(8,128)S(1)}, f32[131,128]{1,0:T(8,128)S(1)}, u32[]{:S(2)}, u32[]{:S(2)}) %collective-permute-start.5) | collective-permute-done | bytes 67104 | tf_op jit(solution)/shard_map/ppermute | solution.py:59
  21.6 1.0 %collective-permute-done.6 = f32[131,128]{1,0:T(8,128)S(1)} collective-permute-done((f32[131,128]{1,0:T(8,128)S(1)}, f32[131,128]{1,0:T(8,128)S(1)}, u32[]{:S(2)}, u32[]{:S(2)}) %collective-permute-start.6) | collective-permute-done | bytes 67104 | tf_op jit(solution)/shard_map/ppermute | solution.py:59
  22.5 0.2 collective-permute-done.7
  22.7 0.1 fusion.90
  22.8 0.1 fusion.34
  22.9 0.9 %collective-permute-start.11 = (f32[128,128]{1,0:T(8,128)S(1)}, f32[128,128]{1,0:T(8,128)S(1)}, u32[]{:S(2)}, u32[]{:S(2)}) collective-permute-start(f32[128,128]{1,0:T(8,128)S(1)} %fusion.34), channel_id=1, source_target_pairs={{0,1},{1,0},{2,3},{3,2},{4,5},{5,4},{6,7},{7,6},{8,9},{9,8},{10,11... | collective-permute-start | bytes 196616 | tf_op jit(solution)/shard_map/ppermute | solution.py:35
  23.9 0.7 %collective-permute-start.8 = (f32[130,128]{1,0:T(8,128)S(1)}, f32[130,128]{1,0:T(8,128)S(1)}, u32[]{:S(2)}, u32[]{:S(2)}) collective-permute-start(f32[130,128]{1,0:T(8,128)S(1)} %get-tuple-element.58), channel_id=1, source_target_pairs={{0,4},{4,8},{8,12},{12,0},{1,5},{5,9},{9,13},{13,1},{2,6},{6,10},{... | collective-permute-start | bytes 199688 | tf_op jit(solution)/shard_map/ppermute | solution.py:41
  24.6 0.3 collective-permute-start.9
  24.9 2.8 %collective-permute-start.10 = (f32[130,128]{1,0:T(8,128)S(1)}, f32[130,128]{1,0:T(8,128)S(1)}, u32[]{:S(2)}, u32[]{:S(2)}) collective-permute-start(f32[130,128]{1,0:T(8,128)S(1)} %get-tuple-element.58), channel_id=1, source_target_pairs={{0,12},{4,0},{8,4},{12,8},{1,13},{5,1},{9,5},{13,9},{2,14},{6,2},{... | collective-permute-start | bytes 199688 | tf_op jit(solution)/shard_map/ppermute | solution.py:41
  27.8 1.6 %collective-permute-start.12 = (f32[2,128,128]{2,1,0:T(8,128)S(1)}, f32[2,128,128]{2,1,0:T(8,128)S(1)}, u32[]{:S(2)}, u32[]{:S(2)}) collective-permute-start(f32[2,128,128]{2,1,0:T(8,128)S(1)} %pad_maximum_fusion.7), channel_id=1, source_target_pairs={{0,2},{1,3},{2,0},{3,1},{4,6},{5,7},{6,4},{7,5},{8,10},{9,11},{10,... | collective-permute-start | bytes 393224 | tf_op jit(solution)/shard_map/ppermute | solution.py:37
  29.3 1.5 %collective-permute-done.8 = f32[130,128]{1,0:T(8,128)S(1)} collective-permute-done((f32[130,128]{1,0:T(8,128)S(1)}, f32[130,128]{1,0:T(8,128)S(1)}, u32[]{:S(2)}, u32[]{:S(2)}) %collective-permute-start.8) | collective-permute-done | bytes 66592 | tf_op jit(solution)/shard_map/ppermute | solution.py:41
  30.8 2.1 %collective-permute-done.9 = f32[130,128]{1,0:T(8,128)S(1)} collective-permute-done((f32[130,128]{1,0:T(8,128)S(1)}, f32[130,128]{1,0:T(8,128)S(1)}, u32[]{:S(2)}, u32[]{:S(2)}) %collective-permute-start.9) | collective-permute-done | bytes 66592 | tf_op jit(solution)/shard_map/ppermute | solution.py:41
  33.0 0.1 multiply_reduce_fusion.3
  33.1 0.2 multiply_subtract_fusion.1
  33.3 1.0 %fusion.83 = f32[4,128,128]{2,1,0:T(8,128)S(1)} fusion(f32[4,128,512]{2,1,0:T(8,128)S(1)} %bitcast.239, f32[512,128,1]{1,0,2:T(8,128)S(1)} %bitcast.245), kind=kOutput, calls=%fused_computation.220 | convolution fusion | flops 402653184 | bytes 1572864 | tf_op jit(solution)/shard_map/dot_general | solution.py:116
  34.4 1.6 %collective-permute-start.14 = (f32[132,128]{1,0:T(8,128)S(1)}, f32[132,128]{1,0:T(8,128)S(1)}, u32[]{:S(2)}, u32[]{:S(2)}) collective-permute-start(f32[132,128]{1,0:T(8,128)S(1)} %concatenate.65), channel_id=1, source_target_pairs={{0,2},{1,3},{2,0},{3,1},{4,6},{5,7},{6,4},{7,5},{8,10},{9,11},{10,... | collective-permute-start | bytes 202760 | tf_op jit(solution)/shard_map/ppermute | solution.py:59
  36.1 0.5 collective-permute-start.13
  36.7 2.2 %collective-permute-done.14 = f32[132,128]{1,0:T(8,128)S(1)} collective-permute-done((f32[132,128]{1,0:T(8,128)S(1)}, f32[132,128]{1,0:T(8,128)S(1)}, u32[]{:S(2)}, u32[]{:S(2)}) %collective-permute-start.14) | collective-permute-done | bytes 67616 | tf_op jit(solution)/shard_map/ppermute | solution.py:59
  38.8 0.5 collective-permute-done.15
  39.3 1.0 %collective-permute-done.13 = f32[132,128]{1,0:T(8,128)S(1)} collective-permute-done((f32[132,128]{1,0:T(8,128)S(1)}, f32[132,128]{1,0:T(8,128)S(1)}, u32[]{:S(2)}, u32[]{:S(2)}) %collective-permute-start.13) | collective-permute-done | bytes 67616 | tf_op jit(solution)/shard_map/ppermute | solution.py:59
  40.3 0.1 multiply_subtract_fusion.3
  40.4 0.1 collective-permute-start.19
  40.6 1.5 %collective-permute-start.16 = (f32[132,128]{1,0:T(8,128)S(1)}, f32[132,128]{1,0:T(8,128)S(1)}, u32[]{:S(2)}, u32[]{:S(2)}) collective-permute-start(f32[132,128]{1,0:T(8,128)S(1)} %get-tuple-element.56), channel_id=1, source_target_pairs={{0,4},{4,8},{8,12},{12,0},{1,5},{5,9},{9,13},{13,1},{2,6},{6,10},{... | collective-permute-start | bytes 202760 | tf_op jit(solution)/shard_map/ppermute | solution.py:41
  42.0 1.0 %collective-permute-start.17 = (f32[132,128]{1,0:T(8,128)S(1)}, f32[132,128]{1,0:T(8,128)S(1)}, u32[]{:S(2)}, u32[]{:S(2)}) collective-permute-start(f32[132,128]{1,0:T(8,128)S(1)} %get-tuple-element.56), channel_id=1, source_target_pairs={{0,8},{4,12},{8,0},{12,4},{1,9},{5,13},{9,1},{13,5},{2,10},{6,14},... | collective-permute-start | bytes 202760 | tf_op jit(solution)/shard_map/ppermute | solution.py:41
  43.0 2.2 %collective-permute-start.18 = (f32[132,128]{1,0:T(8,128)S(1)}, f32[132,128]{1,0:T(8,128)S(1)}, u32[]{:S(2)}, u32[]{:S(2)}) collective-permute-start(f32[132,128]{1,0:T(8,128)S(1)} %get-tuple-element.56), channel_id=1, source_target_pairs={{0,12},{4,0},{8,4},{12,8},{1,13},{5,1},{9,5},{13,9},{2,14},{6,2},{... | collective-permute-start | bytes 202760 | tf_op jit(solution)/shard_map/ppermute | solution.py:41
  45.3 1.4 %collective-permute-start.20 = (f32[2,128,128]{2,1,0:T(8,128)S(1)}, f32[2,128,128]{2,1,0:T(8,128)S(1)}, u32[]{:S(2)}, u32[]{:S(2)}) collective-permute-start(f32[2,128,128]{2,1,0:T(8,128)S(1)} %pad_maximum_fusion.8), channel_id=1, source_target_pairs={{0,2},{1,3},{2,0},{3,1},{4,6},{5,7},{6,4},{7,5},{8,10},{9,11},{10,... | collective-permute-start | bytes 393224 | tf_op jit(solution)/shard_map/ppermute | solution.py:37
  46.6 0.9 %collective-permute-done.16 = f32[132,128]{1,0:T(8,128)S(1)} collective-permute-done((f32[132,128]{1,0:T(8,128)S(1)}, f32[132,128]{1,0:T(8,128)S(1)}, u32[]{:S(2)}, u32[]{:S(2)}) %collective-permute-start.16) | collective-permute-done | bytes 67616 | tf_op jit(solution)/shard_map/ppermute | solution.py:41
  47.5 2.5 %collective-permute-done.17 = f32[132,128]{1,0:T(8,128)S(1)} collective-permute-done((f32[132,128]{1,0:T(8,128)S(1)}, f32[132,128]{1,0:T(8,128)S(1)}, u32[]{:S(2)}, u32[]{:S(2)}) %collective-permute-start.17) | collective-permute-done | bytes 67616 | tf_op jit(solution)/shard_map/ppermute | solution.py:41
  50.1 0.1 multiply_reduce_fusion.2
  50.2 0.2 collective-permute-done.20
  50.4 0.2 fusion.2
  50.6 1.0 %fusion.84 = f32[4,128,128]{2,1,0:T(8,128)S(1)} fusion(f32[4,128,512]{2,1,0:T(8,128)S(1)} %bitcast.240, f32[512,128,1]{1,0,2:T(8,128)S(1)} %bitcast.244), kind=kOutput, calls=%fused_computation.221 | convolution fusion | flops 402653184 | bytes 1572864 | tf_op jit(solution)/shard_map/dot_general | solution.py:116
  51.8 1.3 %collective-permute-start.22 = (f32[132,128]{1,0:T(8,128)S(1)}, f32[132,128]{1,0:T(8,128)S(1)}, u32[]{:S(2)}, u32[]{:S(2)}) collective-permute-start(f32[132,128]{1,0:T(8,128)S(1)} %concatenate.70), channel_id=1, source_target_pairs={{0,2},{1,3},{2,0},{3,1},{4,6},{5,7},{6,4},{7,5},{8,10},{9,11},{10,... | collective-permute-start | bytes 202760 | tf_op jit(solution)/shard_map/ppermute | solution.py:59
  53.1 1.5 %collective-permute-start.23 = (f32[132,128]{1,0:T(8,128)S(1)}, f32[132,128]{1,0:T(8,128)S(1)}, u32[]{:S(2)}, u32[]{:S(2)}) collective-permute-start(f32[132,128]{1,0:T(8,128)S(1)} %concatenate.71), channel_id=1, source_target_pairs={{0,3},{1,0},{2,1},{3,2},{4,7},{5,4},{6,5},{7,6},{8,11},{9,8},{10,9... | collective-permute-start | bytes 202760 | tf_op jit(solution)/shard_map/ppermute | solution.py:59
  54.6 1.0 %collective-permute-done.21 = f32[132,128]{1,0:T(8,128)S(1)} collective-permute-done((f32[132,128]{1,0:T(8,128)S(1)}, f32[132,128]{1,0:T(8,128)S(1)}, u32[]{:S(2)}, u32[]{:S(2)}) %collective-permute-start.21) | collective-permute-done | bytes 67616 | tf_op jit(solution)/shard_map/ppermute | solution.py:59
  55.6 1.1 %collective-permute-done.22 = f32[132,128]{1,0:T(8,128)S(1)} collective-permute-done((f32[132,128]{1,0:T(8,128)S(1)}, f32[132,128]{1,0:T(8,128)S(1)}, u32[]{:S(2)}, u32[]{:S(2)}) %collective-permute-start.22) | collective-permute-done | bytes 67616 | tf_op jit(solution)/shard_map/ppermute | solution.py:59
  56.8 2.1 %collective-permute-start.24 = (f32[4,128]{1,0:T(4,128)S(1)}, f32[4,128]{1,0:T(4,128)S(1)}, u32[]{:S(2)}, u32[]{:S(2)}) collective-permute-start(f32[4,128]{1,0:T(4,128)S(1)} %select_add_fusion.1), channel_id=1, source_target_pairs={{0,4},{4,8},{8,12},{12,0},{1,5},{5,9},{9,13},{13,1},{2,6},{6,10},{... | collective-permute-start | bytes 6152 | tf_op jit(solution)/shard_map/ppermute | solution.py:41
  58.8 1.1 %collective-permute-start.25 = (f32[4,128]{1,0:T(4,128)S(1)}, f32[4,128]{1,0:T(4,128)S(1)}, u32[]{:S(2)}, u32[]{:S(2)}) collective-permute-start(f32[4,128]{1,0:T(4,128)S(1)} %select_add_fusion.1), channel_id=1, source_target_pairs={{0,8},{4,12},{8,0},{12,4},{1,9},{5,13},{9,1},{13,5},{2,10},{6,14},... | collective-permute-start | bytes 6152 | tf_op jit(solution)/shard_map/ppermute | solution.py:41
  59.9 1.4 %collective-permute-start.26 = (f32[4,128]{1,0:T(4,128)S(1)}, f32[4,128]{1,0:T(4,128)S(1)}, u32[]{:S(2)}, u32[]{:S(2)}) collective-permute-start(f32[4,128]{1,0:T(4,128)S(1)} %select_add_fusion.1), channel_id=1, source_target_pairs={{0,12},{4,0},{8,4},{12,8},{1,13},{5,1},{9,5},{13,9},{2,14},{6,2},{... | collective-permute-start | bytes 6152 | tf_op jit(solution)/shard_map/ppermute | solution.py:41
  61.3 0.9 %collective-permute-done.24 = f32[4,128]{1,0:T(4,128)S(1)} collective-permute-done((f32[4,128]{1,0:T(4,128)S(1)}, f32[4,128]{1,0:T(4,128)S(1)}, u32[]{:S(2)}, u32[]{:S(2)}) %collective-permute-start.24) | collective-permute-done | bytes 2080 | tf_op jit(solution)/shard_map/ppermute | solution.py:41
  62.2 1.1 %collective-permute-done.25 = f32[4,128]{1,0:T(4,128)S(1)} collective-permute-done((f32[4,128]{1,0:T(4,128)S(1)}, f32[4,128]{1,0:T(4,128)S(1)}, u32[]{:S(2)}, u32[]{:S(2)}) %collective-permute-start.25) | collective-permute-done | bytes 2080 | tf_op jit(solution)/shard_map/ppermute | solution.py:41
  63.3 0.1 collective-permute-done.26
  63.5 0.8 %fusion.27 = (f32[128,128]{1,0:T(8,128)}, f32[128,128]{1,0:T(8,128)}) fusion(f32[132,128]{1,0:T(8,128)S(1)} %collective-permute-done.23, f32[132,128]{1,0:T(8,128)S(1)} %collective-permute-done.22, f32[132,128]{1,0:T(8,128)S(1)} %collective-permute-done.21, f32[128,128]{1,0:T(8,128)S(1)} %get-tuple-element.36, f32[4,128,128]{2,1,0:T(8,128)S(1)} %fusion.84, ...), kind=kLoop, calls=%fused_computation.79 | loop fusion | flops 425984 | bytes 527876 | tf_op jit(solution)/shard_map/sub | solution.py:170
  (54 shorter events, 0.9 us)
Async XLA Ops:
  0.6 14.6 %collective-permute-start = (s32[128]{0:T(128)}, s32[128]{0:T(128)S(1)}, u32[]{:S(2)}, u32[]{:S(2)}) collective-permute-start(s32[128]{0:T(128)} %bitcast.266), channel_id=1, source_target_pairs={{0,4},{4,8},{8,12},{12,0},{1,5},{5,9},{9,13},{13,1},{2,6},{6,10},{... | collective-permute-start | bytes 1544 | tf_op jit(solution)/shard_map/ppermute | solution.py:41
  3.7 11.5 %collective-permute-start.1 = (s32[128]{0:T(128)}, s32[128]{0:T(128)S(1)}, u32[]{:S(2)}, u32[]{:S(2)}) collective-permute-start(s32[128]{0:T(128)} %bitcast.267), channel_id=1, source_target_pairs={{0,8},{4,12},{8,0},{12,4},{1,9},{5,13},{9,1},{13,5},{2,10},{6,14},... | collective-permute-start | bytes 1544 | tf_op jit(solution)/shard_map/ppermute | solution.py:41
  6.3 8.9 %collective-permute-start.2 = (s32[128]{0:T(128)}, s32[128]{0:T(128)S(1)}, u32[]{:S(2)}, u32[]{:S(2)}) collective-permute-start(s32[128]{0:T(128)} %bitcast.268), channel_id=1, source_target_pairs={{0,12},{4,0},{8,4},{12,8},{1,13},{5,1},{9,5},{13,9},{2,14},{6,2},{... | collective-permute-start | bytes 1544 | tf_op jit(solution)/shard_map/ppermute | solution.py:41
  7.6 6.0 %collective-permute-start.3 = (s32[128]{0:T(128)}, s32[128]{0:T(128)S(1)}, u32[]{:S(2)}, u32[]{:S(2)}) collective-permute-start(s32[128]{0:T(128)} %bitcast.269), channel_id=1, source_target_pairs={{0,1},{1,0},{2,3},{3,2},{4,5},{5,4},{6,7},{7,6},{8,9},{9,8},{10,11... | collective-permute-start | bytes 1544 | tf_op jit(solution)/shard_map/ppermute | solution.py:35
  9.1 3.2 %copy-start = (s32[128,1]{0,1:T(1,128)S(1)}, s32[128,1]{0,1:T(1,128)}, u32[]{:S(2)}) copy-start(s32[128,1]{0,1:T(1,128)} %param.5) | copy-start | bytes 1540
  13.7 3.6 %collective-permute-start.4 = (s32[2,128]{1,0:T(2,128)S(1)}, s32[2,128]{1,0:T(2,128)S(1)}, u32[]{:S(2)}, u32[]{:S(2)}) collective-permute-start(s32[2,128]{1,0:T(2,128)S(1)} %pad_add_fusion.2), channel_id=1, source_target_pairs={{0,2},{1,3},{2,0},{3,1},{4,6},{5,7},{6,4},{7,5},{8,10},{9,11},{10,... | collective-permute-start | bytes 3080 | tf_op jit(solution)/shard_map/ppermute | solution.py:37
  17.7 3.9 %collective-permute-start.5 = (f32[131,128]{1,0:T(8,128)S(1)}, f32[131,128]{1,0:T(8,128)S(1)}, u32[]{:S(2)}, u32[]{:S(2)}) collective-permute-start(f32[131,128]{1,0:T(8,128)S(1)} %get-tuple-element.68), channel_id=1, source_target_pairs={{0,1},{1,2},{2,3},{3,0},{4,5},{5,6},{6,7},{7,4},{8,9},{9,10},{10,1... | collective-permute-start | bytes 201224 | tf_op jit(solution)/shard_map/ppermute | solution.py:59
  17.7 4.8 %collective-permute-start.6 = (f32[131,128]{1,0:T(8,128)S(1)}, f32[131,128]{1,0:T(8,128)S(1)}, u32[]{:S(2)}, u32[]{:S(2)}) collective-permute-start(f32[131,128]{1,0:T(8,128)S(1)} %get-tuple-element.69), channel_id=1, source_target_pairs={{0,2},{1,3},{2,0},{3,1},{4,6},{5,7},{6,4},{7,5},{8,10},{9,11},{10,... | collective-permute-start | bytes 201224 | tf_op jit(solution)/shard_map/ppermute | solution.py:59
  19.3 3.4 %collective-permute-start.7 = (f32[131,128]{1,0:T(8,128)S(1)}, f32[131,128]{1,0:T(8,128)S(1)}, u32[]{:S(2)}, u32[]{:S(2)}) collective-permute-start(f32[131,128]{1,0:T(8,128)S(1)} %get-tuple-element.70), channel_id=1, source_target_pairs={{0,3},{1,0},{2,1},{3,2},{4,7},{5,4},{6,5},{7,6},{8,11},{9,8},{10,9... | collective-permute-start | bytes 201224 | tf_op jit(solution)/shard_map/ppermute | solution.py:59
  22.9 4.8 %collective-permute-start.11 = (f32[128,128]{1,0:T(8,128)S(1)}, f32[128,128]{1,0:T(8,128)S(1)}, u32[]{:S(2)}, u32[]{:S(2)}) collective-permute-start(f32[128,128]{1,0:T(8,128)S(1)} %fusion.34), channel_id=1, source_target_pairs={{0,1},{1,0},{2,3},{3,2},{4,5},{5,4},{6,7},{7,6},{8,9},{9,8},{10,11... | collective-permute-start | bytes 196616 | tf_op jit(solution)/shard_map/ppermute | solution.py:35
  23.9 7.0 %collective-permute-start.8 = (f32[130,128]{1,0:T(8,128)S(1)}, f32[130,128]{1,0:T(8,128)S(1)}, u32[]{:S(2)}, u32[]{:S(2)}) collective-permute-start(f32[130,128]{1,0:T(8,128)S(1)} %get-tuple-element.58), channel_id=1, source_target_pairs={{0,4},{4,8},{8,12},{12,0},{1,5},{5,9},{9,13},{13,1},{2,6},{6,10},{... | collective-permute-start | bytes 199688 | tf_op jit(solution)/shard_map/ppermute | solution.py:41
  24.6 8.3 %collective-permute-start.9 = (f32[130,128]{1,0:T(8,128)S(1)}, f32[130,128]{1,0:T(8,128)S(1)}, u32[]{:S(2)}, u32[]{:S(2)}) collective-permute-start(f32[130,128]{1,0:T(8,128)S(1)} %get-tuple-element.58), channel_id=1, source_target_pairs={{0,8},{4,12},{8,0},{12,4},{1,9},{5,13},{9,1},{13,5},{2,10},{6,14},... | collective-permute-start | bytes 199688 | tf_op jit(solution)/shard_map/ppermute | solution.py:41
  24.9 8.0 %collective-permute-start.10 = (f32[130,128]{1,0:T(8,128)S(1)}, f32[130,128]{1,0:T(8,128)S(1)}, u32[]{:S(2)}, u32[]{:S(2)}) collective-permute-start(f32[130,128]{1,0:T(8,128)S(1)} %get-tuple-element.58), channel_id=1, source_target_pairs={{0,12},{4,0},{8,4},{12,8},{1,13},{5,1},{9,5},{13,9},{2,14},{6,2},{... | collective-permute-start | bytes 199688 | tf_op jit(solution)/shard_map/ppermute | solution.py:41
  27.8 5.3 %collective-permute-start.12 = (f32[2,128,128]{2,1,0:T(8,128)S(1)}, f32[2,128,128]{2,1,0:T(8,128)S(1)}, u32[]{:S(2)}, u32[]{:S(2)}) collective-permute-start(f32[2,128,128]{2,1,0:T(8,128)S(1)} %pad_maximum_fusion.7), channel_id=1, source_target_pairs={{0,2},{1,3},{2,0},{3,1},{4,6},{5,7},{6,4},{7,5},{8,10},{9,11},{10,... | collective-permute-start | bytes 393224 | tf_op jit(solution)/shard_map/ppermute | solution.py:37
  34.4 4.4 %collective-permute-start.14 = (f32[132,128]{1,0:T(8,128)S(1)}, f32[132,128]{1,0:T(8,128)S(1)}, u32[]{:S(2)}, u32[]{:S(2)}) collective-permute-start(f32[132,128]{1,0:T(8,128)S(1)} %concatenate.65), channel_id=1, source_target_pairs={{0,2},{1,3},{2,0},{3,1},{4,6},{5,7},{6,4},{7,5},{8,10},{9,11},{10,... | collective-permute-start | bytes 202760 | tf_op jit(solution)/shard_map/ppermute | solution.py:59
  36.0 3.3 %collective-permute-start.15 = (f32[132,128]{1,0:T(8,128)S(1)}, f32[132,128]{1,0:T(8,128)S(1)}, u32[]{:S(2)}, u32[]{:S(2)}) collective-permute-start(f32[132,128]{1,0:T(8,128)S(1)} %concatenate.66), channel_id=1, source_target_pairs={{0,3},{1,0},{2,1},{3,2},{4,7},{5,4},{6,5},{7,6},{8,11},{9,8},{10,9... | collective-permute-start | bytes 202760 | tf_op jit(solution)/shard_map/ppermute | solution.py:59
  36.1 4.2 %collective-permute-start.13 = (f32[132,128]{1,0:T(8,128)S(1)}, f32[132,128]{1,0:T(8,128)S(1)}, u32[]{:S(2)}, u32[]{:S(2)}) collective-permute-start(f32[132,128]{1,0:T(8,128)S(1)} %concatenate.64), channel_id=1, source_target_pairs={{0,1},{1,2},{2,3},{3,0},{4,5},{5,6},{6,7},{7,4},{8,9},{9,10},{10,1... | collective-permute-start | bytes 202760 | tf_op jit(solution)/shard_map/ppermute | solution.py:59
  40.4 4.8 %collective-permute-start.19 = (f32[128,128]{1,0:T(8,128)S(1)}, f32[128,128]{1,0:T(8,128)S(1)}, u32[]{:S(2)}, u32[]{:S(2)}) collective-permute-start(f32[128,128]{1,0:T(8,128)S(1)} %multiply_subtract_fusion.3), channel_id=1, source_target_pairs={{0,1},{1,0},{2,3},{3,2},{4,5},{5,4},{6,7},{7,6},{8,9},{9,8},{10,11... | collective-permute-start | bytes 196616 | tf_op jit(solution)/shard_map/ppermute | solution.py:35
  40.6 6.9 %collective-permute-start.16 = (f32[132,128]{1,0:T(8,128)S(1)}, f32[132,128]{1,0:T(8,128)S(1)}, u32[]{:S(2)}, u32[]{:S(2)}) collective-permute-start(f32[132,128]{1,0:T(8,128)S(1)} %get-tuple-element.56), channel_id=1, source_target_pairs={{0,4},{4,8},{8,12},{12,0},{1,5},{5,9},{9,13},{13,1},{2,6},{6,10},{... | collective-permute-start | bytes 202760 | tf_op jit(solution)/shard_map/ppermute | solution.py:41
  42.0 8.0 %collective-permute-start.17 = (f32[132,128]{1,0:T(8,128)S(1)}, f32[132,128]{1,0:T(8,128)S(1)}, u32[]{:S(2)}, u32[]{:S(2)}) collective-permute-start(f32[132,128]{1,0:T(8,128)S(1)} %get-tuple-element.56), channel_id=1, source_target_pairs={{0,8},{4,12},{8,0},{12,4},{1,9},{5,13},{9,1},{13,5},{2,10},{6,14},... | collective-permute-start | bytes 202760 | tf_op jit(solution)/shard_map/ppermute | solution.py:41
  43.0 7.0 %collective-permute-start.18 = (f32[132,128]{1,0:T(8,128)S(1)}, f32[132,128]{1,0:T(8,128)S(1)}, u32[]{:S(2)}, u32[]{:S(2)}) collective-permute-start(f32[132,128]{1,0:T(8,128)S(1)} %get-tuple-element.56), channel_id=1, source_target_pairs={{0,12},{4,0},{8,4},{12,8},{1,13},{5,1},{9,5},{13,9},{2,14},{6,2},{... | collective-permute-start | bytes 202760 | tf_op jit(solution)/shard_map/ppermute | solution.py:41
  45.3 5.1 %collective-permute-start.20 = (f32[2,128,128]{2,1,0:T(8,128)S(1)}, f32[2,128,128]{2,1,0:T(8,128)S(1)}, u32[]{:S(2)}, u32[]{:S(2)}) collective-permute-start(f32[2,128,128]{2,1,0:T(8,128)S(1)} %pad_maximum_fusion.8), channel_id=1, source_target_pairs={{0,2},{1,3},{2,0},{3,1},{4,6},{5,7},{6,4},{7,5},{8,10},{9,11},{10,... | collective-permute-start | bytes 393224 | tf_op jit(solution)/shard_map/ppermute | solution.py:37
  51.7 3.9 %collective-permute-start.21 = (f32[132,128]{1,0:T(8,128)S(1)}, f32[132,128]{1,0:T(8,128)S(1)}, u32[]{:S(2)}, u32[]{:S(2)}) collective-permute-start(f32[132,128]{1,0:T(8,128)S(1)} %concatenate.69), channel_id=1, source_target_pairs={{0,1},{1,2},{2,3},{3,0},{4,5},{5,6},{6,7},{7,4},{8,9},{9,10},{10,1... | collective-permute-start | bytes 202760 | tf_op jit(solution)/shard_map/ppermute | solution.py:59
  51.8 4.9 %collective-permute-start.22 = (f32[132,128]{1,0:T(8,128)S(1)}, f32[132,128]{1,0:T(8,128)S(1)}, u32[]{:S(2)}, u32[]{:S(2)}) collective-permute-start(f32[132,128]{1,0:T(8,128)S(1)} %concatenate.70), channel_id=1, source_target_pairs={{0,2},{1,3},{2,0},{3,1},{4,6},{5,7},{6,4},{7,5},{8,10},{9,11},{10,... | collective-permute-start | bytes 202760 | tf_op jit(solution)/shard_map/ppermute | solution.py:59
  53.1 3.6 %collective-permute-start.23 = (f32[132,128]{1,0:T(8,128)S(1)}, f32[132,128]{1,0:T(8,128)S(1)}, u32[]{:S(2)}, u32[]{:S(2)}) collective-permute-start(f32[132,128]{1,0:T(8,128)S(1)} %concatenate.71), channel_id=1, source_target_pairs={{0,3},{1,0},{2,1},{3,2},{4,7},{5,4},{6,5},{7,6},{8,11},{9,8},{10,9... | collective-permute-start | bytes 202760 | tf_op jit(solution)/shard_map/ppermute | solution.py:59
  56.8 5.4 %collective-permute-start.24 = (f32[4,128]{1,0:T(4,128)S(1)}, f32[4,128]{1,0:T(4,128)S(1)}, u32[]{:S(2)}, u32[]{:S(2)}) collective-permute-start(f32[4,128]{1,0:T(4,128)S(1)} %select_add_fusion.1), channel_id=1, source_target_pairs={{0,4},{4,8},{8,12},{12,0},{1,5},{5,9},{9,13},{13,1},{2,6},{6,10},{... | collective-permute-start | bytes 6152 | tf_op jit(solution)/shard_map/ppermute | solution.py:41
  58.8 4.5 %collective-permute-start.25 = (f32[4,128]{1,0:T(4,128)S(1)}, f32[4,128]{1,0:T(4,128)S(1)}, u32[]{:S(2)}, u32[]{:S(2)}) collective-permute-start(f32[4,128]{1,0:T(4,128)S(1)} %select_add_fusion.1), channel_id=1, source_target_pairs={{0,8},{4,12},{8,0},{12,4},{1,9},{5,13},{9,1},{13,5},{2,10},{6,14},... | collective-permute-start | bytes 6152 | tf_op jit(solution)/shard_map/ppermute | solution.py:41
  59.9 3.6 %collective-permute-start.26 = (f32[4,128]{1,0:T(4,128)S(1)}, f32[4,128]{1,0:T(4,128)S(1)}, u32[]{:S(2)}, u32[]{:S(2)}) collective-permute-start(f32[4,128]{1,0:T(4,128)S(1)} %select_add_fusion.1), channel_id=1, source_target_pairs={{0,12},{4,0},{8,4},{12,8},{1,13},{5,1},{9,5},{13,9},{2,14},{6,2},{... | collective-permute-start | bytes 6152 | tf_op jit(solution)/shard_map/ppermute | solution.py:41

commit v10 on v9

--- a/solution.py
+++ b/solution.py
@@ -31,7 +31,7 @@
 def gather_blocks(values, axis, count):
     if count > 4:
         return lax.all_gather(values, axis, axis=0, tiled=False)
-    if axis == "narrow" and count == 4:
+    if count == 4:
         partner = lax.ppermute(values, axis, [(i, i ^ 1) for i in range(count)])
         both = jnp.stack([values, partner])
         return jnp.concatenate([both, lax.ppermute(both, axis, [(i, i ^ 2) for i in range(count)])])
@@ -62,13 +62,13 @@
     return total, jnp.stack(extras)
 
 
-def canonical_sum(extras, axis, count):
+def canonical_sum(extras, axis, count, shifted):
     if count > 4:
         return jnp.sum(extras, axis=0)
     me = lax.axis_index(axis)
     total = None
     for device in range(count):
-        wanted = (me - device) % count
+        wanted = (me - device) % count if shifted else source(axis, count, device)
         term = extras[count - 1]
         for entry in range(count - 2, -1, -1):
             term = jnp.where(wanted == entry, extras[entry], term)
@@ -79,7 +79,7 @@
 def source(axis, count, entry):
     if count > 4:
         return entry
-    if axis == "narrow" and count == 4:
+    if count == 4:
         return lax.axis_index(axis) ^ entry
     return (lax.axis_index(axis) - entry) % count
 
@@ -126,14 +126,14 @@
 
     def narrow_step(partial, partial_sums):
         weighted, extras = scatter_with(partial, partial_sums, "narrow", n_narrow)
-        return weighted, canonical_sum(extras, "narrow", n_narrow)
+        return weighted, canonical_sum(extras, "narrow", n_narrow, True)
 
     def wide_step(applied, narrow_sums, last):
         if last:
-            sums = canonical_sum(gather_blocks(narrow_sums, "wide", n_wide), "wide", n_wide)
+            sums = canonical_sum(gather_blocks(narrow_sums, "wide", n_wide), "wide", n_wide, False)
             return None, None, sums
         got = gather_blocks(jnp.concatenate([applied, narrow_sums], axis=0), "wide", n_wide)
-        sums = canonical_sum(got[:, own_rows:], "wide", n_wide)
+        sums = canonical_sum(got[:, own_rows:], "wide", n_wide, False)
         return got[:, :own_rows], gather_blocks(applied, "narrow", n_narrow), sums
 
     rhs = indicator(labels)

time: 64.5 us -> 72.6 us (1.13)
  waiting for transfers between devices: 18.2 us -> 36.2 us
  starting transfers between devices: 33.5 us -> 22.8 us
    ppermute x12 -> x0, starting transfers between devices: 20.1 us -> none  [gather_blocks(): parts.append(lax.ppermute(values, axis, pairs))]
    ppermute x3 -> x7, waiting for transfers between devices: 1.12 us -> 16 us  [gather_blocks(): lax.ppermute(both, axis, [(i, i ^ 2) for i in range(count)])]
    ppermute x3 -> x7, waiting for transfers between devices: 0.01 us -> 10.8 us  [gather_blocks(): partner = lax.ppermute(values, axis, [(i, i ^ 1) for i in range(count)])]
    ppermute x12 -> x0, waiting for transfers between devices: 9.23 us -> none  [gather_blocks(): parts.append(lax.ppermute(values, axis, pairs))]
    ppermute x3 -> x7, starting transfers between devices: 4.46 us -> 10.6 us  [gather_blocks(): lax.ppermute(both, axis, [(i, i ^ 2) for i in range(count)])]
    ppermute x3 -> x7, starting transfers between devices: 0.95 us -> 5.2 us  [gather_blocks(): partner = lax.ppermute(values, axis, [(i, i ^ 1) for i in range(count)])]
    ppermute x9, waiting for transfers between devices: 7.81 us -> 9.38 us  [scatter_with(): got = lax.ppermute(jnp.concatenate([sent, extra], axis=0), axis, pairs)]
    ppermute x9, starting transfers between devices: 7.95 us -> 6.97 us  [scatter_with(): got = lax.ppermute(jnp.concatenate([sent, extra], axis=0), axis, pairs)]
  transfers between devices with their start and end apart: 27 -> 23, of which waited for: 17 -> 13; matrix products, arithmetic and copies ran while one was open for 12% -> 9% of each run, Pallas kernels for 0% -> 0%
where the time goes in v10:
time: 72.6 us; the launch traced here: 72.4 us
  waiting for transfers between devices  36.2 us (50%)
  starting transfers between devices  22.8 us (31%)
  other arithmetic  8 us (11%)
  matrix products  3.02 us (4%)
  local copies, waits for them, and re-layouts  1.33 us (2%)
  between operations  1.04 us (1%)
    ppermute x7, waiting for transfers between devices, gather_blocks(): lax.ppermute(both, axis, [(i, i ^ 2) for i in range(count)])  16 us
    ppermute x7, waiting for transfers between devices, gather_blocks(): partner = lax.ppermute(values, axis, [(i, i ^ 1) for i in range(count)])  10.8 us
    ppermute x7, starting transfers between devices, gather_blocks(): lax.ppermute(both, axis, [(i, i ^ 2) for i in range(count)])  10.6 us
    ppermute x9, waiting for transfers between devices, scatter_with(): got = lax.ppermute(jnp.concatenate([sent, extra], axis=0), axis, pairs)  9.38 us
    ppermute x9, starting transfers between devices, scatter_with(): got = lax.ppermute(jnp.concatenate([sent, extra], axis=0), axis, pairs)  6.97 us
    ppermute x7, starting transfers between devices, gather_blocks(): partner = lax.ppermute(values, axis, [(i, i ^ 1) for i in range(count)])  5.2 us
    dot_general x3, matrix products, product(): jnp.dot(transposed, row_values.reshape(groups * tile, width), precision=l...  3.02 us
    reduce_sum x1, other arithmetic, local(): column_sums = jnp.sum(dense, axis=(0, 1)).reshape(n_narrow, own_rows)  2.97 us
  transfers between devices with their start and end apart: 23, of which 13 were waited for; matrix products, arithmetic and copies ran while one was open for 9% of the time, Pallas kernels for 0%

profile of v10, /device:TPU:0, one launch (start us, length us, event | category | flops | bytes accessed | tf_op | source)
XLA Modules:
  0.0 72.4 jit_solution(16812761817477699107)
XLA Ops:
  0.6 0.5 collective-permute-start.2
  1.1 2.7 %collective-permute-start = (s32[128]{0:T(128)}, s32[128]{0:T(128)S(1)}, u32[]{:S(2)}, u32[]{:S(2)}) collective-permute-start(s32[128]{0:T(128)} %bitcast.283), channel_id=1, source_target_pairs={{0,4},{4,0},{8,12},{12,8},{1,5},{5,1},{9,13},{13,9},{2,6},{6,2},{1... | collective-permute-start | bytes 1544 | tf_op jit(solution)/shard_map/ppermute | solution.py:35
  3.8 0.7 fusion.83
  4.5 0.1 broadcast_bitcast_fusion
  4.6 0.8 %fusion.32 = (f32[128]{0:T(128)S(1)}, f32[128]{0:T(128)S(1)}) fusion(s32[128]{0:T(128)} %bitcast.284, f32[128]{0:T(128)S(1)} %fusion.83), kind=kLoop, calls=%fused_computation.84 | loop fusion | flops 114432 | bytes 2048 | tf_op jit(solution)/shard_map/reduce_sum | solution.py:156
  5.4 0.7 add_select_fusion
  6.0 0.1 iota_compare_fusion.5
  6.1 3.0 %select_reduce_fusion = (f32[4,128]{1,0:T(4,128)S(1)}, f32[4,128,4,128]{3,1,2,0:T(8,128)S(1)}) fusion(f32[4,8,128,128]{3,2,1,0:T(8,128)} %param.3, pred[4,8,4]{2,1,0:T(8,128)(4,1)S(1)} %iota_compare_fusion.5), kind=kLoop, calls=%fused_computation.1 | loop fusion | flops 6028800 | bytes 3147904 | tf_op jit(solution)/shard_map/reduce_sum | solution.py:102
  9.1 0.1 copy_bitcast_fusion
  9.3 0.0 copy-start
  9.3 0.6 gather_fusion
  9.9 0.1 bitcast_select_fusion
  10.1 0.0 collective-permute-done
  10.1 1.6 %collective-permute-start.3 = (s32[2,128]{1,0:T(2,128)S(1)}, s32[2,128]{1,0:T(2,128)S(1)}, u32[]{:S(2)}, u32[]{:S(2)}) collective-permute-start(s32[2,128]{1,0:T(2,128)S(1)} %get-tuple-element.74), channel_id=1, source_target_pairs={{0,2},{1,3},{2,0},{3,1},{4,6},{5,7},{6,4},{7,5},{8,10},{9,11},{10,... | collective-permute-start | bytes 3080 | tf_op jit(solution)/shard_map/ppermute | solution.py:37
  11.7 2.6 %collective-permute-start.1 = (s32[2,128]{1,0:T(2,128)S(1)}, s32[2,128]{1,0:T(2,128)S(1)}, u32[]{:S(2)}, u32[]{:S(2)}) collective-permute-start(s32[2,128]{1,0:T(2,128)S(1)} %get-tuple-element.75), channel_id=1, source_target_pairs={{0,8},{4,12},{8,0},{12,4},{1,9},{5,13},{9,1},{13,5},{2,10},{6,14},... | collective-permute-start | bytes 3080 | tf_op jit(solution)/shard_map/ppermute | solution.py:37
  14.3 0.3 copy.7
  14.6 1.5 %collective-permute-done.1 = s32[2,128]{1,0:T(2,128)S(1)} collective-permute-done((s32[2,128]{1,0:T(2,128)S(1)}, s32[2,128]{1,0:T(2,128)S(1)}, u32[]{:S(2)}, u32[]{:S(2)}) %collective-permute-start.1) | collective-permute-done | bytes 1056 | tf_op jit(solution)/shard_map/ppermute | solution.py:37
  16.2 0.1 fusion.8
  16.3 1.1 %fusion.5 = f32[4,128,128]{2,1,0:T(8,128)S(1)} fusion(f32[4,128,512]{2,1,0:T(8,128)S(1)} %bitcast.262, s32[512]{0:T(512)S(1)} %get-tuple-element.61), kind=kOutput, calls=%fused_computation.20 | convolution fusion | flops 402784256 | bytes 1312768 | tf_op jit(solution)/shard_map/dot_general | solution.py:116
  17.4 0.2 fusion.29
  17.6 0.1 collective-permute-start.4
  17.7 0.6 collective-permute-start.5
  18.3 1.4 %collective-permute-start.6 = (f32[131,128]{1,0:T(8,128)S(1)}, f32[131,128]{1,0:T(8,128)S(1)}, u32[]{:S(2)}, u32[]{:S(2)}) collective-permute-start(f32[131,128]{1,0:T(8,128)S(1)} %get-tuple-element.70), channel_id=1, source_target_pairs={{0,3},{1,0},{2,1},{3,2},{4,7},{5,4},{6,5},{7,6},{8,11},{9,8},{10,9... | collective-permute-start | bytes 201224 | tf_op jit(solution)/shard_map/ppermute | solution.py:59
  19.7 1.9 %collective-permute-done.4 = f32[131,128]{1,0:T(8,128)S(1)} collective-permute-done((f32[131,128]{1,0:T(8,128)S(1)}, f32[131,128]{1,0:T(8,128)S(1)}, u32[]{:S(2)}, u32[]{:S(2)}) %collective-permute-start.4) | collective-permute-done | bytes 67104 | tf_op jit(solution)/shard_map/ppermute | solution.py:59
  21.5 1.2 %collective-permute-done.5 = f32[131,128]{1,0:T(8,128)S(1)} collective-permute-done((f32[131,128]{1,0:T(8,128)S(1)}, f32[131,128]{1,0:T(8,128)S(1)}, u32[]{:S(2)}, u32[]{:S(2)}) %collective-permute-start.5) | collective-permute-done | bytes 67104 | tf_op jit(solution)/shard_map/ppermute | solution.py:59
  22.8 0.0 collective-permute-done.6
  22.8 0.1 fusion.34
  22.9 0.5 collective-permute-start.7
  23.5 0.4 collective-permute-start.9
  23.9 3.9 %collective-permute-done.7 = f32[130,128]{1,0:T(8,128)S(1)} collective-permute-done((f32[130,128]{1,0:T(8,128)S(1)}, f32[130,128]{1,0:T(8,128)S(1)}, u32[]{:S(2)}, u32[]{:S(2)}) %collective-permute-start.7) | collective-permute-done | bytes 66592 | tf_op jit(solution)/shard_map/ppermute | solution.py:35
  27.8 2.6 %collective-permute-start.8 = (f32[2,130,128]{2,1,0:T(8,128)S(1)}, f32[2,130,128]{2,1,0:T(8,128)S(1)}, u32[]{:S(2)}, u32[]{:S(2)}) collective-permute-start(f32[2,130,128]{2,1,0:T(8,128)S(1)} %pad_maximum_fusion.5), channel_id=1, source_target_pairs={{0,8},{4,12},{8,0},{12,4},{1,9},{5,13},{9,1},{13,5},{2,10},{6,14},... | collective-permute-start | bytes 399368 | tf_op jit(solution)/shard_map/ppermute | solution.py:37
  30.5 0.1 fusion.94
  30.6 0.0 collective-permute-done.9
  30.6 0.6 collective-permute-start.10
  31.2 5.9 %collective-permute-done.8 = f32[2,130,128]{2,1,0:T(8,128)S(1)} collective-permute-done((f32[2,130,128]{2,1,0:T(8,128)S(1)}, f32[2,130,128]{2,1,0:T(8,128)S(1)}, u32[]{:S(2)}, u32[]{:S(2)}) %collective-permute-start.8) | collective-permute-done | bytes 133152 | tf_op jit(solution)/shard_map/ppermute | solution.py:37
  37.1 0.2 multiply_subtract_fusion.1
  37.3 1.0 %fusion.87 = f32[4,128,128]{2,1,0:T(8,128)S(1)} fusion(f32[4,128,512]{2,1,0:T(8,128)S(1)} %bitcast.263, f32[512,128,1]{1,0,2:T(8,128)S(1)} %bitcast.269), kind=kOutput, calls=%fused_computation.223 | convolution fusion | flops 402653184 | bytes 1572864 | tf_op jit(solution)/shard_map/dot_general | solution.py:116
  38.4 0.1 multiply_reduce_fusion.3
  38.6 0.1 collective-permute-start.11
  38.7 1.7 %collective-permute-start.13 = (f32[132,128]{1,0:T(8,128)S(1)}, f32[132,128]{1,0:T(8,128)S(1)}, u32[]{:S(2)}, u32[]{:S(2)}) collective-permute-start(f32[132,128]{1,0:T(8,128)S(1)} %concatenate.80), channel_id=1, source_target_pairs={{0,3},{1,0},{2,1},{3,2},{4,7},{5,4},{6,5},{7,6},{8,11},{9,8},{10,9... | collective-permute-start | bytes 202760 | tf_op jit(solution)/shard_map/ppermute | solution.py:59
  40.4 0.6 collective-permute-start.12
  41.0 1.4 %collective-permute-done.11 = f32[132,128]{1,0:T(8,128)S(1)} collective-permute-done((f32[132,128]{1,0:T(8,128)S(1)}, f32[132,128]{1,0:T(8,128)S(1)}, u32[]{:S(2)}, u32[]{:S(2)}) %collective-permute-start.11) | collective-permute-done | bytes 67616 | tf_op jit(solution)/shard_map/ppermute | solution.py:59
  42.4 0.0 collective-permute-done.13
  42.5 2.3 %collective-permute-done.12 = f32[132,128]{1,0:T(8,128)S(1)} collective-permute-done((f32[132,128]{1,0:T(8,128)S(1)}, f32[132,128]{1,0:T(8,128)S(1)}, u32[]{:S(2)}, u32[]{:S(2)}) %collective-permute-start.12) | collective-permute-done | bytes 67616 | tf_op jit(solution)/shard_map/ppermute | solution.py:59
  44.7 0.1 multiply_subtract_fusion.3
  44.9 0.1 collective-permute-start.14
  45.0 0.1 collective-permute-start.16
  45.1 4.2 %collective-permute-done.14 = f32[132,128]{1,0:T(8,128)S(1)} collective-permute-done((f32[132,128]{1,0:T(8,128)S(1)}, f32[132,128]{1,0:T(8,128)S(1)}, u32[]{:S(2)}, u32[]{:S(2)}) %collective-permute-start.14) | collective-permute-done | bytes 67616 | tf_op jit(solution)/shard_map/ppermute | solution.py:35
  49.3 1.2 %collective-permute-start.15 = (f32[2,132,128]{2,1,0:T(8,128)S(1)}, f32[2,132,128]{2,1,0:T(8,128)S(1)}, u32[]{:S(2)}, u32[]{:S(2)}) collective-permute-start(f32[2,132,128]{2,1,0:T(8,128)S(1)} %pad_maximum_fusion.6), channel_id=1, source_target_pairs={{0,8},{4,12},{8,0},{12,4},{1,9},{5,13},{9,1},{13,5},{2,10},{6,14},... | collective-permute-start | bytes 405512 | tf_op jit(solution)/shard_map/ppermute | solution.py:37
  50.5 1.0 %collective-permute-start.17 = (f32[2,128,128]{2,1,0:T(8,128)S(1)}, f32[2,128,128]{2,1,0:T(8,128)S(1)}, u32[]{:S(2)}, u32[]{:S(2)}) collective-permute-start(f32[2,128,128]{2,1,0:T(8,128)S(1)} %pad_maximum_fusion.8), channel_id=1, source_target_pairs={{0,2},{1,3},{2,0},{3,1},{4,6},{5,7},{6,4},{7,5},{8,10},{9,11},{10,... | collective-permute-start | bytes 393224 | tf_op jit(solution)/shard_map/ppermute | solution.py:37
  51.5 5.1 %collective-permute-done.15 = f32[2,132,128]{2,1,0:T(8,128)S(1)} collective-permute-done((f32[2,132,128]{2,1,0:T(8,128)S(1)}, f32[2,132,128]{2,1,0:T(8,128)S(1)}, u32[]{:S(2)}, u32[]{:S(2)}) %collective-permute-start.15) | collective-permute-done | bytes 135200 | tf_op jit(solution)/shard_map/ppermute | solution.py:37
  56.7 0.2 fusion.2
  56.9 1.0 %fusion.88 = f32[4,128,128]{2,1,0:T(8,128)S(1)} fusion(f32[4,128,512]{2,1,0:T(8,128)S(1)} %bitcast.264, f32[512,128,1]{1,0,2:T(8,128)S(1)} %bitcast.268), kind=kOutput, calls=%fused_computation.224 | convolution fusion | flops 402653184 | bytes 1572864 | tf_op jit(solution)/shard_map/dot_general | solution.py:116
  58.0 0.1 multiply_reduce_fusion.2
  58.2 0.1 collective-permute-start.18
  58.3 1.1 %collective-permute-start.19 = (f32[132,128]{1,0:T(8,128)S(1)}, f32[132,128]{1,0:T(8,128)S(1)}, u32[]{:S(2)}, u32[]{:S(2)}) collective-permute-start(f32[132,128]{1,0:T(8,128)S(1)} %concatenate.85), channel_id=1, source_target_pairs={{0,2},{1,3},{2,0},{3,1},{4,6},{5,7},{6,4},{7,5},{8,10},{9,11},{10,... | collective-permute-start | bytes 202760 | tf_op jit(solution)/shard_map/ppermute | solution.py:59
  59.4 1.4 %collective-permute-start.20 = (f32[132,128]{1,0:T(8,128)S(1)}, f32[132,128]{1,0:T(8,128)S(1)}, u32[]{:S(2)}, u32[]{:S(2)}) collective-permute-start(f32[132,128]{1,0:T(8,128)S(1)} %concatenate.86), channel_id=1, source_target_pairs={{0,3},{1,0},{2,1},{3,2},{4,7},{5,4},{6,5},{7,6},{8,11},{9,8},{10,9... | collective-permute-start | bytes 202760 | tf_op jit(solution)/shard_map/ppermute | solution.py:59
  60.8 1.4 %collective-permute-done.18 = f32[132,128]{1,0:T(8,128)S(1)} collective-permute-done((f32[132,128]{1,0:T(8,128)S(1)}, f32[132,128]{1,0:T(8,128)S(1)}, u32[]{:S(2)}, u32[]{:S(2)}) %collective-permute-start.18) | collective-permute-done | bytes 67616 | tf_op jit(solution)/shard_map/ppermute | solution.py:59
  62.2 1.2 %collective-permute-done.19 = f32[132,128]{1,0:T(8,128)S(1)} collective-permute-done((f32[132,128]{1,0:T(8,128)S(1)}, f32[132,128]{1,0:T(8,128)S(1)}, u32[]{:S(2)}, u32[]{:S(2)}) %collective-permute-start.19) | collective-permute-done | bytes 67616 | tf_op jit(solution)/shard_map/ppermute | solution.py:59
  63.4 1.0 %collective-permute-start.21 = (f32[4,128]{1,0:T(4,128)S(1)}, f32[4,128]{1,0:T(4,128)S(1)}, u32[]{:S(2)}, u32[]{:S(2)}) collective-permute-start(f32[4,128]{1,0:T(4,128)S(1)} %select_add_fusion), channel_id=1, source_target_pairs={{0,4},{4,0},{8,12},{12,8},{1,5},{5,1},{9,13},{13,9},{2,6},{6,2},{1... | collective-permute-start | bytes 6152 | tf_op jit(solution)/shard_map/ppermute | solution.py:35
  64.3 2.7 %collective-permute-done.21 = f32[4,128]{1,0:T(4,128)S(1)} collective-permute-done((f32[4,128]{1,0:T(4,128)S(1)}, f32[4,128]{1,0:T(4,128)S(1)}, u32[]{:S(2)}, u32[]{:S(2)}) %collective-permute-start.21) | collective-permute-done | bytes 2080 | tf_op jit(solution)/shard_map/ppermute | solution.py:35
  67.0 1.0 %collective-permute-start.22 = (f32[2,4,128]{2,1,0:T(4,128)S(1)}, f32[2,4,128]{2,1,0:T(4,128)S(1)}, u32[]{:S(2)}, u32[]{:S(2)}) collective-permute-start(f32[2,4,128]{2,1,0:T(4,128)S(1)} %pad_maximum_fusion.17), channel_id=1, source_target_pairs={{0,8},{4,12},{8,0},{12,4},{1,9},{5,13},{9,1},{13,5},{2,10},{6,14},... | collective-permute-start | bytes 12296 | tf_op jit(solution)/shard_map/ppermute | solution.py:37
  68.1 3.5 %collective-permute-done.22 = f32[2,4,128]{2,1,0:T(4,128)S(1)} collective-permute-done((f32[2,4,128]{2,1,0:T(4,128)S(1)}, f32[2,4,128]{2,1,0:T(4,128)S(1)}, u32[]{:S(2)}, u32[]{:S(2)}) %collective-permute-start.22) | collective-permute-done | bytes 4128 | tf_op jit(solution)/shard_map/ppermute | solution.py:37
  71.6 0.8 %fusion.27 = (f32[128,128]{1,0:T(8,128)}, f32[128,128]{1,0:T(8,128)}) fusion(f32[132,128]{1,0:T(8,128)S(1)} %collective-permute-done.20, f32[132,128]{1,0:T(8,128)S(1)} %collective-permute-done.19, f32[132,128]{1,0:T(8,128)S(1)} %collective-permute-done.18, f32[128,128]{1,0:T(8,128)S(1)} %get-tuple-element.36, f32[4,128,128]{2,1,0:T(8,128)S(1)} %fusion.88, ...), kind=kLoop, calls=%fused_computation.79 | loop fusion | flops 425984 | bytes 527876 | tf_op jit(solution)/shard_map/sub | solution.py:170
  (48 shorter events, 0.8 us)
Async XLA Ops:
  0.6 9.5 %collective-permute-start.2 = (s32[128]{0:T(128)}, s32[128]{0:T(128)S(1)}, u32[]{:S(2)}, u32[]{:S(2)}) collective-permute-start(s32[128]{0:T(128)} %bitcast.282), channel_id=1, source_target_pairs={{0,1},{1,0},{2,3},{3,2},{4,5},{5,4},{6,7},{7,6},{8,9},{9,8},{10,11... | collective-permute-start | bytes 1544 | tf_op jit(solution)/shard_map/ppermute | solution.py:35
  1.1 8.9 %collective-permute-start = (s32[128]{0:T(128)}, s32[128]{0:T(128)S(1)}, u32[]{:S(2)}, u32[]{:S(2)}) collective-permute-start(s32[128]{0:T(128)} %bitcast.283), channel_id=1, source_target_pairs={{0,4},{4,0},{8,12},{12,8},{1,5},{5,1},{9,13},{13,9},{2,6},{6,2},{1... | collective-permute-start | bytes 1544 | tf_op jit(solution)/shard_map/ppermute | solution.py:35
  9.3 0.8 %copy-start = (s32[128,1]{0,1:T(1,128)S(1)}, s32[128,1]{0,1:T(1,128)}, u32[]{:S(2)}) copy-start(s32[128,1]{0,1:T(1,128)} %param.5) | copy-start | bytes 1540
  10.1 4.5 %collective-permute-start.3 = (s32[2,128]{1,0:T(2,128)S(1)}, s32[2,128]{1,0:T(2,128)S(1)}, u32[]{:S(2)}, u32[]{:S(2)}) collective-permute-start(s32[2,128]{1,0:T(2,128)S(1)} %get-tuple-element.74), channel_id=1, source_target_pairs={{0,2},{1,3},{2,0},{3,1},{4,6},{5,7},{6,4},{7,5},{8,10},{9,11},{10,... | collective-permute-start | bytes 3080 | tf_op jit(solution)/shard_map/ppermute | solution.py:37
  11.7 4.5 %collective-permute-start.1 = (s32[2,128]{1,0:T(2,128)S(1)}, s32[2,128]{1,0:T(2,128)S(1)}, u32[]{:S(2)}, u32[]{:S(2)}) collective-permute-start(s32[2,128]{1,0:T(2,128)S(1)} %get-tuple-element.75), channel_id=1, source_target_pairs={{0,8},{4,12},{8,0},{12,4},{1,9},{5,13},{9,1},{13,5},{2,10},{6,14},... | collective-permute-start | bytes 3080 | tf_op jit(solution)/shard_map/ppermute | solution.py:37
  17.6 3.9 %collective-permute-start.4 = (f32[131,128]{1,0:T(8,128)S(1)}, f32[131,128]{1,0:T(8,128)S(1)}, u32[]{:S(2)}, u32[]{:S(2)}) collective-permute-start(f32[131,128]{1,0:T(8,128)S(1)} %get-tuple-element.68), channel_id=1, source_target_pairs={{0,1},{1,2},{2,3},{3,0},{4,5},{5,6},{6,7},{7,4},{8,9},{9,10},{10,1... | collective-permute-start | bytes 201224 | tf_op jit(solution)/shard_map/ppermute | solution.py:59
  17.7 5.1 %collective-permute-start.5 = (f32[131,128]{1,0:T(8,128)S(1)}, f32[131,128]{1,0:T(8,128)S(1)}, u32[]{:S(2)}, u32[]{:S(2)}) collective-permute-start(f32[131,128]{1,0:T(8,128)S(1)} %get-tuple-element.69), channel_id=1, source_target_pairs={{0,2},{1,3},{2,0},{3,1},{4,6},{5,7},{6,4},{7,5},{8,10},{9,11},{10,... | collective-permute-start | bytes 201224 | tf_op jit(solution)/shard_map/ppermute | solution.py:59
  18.3 4.5 %collective-permute-start.6 = (f32[131,128]{1,0:T(8,128)S(1)}, f32[131,128]{1,0:T(8,128)S(1)}, u32[]{:S(2)}, u32[]{:S(2)}) collective-permute-start(f32[131,128]{1,0:T(8,128)S(1)} %get-tuple-element.70), channel_id=1, source_target_pairs={{0,3},{1,0},{2,1},{3,2},{4,7},{5,4},{6,5},{7,6},{8,11},{9,8},{10,9... | collective-permute-start | bytes 201224 | tf_op jit(solution)/shard_map/ppermute | solution.py:59
  22.9 4.9 %collective-permute-start.7 = (f32[130,128]{1,0:T(8,128)S(1)}, f32[130,128]{1,0:T(8,128)S(1)}, u32[]{:S(2)}, u32[]{:S(2)}) collective-permute-start(f32[130,128]{1,0:T(8,128)S(1)} %get-tuple-element.58), channel_id=1, source_target_pairs={{0,4},{4,0},{8,12},{12,8},{1,5},{5,1},{9,13},{13,9},{2,6},{6,2},{1... | collective-permute-start | bytes 199688 | tf_op jit(solution)/shard_map/ppermute | solution.py:35
  23.5 7.1 %collective-permute-start.9 = (f32[128,128]{1,0:T(8,128)S(1)}, f32[128,128]{1,0:T(8,128)S(1)}, u32[]{:S(2)}, u32[]{:S(2)}) collective-permute-start(f32[128,128]{1,0:T(8,128)S(1)} %fusion.34), channel_id=1, source_target_pairs={{0,1},{1,0},{2,3},{3,2},{4,5},{5,4},{6,7},{7,6},{8,9},{9,8},{10,11... | collective-permute-start | bytes 196616 | tf_op jit(solution)/shard_map/ppermute | solution.py:35
  27.8 9.3 %collective-permute-start.8 = (f32[2,130,128]{2,1,0:T(8,128)S(1)}, f32[2,130,128]{2,1,0:T(8,128)S(1)}, u32[]{:S(2)}, u32[]{:S(2)}) collective-permute-start(f32[2,130,128]{2,1,0:T(8,128)S(1)} %pad_maximum_fusion.5), channel_id=1, source_target_pairs={{0,8},{4,12},{8,0},{12,4},{1,9},{5,13},{9,1},{13,5},{2,10},{6,14},... | collective-permute-start | bytes 399368 | tf_op jit(solution)/shard_map/ppermute | solution.py:37
  30.6 6.5 %collective-permute-start.10 = (f32[2,128,128]{2,1,0:T(8,128)S(1)}, f32[2,128,128]{2,1,0:T(8,128)S(1)}, u32[]{:S(2)}, u32[]{:S(2)}) collective-permute-start(f32[2,128,128]{2,1,0:T(8,128)S(1)} %pad_maximum_fusion.7), channel_id=1, source_target_pairs={{0,2},{1,3},{2,0},{3,1},{4,6},{5,7},{6,4},{7,5},{8,10},{9,11},{10,... | collective-permute-start | bytes 393224 | tf_op jit(solution)/shard_map/ppermute | solution.py:37
  38.6 3.8 %collective-permute-start.11 = (f32[132,128]{1,0:T(8,128)S(1)}, f32[132,128]{1,0:T(8,128)S(1)}, u32[]{:S(2)}, u32[]{:S(2)}) collective-permute-start(f32[132,128]{1,0:T(8,128)S(1)} %concatenate.78), channel_id=1, source_target_pairs={{0,1},{1,2},{2,3},{3,0},{4,5},{5,6},{6,7},{7,4},{8,9},{9,10},{10,1... | collective-permute-start | bytes 202760 | tf_op jit(solution)/shard_map/ppermute | solution.py:59
  38.7 3.8 %collective-permute-start.13 = (f32[132,128]{1,0:T(8,128)S(1)}, f32[132,128]{1,0:T(8,128)S(1)}, u32[]{:S(2)}, u32[]{:S(2)}) collective-permute-start(f32[132,128]{1,0:T(8,128)S(1)} %concatenate.80), channel_id=1, source_target_pairs={{0,3},{1,0},{2,1},{3,2},{4,7},{5,4},{6,5},{7,6},{8,11},{9,8},{10,9... | collective-permute-start | bytes 202760 | tf_op jit(solution)/shard_map/ppermute | solution.py:59
  40.4 4.3 %collective-permute-start.12 = (f32[132,128]{1,0:T(8,128)S(1)}, f32[132,128]{1,0:T(8,128)S(1)}, u32[]{:S(2)}, u32[]{:S(2)}) collective-permute-start(f32[132,128]{1,0:T(8,128)S(1)} %concatenate.79), channel_id=1, source_target_pairs={{0,2},{1,3},{2,0},{3,1},{4,6},{5,7},{6,4},{7,5},{8,10},{9,11},{10,... | collective-permute-start | bytes 202760 | tf_op jit(solution)/shard_map/ppermute | solution.py:59
  44.9 4.4 %collective-permute-start.14 = (f32[132,128]{1,0:T(8,128)S(1)}, f32[132,128]{1,0:T(8,128)S(1)}, u32[]{:S(2)}, u32[]{:S(2)}) collective-permute-start(f32[132,128]{1,0:T(8,128)S(1)} %get-tuple-element.56), channel_id=1, source_target_pairs={{0,4},{4,0},{8,12},{12,8},{1,5},{5,1},{9,13},{13,9},{2,6},{6,2},{1... | collective-permute-start | bytes 202760 | tf_op jit(solution)/shard_map/ppermute | solution.py:35
  45.0 5.5 %collective-permute-start.16 = (f32[128,128]{1,0:T(8,128)S(1)}, f32[128,128]{1,0:T(8,128)S(1)}, u32[]{:S(2)}, u32[]{:S(2)}) collective-permute-start(f32[128,128]{1,0:T(8,128)S(1)} %multiply_subtract_fusion.3), channel_id=1, source_target_pairs={{0,1},{1,0},{2,3},{3,2},{4,5},{5,4},{6,7},{7,6},{8,9},{9,8},{10,11... | collective-permute-start | bytes 196616 | tf_op jit(solution)/shard_map/ppermute | solution.py:35
  49.3 7.3 %collective-permute-start.15 = (f32[2,132,128]{2,1,0:T(8,128)S(1)}, f32[2,132,128]{2,1,0:T(8,128)S(1)}, u32[]{:S(2)}, u32[]{:S(2)}) collective-permute-start(f32[2,132,128]{2,1,0:T(8,128)S(1)} %pad_maximum_fusion.6), channel_id=1, source_target_pairs={{0,8},{4,12},{8,0},{12,4},{1,9},{5,13},{9,1},{13,5},{2,10},{6,14},... | collective-permute-start | bytes 405512 | tf_op jit(solution)/shard_map/ppermute | solution.py:37
  50.5 6.2 %collective-permute-start.17 = (f32[2,128,128]{2,1,0:T(8,128)S(1)}, f32[2,128,128]{2,1,0:T(8,128)S(1)}, u32[]{:S(2)}, u32[]{:S(2)}) collective-permute-start(f32[2,128,128]{2,1,0:T(8,128)S(1)} %pad_maximum_fusion.8), channel_id=1, source_target_pairs={{0,2},{1,3},{2,0},{3,1},{4,6},{5,7},{6,4},{7,5},{8,10},{9,11},{10,... | collective-permute-start | bytes 393224 | tf_op jit(solution)/shard_map/ppermute | solution.py:37
  58.2 3.9 %collective-permute-start.18 = (f32[132,128]{1,0:T(8,128)S(1)}, f32[132,128]{1,0:T(8,128)S(1)}, u32[]{:S(2)}, u32[]{:S(2)}) collective-permute-start(f32[132,128]{1,0:T(8,128)S(1)} %concatenate.84), channel_id=1, source_target_pairs={{0,1},{1,2},{2,3},{3,0},{4,5},{5,6},{6,7},{7,4},{8,9},{9,10},{10,1... | collective-permute-start | bytes 202760 | tf_op jit(solution)/shard_map/ppermute | solution.py:59
  58.3 5.1 %collective-permute-start.19 = (f32[132,128]{1,0:T(8,128)S(1)}, f32[132,128]{1,0:T(8,128)S(1)}, u32[]{:S(2)}, u32[]{:S(2)}) collective-permute-start(f32[132,128]{1,0:T(8,128)S(1)} %concatenate.85), channel_id=1, source_target_pairs={{0,2},{1,3},{2,0},{3,1},{4,6},{5,7},{6,4},{7,5},{8,10},{9,11},{10,... | collective-permute-start | bytes 202760 | tf_op jit(solution)/shard_map/ppermute | solution.py:59
  59.4 4.0 %collective-permute-start.20 = (f32[132,128]{1,0:T(8,128)S(1)}, f32[132,128]{1,0:T(8,128)S(1)}, u32[]{:S(2)}, u32[]{:S(2)}) collective-permute-start(f32[132,128]{1,0:T(8,128)S(1)} %concatenate.86), channel_id=1, source_target_pairs={{0,3},{1,0},{2,1},{3,2},{4,7},{5,4},{6,5},{7,6},{8,11},{9,8},{10,9... | collective-permute-start | bytes 202760 | tf_op jit(solution)/shard_map/ppermute | solution.py:59
  63.4 3.7 %collective-permute-start.21 = (f32[4,128]{1,0:T(4,128)S(1)}, f32[4,128]{1,0:T(4,128)S(1)}, u32[]{:S(2)}, u32[]{:S(2)}) collective-permute-start(f32[4,128]{1,0:T(4,128)S(1)} %select_add_fusion), channel_id=1, source_target_pairs={{0,4},{4,0},{8,12},{12,8},{1,5},{5,1},{9,13},{13,9},{2,6},{6,2},{1... | collective-permute-start | bytes 6152 | tf_op jit(solution)/shard_map/ppermute | solution.py:35
  67.0 4.5 %collective-permute-start.22 = (f32[2,4,128]{2,1,0:T(4,128)S(1)}, f32[2,4,128]{2,1,0:T(4,128)S(1)}, u32[]{:S(2)}, u32[]{:S(2)}) collective-permute-start(f32[2,4,128]{2,1,0:T(4,128)S(1)} %pad_maximum_fusion.17), channel_id=1, source_target_pairs={{0,8},{4,12},{8,0},{12,4},{1,9},{5,13},{9,1},{13,5},{2,10},{6,14},... | collective-permute-start | bytes 12296 | tf_op jit(solution)/shard_map/ppermute | solution.py:37

commit v11 on v9

--- a/solution.py
+++ b/solution.py
@@ -60,6 +60,20 @@
         total = total + got[:rows]
         extras.append(got[rows:])
     return total, jnp.stack(extras)
+
+
+def natural(blocks, axis, count):
+    if count > 4:
+        return blocks
+    me = lax.axis_index(axis)
+    ordered = []
+    for device in range(count):
+        wanted = (me - device) % count
+        block = blocks[count - 1]
+        for entry in range(count - 2, -1, -1):
+            block = jnp.where(wanted == entry, blocks[entry], block)
+        ordered.append(block)
+    return jnp.stack(ordered)
 
 
 def canonical_sum(extras, axis, count):
@@ -95,14 +109,12 @@
     width = SEED_CLASSES
     column_blocks = n_narrow * br_local
     local_column = pattern // groups * br_local + pattern % br_local
-    pick = local_column[:, :, None] == jnp.arange(column_blocks, dtype=local_column.dtype)
-    dense = jnp.sum(
-        jnp.where(pick[:, :, None, :, None], tiles[:, :, :, None, :], 0.0), axis=1
-    )
-    column_sums = jnp.sum(dense, axis=(0, 1)).reshape(n_narrow, own_rows)
-    order = source("wide", n_wide, jnp.arange(n_wide))
-    dense = jnp.take(dense.reshape(n_wide, own_rows, column_blocks * tile), order, axis=0)
-    transposed = dense.reshape(groups * tile, column_blocks * tile).T
+    pick = (
+        local_column[:, :, None] == jnp.arange(column_blocks, dtype=local_column.dtype)
+    ).astype(jnp.float32)
+    transposed = jnp.einsum("mkt,mkab->tbma", pick, tiles, precision=lax.Precision.HIGHEST)
+    column_sums = jnp.sum(transposed, axis=(2, 3)).reshape(n_narrow, own_rows)
+    transposed = transposed.reshape(column_blocks * tile, groups * tile)
 
     labels = seed_label[:, 0]
     seeded = (labels < SEED_CLASSES).astype(jnp.float32)
@@ -134,13 +146,14 @@
             return None, None, sums
         got = gather_blocks(jnp.concatenate([applied, narrow_sums], axis=0), "wide", n_wide)
         sums = canonical_sum(got[:, own_rows:], "wide", n_wide)
-        return got[:, :own_rows], gather_blocks(applied, "narrow", n_narrow), sums
+        rows = natural(got[:, :own_rows], "wide", n_wide)
+        return rows, gather_blocks(applied, "narrow", n_narrow), sums
 
     rhs = indicator(labels)
     solution = jnp.zeros_like(rhs)
     residual = rhs
     direction = rhs
-    rows_residual = indicator(gather_blocks(labels, "wide", n_wide))
+    rows_residual = indicator(natural(gather_blocks(labels, "wide", n_wide), "wide", n_wide))
     columns_residual = indicator(gather_blocks(labels, "narrow", n_narrow))
     partial, quad = product(rows_residual, columns_residual)
     degree_part = jnp.zeros((width,), jnp.float32)

time: 64.5 us -> 86.1 us (1.33)
  local copies, waits for them, and re-layouts: 1.34 us -> 12.3 us
  other arithmetic: 7.31 us -> 14.8 us
  matrix products: 3.02 us -> 7.47 us
  starting transfers between devices: 33.5 us -> 30.7 us
    concatenate x6, local copies, waits for them, and re-layouts: 0.17 us -> 10.4 us  [scatter_with(): got = lax.ppermute(jnp.concatenate([sent, extra], axis=0), axis, pairs)]
    reduce_sum x1 -> x0, other arithmetic: 2.97 us -> none  [local(): column_sums = jnp.sum(dense, axis=(0, 1)).reshape(n_narrow, own_rows)]
    reduce_sum x2, other arithmetic: 0.26 us -> 2.77 us  [local(): jnp.sum(residual * residual, axis=0)]
    dot_general x0 -> x1, matrix products: none -> 2.52 us  [local(): jnp.einsum('mkt,mkab->tbma', pick, tiles, precision=lax.Precision.HIGHEST)]
    dot_general x3, matrix products: 3.02 us -> 4.95 us  [product(): jnp.dot(transposed, row_values.reshape(groups * tile, width), precision=l...]
    ppermute x9, waiting for transfers between devices: 7.81 us -> 9.36 us  [scatter_with(): got = lax.ppermute(jnp.concatenate([sent, extra], axis=0), axis, pairs)]
    add x6, other arithmetic: 0.08 us -> 1.52 us  [canonical_sum(): total = term if total is None else total + term]
    transpose x0 -> x1, local copies, waits for them, and re-layouts: none -> 1.35 us  [local(): jnp.einsum('mkt,mkab->tbma', pick, tiles, precision=lax.Precision.HIGHEST)]
  transfers between devices with their start and end apart: 27 -> 27, of which waited for: 17 -> 10; matrix products, arithmetic and copies ran while one was open for 12% -> 28% of each run, Pallas kernels for 0% -> 0%
where the time goes in v11:
time: 86.1 us; the launch traced here: 85.4 us
  starting transfers between devices  30.7 us (36%)
  waiting for transfers between devices  18.9 us (22%)
  other arithmetic  14.8 us (17%)
  local copies, waits for them, and re-layouts  12.3 us (14%)
  matrix products  7.47 us (9%)
  between operations  1.23 us (1%)
    ppermute x12, starting transfers between devices, gather_blocks(): parts.append(lax.ppermute(values, axis, pairs))  19.7 us
    concatenate x6, local copies, waits for them, and re-layouts, scatter_with(): got = lax.ppermute(jnp.concatenate([sent, extra], axis=0), axis, pairs)  10.4 us
    ppermute x9, waiting for transfers between devices, scatter_with(): got = lax.ppermute(jnp.concatenate([sent, extra], axis=0), axis, pairs)  9.36 us
    ppermute x12, waiting for transfers between devices, gather_blocks(): parts.append(lax.ppermute(values, axis, pairs))  8.41 us
    ppermute x9, starting transfers between devices, scatter_with(): got = lax.ppermute(jnp.concatenate([sent, extra], axis=0), axis, pairs)  6.76 us
    dot_general x3, matrix products, product(): jnp.dot(transposed, row_values.reshape(groups * tile, width), precision=l...  4.95 us
    ppermute x3, starting transfers between devices, gather_blocks(): lax.ppermute(both, axis, [(i, i ^ 2) for i in range(count)])  3.67 us
    reduce_sum x2, other arithmetic, local(): jnp.sum(residual * residual, axis=0)  2.77 us
  transfers between devices with their start and end apart: 27, of which 10 were waited for; matrix products, arithmetic and copies ran while one was open for 28% of the time, Pallas kernels for 0%

profile of v11, /device:TPU:0, one launch (start us, length us, event | category | flops | bytes accessed | tf_op | source)
XLA Modules:
  0.0 85.4 jit_solution(4058476744451968186)
XLA Ops:
  0.7 0.5 collective-permute-start.3
  1.2 2.6 %collective-permute-start = (s32[128]{0:T(128)}, s32[128]{0:T(128)S(1)}, u32[]{:S(2)}, u32[]{:S(2)}) collective-permute-start(s32[128]{0:T(128)} %bitcast.276), channel_id=1, source_target_pairs={{0,4},{4,8},{8,12},{12,0},{1,5},{5,9},{9,13},{13,1},{2,6},{6,10},{... | collective-permute-start | bytes 1544 | tf_op jit(solution)/shard_map/ppermute | solution.py:41
  3.8 2.6 %collective-permute-start.1 = (s32[128]{0:T(128)}, s32[128]{0:T(128)S(1)}, u32[]{:S(2)}, u32[]{:S(2)}) collective-permute-start(s32[128]{0:T(128)} %bitcast.277), channel_id=1, source_target_pairs={{0,8},{4,12},{8,0},{12,4},{1,9},{5,13},{9,1},{13,5},{2,10},{6,14},... | collective-permute-start | bytes 1544 | tf_op jit(solution)/shard_map/ppermute | solution.py:41
  6.4 1.3 %collective-permute-start.2 = (s32[128]{0:T(128)}, s32[128]{0:T(128)S(1)}, u32[]{:S(2)}, u32[]{:S(2)}) collective-permute-start(s32[128]{0:T(128)} %bitcast.278), channel_id=1, source_target_pairs={{0,12},{4,0},{8,4},{12,8},{1,13},{5,1},{9,5},{13,9},{2,14},{6,2},{... | collective-permute-start | bytes 1544 | tf_op jit(solution)/shard_map/ppermute | solution.py:41
  7.7 0.7 fusion.108
  8.4 0.7 add_select_fusion
  9.1 0.8 fusion.54
  9.9 2.5 %bitcast_reduce_fusion = (f32[4,128]{1,0:T(4,128)S(1)}, f32[4,4,128,128]{3,1,2,0:T(4,128)S(1)}) fusion(f32[4,8,128,128]{3,2,1,0:T(8,128)S(1)} %copy-done, s32[4,8]{1,0:T(4,128)S(1)} %add_select_fusion), kind=kOutput, calls=%fused_computation.239 | convolution fusion | flops 25427584 | bytes 3147904 | tf_op jit(solution)/shard_map/mkt,mkab->tbma/dot_general | solution.py:115
  12.5 1.6 %collective-permute-start.4 = (s32[2,128]{1,0:T(2,128)S(1)}, s32[2,128]{1,0:T(2,128)S(1)}, u32[]{:S(2)}, u32[]{:S(2)}) collective-permute-start(s32[2,128]{1,0:T(2,128)S(1)} %pad_add_fusion.2), channel_id=1, source_target_pairs={{0,2},{1,3},{2,0},{3,1},{4,6},{5,7},{6,4},{7,5},{8,10},{9,11},{10,... | collective-permute-start | bytes 3080 | tf_op jit(solution)/shard_map/ppermute | solution.py:37
  14.1 0.6 pad_add_fusion
  14.7 1.9 %fusion.2 = f32[4,128,128]{2,1,0:T(8,128)S(1)} fusion(f32[4,128,512]{1,0,2:T(4,128)S(1)} %bitcast.248, s32[512]{0:T(512)S(1)} %get-tuple-element.67), kind=kOutput, calls=%fused_computation.4 | convolution fusion | flops 402784256 | bytes 1312768 | tf_op jit(solution)/shard_map/dot_general | solution.py:128
  16.7 0.1 fusion.20
  16.8 0.2 fusion.51
  17.0 0.7 pad_maximum_fusion.8
  17.7 1.7 %collective-permute-start.7 = (f32[131,128]{1,0:T(8,128)}, f32[131,128]{1,0:T(8,128)}, u32[]{:S(2)}, u32[]{:S(2)}) collective-permute-start(f32[131,128]{1,0:T(8,128)} %get-tuple-element.78), channel_id=1, source_target_pairs={{0,3},{1,0},{2,1},{3,2},{4,7},{5,4},{6,5},{7,6},{8,11},{9,8},{10,9... | collective-permute-start | bytes 201224 | tf_op jit(solution)/shard_map/ppermute | solution.py:59
  19.5 1.0 %collective-permute-start.6 = (f32[131,128]{1,0:T(8,128)}, f32[131,128]{1,0:T(8,128)}, u32[]{:S(2)}, u32[]{:S(2)}) collective-permute-start(f32[131,128]{1,0:T(8,128)} %get-tuple-element.77), channel_id=1, source_target_pairs={{0,2},{1,3},{2,0},{3,1},{4,6},{5,7},{6,4},{7,5},{8,10},{9,11},{10,... | collective-permute-start | bytes 201224 | tf_op jit(solution)/shard_map/ppermute | solution.py:59
  20.5 1.4 %copy.7 = f32[4,128,4,128]{3,1,2,0:T(8,128)} copy(f32[4,128,4,128]{1,0,3,2:T(4,128)S(1)} %bitcast.249) | data formatting | bytes 2097152 | tf_op jit(solution)/shard_map/mkt,mkab->tbma/transpose | solution.py:115
  21.8 2.3 %collective-permute-done.6 = f32[131,128]{1,0:T(8,128)} collective-permute-done((f32[131,128]{1,0:T(8,128)}, f32[131,128]{1,0:T(8,128)}, u32[]{:S(2)}, u32[]{:S(2)}) %collective-permute-start.6) | collective-permute-done | bytes 67104 | tf_op jit(solution)/shard_map/ppermute | solution.py:59
  24.1 0.9 %fusion.40 = f32[129,128]{1,0:T(8,128)S(1)} fusion(s32[]{:T(128)S(6)} %select_n.863, f32[4,128,128]{2,1,0:T(8,128)S(1)} %fusion.2, f32[4,1,128]{2,1,0:T(1,128)S(1)} %bitcast.289, f32[131,128]{1,0:T(8,128)} %collective-permute-done.7, f32[131,128]{1,0:T(8,128)} %collective-permute-done.6, f32[131,128]{1,0:T(8,128)S(1)} %collective-permute-done.5), kind=kLoop, calls=%fused_computation.82 | loop fusion | flops 66048 | bytes 528388 | tf_op jit(solution)/shard_map/add | solution.py:60
  25.1 0.1 fusion.56
  25.2 0.7 select_add_fusion.3
  25.9 0.7 collective-permute-start.8
  26.7 3.1 %collective-permute-start.10 = (f32[130,128]{1,0:T(8,128)S(1)}, f32[130,128]{1,0:T(8,128)S(1)}, u32[]{:S(2)}, u32[]{:S(2)}) collective-permute-start(f32[130,128]{1,0:T(8,128)S(1)} %get-tuple-element.64), channel_id=1, source_target_pairs={{0,12},{4,0},{8,4},{12,8},{1,13},{5,1},{9,5},{13,9},{2,14},{6,2},{... | collective-permute-start | bytes 199688 | tf_op jit(solution)/shard_map/ppermute | solution.py:41
  29.8 0.1 fusion.114
  29.9 1.1 %collective-permute-done.11 = f32[128,128]{1,0:T(8,128)S(1)} collective-permute-done((f32[128,128]{1,0:T(8,128)S(1)}, f32[128,128]{1,0:T(8,128)S(1)}, u32[]{:S(2)}, u32[]{:S(2)}) %collective-permute-start.11) | collective-permute-done | bytes 65568 | tf_op jit(solution)/shard_map/ppermute | solution.py:35
  31.1 1.1 %collective-permute-start.12 = (f32[2,128,128]{2,1,0:T(8,128)S(1)}, f32[2,128,128]{2,1,0:T(8,128)S(1)}, u32[]{:S(2)}, u32[]{:S(2)}) collective-permute-start(f32[2,128,128]{2,1,0:T(8,128)S(1)} %pad_maximum_fusion.4), channel_id=1, source_target_pairs={{0,2},{1,3},{2,0},{3,1},{4,6},{5,7},{6,4},{7,5},{8,10},{9,11},{10,... | collective-permute-start | bytes 393224 | tf_op jit(solution)/shard_map/ppermute | solution.py:37
  32.1 0.3 collective-permute-done.8
  32.4 2.6 %collective-permute-done.9 = f32[130,128]{1,0:T(8,128)S(1)} collective-permute-done((f32[130,128]{1,0:T(8,128)S(1)}, f32[130,128]{1,0:T(8,128)S(1)}, u32[]{:S(2)}, u32[]{:S(2)}) %collective-permute-start.9) | collective-permute-done | bytes 66592 | tf_op jit(solution)/shard_map/ppermute | solution.py:41
  35.2 0.4 copy-done.29
  35.6 1.1 %convolution_bitcast_fusion.1 = f32[4,128,128]{2,1,0:T(8,128)S(1)} fusion(f32[4,128,4,128]{3,1,2,0:T(8,128)S(1)} %copy-done.1, f32[1,128,128]{2,1,0:T(8,128)S(1)} %get-tuple-element.44, f32[1,128,128]{2,1,0:T(8,128)S(1)} %get-tuple-element.43, f32[1,128,128]{2,1,0:T(8,128)S(1)} %get-tuple-element.42, f32[1,128,128]{2,1,0:T(8,128)S(1)} %get-tuple-element.41, ...), kind=kOutput, calls=%fused_computation.3 | convolution fusion | flops 403111936 | bytes 1575424 | tf_op jit(solution)/shard_map/dot_general | solution.py:128
  36.7 0.7 multiply_reduce_fusion.3
  37.4 0.1 multiply_subtract_fusion
  37.6 0.7 dynamic-slice_bitcast_fusion.4
  38.3 0.6 subtract_bitcast_fusion.2
  38.9 2.8 %concatenate.64 = f32[132,128]{1,0:T(8,128)} concatenate(f32[128,128]{1,0:T(8,128)} %get-tuple-element.59, f32[1,128]{1,0:T(1,128)} %bitcast.306, f32[1,128]{1,0:T(1,128)} %subtract_bitcast_fusion.2, f32[1,128]{1,0:T(1,128)} %bitcast.302, f32[1,128]{1,0:T(1,128)} %bitcast.310), dimensions={0} | concatenate | bytes 135168 | tf_op jit(solution)/shard_map/concatenate | solution.py:59
  41.6 2.8 %concatenate.66 = f32[132,128]{1,0:T(8,128)} concatenate(f32[128,128]{1,0:T(8,128)} %get-tuple-element.55, f32[1,128]{1,0:T(1,128)} %bitcast.307, f32[1,128]{1,0:T(1,128)} %subtract_bitcast_fusion.2, f32[1,128]{1,0:T(1,128)} %bitcast.303, f32[1,128]{1,0:T(1,128)} %bitcast.311), dimensions={0} | concatenate | bytes 135168 | tf_op jit(solution)/shard_map/concatenate | solution.py:59
  44.4 1.7 %collective-permute-start.15 = (f32[132,128]{1,0:T(8,128)}, f32[132,128]{1,0:T(8,128)}, u32[]{:S(2)}, u32[]{:S(2)}) collective-permute-start(f32[132,128]{1,0:T(8,128)} %concatenate.66), channel_id=1, source_target_pairs={{0,3},{1,0},{2,1},{3,2},{4,7},{5,4},{6,5},{7,6},{8,11},{9,8},{10,9... | collective-permute-start | bytes 202760 | tf_op jit(solution)/shard_map/ppermute | solution.py:59
  46.1 2.7 %concatenate.65 = f32[132,128]{1,0:T(8,128)} concatenate(f32[128,128]{1,0:T(8,128)} %get-tuple-element.54, f32[1,128]{1,0:T(1,128)} %bitcast.308, f32[1,128]{1,0:T(1,128)} %subtract_bitcast_fusion.2, f32[1,128]{1,0:T(1,128)} %bitcast.304, f32[1,128]{1,0:T(1,128)} %bitcast.312), dimensions={0} | concatenate | bytes 135168 | tf_op jit(solution)/shard_map/concatenate | solution.py:59
  48.9 1.0 %collective-permute-start.14 = (f32[132,128]{1,0:T(8,128)}, f32[132,128]{1,0:T(8,128)S(1)}, u32[]{:S(2)}, u32[]{:S(2)}) collective-permute-start(f32[132,128]{1,0:T(8,128)} %concatenate.65), channel_id=1, source_target_pairs={{0,2},{1,3},{2,0},{3,1},{4,6},{5,7},{6,4},{7,5},{8,10},{9,11},{10,... | collective-permute-start | bytes 202760 | tf_op jit(solution)/shard_map/ppermute | solution.py:59
  49.9 3.5 %collective-permute-done.14 = f32[132,128]{1,0:T(8,128)S(1)} collective-permute-done((f32[132,128]{1,0:T(8,128)}, f32[132,128]{1,0:T(8,128)S(1)}, u32[]{:S(2)}, u32[]{:S(2)}) %collective-permute-start.14) | collective-permute-done | bytes 67616 | tf_op jit(solution)/shard_map/ppermute | solution.py:59
  53.5 1.0 %multiply_subtract_fusion.5 = f32[128,128]{1,0:T(8,128)S(1)} fusion(f32[132,128]{1,0:T(8,128)} %collective-permute-done.15, f32[132,128]{1,0:T(8,128)S(1)} %collective-permute-done.14, f32[132,128]{1,0:T(8,128)} %collective-permute-done.13, f32[4,128,128]{2,1,0:T(8,128)S(1)} %convolution_bitcast_fusion.1, s32[]{:T(128)S(6)} %select_n.863, ...), kind=kLoop, calls=%fused_computation.74 | loop fusion | flops 180224 | bytes 394756 | tf_op jit(solution)/shard_map/sub | solution.py:198
  54.5 0.7 select_add_fusion.2
  55.3 1.0 %collective-permute-start.18 = (f32[132,128]{1,0:T(8,128)S(1)}, f32[132,128]{1,0:T(8,128)S(1)}, u32[]{:S(2)}, u32[]{:S(2)}) collective-permute-start(f32[132,128]{1,0:T(8,128)S(1)} %get-tuple-element.62), channel_id=1, source_target_pairs={{0,12},{4,0},{8,4},{12,8},{1,13},{5,1},{9,5},{13,9},{2,14},{6,2},{... | collective-permute-start | bytes 202760 | tf_op jit(solution)/shard_map/ppermute | solution.py:41
  56.2 1.4 %collective-permute-start.17 = (f32[132,128]{1,0:T(8,128)S(1)}, f32[132,128]{1,0:T(8,128)S(1)}, u32[]{:S(2)}, u32[]{:S(2)}) collective-permute-start(f32[132,128]{1,0:T(8,128)S(1)} %get-tuple-element.62), channel_id=1, source_target_pairs={{0,8},{4,12},{8,0},{12,4},{1,9},{5,13},{9,1},{13,5},{2,10},{6,14},... | collective-permute-start | bytes 202760 | tf_op jit(solution)/shard_map/ppermute | solution.py:41
  57.6 1.9 %collective-permute-start.16 = (f32[132,128]{1,0:T(8,128)S(1)}, f32[132,128]{1,0:T(8,128)S(1)}, u32[]{:S(2)}, u32[]{:S(2)}) collective-permute-start(f32[132,128]{1,0:T(8,128)S(1)} %get-tuple-element.62), channel_id=1, source_target_pairs={{0,4},{4,8},{8,12},{12,0},{1,5},{5,9},{9,13},{13,1},{2,6},{6,10},{... | collective-permute-start | bytes 202760 | tf_op jit(solution)/shard_map/ppermute | solution.py:41
  59.6 1.1 %collective-permute-start.20 = (f32[2,128,128]{2,1,0:T(8,128)S(1)}, f32[2,128,128]{2,1,0:T(8,128)S(1)}, u32[]{:S(2)}, u32[]{:S(2)}) collective-permute-start(f32[2,128,128]{2,1,0:T(8,128)S(1)} %pad_maximum_fusion.5), channel_id=1, source_target_pairs={{0,2},{1,3},{2,0},{3,1},{4,6},{5,7},{6,4},{7,5},{8,10},{9,11},{10,... | collective-permute-start | bytes 393224 | tf_op jit(solution)/shard_map/ppermute | solution.py:37
  60.6 4.2 %collective-permute-done.17 = f32[132,128]{1,0:T(8,128)S(1)} collective-permute-done((f32[132,128]{1,0:T(8,128)S(1)}, f32[132,128]{1,0:T(8,128)S(1)}, u32[]{:S(2)}, u32[]{:S(2)}) %collective-permute-start.17) | collective-permute-done | bytes 67616 | tf_op jit(solution)/shard_map/ppermute | solution.py:41
  64.9 0.7 bitcast_divide_fusion
  65.6 0.7 fusion.98
  66.3 2.0 %multiply_reduce_fusion.2 = (f32[128]{0:T(128)}, f32[128]{0:T(128)S(1)}, f32[128]{0:T(128)}, f32[128]{0:T(128)}, f32[128,128]{1,0:T(8,128)}) fusion(f32[128]{0:T(128)S(1)} %get-tuple-element.35, f32[128]{0:T(128)} %copy-done.20, s32[128]{0:T(128)S(1)} %bitcast.286, f32[128]{0:T(128)} %copy-done.16, f32[128]{0:T(128)S(1)} %bitcast.316, ...), kind=kLoop, calls=%fused_computation.150 | loop fusion | flops 343552 | bytes 201216 | tf_op jit(solution)/shard_map/reduce_sum | solution.py:191
  68.3 2.0 %convolution_bitcast_fusion = f32[4,128,128]{2,1,0:T(8,128)S(1)} fusion(f32[4,128,4,128]{3,1,2,0:T(8,128)S(1)} %copy-done.1, f32[1,128,128]{2,1,0:T(8,128)S(1)} %get-tuple-element.40, f32[1,128,128]{2,1,0:T(8,128)S(1)} %get-tuple-element.39, f32[1,128,128]{2,1,0:T(8,128)S(1)} %get-tuple-element.38, f32[1,128,128]{2,1,0:T(8,128)S(1)} %get-tuple-element.37, ...), kind=kOutput, calls=%fused_computation.2 | convolution fusion | flops 403570688 | bytes 1838592 | tf_op jit(solution)/shard_map/dot_general | solution.py:128
  70.4 0.1 fusion.5
  70.7 0.7 concatenate.71
  71.4 0.7 concatenate.70
  72.1 1.0 %collective-permute-start.22 = (f32[132,128]{1,0:T(8,128)S(1)}, f32[132,128]{1,0:T(8,128)S(1)}, u32[]{:S(2)}, u32[]{:S(2)}) collective-permute-start(f32[132,128]{1,0:T(8,128)S(1)} %concatenate.70), channel_id=1, source_target_pairs={{0,2},{1,3},{2,0},{3,1},{4,6},{5,7},{6,4},{7,5},{8,10},{9,11},{10,... | collective-permute-start | bytes 202760 | tf_op jit(solution)/shard_map/ppermute | solution.py:59
  73.2 0.7 concatenate.69
  73.9 0.2 collective-permute-start.21
  74.1 2.7 %collective-permute-done.22 = f32[132,128]{1,0:T(8,128)S(1)} collective-permute-done((f32[132,128]{1,0:T(8,128)S(1)}, f32[132,128]{1,0:T(8,128)S(1)}, u32[]{:S(2)}, u32[]{:S(2)}) %collective-permute-start.22) | collective-permute-done | bytes 67616 | tf_op jit(solution)/shard_map/ppermute | solution.py:59
  76.7 0.9 %collective-permute-done.21 = f32[132,128]{1,0:T(8,128)S(1)} collective-permute-done((f32[132,128]{1,0:T(8,128)S(1)}, f32[132,128]{1,0:T(8,128)S(1)}, u32[]{:S(2)}, u32[]{:S(2)}) %collective-permute-start.21) | collective-permute-done | bytes 67616 | tf_op jit(solution)/shard_map/ppermute | solution.py:59
  77.7 2.0 %collective-permute-start.25 = (f32[4,128]{1,0:T(4,128)S(1)}, f32[4,128]{1,0:T(4,128)S(1)}, u32[]{:S(2)}, u32[]{:S(2)}) collective-permute-start(f32[4,128]{1,0:T(4,128)S(1)} %select_add_fusion.1), channel_id=1, source_target_pairs={{0,8},{4,12},{8,0},{12,4},{1,9},{5,13},{9,1},{13,5},{2,10},{6,14},... | collective-permute-start | bytes 6152 | tf_op jit(solution)/shard_map/ppermute | solution.py:41
  79.7 2.8 %collective-permute-start.26 = (f32[4,128]{1,0:T(4,128)S(1)}, f32[4,128]{1,0:T(4,128)S(1)}, u32[]{:S(2)}, u32[]{:S(2)}) collective-permute-start(f32[4,128]{1,0:T(4,128)S(1)} %select_add_fusion.1), channel_id=1, source_target_pairs={{0,12},{4,0},{8,4},{12,8},{1,13},{5,1},{9,5},{13,9},{2,14},{6,2},{... | collective-permute-start | bytes 6152 | tf_op jit(solution)/shard_map/ppermute | solution.py:41
  82.6 0.5 collective-permute-done.24
  83.1 0.8 collective-permute-done.26
  84.0 1.5 %fusion.49 = (f32[128,128]{1,0:T(8,128)}, f32[128,128]{1,0:T(8,128)}) fusion(f32[132,128]{1,0:T(8,128)S(1)} %collective-permute-done.23, f32[132,128]{1,0:T(8,128)S(1)} %collective-permute-done.22, f32[132,128]{1,0:T(8,128)S(1)} %collective-permute-done.21, f32[128,128]{1,0:T(8,128)S(1)} %copy-done.10, f32[4,128,128]{2,1,0:T(8,128)S(1)} %convolution_bitcast_fusion, ...), kind=kLoop, calls=%fused_computation.93 | loop fusion | flops 425984 | bytes 527876 | tf_op jit(solution)/shard_map/sub | solution.py:183
  (109 shorter events, 0.8 us)
Async XLA Ops:
  0.6 9.3 %copy-start = (f32[4,8,128,128]{3,2,1,0:T(8,128)S(1)}, f32[4,8,128,128]{3,2,1,0:T(8,128)}, u32[]{:S(2)}) copy-start(f32[4,8,128,128]{3,2,1,0:T(8,128)} %param.3) | copy-start | bytes 6291460
  0.6 11.9 %copy-start.11 = (s32[128,1]{0,1:T(1,128)S(1)}, s32[128,1]{0,1:T(1,128)}, u32[]{:S(2)}) copy-start(s32[128,1]{0,1:T(1,128)} %param.5) | copy-start | bytes 1540
  0.7 11.9 %collective-permute-start.3 = (s32[128]{0:T(128)}, s32[128]{0:T(128)S(1)}, u32[]{:S(2)}, u32[]{:S(2)}) collective-permute-start(s32[128]{0:T(128)} %bitcast.275), channel_id=1, source_target_pairs={{0,1},{1,0},{2,3},{3,2},{4,5},{5,4},{6,7},{7,6},{8,9},{9,8},{10,11... | collective-permute-start | bytes 1544 | tf_op jit(solution)/shard_map/ppermute | solution.py:35
  1.2 12.9 %collective-permute-start = (s32[128]{0:T(128)}, s32[128]{0:T(128)S(1)}, u32[]{:S(2)}, u32[]{:S(2)}) collective-permute-start(s32[128]{0:T(128)} %bitcast.276), channel_id=1, source_target_pairs={{0,4},{4,8},{8,12},{12,0},{1,5},{5,9},{9,13},{13,1},{2,6},{6,10},{... | collective-permute-start | bytes 1544 | tf_op jit(solution)/shard_map/ppermute | solution.py:41
  3.8 10.3 %collective-permute-start.1 = (s32[128]{0:T(128)}, s32[128]{0:T(128)S(1)}, u32[]{:S(2)}, u32[]{:S(2)}) collective-permute-start(s32[128]{0:T(128)} %bitcast.277), channel_id=1, source_target_pairs={{0,8},{4,12},{8,0},{12,4},{1,9},{5,13},{9,1},{13,5},{2,10},{6,14},... | collective-permute-start | bytes 1544 | tf_op jit(solution)/shard_map/ppermute | solution.py:41
  6.4 7.7 %collective-permute-start.2 = (s32[128]{0:T(128)}, s32[128]{0:T(128)S(1)}, u32[]{:S(2)}, u32[]{:S(2)}) collective-permute-start(s32[128]{0:T(128)} %bitcast.278), channel_id=1, source_target_pairs={{0,12},{4,0},{8,4},{12,8},{1,13},{5,1},{9,5},{13,9},{2,14},{6,2},{... | collective-permute-start | bytes 1544 | tf_op jit(solution)/shard_map/ppermute | solution.py:41
  9.9 7.1 %copy-start.24 = (f32[128]{0:T(128)}, f32[128]{0:T(128)S(1)}, u32[]{:S(2)}) copy-start(f32[128]{0:T(128)S(1)} %get-tuple-element.28) | copy-start | bytes 1540
  12.5 4.1 %collective-permute-start.4 = (s32[2,128]{1,0:T(2,128)S(1)}, s32[2,128]{1,0:T(2,128)S(1)}, u32[]{:S(2)}, u32[]{:S(2)}) collective-permute-start(s32[2,128]{1,0:T(2,128)S(1)} %pad_add_fusion.2), channel_id=1, source_target_pairs={{0,2},{1,3},{2,0},{3,1},{4,6},{5,7},{6,4},{7,5},{8,10},{9,11},{10,... | collective-permute-start | bytes 3080 | tf_op jit(solution)/shard_map/ppermute | solution.py:37
  16.7 1.0 %copy-start.12 = (s32[4,128]{1,0:T(4,128)}, s32[4,128]{1,0:T(4,128)S(1)}, u32[]{:S(2)}) copy-start(s32[4,128]{1,0:T(4,128)S(1)} %pad_add_fusion.1) | copy-start | bytes 6148
  17.0 0.7 copy-start.23
  17.7 4.1 %collective-permute-start.5 = (f32[131,128]{1,0:T(8,128)}, f32[131,128]{1,0:T(8,128)S(1)}, u32[]{:S(2)}, u32[]{:S(2)}) collective-permute-start(f32[131,128]{1,0:T(8,128)} %get-tuple-element.76), channel_id=1, source_target_pairs={{0,1},{1,2},{2,3},{3,0},{4,5},{5,6},{6,7},{7,4},{8,9},{9,10},{10,1... | collective-permute-start | bytes 201224 | tf_op jit(solution)/shard_map/ppermute | solution.py:59
  17.7 4.1 %collective-permute-start.7 = (f32[131,128]{1,0:T(8,128)}, f32[131,128]{1,0:T(8,128)}, u32[]{:S(2)}, u32[]{:S(2)}) collective-permute-start(f32[131,128]{1,0:T(8,128)} %get-tuple-element.78), channel_id=1, source_target_pairs={{0,3},{1,0},{2,1},{3,2},{4,7},{5,4},{6,5},{7,6},{8,11},{9,8},{10,9... | collective-permute-start | bytes 201224 | tf_op jit(solution)/shard_map/ppermute | solution.py:59
  19.5 4.6 %collective-permute-start.6 = (f32[131,128]{1,0:T(8,128)}, f32[131,128]{1,0:T(8,128)}, u32[]{:S(2)}, u32[]{:S(2)}) collective-permute-start(f32[131,128]{1,0:T(8,128)} %get-tuple-element.77), channel_id=1, source_target_pairs={{0,2},{1,3},{2,0},{3,1},{4,6},{5,7},{6,4},{7,5},{8,10},{9,11},{10,... | collective-permute-start | bytes 201224 | tf_op jit(solution)/shard_map/ppermute | solution.py:59
  21.8 13.8 %copy-start.1 = (f32[4,128,4,128]{3,1,2,0:T(8,128)S(1)}, f32[4,128,4,128]{3,1,2,0:T(8,128)}, u32[]{:S(2)}) copy-start(f32[4,128,4,128]{3,1,2,0:T(8,128)} %copy.7) | copy-start | bytes 3145732
  21.8 13.8 %copy-start.15 = (s32[4,128]{1,0:T(4,128)S(1)}, s32[4,128]{1,0:T(4,128)}, u32[]{:S(2)}) copy-start(s32[4,128]{1,0:T(4,128)} %get-tuple-element.66) | copy-start | bytes 6148
  21.8 15.6 %copy-start.13 = (s32[4,128]{1,0:T(4,128)S(1)}, s32[4,128]{1,0:T(4,128)}, u32[]{:S(2)}) copy-start(s32[4,128]{1,0:T(4,128)} %copy-done.12) | copy-start | bytes 6148
  25.1 28.4 %copy-start.16 = (f32[128]{0:T(128)}, f32[128]{0:T(128)S(1)}, u32[]{:S(2)}) copy-start(f32[128]{0:T(128)S(1)} %fusion.90) | copy-start | bytes 1540
  25.9 6.5 %collective-permute-start.8 = (f32[130,128]{1,0:T(8,128)S(1)}, f32[130,128]{1,0:T(8,128)S(1)}, u32[]{:S(2)}, u32[]{:S(2)}) collective-permute-start(f32[130,128]{1,0:T(8,128)S(1)} %get-tuple-element.64), channel_id=1, source_target_pairs={{0,4},{4,8},{8,12},{12,0},{1,5},{5,9},{9,13},{13,1},{2,6},{6,10},{... | collective-permute-start | bytes 199688 | tf_op jit(solution)/shard_map/ppermute | solution.py:41
  26.7 5.8 %collective-permute-start.10 = (f32[130,128]{1,0:T(8,128)S(1)}, f32[130,128]{1,0:T(8,128)S(1)}, u32[]{:S(2)}, u32[]{:S(2)}) collective-permute-start(f32[130,128]{1,0:T(8,128)S(1)} %get-tuple-element.64), channel_id=1, source_target_pairs={{0,12},{4,0},{8,4},{12,8},{1,13},{5,1},{9,5},{13,9},{2,14},{6,2},{... | collective-permute-start | bytes 199688 | tf_op jit(solution)/shard_map/ppermute | solution.py:41
  29.8 5.2 %collective-permute-start.9 = (f32[130,128]{1,0:T(8,128)S(1)}, f32[130,128]{1,0:T(8,128)S(1)}, u32[]{:S(2)}, u32[]{:S(2)}) collective-permute-start(f32[130,128]{1,0:T(8,128)S(1)} %get-tuple-element.64), channel_id=1, source_target_pairs={{0,8},{4,12},{8,0},{12,4},{1,9},{5,13},{9,1},{13,5},{2,10},{6,14},... | collective-permute-start | bytes 199688 | tf_op jit(solution)/shard_map/ppermute | solution.py:41
  29.8 1.3 %collective-permute-start.11 = (f32[128,128]{1,0:T(8,128)S(1)}, f32[128,128]{1,0:T(8,128)S(1)}, u32[]{:S(2)}, u32[]{:S(2)}) collective-permute-start(f32[128,128]{1,0:T(8,128)S(1)} %fusion.56), channel_id=1, source_target_pairs={{0,1},{1,0},{2,3},{3,2},{4,5},{5,4},{6,7},{7,6},{8,9},{9,8},{10,11... | collective-permute-start | bytes 196616 | tf_op jit(solution)/shard_map/ppermute | solution.py:35
  31.1 7.8 %copy-start.6 = (f32[128,128]{1,0:T(8,128)}, f32[128,128]{1,0:T(8,128)S(1)}, u32[]{:S(2)}) copy-start(f32[128,128]{1,0:T(8,128)S(1)} %collective-permute-done.11) | copy-start | bytes 196612
  31.1 6.3 %collective-permute-start.12 = (f32[2,128,128]{2,1,0:T(8,128)S(1)}, f32[2,128,128]{2,1,0:T(8,128)S(1)}, u32[]{:S(2)}, u32[]{:S(2)}) collective-permute-start(f32[2,128,128]{2,1,0:T(8,128)S(1)} %pad_maximum_fusion.4), channel_id=1, source_target_pairs={{0,2},{1,3},{2,0},{3,1},{4,6},{5,7},{6,4},{7,5},{8,10},{9,11},{10,... | collective-permute-start | bytes 393224 | tf_op jit(solution)/shard_map/ppermute | solution.py:37
  35.0 0.6 copy-start.29
  35.1 2.3 %copy-start.2 = (f32[1,128,128]{2,1,0:T(8,128)}, f32[1,128,128]{2,1,0:T(8,128)S(1)}, u32[]{:S(2)}) copy-start(f32[1,128,128]{2,1,0:T(8,128)S(1)} %get-tuple-element.43) | copy-start | bytes 196612
  35.1 2.3 %copy-start.3 = (f32[1,128,128]{2,1,0:T(8,128)}, f32[1,128,128]{2,1,0:T(8,128)S(1)}, u32[]{:S(2)}) copy-start(f32[1,128,128]{2,1,0:T(8,128)S(1)} %get-tuple-element.44) | copy-start | bytes 196612
  35.1 2.3 %copy-start.4 = (f32[1,128,128]{2,1,0:T(8,128)}, f32[1,128,128]{2,1,0:T(8,128)S(1)}, u32[]{:S(2)}) copy-start(f32[1,128,128]{2,1,0:T(8,128)S(1)} %get-tuple-element.41) | copy-start | bytes 196612
  35.1 2.3 %copy-start.5 = (f32[1,128,128]{2,1,0:T(8,128)}, f32[1,128,128]{2,1,0:T(8,128)S(1)}, u32[]{:S(2)}) copy-start(f32[1,128,128]{2,1,0:T(8,128)S(1)} %get-tuple-element.42) | copy-start | bytes 196612
  35.1 3.7 %copy-start.20 = (f32[128]{0:T(128)}, f32[128]{0:T(128)S(1)}, u32[]{:S(2)}) copy-start(f32[128]{0:T(128)S(1)} %fusion.97) | copy-start | bytes 1540
  35.2 3.7 %copy-start.21 = (f32[128]{0:T(128)}, f32[128]{0:T(128)S(1)}, u32[]{:S(2)}) copy-start(f32[128]{0:T(128)S(1)} %bitcast_divide_fusion.5) | copy-start | bytes 1540
  37.4 1.5 %copy-start.8 = (f32[2,128,128]{2,1,0:T(8,128)}, f32[2,128,128]{2,1,0:T(8,128)S(1)}, u32[]{:S(2)}) copy-start(f32[2,128,128]{2,1,0:T(8,128)S(1)} %collective-permute-done.12) | copy-start | bytes 393220
  38.9 31.5 %copy-start.14 = (s32[4,128]{1,0:T(4,128)S(1)}, s32[4,128]{1,0:T(4,128)}, u32[]{:S(2)}) copy-start(s32[4,128]{1,0:T(4,128)} %copy-done.12) | copy-start | bytes 6148
  41.6 8.3 %collective-permute-start.13 = (f32[132,128]{1,0:T(8,128)}, f32[132,128]{1,0:T(8,128)}, u32[]{:S(2)}, u32[]{:S(2)}) collective-permute-start(f32[132,128]{1,0:T(8,128)} %concatenate.64), channel_id=1, source_target_pairs={{0,1},{1,2},{2,3},{3,0},{4,5},{5,6},{6,7},{7,4},{8,9},{9,10},{10,1... | collective-permute-start | bytes 202760 | tf_op jit(solution)/shard_map/ppermute | solution.py:59
  44.4 5.5 %collective-permute-start.15 = (f32[132,128]{1,0:T(8,128)}, f32[132,128]{1,0:T(8,128)}, u32[]{:S(2)}, u32[]{:S(2)}) collective-permute-start(f32[132,128]{1,0:T(8,128)} %concatenate.66), channel_id=1, source_target_pairs={{0,3},{1,0},{2,1},{3,2},{4,7},{5,4},{6,5},{7,6},{8,11},{9,8},{10,9... | collective-permute-start | bytes 202760 | tf_op jit(solution)/shard_map/ppermute | solution.py:59
  48.9 21.5 %copy-start.7 = (f32[128,128]{1,0:T(8,128)S(1)}, f32[128,128]{1,0:T(8,128)}, u32[]{:S(2)}) copy-start(f32[128,128]{1,0:T(8,128)} %copy-done.6) | copy-start | bytes 196612
  48.9 21.5 %copy-start.9 = (f32[2,128,128]{2,1,0:T(8,128)S(1)}, f32[2,128,128]{2,1,0:T(8,128)}, u32[]{:S(2)}) copy-start(f32[2,128,128]{2,1,0:T(8,128)} %copy-done.8) | copy-start | bytes 393220
  48.9 21.6 %copy-start.22 = (f32[128]{0:T(128)S(1)}, f32[128]{0:T(128)}, u32[]{:S(2)}) copy-start(f32[128]{0:T(128)} %copy-done.21) | copy-start | bytes 1540
  48.9 4.6 %collective-permute-start.14 = (f32[132,128]{1,0:T(8,128)}, f32[132,128]{1,0:T(8,128)S(1)}, u32[]{:S(2)}, u32[]{:S(2)}) collective-permute-start(f32[132,128]{1,0:T(8,128)} %concatenate.65), channel_id=1, source_target_pairs={{0,2},{1,3},{2,0},{3,1},{4,6},{5,7},{6,4},{7,5},{8,10},{9,11},{10,... | collective-permute-start | bytes 202760 | tf_op jit(solution)/shard_map/ppermute | solution.py:59
  54.5 5.1 %collective-permute-start.19 = (f32[128,128]{1,0:T(8,128)S(1)}, f32[128,128]{1,0:T(8,128)S(1)}, u32[]{:S(2)}, u32[]{:S(2)}) collective-permute-start(f32[128,128]{1,0:T(8,128)S(1)} %multiply_subtract_fusion.5), channel_id=1, source_target_pairs={{0,1},{1,0},{2,3},{3,2},{4,5},{5,4},{6,7},{7,6},{8,9},{9,8},{10,11... | collective-permute-start | bytes 196616 | tf_op jit(solution)/shard_map/ppermute | solution.py:35
  55.3 5.4 %collective-permute-start.18 = (f32[132,128]{1,0:T(8,128)S(1)}, f32[132,128]{1,0:T(8,128)S(1)}, u32[]{:S(2)}, u32[]{:S(2)}) collective-permute-start(f32[132,128]{1,0:T(8,128)S(1)} %get-tuple-element.62), channel_id=1, source_target_pairs={{0,12},{4,0},{8,4},{12,8},{1,13},{5,1},{9,5},{13,9},{2,14},{6,2},{... | collective-permute-start | bytes 202760 | tf_op jit(solution)/shard_map/ppermute | solution.py:41
  56.2 8.6 %collective-permute-start.17 = (f32[132,128]{1,0:T(8,128)S(1)}, f32[132,128]{1,0:T(8,128)S(1)}, u32[]{:S(2)}, u32[]{:S(2)}) collective-permute-start(f32[132,128]{1,0:T(8,128)S(1)} %get-tuple-element.62), channel_id=1, source_target_pairs={{0,8},{4,12},{8,0},{12,4},{1,9},{5,13},{9,1},{13,5},{2,10},{6,14},... | collective-permute-start | bytes 202760 | tf_op jit(solution)/shard_map/ppermute | solution.py:41
  57.6 7.2 %collective-permute-start.16 = (f32[132,128]{1,0:T(8,128)S(1)}, f32[132,128]{1,0:T(8,128)S(1)}, u32[]{:S(2)}, u32[]{:S(2)}) collective-permute-start(f32[132,128]{1,0:T(8,128)S(1)} %get-tuple-element.62), channel_id=1, source_target_pairs={{0,4},{4,8},{8,12},{12,0},{1,5},{5,9},{9,13},{13,1},{2,6},{6,10},{... | collective-permute-start | bytes 202760 | tf_op jit(solution)/shard_map/ppermute | solution.py:41
  59.6 10.8 %collective-permute-start.20 = (f32[2,128,128]{2,1,0:T(8,128)S(1)}, f32[2,128,128]{2,1,0:T(8,128)S(1)}, u32[]{:S(2)}, u32[]{:S(2)}) collective-permute-start(f32[2,128,128]{2,1,0:T(8,128)S(1)} %pad_maximum_fusion.5), channel_id=1, source_target_pairs={{0,2},{1,3},{2,0},{3,1},{4,6},{5,7},{6,4},{7,5},{8,10},{9,11},{10,... | collective-permute-start | bytes 393224 | tf_op jit(solution)/shard_map/ppermute | solution.py:37
  66.3 2.0 %copy-start.25 = (f32[128]{0:T(128)}, f32[128]{0:T(128)S(1)}, u32[]{:S(2)}) copy-start(f32[128]{0:T(128)S(1)} %get-tuple-element.35) | copy-start | bytes 1540
  66.3 2.0 %copy-start.27 = (f32[1,128]{1,0:T(1,128)}, f32[1,128]{1,0:T(1,128)S(1)}, u32[]{:S(2)}) copy-start(f32[1,128]{1,0:T(1,128)S(1)} %get-tuple-element.36) | copy-start | bytes 1540
  70.3 7.3 %copy-start.17 = (f32[128]{0:T(128)S(1)}, f32[128]{0:T(128)}, u32[]{:S(2)}) copy-start(f32[128]{0:T(128)} %get-tuple-element.20) | copy-start | bytes 1540
  70.3 7.3 %copy-start.18 = (f32[128]{0:T(128)S(1)}, f32[128]{0:T(128)}, u32[]{:S(2)}) copy-start(f32[128]{0:T(128)} %get-tuple-element.22) | copy-start | bytes 1540
  70.4 7.3 %copy-start.19 = (f32[128]{0:T(128)S(1)}, f32[128]{0:T(128)}, u32[]{:S(2)}) copy-start(f32[128]{0:T(128)} %get-tuple-element.23) | copy-start | bytes 1540
  70.4 13.6 %copy-start.10 = (f32[128,128]{1,0:T(8,128)S(1)}, f32[128,128]{1,0:T(8,128)}, u32[]{:S(2)}) copy-start(f32[128,128]{1,0:T(8,128)} %get-tuple-element.34) | copy-start | bytes 196612
  70.4 13.6 %copy-start.26 = (f32[128]{0:T(128)S(1)}, f32[128]{0:T(128)}, u32[]{:S(2)}) copy-start(f32[128]{0:T(128)} %copy-done.25) | copy-start | bytes 1540
  70.4 13.6 %copy-start.28 = (f32[1,128]{1,0:T(1,128)S(1)}, f32[1,128]{1,0:T(1,128)}, u32[]{:S(2)}) copy-start(f32[1,128]{1,0:T(1,128)} %copy-done.27) | copy-start | bytes 1540
  71.4 2.7 %collective-permute-start.23 = (f32[132,128]{1,0:T(8,128)S(1)}, f32[132,128]{1,0:T(8,128)S(1)}, u32[]{:S(2)}, u32[]{:S(2)}) collective-permute-start(f32[132,128]{1,0:T(8,128)S(1)} %concatenate.71), channel_id=1, source_target_pairs={{0,3},{1,0},{2,1},{3,2},{4,7},{5,4},{6,5},{7,6},{8,11},{9,8},{10,9... | collective-permute-start | bytes 202760 | tf_op jit(solution)/shard_map/ppermute | solution.py:59
  72.1 4.6 %collective-permute-start.22 = (f32[132,128]{1,0:T(8,128)S(1)}, f32[132,128]{1,0:T(8,128)S(1)}, u32[]{:S(2)}, u32[]{:S(2)}) collective-permute-start(f32[132,128]{1,0:T(8,128)S(1)} %concatenate.70), channel_id=1, source_target_pairs={{0,2},{1,3},{2,0},{3,1},{4,6},{5,7},{6,4},{7,5},{8,10},{9,11},{10,... | collective-permute-start | bytes 202760 | tf_op jit(solution)/shard_map/ppermute | solution.py:59
  73.9 3.7 %collective-permute-start.21 = (f32[132,128]{1,0:T(8,128)S(1)}, f32[132,128]{1,0:T(8,128)S(1)}, u32[]{:S(2)}, u32[]{:S(2)}) collective-permute-start(f32[132,128]{1,0:T(8,128)S(1)} %concatenate.69), channel_id=1, source_target_pairs={{0,1},{1,2},{2,3},{3,0},{4,5},{5,6},{6,7},{7,4},{8,9},{9,10},{10,1... | collective-permute-start | bytes 202760 | tf_op jit(solution)/shard_map/ppermute | solution.py:59
  77.7 5.4 %collective-permute-start.24 = (f32[4,128]{1,0:T(4,128)S(1)}, f32[4,128]{1,0:T(4,128)S(1)}, u32[]{:S(2)}, u32[]{:S(2)}) collective-permute-start(f32[4,128]{1,0:T(4,128)S(1)} %select_add_fusion.1), channel_id=1, source_target_pairs={{0,4},{4,8},{8,12},{12,0},{1,5},{5,9},{9,13},{13,1},{2,6},{6,10},{... | collective-permute-start | bytes 6152 | tf_op jit(solution)/shard_map/ppermute | solution.py:41
  77.7 5.4 %collective-permute-start.25 = (f32[4,128]{1,0:T(4,128)S(1)}, f32[4,128]{1,0:T(4,128)S(1)}, u32[]{:S(2)}, u32[]{:S(2)}) collective-permute-start(f32[4,128]{1,0:T(4,128)S(1)} %select_add_fusion.1), channel_id=1, source_target_pairs={{0,8},{4,12},{8,0},{12,4},{1,9},{5,13},{9,1},{13,5},{2,10},{6,14},... | collective-permute-start | bytes 6152 | tf_op jit(solution)/shard_map/ppermute | solution.py:41
  79.7 4.2 %collective-permute-start.26 = (f32[4,128]{1,0:T(4,128)S(1)}, f32[4,128]{1,0:T(4,128)S(1)}, u32[]{:S(2)}, u32[]{:S(2)}) collective-permute-start(f32[4,128]{1,0:T(4,128)S(1)} %select_add_fusion.1), channel_id=1, source_target_pairs={{0,12},{4,0},{8,4},{12,8},{1,13},{5,1},{9,5},{13,9},{2,14},{6,2},{... | collective-permute-start | bytes 6152 | tf_op jit(solution)/shard_map/ppermute | solution.py:41

commit v12 on v9

--- a/solution.py
+++ b/solution.py
@@ -44,6 +44,24 @@
 
 def scatter_with(blocks, extra, axis, count):
     rows = blocks.shape[1]
+    if count == 4:
+        me = lax.axis_index(axis)
+        far = jnp.stack(
+            [lax.dynamic_index_in_dim(blocks, me ^ 2, 0, keepdims=False),
+             lax.dynamic_index_in_dim(blocks, me ^ 3, 0, keepdims=False)]
+        )
+        near = jnp.stack(
+            [lax.dynamic_index_in_dim(blocks, me, 0, keepdims=False),
+             lax.dynamic_index_in_dim(blocks, me ^ 1, 0, keepdims=False)]
+        )
+        sent = jnp.concatenate([far, jnp.broadcast_to(extra[None], (2,) + extra.shape)], axis=1)
+        got = lax.ppermute(sent, axis, [(i, i ^ 2) for i in range(count)])
+        near = near + got[:, :rows]
+        pair = extra + got[0, rows:]
+        got = lax.ppermute(
+            jnp.concatenate([near[1], pair], axis=0), axis, [(i, i ^ 1) for i in range(count)]
+        )
+        return near[0] + got[:rows], pair + got[rows:]
     if count > 4:
         payload = jnp.concatenate(
             [blocks, jnp.broadcast_to(extra[None], (count,) + extra.shape)], axis=1
@@ -126,6 +144,8 @@
 
     def narrow_step(partial, partial_sums):
         weighted, extras = scatter_with(partial, partial_sums, "narrow", n_narrow)
+        if n_narrow == 4:
+            return weighted, extras
         return weighted, canonical_sum(extras, "narrow", n_narrow)
 
     def wide_step(applied, narrow_sums, last):

time: 64.5 us -> 67.9 us (1.053)
  waiting for transfers between devices: 18.2 us -> 25.2 us
  starting transfers between devices: 33.5 us -> 29.8 us
    ppermute x9 -> x6, waiting for transfers between devices: 7.81 us -> 14.8 us  [the longest x3 11.2 us: scatter_with(): got = lax.ppermute(sent, axis, [(i, i ^ 2) for i in range(count)])]
    ppermute x9 -> x6, starting transfers between devices: 7.95 us -> 4.88 us  [the longest x3 4.67 us: scatter_with(): got = lax.ppermute(sent, axis, [(i, i ^ 2) for i in range(count)])]
  transfers between devices with their start and end apart: 27 -> 24, of which waited for: 17 -> 13; matrix products, arithmetic and copies ran while one was open for 12% -> 11% of each run, Pallas kernels for 0% -> 0%
where the time goes in v12:
time: 67.9 us; the launch traced here: 67.8 us
  starting transfers between devices  29.8 us (44%)
  waiting for transfers between devices  25.2 us (37%)
  other arithmetic  7.39 us (11%)
  matrix products  3.03 us (4%)
  local copies, waits for them, and re-layouts  1.19 us (2%)
  between operations  1.18 us (2%)
    ppermute x12, starting transfers between devices, gather_blocks(): parts.append(lax.ppermute(values, axis, pairs))  19.8 us
    ppermute x3, waiting for transfers between devices, scatter_with(): got = lax.ppermute(sent, axis, [(i, i ^ 2) for i in range(count)])  11.2 us
    ppermute x12, waiting for transfers between devices, gather_blocks(): parts.append(lax.ppermute(values, axis, pairs))  9.37 us
    ppermute x3, starting transfers between devices, scatter_with(): got = lax.ppermute(sent, axis, [(i, i ^ 2) for i in range(count)])  4.67 us
    ppermute x3, starting transfers between devices, gather_blocks(): lax.ppermute(both, axis, [(i, i ^ 2) for i in range(count)])  4.66 us
    ppermute x3, waiting for transfers between devices, scatter_with(): lax.ppermute(jnp.concatenate([near[1], pair], axis=0), axis, [(i, i ^ 1)...  3.66 us
    dot_general x3, matrix products, product(): jnp.dot(transposed, row_values.reshape(groups * tile, width), precision=l...  3.03 us
    reduce_sum x1, other arithmetic, local(): column_sums = jnp.sum(dense, axis=(0, 1)).reshape(n_narrow, own_rows)  2.97 us
  transfers between devices with their start and end apart: 24, of which 13 were waited for; matrix products, arithmetic and copies ran while one was open for 11% of the time, Pallas kernels for 0%

profile of v12, /device:TPU:0, one launch (start us, length us, event | category | flops | bytes accessed | tf_op | source)
XLA Modules:
  0.0 67.8 jit_solution(11005036896878668257)
XLA Ops:
  0.6 3.1 %collective-permute-start = (s32[128]{0:T(128)}, s32[128]{0:T(128)S(1)}, u32[]{:S(2)}, u32[]{:S(2)}) collective-permute-start(s32[128]{0:T(128)} %bitcast.258), channel_id=1, source_target_pairs={{0,4},{4,8},{8,12},{12,0},{1,5},{5,9},{9,13},{13,1},{2,6},{6,10},{... | collective-permute-start | bytes 1544 | tf_op jit(solution)/shard_map/ppermute | solution.py:41
  3.7 2.6 %collective-permute-start.1 = (s32[128]{0:T(128)}, s32[128]{0:T(128)S(1)}, u32[]{:S(2)}, u32[]{:S(2)}) collective-permute-start(s32[128]{0:T(128)} %bitcast.259), channel_id=1, source_target_pairs={{0,8},{4,12},{8,0},{12,4},{1,9},{5,13},{9,1},{13,5},{2,10},{6,14},... | collective-permute-start | bytes 1544 | tf_op jit(solution)/shard_map/ppermute | solution.py:41
  6.3 1.3 %collective-permute-start.2 = (s32[128]{0:T(128)}, s32[128]{0:T(128)S(1)}, u32[]{:S(2)}, u32[]{:S(2)}) collective-permute-start(s32[128]{0:T(128)} %bitcast.260), channel_id=1, source_target_pairs={{0,12},{4,0},{8,4},{12,8},{1,13},{5,1},{9,5},{13,9},{2,14},{6,2},{... | collective-permute-start | bytes 1544 | tf_op jit(solution)/shard_map/ppermute | solution.py:41
  7.6 0.0 collective-permute-start.3
  7.7 0.7 %fusion.73 = f32[128]{0:T(128)S(1)} fusion(s32[128,1]{0,1:T(1,128)} %param.5), kind=kLoop, calls=%fused_computation.221 | loop fusion | flops 384 | bytes 1024 | tf_op jit(solution)/shard_map/mul | solution.py:177
  8.4 0.7 %add_select_fusion = s32[4,8]{1,0:T(4,128)S(1)} fusion(s32[4,8]{1,0:T(4,128)} %param.4), kind=kLoop, calls=%fused_computation.146 | loop fusion | flops 480 | bytes 256 | tf_op jit(solution)/shard_map/jit(floor_divide)/jit(_where)/select_n | solution.py:115
  9.1 0.1 iota_compare_fusion.5
  9.1 0.0 copy-start
  9.2 3.0 %select_reduce_fusion = (f32[4,128]{1,0:T(4,128)S(1)}, f32[4,128,4,128]{3,1,2,0:T(8,128)S(1)}) fusion(f32[4,8,128,128]{3,2,1,0:T(8,128)} %param.3, pred[4,8,4]{2,1,0:T(8,128)(4,1)S(1)} %iota_compare_fusion.5), kind=kLoop, calls=%fused_computation.1 | loop fusion | flops 6028800 | bytes 3147904 | tf_op jit(solution)/shard_map/reduce_sum | solution.py:120
  12.1 0.1 copy_bitcast_fusion
  12.3 0.1 broadcast_bitcast_fusion
  12.3 0.1 fusion.25
  12.5 0.6 gather_fusion
  13.1 0.1 bitcast_select_fusion
  13.3 0.3 copy.7
  13.6 1.6 %collective-permute-start.4 = (s32[2,128]{1,0:T(2,128)S(1)}, s32[2,128]{1,0:T(2,128)S(1)}, u32[]{:S(2)}, u32[]{:S(2)}) collective-permute-start(s32[2,128]{1,0:T(2,128)S(1)} %pad_add_fusion.2), channel_id=1, source_target_pairs={{0,2},{1,3},{2,0},{3,1},{4,6},{5,7},{6,4},{7,5},{8,10},{9,11},{10,... | collective-permute-start | bytes 3080 | tf_op jit(solution)/shard_map/ppermute | solution.py:37
  15.2 0.0 collective-permute-done
  15.2 1.1 %fusion.5 = f32[4,128,128]{2,1,0:T(8,128)S(1)} fusion(f32[4,128,512]{2,1,0:T(8,128)S(1)} %bitcast.230, s32[512]{0:T(512)S(1)} %get-tuple-element.60), kind=kOutput, calls=%fused_computation.22 | convolution fusion | flops 402784256 | bytes 1312768 | tf_op jit(solution)/shard_map/dot_general | solution.py:134
  16.3 1.0 %collective-permute-done.4 = s32[2,128]{1,0:T(2,128)S(1)} collective-permute-done((s32[2,128]{1,0:T(2,128)S(1)}, s32[2,128]{1,0:T(2,128)S(1)}, u32[]{:S(2)}, u32[]{:S(2)}) %collective-permute-start.4) | collective-permute-done | bytes 1056 | tf_op jit(solution)/shard_map/ppermute | solution.py:37
  17.3 0.1 fusion.8
  17.4 0.2 fusion.22
  17.7 1.6 %collective-permute-start.5 = (f32[2,131,128]{2,1,0:T(8,128)S(1)}, f32[2,131,128]{2,1,0:T(8,128)S(1)}, u32[]{:S(2)}, u32[]{:S(2)}) collective-permute-start(f32[2,131,128]{2,1,0:T(8,128)S(1)} %pad_maximum_fusion.7), channel_id=1, source_target_pairs={{0,2},{1,3},{2,0},{3,1},{4,6},{5,7},{6,4},{7,5},{8,10},{9,11},{10,... | collective-permute-start | bytes 402440 | tf_op jit(solution)/shard_map/ppermute | solution.py:58
  19.2 3.6 %collective-permute-done.5 = f32[2,131,128]{2,1,0:T(8,128)S(1)} collective-permute-done((f32[2,131,128]{2,1,0:T(8,128)S(1)}, f32[2,131,128]{2,1,0:T(8,128)S(1)}, u32[]{:S(2)}, u32[]{:S(2)}) %collective-permute-start.5) | collective-permute-done | bytes 134176 | tf_op jit(solution)/shard_map/ppermute | solution.py:58
  22.9 0.1 collective-permute-start.6
  23.0 1.2 %collective-permute-done.6 = f32[131,128]{1,0:T(8,128)S(1)} collective-permute-done((f32[131,128]{1,0:T(8,128)S(1)}, f32[131,128]{1,0:T(8,128)S(1)}, u32[]{:S(2)}, u32[]{:S(2)}) %collective-permute-start.6) | collective-permute-done | bytes 67104 | tf_op jit(solution)/shard_map/ppermute | solution.py:61
  24.2 0.1 fusion.84
  24.3 0.1 fusion.27
  24.4 0.2 collective-permute-start.10
  24.7 0.7 %collective-permute-start.7 = (f32[130,128]{1,0:T(8,128)S(1)}, f32[130,128]{1,0:T(8,128)S(1)}, u32[]{:S(2)}, u32[]{:S(2)}) collective-permute-start(f32[130,128]{1,0:T(8,128)S(1)} %get-tuple-element.57), channel_id=1, source_target_pairs={{0,4},{4,8},{8,12},{12,0},{1,5},{5,9},{9,13},{13,1},{2,6},{6,10},{... | collective-permute-start | bytes 199688 | tf_op jit(solution)/shard_map/ppermute | solution.py:41
  25.4 0.3 collective-permute-start.8
  25.7 2.8 %collective-permute-start.9 = (f32[130,128]{1,0:T(8,128)S(1)}, f32[130,128]{1,0:T(8,128)S(1)}, u32[]{:S(2)}, u32[]{:S(2)}) collective-permute-start(f32[130,128]{1,0:T(8,128)S(1)} %get-tuple-element.57), channel_id=1, source_target_pairs={{0,12},{4,0},{8,4},{12,8},{1,13},{5,1},{9,5},{13,9},{2,14},{6,2},{... | collective-permute-start | bytes 199688 | tf_op jit(solution)/shard_map/ppermute | solution.py:41
  28.6 1.6 %collective-permute-start.11 = (f32[2,128,128]{2,1,0:T(8,128)S(1)}, f32[2,128,128]{2,1,0:T(8,128)S(1)}, u32[]{:S(2)}, u32[]{:S(2)}) collective-permute-start(f32[2,128,128]{2,1,0:T(8,128)S(1)} %pad_maximum_fusion.10), channel_id=1, source_target_pairs={{0,2},{1,3},{2,0},{3,1},{4,6},{5,7},{6,4},{7,5},{8,10},{9,11},{10,... | collective-permute-start | bytes 393224 | tf_op jit(solution)/shard_map/ppermute | solution.py:37
  30.1 1.5 %collective-permute-done.7 = f32[130,128]{1,0:T(8,128)S(1)} collective-permute-done((f32[130,128]{1,0:T(8,128)S(1)}, f32[130,128]{1,0:T(8,128)S(1)}, u32[]{:S(2)}, u32[]{:S(2)}) %collective-permute-start.7) | collective-permute-done | bytes 66592 | tf_op jit(solution)/shard_map/ppermute | solution.py:41
  31.6 2.4 %collective-permute-done.8 = f32[130,128]{1,0:T(8,128)S(1)} collective-permute-done((f32[130,128]{1,0:T(8,128)S(1)}, f32[130,128]{1,0:T(8,128)S(1)}, u32[]{:S(2)}, u32[]{:S(2)}) %collective-permute-start.8) | collective-permute-done | bytes 66592 | tf_op jit(solution)/shard_map/ppermute | solution.py:41
  34.1 0.1 multiply_reduce_fusion.4
  34.2 0.2 multiply_subtract_fusion.1
  34.4 1.0 %fusion.77 = f32[4,128,128]{2,1,0:T(8,128)S(1)} fusion(f32[4,128,512]{2,1,0:T(8,128)S(1)} %bitcast.231, f32[512,128,1]{1,0,2:T(8,128)S(1)} %bitcast.237), kind=kOutput, calls=%fused_computation.225 | convolution fusion | flops 402653184 | bytes 1572864 | tf_op jit(solution)/shard_map/dot_general | solution.py:134
  35.4 0.1 fusion.38
  35.5 1.6 %collective-permute-start.12 = (f32[2,132,128]{2,1,0:T(8,128)S(1)}, f32[2,132,128]{2,1,0:T(8,128)S(1)}, u32[]{:S(2)}, u32[]{:S(2)}) collective-permute-start(f32[2,132,128]{2,1,0:T(8,128)S(1)} %pad_maximum_fusion.8), channel_id=1, source_target_pairs={{0,2},{1,3},{2,0},{3,1},{4,6},{5,7},{6,4},{7,5},{8,10},{9,11},{10,... | collective-permute-start | bytes 405512 | tf_op jit(solution)/shard_map/ppermute | solution.py:58
  37.1 3.6 %collective-permute-done.12 = f32[2,132,128]{2,1,0:T(8,128)S(1)} collective-permute-done((f32[2,132,128]{2,1,0:T(8,128)S(1)}, f32[2,132,128]{2,1,0:T(8,128)S(1)}, u32[]{:S(2)}, u32[]{:S(2)}) %collective-permute-start.12) | collective-permute-done | bytes 135200 | tf_op jit(solution)/shard_map/ppermute | solution.py:58
  40.7 0.1 collective-permute-start.13
  40.8 1.2 %collective-permute-done.13 = f32[132,128]{1,0:T(8,128)S(1)} collective-permute-done((f32[132,128]{1,0:T(8,128)S(1)}, f32[132,128]{1,0:T(8,128)S(1)}, u32[]{:S(2)}, u32[]{:S(2)}) %collective-permute-start.13) | collective-permute-done | bytes 67616 | tf_op jit(solution)/shard_map/ppermute | solution.py:61
  42.0 0.1 multiply_subtract_fusion.3
  42.2 0.2 collective-permute-start.17
  42.4 1.6 %collective-permute-start.14 = (f32[132,128]{1,0:T(8,128)S(1)}, f32[132,128]{1,0:T(8,128)S(1)}, u32[]{:S(2)}, u32[]{:S(2)}) collective-permute-start(f32[132,128]{1,0:T(8,128)S(1)} %get-tuple-element.55), channel_id=1, source_target_pairs={{0,4},{4,8},{8,12},{12,0},{1,5},{5,9},{9,13},{13,1},{2,6},{6,10},{... | collective-permute-start | bytes 202760 | tf_op jit(solution)/shard_map/ppermute | solution.py:41
  44.0 1.6 %collective-permute-start.15 = (f32[132,128]{1,0:T(8,128)S(1)}, f32[132,128]{1,0:T(8,128)S(1)}, u32[]{:S(2)}, u32[]{:S(2)}) collective-permute-start(f32[132,128]{1,0:T(8,128)S(1)} %get-tuple-element.55), channel_id=1, source_target_pairs={{0,8},{4,12},{8,0},{12,4},{1,9},{5,13},{9,1},{13,5},{2,10},{6,14},... | collective-permute-start | bytes 202760 | tf_op jit(solution)/shard_map/ppermute | solution.py:41
  45.6 1.2 %collective-permute-start.16 = (f32[132,128]{1,0:T(8,128)S(1)}, f32[132,128]{1,0:T(8,128)S(1)}, u32[]{:S(2)}, u32[]{:S(2)}) collective-permute-start(f32[132,128]{1,0:T(8,128)S(1)} %get-tuple-element.55), channel_id=1, source_target_pairs={{0,12},{4,0},{8,4},{12,8},{1,13},{5,1},{9,5},{13,9},{2,14},{6,2},{... | collective-permute-start | bytes 202760 | tf_op jit(solution)/shard_map/ppermute | solution.py:41
  46.8 1.6 %collective-permute-start.18 = (f32[2,128,128]{2,1,0:T(8,128)S(1)}, f32[2,128,128]{2,1,0:T(8,128)S(1)}, u32[]{:S(2)}, u32[]{:S(2)}) collective-permute-start(f32[2,128,128]{2,1,0:T(8,128)S(1)} %pad_maximum_fusion.11), channel_id=1, source_target_pairs={{0,2},{1,3},{2,0},{3,1},{4,6},{5,7},{6,4},{7,5},{8,10},{9,11},{10,... | collective-permute-start | bytes 393224 | tf_op jit(solution)/shard_map/ppermute | solution.py:37
  48.4 1.0 %collective-permute-done.14 = f32[132,128]{1,0:T(8,128)S(1)} collective-permute-done((f32[132,128]{1,0:T(8,128)S(1)}, f32[132,128]{1,0:T(8,128)S(1)}, u32[]{:S(2)}, u32[]{:S(2)}) %collective-permute-start.14) | collective-permute-done | bytes 67616 | tf_op jit(solution)/shard_map/ppermute | solution.py:41
  49.4 2.4 %collective-permute-done.15 = f32[132,128]{1,0:T(8,128)S(1)} collective-permute-done((f32[132,128]{1,0:T(8,128)S(1)}, f32[132,128]{1,0:T(8,128)S(1)}, u32[]{:S(2)}, u32[]{:S(2)}) %collective-permute-start.15) | collective-permute-done | bytes 67616 | tf_op jit(solution)/shard_map/ppermute | solution.py:41
  51.8 0.1 multiply_reduce_fusion.2
  52.0 0.2 fusion.2
  52.2 1.0 %fusion.78 = f32[4,128,128]{2,1,0:T(8,128)S(1)} fusion(f32[4,128,512]{2,1,0:T(8,128)S(1)} %bitcast.232, f32[512,128,1]{1,0,2:T(8,128)S(1)} %bitcast.236), kind=kOutput, calls=%fused_computation.226 | convolution fusion | flops 402653184 | bytes 1572864 | tf_op jit(solution)/shard_map/dot_general | solution.py:134
  53.2 0.1 fusion.34
  53.3 1.6 %collective-permute-start.19 = (f32[2,132,128]{2,1,0:T(8,128)S(1)}, f32[2,132,128]{2,1,0:T(8,128)S(1)}, u32[]{:S(2)}, u32[]{:S(2)}) collective-permute-start(f32[2,132,128]{2,1,0:T(8,128)S(1)} %pad_maximum_fusion.9), channel_id=1, source_target_pairs={{0,2},{1,3},{2,0},{3,1},{4,6},{5,7},{6,4},{7,5},{8,10},{9,11},{10,... | collective-permute-start | bytes 405512 | tf_op jit(solution)/shard_map/ppermute | solution.py:58
  54.9 4.0 %collective-permute-done.19 = f32[2,132,128]{2,1,0:T(8,128)S(1)} collective-permute-done((f32[2,132,128]{2,1,0:T(8,128)S(1)}, f32[2,132,128]{2,1,0:T(8,128)S(1)}, u32[]{:S(2)}, u32[]{:S(2)}) %collective-permute-start.19) | collective-permute-done | bytes 135200 | tf_op jit(solution)/shard_map/ppermute | solution.py:58
  59.0 0.1 collective-permute-start.20
  59.1 1.2 %collective-permute-done.20 = f32[132,128]{1,0:T(8,128)S(1)} collective-permute-done((f32[132,128]{1,0:T(8,128)S(1)}, f32[132,128]{1,0:T(8,128)S(1)}, u32[]{:S(2)}, u32[]{:S(2)}) %collective-permute-start.20) | collective-permute-done | bytes 67616 | tf_op jit(solution)/shard_map/ppermute | solution.py:61
  60.3 2.1 %collective-permute-start.21 = (f32[4,128]{1,0:T(4,128)S(1)}, f32[4,128]{1,0:T(4,128)S(1)}, u32[]{:S(2)}, u32[]{:S(2)}) collective-permute-start(f32[4,128]{1,0:T(4,128)S(1)} %slice_add_fusion.6), channel_id=1, source_target_pairs={{0,4},{4,8},{8,12},{12,0},{1,5},{5,9},{9,13},{13,1},{2,6},{6,10},{... | collective-permute-start | bytes 6152 | tf_op jit(solution)/shard_map/ppermute | solution.py:41
  62.4 0.9 %collective-permute-start.22 = (f32[4,128]{1,0:T(4,128)S(1)}, f32[4,128]{1,0:T(4,128)S(1)}, u32[]{:S(2)}, u32[]{:S(2)}) collective-permute-start(f32[4,128]{1,0:T(4,128)S(1)} %slice_add_fusion.6), channel_id=1, source_target_pairs={{0,8},{4,12},{8,0},{12,4},{1,9},{5,13},{9,1},{13,5},{2,10},{6,14},... | collective-permute-start | bytes 6152 | tf_op jit(solution)/shard_map/ppermute | solution.py:41
  63.3 1.5 %collective-permute-start.23 = (f32[4,128]{1,0:T(4,128)S(1)}, f32[4,128]{1,0:T(4,128)S(1)}, u32[]{:S(2)}, u32[]{:S(2)}) collective-permute-start(f32[4,128]{1,0:T(4,128)S(1)} %slice_add_fusion.6), channel_id=1, source_target_pairs={{0,12},{4,0},{8,4},{12,8},{1,13},{5,1},{9,5},{13,9},{2,14},{6,2},{... | collective-permute-start | bytes 6152 | tf_op jit(solution)/shard_map/ppermute | solution.py:41
  64.9 0.9 %collective-permute-done.21 = f32[4,128]{1,0:T(4,128)S(1)} collective-permute-done((f32[4,128]{1,0:T(4,128)S(1)}, f32[4,128]{1,0:T(4,128)S(1)}, u32[]{:S(2)}, u32[]{:S(2)}) %collective-permute-start.21) | collective-permute-done | bytes 2080 | tf_op jit(solution)/shard_map/ppermute | solution.py:41
  65.8 1.2 %collective-permute-done.22 = f32[4,128]{1,0:T(4,128)S(1)} collective-permute-done((f32[4,128]{1,0:T(4,128)S(1)}, f32[4,128]{1,0:T(4,128)S(1)}, u32[]{:S(2)}, u32[]{:S(2)}) %collective-permute-start.22) | collective-permute-done | bytes 2080 | tf_op jit(solution)/shard_map/ppermute | solution.py:41
  67.0 0.8 %fusion.20 = (f32[128,128]{1,0:T(8,128)}, f32[128,128]{1,0:T(8,128)}) fusion(f32[132,128]{1,0:T(8,128)S(1)} %collective-permute-done.20, f32[2,128,128]{2,1,0:T(8,128)S(1)} %slice_add_fusion.1, f32[128,128]{1,0:T(8,128)S(1)} %get-tuple-element.42, f32[128]{0:T(128)S(1)} %bitcast.296, f32[128]{0:T(128)S(1)} %get-tuple-element.34, f32[128]{0:T(128)S(1)} %fusion.61, ...), kind=kLoop, calls=%fused_computation.78 | loop fusion | flops 393216 | bytes 396800 | tf_op jit(solution)/shard_map/sub | solution.py:190
  (60 shorter events, 0.6 us)
Async XLA Ops:
  0.6 14.6 %collective-permute-start = (s32[128]{0:T(128)}, s32[128]{0:T(128)S(1)}, u32[]{:S(2)}, u32[]{:S(2)}) collective-permute-start(s32[128]{0:T(128)} %bitcast.258), channel_id=1, source_target_pairs={{0,4},{4,8},{8,12},{12,0},{1,5},{5,9},{9,13},{13,1},{2,6},{6,10},{... | collective-permute-start | bytes 1544 | tf_op jit(solution)/shard_map/ppermute | solution.py:41
  3.7 11.5 %collective-permute-start.1 = (s32[128]{0:T(128)}, s32[128]{0:T(128)S(1)}, u32[]{:S(2)}, u32[]{:S(2)}) collective-permute-start(s32[128]{0:T(128)} %bitcast.259), channel_id=1, source_target_pairs={{0,8},{4,12},{8,0},{12,4},{1,9},{5,13},{9,1},{13,5},{2,10},{6,14},... | collective-permute-start | bytes 1544 | tf_op jit(solution)/shard_map/ppermute | solution.py:41
  6.3 8.9 %collective-permute-start.2 = (s32[128]{0:T(128)}, s32[128]{0:T(128)S(1)}, u32[]{:S(2)}, u32[]{:S(2)}) collective-permute-start(s32[128]{0:T(128)} %bitcast.260), channel_id=1, source_target_pairs={{0,12},{4,0},{8,4},{12,8},{1,13},{5,1},{9,5},{13,9},{2,14},{6,2},{... | collective-permute-start | bytes 1544 | tf_op jit(solution)/shard_map/ppermute | solution.py:41
  7.6 6.0 %collective-permute-start.3 = (s32[128]{0:T(128)}, s32[128]{0:T(128)S(1)}, u32[]{:S(2)}, u32[]{:S(2)}) collective-permute-start(s32[128]{0:T(128)} %bitcast.261), channel_id=1, source_target_pairs={{0,1},{1,0},{2,3},{3,2},{4,5},{5,4},{6,7},{7,6},{8,9},{9,8},{10,11... | collective-permute-start | bytes 1544 | tf_op jit(solution)/shard_map/ppermute | solution.py:35
  9.1 3.2 %copy-start = (s32[128,1]{0,1:T(1,128)S(1)}, s32[128,1]{0,1:T(1,128)}, u32[]{:S(2)}) copy-start(s32[128,1]{0,1:T(1,128)} %param.5) | copy-start | bytes 1540
  13.6 3.6 %collective-permute-start.4 = (s32[2,128]{1,0:T(2,128)S(1)}, s32[2,128]{1,0:T(2,128)S(1)}, u32[]{:S(2)}, u32[]{:S(2)}) collective-permute-start(s32[2,128]{1,0:T(2,128)S(1)} %pad_add_fusion.2), channel_id=1, source_target_pairs={{0,2},{1,3},{2,0},{3,1},{4,6},{5,7},{6,4},{7,5},{8,10},{9,11},{10,... | collective-permute-start | bytes 3080 | tf_op jit(solution)/shard_map/ppermute | solution.py:37
  17.7 5.1 %collective-permute-start.5 = (f32[2,131,128]{2,1,0:T(8,128)S(1)}, f32[2,131,128]{2,1,0:T(8,128)S(1)}, u32[]{:S(2)}, u32[]{:S(2)}) collective-permute-start(f32[2,131,128]{2,1,0:T(8,128)S(1)} %pad_maximum_fusion.7), channel_id=1, source_target_pairs={{0,2},{1,3},{2,0},{3,1},{4,6},{5,7},{6,4},{7,5},{8,10},{9,11},{10,... | collective-permute-start | bytes 402440 | tf_op jit(solution)/shard_map/ppermute | solution.py:58
  22.9 1.3 %collective-permute-start.6 = (f32[131,128]{1,0:T(8,128)S(1)}, f32[131,128]{1,0:T(8,128)S(1)}, u32[]{:S(2)}, u32[]{:S(2)}) collective-permute-start(f32[131,128]{1,0:T(8,128)S(1)} %pad_maximum_fusion.12), channel_id=1, source_target_pairs={{0,1},{1,0},{2,3},{3,2},{4,5},{5,4},{6,7},{7,6},{8,9},{9,8},{10,11... | collective-permute-start | bytes 201224 | tf_op jit(solution)/shard_map/ppermute | solution.py:61
  24.4 4.1 %collective-permute-start.10 = (f32[128,128]{1,0:T(8,128)S(1)}, f32[128,128]{1,0:T(8,128)S(1)}, u32[]{:S(2)}, u32[]{:S(2)}) collective-permute-start(f32[128,128]{1,0:T(8,128)S(1)} %fusion.27), channel_id=1, source_target_pairs={{0,1},{1,0},{2,3},{3,2},{4,5},{5,4},{6,7},{7,6},{8,9},{9,8},{10,11... | collective-permute-start | bytes 196616 | tf_op jit(solution)/shard_map/ppermute | solution.py:35
  24.7 7.0 %collective-permute-start.7 = (f32[130,128]{1,0:T(8,128)S(1)}, f32[130,128]{1,0:T(8,128)S(1)}, u32[]{:S(2)}, u32[]{:S(2)}) collective-permute-start(f32[130,128]{1,0:T(8,128)S(1)} %get-tuple-element.57), channel_id=1, source_target_pairs={{0,4},{4,8},{8,12},{12,0},{1,5},{5,9},{9,13},{13,1},{2,6},{6,10},{... | collective-permute-start | bytes 199688 | tf_op jit(solution)/shard_map/ppermute | solution.py:41
  25.4 8.6 %collective-permute-start.8 = (f32[130,128]{1,0:T(8,128)S(1)}, f32[130,128]{1,0:T(8,128)S(1)}, u32[]{:S(2)}, u32[]{:S(2)}) collective-permute-start(f32[130,128]{1,0:T(8,128)S(1)} %get-tuple-element.57), channel_id=1, source_target_pairs={{0,8},{4,12},{8,0},{12,4},{1,9},{5,13},{9,1},{13,5},{2,10},{6,14},... | collective-permute-start | bytes 199688 | tf_op jit(solution)/shard_map/ppermute | solution.py:41
  25.7 8.3 %collective-permute-start.9 = (f32[130,128]{1,0:T(8,128)S(1)}, f32[130,128]{1,0:T(8,128)S(1)}, u32[]{:S(2)}, u32[]{:S(2)}) collective-permute-start(f32[130,128]{1,0:T(8,128)S(1)} %get-tuple-element.57), channel_id=1, source_target_pairs={{0,12},{4,0},{8,4},{12,8},{1,13},{5,1},{9,5},{13,9},{2,14},{6,2},{... | collective-permute-start | bytes 199688 | tf_op jit(solution)/shard_map/ppermute | solution.py:41
  28.6 5.6 %collective-permute-start.11 = (f32[2,128,128]{2,1,0:T(8,128)S(1)}, f32[2,128,128]{2,1,0:T(8,128)S(1)}, u32[]{:S(2)}, u32[]{:S(2)}) collective-permute-start(f32[2,128,128]{2,1,0:T(8,128)S(1)} %pad_maximum_fusion.10), channel_id=1, source_target_pairs={{0,2},{1,3},{2,0},{3,1},{4,6},{5,7},{6,4},{7,5},{8,10},{9,11},{10,... | collective-permute-start | bytes 393224 | tf_op jit(solution)/shard_map/ppermute | solution.py:37
  35.5 5.1 %collective-permute-start.12 = (f32[2,132,128]{2,1,0:T(8,128)S(1)}, f32[2,132,128]{2,1,0:T(8,128)S(1)}, u32[]{:S(2)}, u32[]{:S(2)}) collective-permute-start(f32[2,132,128]{2,1,0:T(8,128)S(1)} %pad_maximum_fusion.8), channel_id=1, source_target_pairs={{0,2},{1,3},{2,0},{3,1},{4,6},{5,7},{6,4},{7,5},{8,10},{9,11},{10,... | collective-permute-start | bytes 405512 | tf_op jit(solution)/shard_map/ppermute | solution.py:58
  40.7 1.3 %collective-permute-start.13 = (f32[132,128]{1,0:T(8,128)S(1)}, f32[132,128]{1,0:T(8,128)S(1)}, u32[]{:S(2)}, u32[]{:S(2)}) collective-permute-start(f32[132,128]{1,0:T(8,128)S(1)} %pad_maximum_fusion.14), channel_id=1, source_target_pairs={{0,1},{1,0},{2,3},{3,2},{4,5},{5,4},{6,7},{7,6},{8,9},{9,8},{10,11... | collective-permute-start | bytes 202760 | tf_op jit(solution)/shard_map/ppermute | solution.py:61
  42.2 4.6 %collective-permute-start.17 = (f32[128,128]{1,0:T(8,128)S(1)}, f32[128,128]{1,0:T(8,128)S(1)}, u32[]{:S(2)}, u32[]{:S(2)}) collective-permute-start(f32[128,128]{1,0:T(8,128)S(1)} %multiply_subtract_fusion.3), channel_id=1, source_target_pairs={{0,1},{1,0},{2,3},{3,2},{4,5},{5,4},{6,7},{7,6},{8,9},{9,8},{10,11... | collective-permute-start | bytes 196616 | tf_op jit(solution)/shard_map/ppermute | solution.py:35
  42.4 6.9 %collective-permute-start.14 = (f32[132,128]{1,0:T(8,128)S(1)}, f32[132,128]{1,0:T(8,128)S(1)}, u32[]{:S(2)}, u32[]{:S(2)}) collective-permute-start(f32[132,128]{1,0:T(8,128)S(1)} %get-tuple-element.55), channel_id=1, source_target_pairs={{0,4},{4,8},{8,12},{12,0},{1,5},{5,9},{9,13},{13,1},{2,6},{6,10},{... | collective-permute-start | bytes 202760 | tf_op jit(solution)/shard_map/ppermute | solution.py:41
  44.0 7.8 %collective-permute-start.15 = (f32[132,128]{1,0:T(8,128)S(1)}, f32[132,128]{1,0:T(8,128)S(1)}, u32[]{:S(2)}, u32[]{:S(2)}) collective-permute-start(f32[132,128]{1,0:T(8,128)S(1)} %get-tuple-element.55), channel_id=1, source_target_pairs={{0,8},{4,12},{8,0},{12,4},{1,9},{5,13},{9,1},{13,5},{2,10},{6,14},... | collective-permute-start | bytes 202760 | tf_op jit(solution)/shard_map/ppermute | solution.py:41
  45.6 6.2 %collective-permute-start.16 = (f32[132,128]{1,0:T(8,128)S(1)}, f32[132,128]{1,0:T(8,128)S(1)}, u32[]{:S(2)}, u32[]{:S(2)}) collective-permute-start(f32[132,128]{1,0:T(8,128)S(1)} %get-tuple-element.55), channel_id=1, source_target_pairs={{0,12},{4,0},{8,4},{12,8},{1,13},{5,1},{9,5},{13,9},{2,14},{6,2},{... | collective-permute-start | bytes 202760 | tf_op jit(solution)/shard_map/ppermute | solution.py:41
  46.8 5.1 %collective-permute-start.18 = (f32[2,128,128]{2,1,0:T(8,128)S(1)}, f32[2,128,128]{2,1,0:T(8,128)S(1)}, u32[]{:S(2)}, u32[]{:S(2)}) collective-permute-start(f32[2,128,128]{2,1,0:T(8,128)S(1)} %pad_maximum_fusion.11), channel_id=1, source_target_pairs={{0,2},{1,3},{2,0},{3,1},{4,6},{5,7},{6,4},{7,5},{8,10},{9,11},{10,... | collective-permute-start | bytes 393224 | tf_op jit(solution)/shard_map/ppermute | solution.py:37
  53.3 5.6 %collective-permute-start.19 = (f32[2,132,128]{2,1,0:T(8,128)S(1)}, f32[2,132,128]{2,1,0:T(8,128)S(1)}, u32[]{:S(2)}, u32[]{:S(2)}) collective-permute-start(f32[2,132,128]{2,1,0:T(8,128)S(1)} %pad_maximum_fusion.9), channel_id=1, source_target_pairs={{0,2},{1,3},{2,0},{3,1},{4,6},{5,7},{6,4},{7,5},{8,10},{9,11},{10,... | collective-permute-start | bytes 405512 | tf_op jit(solution)/shard_map/ppermute | solution.py:58
  59.0 1.3 %collective-permute-start.20 = (f32[132,128]{1,0:T(8,128)S(1)}, f32[132,128]{1,0:T(8,128)S(1)}, u32[]{:S(2)}, u32[]{:S(2)}) collective-permute-start(f32[132,128]{1,0:T(8,128)S(1)} %pad_maximum_fusion.16), channel_id=1, source_target_pairs={{0,1},{1,0},{2,3},{3,2},{4,5},{5,4},{6,7},{7,6},{8,9},{9,8},{10,11... | collective-permute-start | bytes 202760 | tf_op jit(solution)/shard_map/ppermute | solution.py:61
  60.3 5.4 %collective-permute-start.21 = (f32[4,128]{1,0:T(4,128)S(1)}, f32[4,128]{1,0:T(4,128)S(1)}, u32[]{:S(2)}, u32[]{:S(2)}) collective-permute-start(f32[4,128]{1,0:T(4,128)S(1)} %slice_add_fusion.6), channel_id=1, source_target_pairs={{0,4},{4,8},{8,12},{12,0},{1,5},{5,9},{9,13},{13,1},{2,6},{6,10},{... | collective-permute-start | bytes 6152 | tf_op jit(solution)/shard_map/ppermute | solution.py:41
  62.4 4.5 %collective-permute-start.22 = (f32[4,128]{1,0:T(4,128)S(1)}, f32[4,128]{1,0:T(4,128)S(1)}, u32[]{:S(2)}, u32[]{:S(2)}) collective-permute-start(f32[4,128]{1,0:T(4,128)S(1)} %slice_add_fusion.6), channel_id=1, source_target_pairs={{0,8},{4,12},{8,0},{12,4},{1,9},{5,13},{9,1},{13,5},{2,10},{6,14},... | collective-permute-start | bytes 6152 | tf_op jit(solution)/shard_map/ppermute | solution.py:41
  63.3 3.6 %collective-permute-start.23 = (f32[4,128]{1,0:T(4,128)S(1)}, f32[4,128]{1,0:T(4,128)S(1)}, u32[]{:S(2)}, u32[]{:S(2)}) collective-permute-start(f32[4,128]{1,0:T(4,128)S(1)} %slice_add_fusion.6), channel_id=1, source_target_pairs={{0,12},{4,0},{8,4},{12,8},{1,13},{5,1},{9,5},{13,9},{2,14},{6,2},{... | collective-permute-start | bytes 6152 | tf_op jit(solution)/shard_map/ppermute | solution.py:41

commit v13 on v9

--- a/solution.py
+++ b/solution.py
@@ -105,6 +105,7 @@
     transposed = dense.reshape(groups * tile, column_blocks * tile).T
 
     labels = seed_label[:, 0]
+    sent_labels = labels + (column_sums[0, 0] < 0).astype(labels.dtype)
     seeded = (labels < SEED_CLASSES).astype(jnp.float32)
     fixed_column = (SEED_WEIGHT * seeded + PRIOR)[:, None]
     classes = jnp.arange(SEED_CLASSES, dtype=jnp.int32)
@@ -140,8 +141,8 @@
     solution = jnp.zeros_like(rhs)
     residual = rhs
     direction = rhs
-    rows_residual = indicator(gather_blocks(labels, "wide", n_wide))
-    columns_residual = indicator(gather_blocks(labels, "narrow", n_narrow))
+    rows_residual = indicator(gather_blocks(sent_labels, "wide", n_wide))
+    columns_residual = indicator(gather_blocks(sent_labels, "narrow", n_narrow))
     partial, quad = product(rows_residual, columns_residual)
     degree_part = jnp.zeros((width,), jnp.float32)
     for entry in range(n_narrow):

time: 64.5 us -> 65.4 us (1.014)
  waiting for transfers between devices: 18.2 us -> 19.1 us
  other arithmetic: 7.31 us -> 6.61 us
  between operations: 1.01 us -> 1.7 us
    mul x1, other arithmetic: 0.68 us -> 0.01 us  [local(): fixed_column * direction * direction]
  transfers between devices with their start and end apart: 27 -> 27, of which waited for: 17 -> 16; matrix products, arithmetic and copies ran while one was open for 12% -> 5% of each run, Pallas kernels for 0% -> 0%
where the time goes in v13:
time: 65.4 us; the launch traced here: 65.2 us
  starting transfers between devices  32.9 us (50%)
  waiting for transfers between devices  19.1 us (29%)
  other arithmetic  6.61 us (10%)
  matrix products  3.03 us (5%)
  local copies, waits for them, and re-layouts  1.85 us (3%)
  between operations  1.7 us (3%)
    ppermute x12, starting transfers between devices, gather_blocks(): parts.append(lax.ppermute(values, axis, pairs))  19.8 us
    ppermute x12, waiting for transfers between devices, gather_blocks(): parts.append(lax.ppermute(values, axis, pairs))  9.75 us
    ppermute x9, waiting for transfers between devices, scatter_with(): got = lax.ppermute(jnp.concatenate([sent, extra], axis=0), axis, pairs)  8.29 us
    ppermute x9, starting transfers between devices, scatter_with(): got = lax.ppermute(jnp.concatenate([sent, extra], axis=0), axis, pairs)  7.62 us
    ppermute x3, starting transfers between devices, gather_blocks(): lax.ppermute(both, axis, [(i, i ^ 2) for i in range(count)])  4.46 us
    dot_general x3, matrix products, product(): jnp.dot(transposed, row_values.reshape(groups * tile, width), precision=l...  3.03 us
    reduce_sum x1, other arithmetic, local(): column_sums = jnp.sum(dense, axis=(0, 1)).reshape(n_narrow, own_rows)  2.94 us
  transfers between devices with their start and end apart: 27, of which 16 were waited for; matrix products, arithmetic and copies ran while one was open for 5% of the time, Pallas kernels for 0%

profile of v13, /device:TPU:0, one launch (start us, length us, event | category | flops | bytes accessed | tf_op | source)
XLA Modules:
  0.0 65.2 jit_solution(17988650423771113422)
XLA Ops:
  0.6 0.7 %add_select_fusion = s32[4,8]{1,0:T(4,128)S(1)} fusion(s32[4,8]{1,0:T(4,128)} %param.4), kind=kLoop, calls=%fused_computation.147 | loop fusion | flops 480 | bytes 256 | tf_op jit(solution)/shard_map/jit(floor_divide)/jit(_where)/select_n | solution.py:97
  1.3 0.1 iota_compare_fusion.5
  1.4 2.9 %select_reduce_fusion = (f32[4,128]{1,0:T(4,128)S(1)}, f32[4,128,4,128]{3,1,2,0:T(8,128)S(1)}) fusion(f32[4,8,128,128]{3,2,1,0:T(8,128)} %param.3, pred[4,8,4]{2,1,0:T(8,128)(4,1)S(1)} %iota_compare_fusion.5), kind=kLoop, calls=%fused_computation.1 | loop fusion | flops 6028800 | bytes 3147904 | tf_op jit(solution)/shard_map/reduce_sum | solution.py:102
  4.4 0.5 slice.209
  5.5 5.1 %collective-permute-start.2 = (s32[128]{0:T(128)S(1)}, s32[128]{0:T(128)S(1)}, u32[]{:S(2)}, u32[]{:S(2)}) collective-permute-start(s32[128]{0:T(128)S(1)} %broadcast_add_fusion), channel_id=1, source_target_pairs={{0,12},{4,0},{8,4},{12,8},{1,13},{5,1},{9,5},{13,9},{2,14},{6,2},{... | collective-permute-start | bytes 1544 | tf_op jit(solution)/shard_map/ppermute | solution.py:41
  10.7 1.0 %collective-permute-start.1 = (s32[128]{0:T(128)S(1)}, s32[128]{0:T(128)S(1)}, u32[]{:S(2)}, u32[]{:S(2)}) collective-permute-start(s32[128]{0:T(128)S(1)} %broadcast_add_fusion), channel_id=1, source_target_pairs={{0,8},{4,12},{8,0},{12,4},{1,9},{5,13},{9,1},{13,5},{2,10},{6,14},... | collective-permute-start | bytes 1544 | tf_op jit(solution)/shard_map/ppermute | solution.py:41
  11.7 0.1 copy_bitcast_fusion
  11.9 0.1 broadcast_bitcast_fusion
  12.0 0.6 gather_fusion
  12.6 0.1 bitcast_select_fusion
  12.7 0.1 fusion.32
  12.9 0.3 copy.7
  13.3 1.6 %collective-permute-start.4 = (s32[2,128]{1,0:T(2,128)S(1)}, s32[2,128]{1,0:T(2,128)S(1)}, u32[]{:S(2)}, u32[]{:S(2)}) collective-permute-start(s32[2,128]{1,0:T(2,128)S(1)} %pad_add_fusion.2), channel_id=1, source_target_pairs={{0,2},{1,3},{2,0},{3,1},{4,6},{5,7},{6,4},{7,5},{8,10},{9,11},{10,... | collective-permute-start | bytes 3080 | tf_op jit(solution)/shard_map/ppermute | solution.py:37
  14.8 1.2 %collective-permute-done = s32[128]{0:T(128)S(1)} collective-permute-done((s32[128]{0:T(128)S(1)}, s32[128]{0:T(128)S(1)}, u32[]{:S(2)}, u32[]{:S(2)}) %collective-permute-start) | collective-permute-done | bytes 544 | tf_op jit(solution)/shard_map/ppermute | solution.py:41
  16.0 1.1 %fusion.5 = f32[4,128,128]{2,1,0:T(8,128)S(1)} fusion(f32[4,128,512]{2,1,0:T(8,128)S(1)} %bitcast.241, s32[512]{0:T(512)S(1)} %get-tuple-element.61), kind=kOutput, calls=%fused_computation.22 | convolution fusion | flops 402784256 | bytes 1312768 | tf_op jit(solution)/shard_map/dot_general | solution.py:117
  17.1 0.1 fusion.8
  17.3 0.2 fusion.29
  17.5 0.1 collective-permute-start.5
  17.5 1.6 %collective-permute-start.6 = (f32[131,128]{1,0:T(8,128)S(1)}, f32[131,128]{1,0:T(8,128)S(1)}, u32[]{:S(2)}, u32[]{:S(2)}) collective-permute-start(f32[131,128]{1,0:T(8,128)S(1)} %get-tuple-element.69), channel_id=1, source_target_pairs={{0,2},{1,3},{2,0},{3,1},{4,6},{5,7},{6,4},{7,5},{8,10},{9,11},{10,... | collective-permute-start | bytes 201224 | tf_op jit(solution)/shard_map/ppermute | solution.py:59
  19.1 1.4 %collective-permute-start.7 = (f32[131,128]{1,0:T(8,128)S(1)}, f32[131,128]{1,0:T(8,128)S(1)}, u32[]{:S(2)}, u32[]{:S(2)}) collective-permute-start(f32[131,128]{1,0:T(8,128)S(1)} %get-tuple-element.70), channel_id=1, source_target_pairs={{0,3},{1,0},{2,1},{3,2},{4,7},{5,4},{6,5},{7,6},{8,11},{9,8},{10,9... | collective-permute-start | bytes 201224 | tf_op jit(solution)/shard_map/ppermute | solution.py:59
  20.5 0.9 %collective-permute-done.5 = f32[131,128]{1,0:T(8,128)S(1)} collective-permute-done((f32[131,128]{1,0:T(8,128)S(1)}, f32[131,128]{1,0:T(8,128)S(1)}, u32[]{:S(2)}, u32[]{:S(2)}) %collective-permute-start.5) | collective-permute-done | bytes 67104 | tf_op jit(solution)/shard_map/ppermute | solution.py:59
  21.4 0.9 %collective-permute-done.6 = f32[131,128]{1,0:T(8,128)S(1)} collective-permute-done((f32[131,128]{1,0:T(8,128)S(1)}, f32[131,128]{1,0:T(8,128)S(1)}, u32[]{:S(2)}, u32[]{:S(2)}) %collective-permute-start.6) | collective-permute-done | bytes 67104 | tf_op jit(solution)/shard_map/ppermute | solution.py:59
  22.4 0.2 collective-permute-done.7
  22.6 0.1 fusion.90
  22.7 0.1 fusion.34
  22.8 0.9 %collective-permute-start.11 = (f32[128,128]{1,0:T(8,128)S(1)}, f32[128,128]{1,0:T(8,128)S(1)}, u32[]{:S(2)}, u32[]{:S(2)}) collective-permute-start(f32[128,128]{1,0:T(8,128)S(1)} %fusion.34), channel_id=1, source_target_pairs={{0,1},{1,0},{2,3},{3,2},{4,5},{5,4},{6,7},{7,6},{8,9},{9,8},{10,11... | collective-permute-start | bytes 196616 | tf_op jit(solution)/shard_map/ppermute | solution.py:35
  23.7 3.2 %collective-permute-start.8 = (f32[130,128]{1,0:T(8,128)S(1)}, f32[130,128]{1,0:T(8,128)S(1)}, u32[]{:S(2)}, u32[]{:S(2)}) collective-permute-start(f32[130,128]{1,0:T(8,128)S(1)} %get-tuple-element.58), channel_id=1, source_target_pairs={{0,4},{4,8},{8,12},{12,0},{1,5},{5,9},{9,13},{13,1},{2,6},{6,10},{... | collective-permute-start | bytes 199688 | tf_op jit(solution)/shard_map/ppermute | solution.py:41
  26.9 0.3 collective-permute-start.9
  27.2 2.1 %collective-permute-start.10 = (f32[130,128]{1,0:T(8,128)S(1)}, f32[130,128]{1,0:T(8,128)S(1)}, u32[]{:S(2)}, u32[]{:S(2)}) collective-permute-start(f32[130,128]{1,0:T(8,128)S(1)} %get-tuple-element.58), channel_id=1, source_target_pairs={{0,12},{4,0},{8,4},{12,8},{1,13},{5,1},{9,5},{13,9},{2,14},{6,2},{... | collective-permute-start | bytes 199688 | tf_op jit(solution)/shard_map/ppermute | solution.py:41
  29.4 1.6 %collective-permute-start.12 = (f32[2,128,128]{2,1,0:T(8,128)S(1)}, f32[2,128,128]{2,1,0:T(8,128)S(1)}, u32[]{:S(2)}, u32[]{:S(2)}) collective-permute-start(f32[2,128,128]{2,1,0:T(8,128)S(1)} %pad_maximum_fusion.7), channel_id=1, source_target_pairs={{0,2},{1,3},{2,0},{3,1},{4,6},{5,7},{6,4},{7,5},{8,10},{9,11},{10,... | collective-permute-start | bytes 393224 | tf_op jit(solution)/shard_map/ppermute | solution.py:37
  30.9 2.2 %collective-permute-done.9 = f32[130,128]{1,0:T(8,128)S(1)} collective-permute-done((f32[130,128]{1,0:T(8,128)S(1)}, f32[130,128]{1,0:T(8,128)S(1)}, u32[]{:S(2)}, u32[]{:S(2)}) %collective-permute-start.9) | collective-permute-done | bytes 66592 | tf_op jit(solution)/shard_map/ppermute | solution.py:41
  33.2 0.1 multiply_reduce_fusion.3
  33.3 1.1 %collective-permute-done.12 = f32[2,128,128]{2,1,0:T(8,128)S(1)} collective-permute-done((f32[2,128,128]{2,1,0:T(8,128)S(1)}, f32[2,128,128]{2,1,0:T(8,128)S(1)}, u32[]{:S(2)}, u32[]{:S(2)}) %collective-permute-start.12) | collective-permute-done | bytes 131104 | tf_op jit(solution)/shard_map/ppermute | solution.py:37
  34.4 0.2 multiply_subtract_fusion.1
  34.6 1.0 %fusion.83 = f32[4,128,128]{2,1,0:T(8,128)S(1)} fusion(f32[4,128,512]{2,1,0:T(8,128)S(1)} %bitcast.242, f32[512,128,1]{1,0,2:T(8,128)S(1)} %bitcast.248), kind=kOutput, calls=%fused_computation.222 | convolution fusion | flops 402653184 | bytes 1572864 | tf_op jit(solution)/shard_map/dot_general | solution.py:117
  35.7 1.6 %collective-permute-start.14 = (f32[132,128]{1,0:T(8,128)S(1)}, f32[132,128]{1,0:T(8,128)S(1)}, u32[]{:S(2)}, u32[]{:S(2)}) collective-permute-start(f32[132,128]{1,0:T(8,128)S(1)} %concatenate.65), channel_id=1, source_target_pairs={{0,2},{1,3},{2,0},{3,1},{4,6},{5,7},{6,4},{7,5},{8,10},{9,11},{10,... | collective-permute-start | bytes 202760 | tf_op jit(solution)/shard_map/ppermute | solution.py:59
  37.3 0.0 collective-permute-start.15
  37.4 0.5 collective-permute-start.13
  37.9 2.2 %collective-permute-done.14 = f32[132,128]{1,0:T(8,128)S(1)} collective-permute-done((f32[132,128]{1,0:T(8,128)S(1)}, f32[132,128]{1,0:T(8,128)S(1)}, u32[]{:S(2)}, u32[]{:S(2)}) %collective-permute-start.14) | collective-permute-done | bytes 67616 | tf_op jit(solution)/shard_map/ppermute | solution.py:59
  40.1 0.5 collective-permute-done.15
  40.6 1.0 %collective-permute-done.13 = f32[132,128]{1,0:T(8,128)S(1)} collective-permute-done((f32[132,128]{1,0:T(8,128)S(1)}, f32[132,128]{1,0:T(8,128)S(1)}, u32[]{:S(2)}, u32[]{:S(2)}) %collective-permute-start.13) | collective-permute-done | bytes 67616 | tf_op jit(solution)/shard_map/ppermute | solution.py:59
  41.6 0.1 multiply_subtract_fusion.3
  41.7 0.1 collective-permute-start.19
  41.8 0.8 %collective-permute-start.16 = (f32[132,128]{1,0:T(8,128)S(1)}, f32[132,128]{1,0:T(8,128)S(1)}, u32[]{:S(2)}, u32[]{:S(2)}) collective-permute-start(f32[132,128]{1,0:T(8,128)S(1)} %get-tuple-element.56), channel_id=1, source_target_pairs={{0,4},{4,8},{8,12},{12,0},{1,5},{5,9},{9,13},{13,1},{2,6},{6,10},{... | collective-permute-start | bytes 202760 | tf_op jit(solution)/shard_map/ppermute | solution.py:41
  42.7 1.7 %collective-permute-start.17 = (f32[132,128]{1,0:T(8,128)S(1)}, f32[132,128]{1,0:T(8,128)S(1)}, u32[]{:S(2)}, u32[]{:S(2)}) collective-permute-start(f32[132,128]{1,0:T(8,128)S(1)} %get-tuple-element.56), channel_id=1, source_target_pairs={{0,8},{4,12},{8,0},{12,4},{1,9},{5,13},{9,1},{13,5},{2,10},{6,14},... | collective-permute-start | bytes 202760 | tf_op jit(solution)/shard_map/ppermute | solution.py:41
  44.4 1.3 %collective-permute-start.18 = (f32[132,128]{1,0:T(8,128)S(1)}, f32[132,128]{1,0:T(8,128)S(1)}, u32[]{:S(2)}, u32[]{:S(2)}) collective-permute-start(f32[132,128]{1,0:T(8,128)S(1)} %get-tuple-element.56), channel_id=1, source_target_pairs={{0,12},{4,0},{8,4},{12,8},{1,13},{5,1},{9,5},{13,9},{2,14},{6,2},{... | collective-permute-start | bytes 202760 | tf_op jit(solution)/shard_map/ppermute | solution.py:41
  45.7 1.4 %collective-permute-start.20 = (f32[2,128,128]{2,1,0:T(8,128)S(1)}, f32[2,128,128]{2,1,0:T(8,128)S(1)}, u32[]{:S(2)}, u32[]{:S(2)}) collective-permute-start(f32[2,128,128]{2,1,0:T(8,128)S(1)} %pad_maximum_fusion.8), channel_id=1, source_target_pairs={{0,2},{1,3},{2,0},{3,1},{4,6},{5,7},{6,4},{7,5},{8,10},{9,11},{10,... | collective-permute-start | bytes 393224 | tf_op jit(solution)/shard_map/ppermute | solution.py:37
  47.1 1.7 %collective-permute-done.16 = f32[132,128]{1,0:T(8,128)S(1)} collective-permute-done((f32[132,128]{1,0:T(8,128)S(1)}, f32[132,128]{1,0:T(8,128)S(1)}, u32[]{:S(2)}, u32[]{:S(2)}) %collective-permute-start.16) | collective-permute-done | bytes 67616 | tf_op jit(solution)/shard_map/ppermute | solution.py:41
  48.8 2.5 %collective-permute-done.17 = f32[132,128]{1,0:T(8,128)S(1)} collective-permute-done((f32[132,128]{1,0:T(8,128)S(1)}, f32[132,128]{1,0:T(8,128)S(1)}, u32[]{:S(2)}, u32[]{:S(2)}) %collective-permute-start.17) | collective-permute-done | bytes 67616 | tf_op jit(solution)/shard_map/ppermute | solution.py:41
  51.3 0.1 multiply_reduce_fusion.2
  51.5 0.2 fusion.2
  51.7 1.0 %fusion.84 = f32[4,128,128]{2,1,0:T(8,128)S(1)} fusion(f32[4,128,512]{2,1,0:T(8,128)S(1)} %bitcast.243, f32[512,128,1]{1,0,2:T(8,128)S(1)} %bitcast.247), kind=kOutput, calls=%fused_computation.223 | convolution fusion | flops 402653184 | bytes 1572864 | tf_op jit(solution)/shard_map/dot_general | solution.py:117
  52.9 0.1 collective-permute-start.21
  53.0 0.9 %collective-permute-start.22 = (f32[132,128]{1,0:T(8,128)S(1)}, f32[132,128]{1,0:T(8,128)S(1)}, u32[]{:S(2)}, u32[]{:S(2)}) collective-permute-start(f32[132,128]{1,0:T(8,128)S(1)} %concatenate.70), channel_id=1, source_target_pairs={{0,2},{1,3},{2,0},{3,1},{4,6},{5,7},{6,4},{7,5},{8,10},{9,11},{10,... | collective-permute-start | bytes 202760 | tf_op jit(solution)/shard_map/ppermute | solution.py:59
  53.9 1.5 %collective-permute-start.23 = (f32[132,128]{1,0:T(8,128)S(1)}, f32[132,128]{1,0:T(8,128)S(1)}, u32[]{:S(2)}, u32[]{:S(2)}) collective-permute-start(f32[132,128]{1,0:T(8,128)S(1)} %concatenate.71), channel_id=1, source_target_pairs={{0,3},{1,0},{2,1},{3,2},{4,7},{5,4},{6,5},{7,6},{8,11},{9,8},{10,9... | collective-permute-start | bytes 202760 | tf_op jit(solution)/shard_map/ppermute | solution.py:59
  55.4 1.4 %collective-permute-done.21 = f32[132,128]{1,0:T(8,128)S(1)} collective-permute-done((f32[132,128]{1,0:T(8,128)S(1)}, f32[132,128]{1,0:T(8,128)S(1)}, u32[]{:S(2)}, u32[]{:S(2)}) %collective-permute-start.21) | collective-permute-done | bytes 67616 | tf_op jit(solution)/shard_map/ppermute | solution.py:59
  56.8 1.3 %collective-permute-done.22 = f32[132,128]{1,0:T(8,128)S(1)} collective-permute-done((f32[132,128]{1,0:T(8,128)S(1)}, f32[132,128]{1,0:T(8,128)S(1)}, u32[]{:S(2)}, u32[]{:S(2)}) %collective-permute-start.22) | collective-permute-done | bytes 67616 | tf_op jit(solution)/shard_map/ppermute | solution.py:59
  58.0 1.4 %collective-permute-start.24 = (f32[4,128]{1,0:T(4,128)S(1)}, f32[4,128]{1,0:T(4,128)S(1)}, u32[]{:S(2)}, u32[]{:S(2)}) collective-permute-start(f32[4,128]{1,0:T(4,128)S(1)} %select_add_fusion.1), channel_id=1, source_target_pairs={{0,4},{4,8},{8,12},{12,0},{1,5},{5,9},{9,13},{13,1},{2,6},{6,10},{... | collective-permute-start | bytes 6152 | tf_op jit(solution)/shard_map/ppermute | solution.py:41
  59.5 1.3 %collective-permute-start.25 = (f32[4,128]{1,0:T(4,128)S(1)}, f32[4,128]{1,0:T(4,128)S(1)}, u32[]{:S(2)}, u32[]{:S(2)}) collective-permute-start(f32[4,128]{1,0:T(4,128)S(1)} %select_add_fusion.1), channel_id=1, source_target_pairs={{0,8},{4,12},{8,0},{12,4},{1,9},{5,13},{9,1},{13,5},{2,10},{6,14},... | collective-permute-start | bytes 6152 | tf_op jit(solution)/shard_map/ppermute | solution.py:41
  60.8 1.4 %collective-permute-start.26 = (f32[4,128]{1,0:T(4,128)S(1)}, f32[4,128]{1,0:T(4,128)S(1)}, u32[]{:S(2)}, u32[]{:S(2)}) collective-permute-start(f32[4,128]{1,0:T(4,128)S(1)} %select_add_fusion.1), channel_id=1, source_target_pairs={{0,12},{4,0},{8,4},{12,8},{1,13},{5,1},{9,5},{13,9},{2,14},{6,2},{... | collective-permute-start | bytes 6152 | tf_op jit(solution)/shard_map/ppermute | solution.py:41
  62.2 1.2 %collective-permute-done.24 = f32[4,128]{1,0:T(4,128)S(1)} collective-permute-done((f32[4,128]{1,0:T(4,128)S(1)}, f32[4,128]{1,0:T(4,128)S(1)}, u32[]{:S(2)}, u32[]{:S(2)}) %collective-permute-start.24) | collective-permute-done | bytes 2080 | tf_op jit(solution)/shard_map/ppermute | solution.py:41
  63.5 0.5 collective-permute-done.25
  64.0 0.4 collective-permute-done.26
  64.4 0.8 %fusion.27 = (f32[128,128]{1,0:T(8,128)}, f32[128,128]{1,0:T(8,128)}) fusion(f32[132,128]{1,0:T(8,128)S(1)} %collective-permute-done.23, f32[132,128]{1,0:T(8,128)S(1)} %collective-permute-done.22, f32[132,128]{1,0:T(8,128)S(1)} %collective-permute-done.21, f32[128,128]{1,0:T(8,128)S(1)} %get-tuple-element.36, f32[4,128,128]{2,1,0:T(8,128)S(1)} %fusion.84, ...), kind=kLoop, calls=%fused_computation.79 | loop fusion | flops 425984 | bytes 527876 | tf_op jit(solution)/shard_map/sub | solution.py:171
  (57 shorter events, 0.8 us)
Async XLA Ops:
  0.6 4.9 %copy-start = (s32[128,1]{0,1:T(1,128)S(1)}, s32[128,1]{0,1:T(1,128)}, u32[]{:S(2)}) copy-start(s32[128,1]{0,1:T(1,128)} %param.5) | copy-start | bytes 1540
  5.5 9.3 %collective-permute-start.2 = (s32[128]{0:T(128)S(1)}, s32[128]{0:T(128)S(1)}, u32[]{:S(2)}, u32[]{:S(2)}) collective-permute-start(s32[128]{0:T(128)S(1)} %broadcast_add_fusion), channel_id=1, source_target_pairs={{0,12},{4,0},{8,4},{12,8},{1,13},{5,1},{9,5},{13,9},{2,14},{6,2},{... | collective-permute-start | bytes 1544 | tf_op jit(solution)/shard_map/ppermute | solution.py:41
  10.7 5.3 %collective-permute-start = (s32[128]{0:T(128)S(1)}, s32[128]{0:T(128)S(1)}, u32[]{:S(2)}, u32[]{:S(2)}) collective-permute-start(s32[128]{0:T(128)S(1)} %broadcast_add_fusion), channel_id=1, source_target_pairs={{0,4},{4,8},{8,12},{12,0},{1,5},{5,9},{9,13},{13,1},{2,6},{6,10},{... | collective-permute-start | bytes 1544 | tf_op jit(solution)/shard_map/ppermute | solution.py:41
  10.7 5.3 %collective-permute-start.1 = (s32[128]{0:T(128)S(1)}, s32[128]{0:T(128)S(1)}, u32[]{:S(2)}, u32[]{:S(2)}) collective-permute-start(s32[128]{0:T(128)S(1)} %broadcast_add_fusion), channel_id=1, source_target_pairs={{0,8},{4,12},{8,0},{12,4},{1,9},{5,13},{9,1},{13,5},{2,10},{6,14},... | collective-permute-start | bytes 1544 | tf_op jit(solution)/shard_map/ppermute | solution.py:41
  11.7 1.6 %collective-permute-start.3 = (s32[128]{0:T(128)S(1)}, s32[128]{0:T(128)S(1)}, u32[]{:S(2)}, u32[]{:S(2)}) collective-permute-start(s32[128]{0:T(128)S(1)} %broadcast_add_fusion), channel_id=1, source_target_pairs={{0,1},{1,0},{2,3},{3,2},{4,5},{5,4},{6,7},{7,6},{8,9},{9,8},{10,11... | collective-permute-start | bytes 1544 | tf_op jit(solution)/shard_map/ppermute | solution.py:35
  13.3 3.8 %collective-permute-start.4 = (s32[2,128]{1,0:T(2,128)S(1)}, s32[2,128]{1,0:T(2,128)S(1)}, u32[]{:S(2)}, u32[]{:S(2)}) collective-permute-start(s32[2,128]{1,0:T(2,128)S(1)} %pad_add_fusion.2), channel_id=1, source_target_pairs={{0,2},{1,3},{2,0},{3,1},{4,6},{5,7},{6,4},{7,5},{8,10},{9,11},{10,... | collective-permute-start | bytes 3080 | tf_op jit(solution)/shard_map/ppermute | solution.py:37
  17.5 3.9 %collective-permute-start.5 = (f32[131,128]{1,0:T(8,128)S(1)}, f32[131,128]{1,0:T(8,128)S(1)}, u32[]{:S(2)}, u32[]{:S(2)}) collective-permute-start(f32[131,128]{1,0:T(8,128)S(1)} %get-tuple-element.68), channel_id=1, source_target_pairs={{0,1},{1,2},{2,3},{3,0},{4,5},{5,6},{6,7},{7,4},{8,9},{9,10},{10,1... | collective-permute-start | bytes 201224 | tf_op jit(solution)/shard_map/ppermute | solution.py:59
  17.5 4.8 %collective-permute-start.6 = (f32[131,128]{1,0:T(8,128)S(1)}, f32[131,128]{1,0:T(8,128)S(1)}, u32[]{:S(2)}, u32[]{:S(2)}) collective-permute-start(f32[131,128]{1,0:T(8,128)S(1)} %get-tuple-element.69), channel_id=1, source_target_pairs={{0,2},{1,3},{2,0},{3,1},{4,6},{5,7},{6,4},{7,5},{8,10},{9,11},{10,... | collective-permute-start | bytes 201224 | tf_op jit(solution)/shard_map/ppermute | solution.py:59
  19.1 3.4 %collective-permute-start.7 = (f32[131,128]{1,0:T(8,128)S(1)}, f32[131,128]{1,0:T(8,128)S(1)}, u32[]{:S(2)}, u32[]{:S(2)}) collective-permute-start(f32[131,128]{1,0:T(8,128)S(1)} %get-tuple-element.70), channel_id=1, source_target_pairs={{0,3},{1,0},{2,1},{3,2},{4,7},{5,4},{6,5},{7,6},{8,11},{9,8},{10,9... | collective-permute-start | bytes 201224 | tf_op jit(solution)/shard_map/ppermute | solution.py:59
  22.8 6.6 %collective-permute-start.11 = (f32[128,128]{1,0:T(8,128)S(1)}, f32[128,128]{1,0:T(8,128)S(1)}, u32[]{:S(2)}, u32[]{:S(2)}) collective-permute-start(f32[128,128]{1,0:T(8,128)S(1)} %fusion.34), channel_id=1, source_target_pairs={{0,1},{1,0},{2,3},{3,2},{4,5},{5,4},{6,7},{7,6},{8,9},{9,8},{10,11... | collective-permute-start | bytes 196616 | tf_op jit(solution)/shard_map/ppermute | solution.py:35
  23.7 7.2 %collective-permute-start.8 = (f32[130,128]{1,0:T(8,128)S(1)}, f32[130,128]{1,0:T(8,128)S(1)}, u32[]{:S(2)}, u32[]{:S(2)}) collective-permute-start(f32[130,128]{1,0:T(8,128)S(1)} %get-tuple-element.58), channel_id=1, source_target_pairs={{0,4},{4,8},{8,12},{12,0},{1,5},{5,9},{9,13},{13,1},{2,6},{6,10},{... | collective-permute-start | bytes 199688 | tf_op jit(solution)/shard_map/ppermute | solution.py:41
  26.9 6.3 %collective-permute-start.9 = (f32[130,128]{1,0:T(8,128)S(1)}, f32[130,128]{1,0:T(8,128)S(1)}, u32[]{:S(2)}, u32[]{:S(2)}) collective-permute-start(f32[130,128]{1,0:T(8,128)S(1)} %get-tuple-element.58), channel_id=1, source_target_pairs={{0,8},{4,12},{8,0},{12,4},{1,9},{5,13},{9,1},{13,5},{2,10},{6,14},... | collective-permute-start | bytes 199688 | tf_op jit(solution)/shard_map/ppermute | solution.py:41
  27.2 5.9 %collective-permute-start.10 = (f32[130,128]{1,0:T(8,128)S(1)}, f32[130,128]{1,0:T(8,128)S(1)}, u32[]{:S(2)}, u32[]{:S(2)}) collective-permute-start(f32[130,128]{1,0:T(8,128)S(1)} %get-tuple-element.58), channel_id=1, source_target_pairs={{0,12},{4,0},{8,4},{12,8},{1,13},{5,1},{9,5},{13,9},{2,14},{6,2},{... | collective-permute-start | bytes 199688 | tf_op jit(solution)/shard_map/ppermute | solution.py:41
  29.4 5.0 %collective-permute-start.12 = (f32[2,128,128]{2,1,0:T(8,128)S(1)}, f32[2,128,128]{2,1,0:T(8,128)S(1)}, u32[]{:S(2)}, u32[]{:S(2)}) collective-permute-start(f32[2,128,128]{2,1,0:T(8,128)S(1)} %pad_maximum_fusion.7), channel_id=1, source_target_pairs={{0,2},{1,3},{2,0},{3,1},{4,6},{5,7},{6,4},{7,5},{8,10},{9,11},{10,... | collective-permute-start | bytes 393224 | tf_op jit(solution)/shard_map/ppermute | solution.py:37
  35.7 4.4 %collective-permute-start.14 = (f32[132,128]{1,0:T(8,128)S(1)}, f32[132,128]{1,0:T(8,128)S(1)}, u32[]{:S(2)}, u32[]{:S(2)}) collective-permute-start(f32[132,128]{1,0:T(8,128)S(1)} %concatenate.65), channel_id=1, source_target_pairs={{0,2},{1,3},{2,0},{3,1},{4,6},{5,7},{6,4},{7,5},{8,10},{9,11},{10,... | collective-permute-start | bytes 202760 | tf_op jit(solution)/shard_map/ppermute | solution.py:59
  37.3 3.3 %collective-permute-start.15 = (f32[132,128]{1,0:T(8,128)S(1)}, f32[132,128]{1,0:T(8,128)S(1)}, u32[]{:S(2)}, u32[]{:S(2)}) collective-permute-start(f32[132,128]{1,0:T(8,128)S(1)} %concatenate.66), channel_id=1, source_target_pairs={{0,3},{1,0},{2,1},{3,2},{4,7},{5,4},{6,5},{7,6},{8,11},{9,8},{10,9... | collective-permute-start | bytes 202760 | tf_op jit(solution)/shard_map/ppermute | solution.py:59
  37.4 4.2 %collective-permute-start.13 = (f32[132,128]{1,0:T(8,128)S(1)}, f32[132,128]{1,0:T(8,128)S(1)}, u32[]{:S(2)}, u32[]{:S(2)}) collective-permute-start(f32[132,128]{1,0:T(8,128)S(1)} %concatenate.64), channel_id=1, source_target_pairs={{0,1},{1,2},{2,3},{3,0},{4,5},{5,6},{6,7},{7,4},{8,9},{9,10},{10,1... | collective-permute-start | bytes 202760 | tf_op jit(solution)/shard_map/ppermute | solution.py:59
  41.7 4.0 %collective-permute-start.19 = (f32[128,128]{1,0:T(8,128)S(1)}, f32[128,128]{1,0:T(8,128)S(1)}, u32[]{:S(2)}, u32[]{:S(2)}) collective-permute-start(f32[128,128]{1,0:T(8,128)S(1)} %multiply_subtract_fusion.3), channel_id=1, source_target_pairs={{0,1},{1,0},{2,3},{3,2},{4,5},{5,4},{6,7},{7,6},{8,9},{9,8},{10,11... | collective-permute-start | bytes 196616 | tf_op jit(solution)/shard_map/ppermute | solution.py:35
  41.8 6.9 %collective-permute-start.16 = (f32[132,128]{1,0:T(8,128)S(1)}, f32[132,128]{1,0:T(8,128)S(1)}, u32[]{:S(2)}, u32[]{:S(2)}) collective-permute-start(f32[132,128]{1,0:T(8,128)S(1)} %get-tuple-element.56), channel_id=1, source_target_pairs={{0,4},{4,8},{8,12},{12,0},{1,5},{5,9},{9,13},{13,1},{2,6},{6,10},{... | collective-permute-start | bytes 202760 | tf_op jit(solution)/shard_map/ppermute | solution.py:41
  42.7 8.6 %collective-permute-start.17 = (f32[132,128]{1,0:T(8,128)S(1)}, f32[132,128]{1,0:T(8,128)S(1)}, u32[]{:S(2)}, u32[]{:S(2)}) collective-permute-start(f32[132,128]{1,0:T(8,128)S(1)} %get-tuple-element.56), channel_id=1, source_target_pairs={{0,8},{4,12},{8,0},{12,4},{1,9},{5,13},{9,1},{13,5},{2,10},{6,14},... | collective-permute-start | bytes 202760 | tf_op jit(solution)/shard_map/ppermute | solution.py:41
  44.4 6.9 %collective-permute-start.18 = (f32[132,128]{1,0:T(8,128)S(1)}, f32[132,128]{1,0:T(8,128)S(1)}, u32[]{:S(2)}, u32[]{:S(2)}) collective-permute-start(f32[132,128]{1,0:T(8,128)S(1)} %get-tuple-element.56), channel_id=1, source_target_pairs={{0,12},{4,0},{8,4},{12,8},{1,13},{5,1},{9,5},{13,9},{2,14},{6,2},{... | collective-permute-start | bytes 202760 | tf_op jit(solution)/shard_map/ppermute | solution.py:41
  45.7 5.8 %collective-permute-start.20 = (f32[2,128,128]{2,1,0:T(8,128)S(1)}, f32[2,128,128]{2,1,0:T(8,128)S(1)}, u32[]{:S(2)}, u32[]{:S(2)}) collective-permute-start(f32[2,128,128]{2,1,0:T(8,128)S(1)} %pad_maximum_fusion.8), channel_id=1, source_target_pairs={{0,2},{1,3},{2,0},{3,1},{4,6},{5,7},{6,4},{7,5},{8,10},{9,11},{10,... | collective-permute-start | bytes 393224 | tf_op jit(solution)/shard_map/ppermute | solution.py:37
  52.9 3.9 %collective-permute-start.21 = (f32[132,128]{1,0:T(8,128)S(1)}, f32[132,128]{1,0:T(8,128)S(1)}, u32[]{:S(2)}, u32[]{:S(2)}) collective-permute-start(f32[132,128]{1,0:T(8,128)S(1)} %concatenate.69), channel_id=1, source_target_pairs={{0,1},{1,2},{2,3},{3,0},{4,5},{5,6},{6,7},{7,4},{8,9},{9,10},{10,1... | collective-permute-start | bytes 202760 | tf_op jit(solution)/shard_map/ppermute | solution.py:59
  53.0 5.1 %collective-permute-start.22 = (f32[132,128]{1,0:T(8,128)S(1)}, f32[132,128]{1,0:T(8,128)S(1)}, u32[]{:S(2)}, u32[]{:S(2)}) collective-permute-start(f32[132,128]{1,0:T(8,128)S(1)} %concatenate.70), channel_id=1, source_target_pairs={{0,2},{1,3},{2,0},{3,1},{4,6},{5,7},{6,4},{7,5},{8,10},{9,11},{10,... | collective-permute-start | bytes 202760 | tf_op jit(solution)/shard_map/ppermute | solution.py:59
  53.9 4.1 %collective-permute-start.23 = (f32[132,128]{1,0:T(8,128)S(1)}, f32[132,128]{1,0:T(8,128)S(1)}, u32[]{:S(2)}, u32[]{:S(2)}) collective-permute-start(f32[132,128]{1,0:T(8,128)S(1)} %concatenate.71), channel_id=1, source_target_pairs={{0,3},{1,0},{2,1},{3,2},{4,7},{5,4},{6,5},{7,6},{8,11},{9,8},{10,9... | collective-permute-start | bytes 202760 | tf_op jit(solution)/shard_map/ppermute | solution.py:59
  58.0 5.4 %collective-permute-start.24 = (f32[4,128]{1,0:T(4,128)S(1)}, f32[4,128]{1,0:T(4,128)S(1)}, u32[]{:S(2)}, u32[]{:S(2)}) collective-permute-start(f32[4,128]{1,0:T(4,128)S(1)} %select_add_fusion.1), channel_id=1, source_target_pairs={{0,4},{4,8},{8,12},{12,0},{1,5},{5,9},{9,13},{13,1},{2,6},{6,10},{... | collective-permute-start | bytes 6152 | tf_op jit(solution)/shard_map/ppermute | solution.py:41
  59.5 4.5 %collective-permute-start.25 = (f32[4,128]{1,0:T(4,128)S(1)}, f32[4,128]{1,0:T(4,128)S(1)}, u32[]{:S(2)}, u32[]{:S(2)}) collective-permute-start(f32[4,128]{1,0:T(4,128)S(1)} %select_add_fusion.1), channel_id=1, source_target_pairs={{0,8},{4,12},{8,0},{12,4},{1,9},{5,13},{9,1},{13,5},{2,10},{6,14},... | collective-permute-start | bytes 6152 | tf_op jit(solution)/shard_map/ppermute | solution.py:41
  60.8 3.6 %collective-permute-start.26 = (f32[4,128]{1,0:T(4,128)S(1)}, f32[4,128]{1,0:T(4,128)S(1)}, u32[]{:S(2)}, u32[]{:S(2)}) collective-permute-start(f32[4,128]{1,0:T(4,128)S(1)} %select_add_fusion.1), channel_id=1, source_target_pairs={{0,12},{4,0},{8,4},{12,8},{1,13},{5,1},{9,5},{13,9},{2,14},{6,2},{... | collective-permute-start | bytes 6152 | tf_op jit(solution)/shard_map/ppermute | solution.py:41

commit v14 on v9

--- a/solution.py
+++ b/solution.py
@@ -94,8 +94,13 @@
     n_all = n_wide * n_narrow
     width = SEED_CLASSES
     column_blocks = n_narrow * br_local
-    local_column = pattern // groups * br_local + pattern % br_local
-    pick = local_column[:, :, None] == jnp.arange(column_blocks, dtype=local_column.dtype)
+    blocks_of = jnp.arange(column_blocks, dtype=pattern.dtype)
+    if br_local == 1:
+        low = pattern[:, :, None] >= blocks_of * groups
+        pick = low & (pattern[:, :, None] < (blocks_of + 1) * groups)
+    else:
+        local_column = pattern // groups * br_local + pattern % br_local
+        pick = local_column[:, :, None] == blocks_of
     dense = jnp.sum(
         jnp.where(pick[:, :, None, :, None], tiles[:, :, :, None, :], 0.0), axis=1
     )

time: 64.5 us -> 64.5 us (level)
    and x0 -> x1, other arithmetic: none -> 0.75 us  [local(): pick = low & (pattern[:, :, None] < (blocks_of + 1) * groups)]
    select_n x1 -> x0, other arithmetic: 0.69 us -> none  [local(): local_column = pattern // groups * br_local + pattern % br_local]
where the time goes in v14:
time: 64.5 us; the launch traced here: 64.3 us
  starting transfers between devices  33.5 us (52%)
  waiting for transfers between devices  18.2 us (28%)
  other arithmetic  7.3 us (11%)
  matrix products  3.02 us (5%)
  local copies, waits for them, and re-layouts  1.34 us (2%)
  between operations  1.01 us (2%)
    ppermute x12, starting transfers between devices, gather_blocks(): parts.append(lax.ppermute(values, axis, pairs))  20.1 us
    ppermute x12, waiting for transfers between devices, gather_blocks(): parts.append(lax.ppermute(values, axis, pairs))  9.23 us
    ppermute x9, starting transfers between devices, scatter_with(): got = lax.ppermute(jnp.concatenate([sent, extra], axis=0), axis, pairs)  7.95 us
    ppermute x9, waiting for transfers between devices, scatter_with(): got = lax.ppermute(jnp.concatenate([sent, extra], axis=0), axis, pairs)  7.81 us
    ppermute x3, starting transfers between devices, gather_blocks(): lax.ppermute(both, axis, [(i, i ^ 2) for i in range(count)])  4.47 us
    dot_general x3, matrix products, product(): jnp.dot(transposed, row_values.reshape(groups * tile, width), precision=l...  3.02 us
    reduce_sum x1, other arithmetic, local(): column_sums = jnp.sum(dense, axis=(0, 1)).reshape(n_narrow, own_rows)  2.97 us
  transfers between devices with their start and end apart: 27, of which 17 were waited for; matrix products, arithmetic and copies ran while one was open for 12% of the time, Pallas kernels for 0%

profile of v14, /device:TPU:0, one launch (start us, length us, event | category | flops | bytes accessed | tf_op | source)
XLA Modules:
  0.0 64.3 jit_solution(4813360150787322959)
XLA Ops:
  0.6 3.1 %collective-permute-start = (s32[128]{0:T(128)}, s32[128]{0:T(128)S(1)}, u32[]{:S(2)}, u32[]{:S(2)}) collective-permute-start(s32[128]{0:T(128)} %bitcast.266), channel_id=1, source_target_pairs={{0,4},{4,8},{8,12},{12,0},{1,5},{5,9},{9,13},{13,1},{2,6},{6,10},{... | collective-permute-start | bytes 1544 | tf_op jit(solution)/shard_map/ppermute | solution.py:41
  3.7 2.6 %collective-permute-start.1 = (s32[128]{0:T(128)}, s32[128]{0:T(128)S(1)}, u32[]{:S(2)}, u32[]{:S(2)}) collective-permute-start(s32[128]{0:T(128)} %bitcast.267), channel_id=1, source_target_pairs={{0,8},{4,12},{8,0},{12,4},{1,9},{5,13},{9,1},{13,5},{2,10},{6,14},... | collective-permute-start | bytes 1544 | tf_op jit(solution)/shard_map/ppermute | solution.py:41
  6.3 1.3 %collective-permute-start.2 = (s32[128]{0:T(128)}, s32[128]{0:T(128)S(1)}, u32[]{:S(2)}, u32[]{:S(2)}) collective-permute-start(s32[128]{0:T(128)} %bitcast.268), channel_id=1, source_target_pairs={{0,12},{4,0},{8,4},{12,8},{1,13},{5,1},{9,5},{13,9},{2,14},{6,2},{... | collective-permute-start | bytes 1544 | tf_op jit(solution)/shard_map/ppermute | solution.py:41
  7.7 0.7 %fusion.77 = f32[128]{0:T(128)S(1)} fusion(s32[128,1]{0,1:T(1,128)} %param.5), kind=kLoop, calls=%fused_computation.211 | loop fusion | flops 384 | bytes 1024 | tf_op jit(solution)/shard_map/mul | solution.py:162
  8.4 0.8 %compare_and_fusion = pred[4,8,4]{2,1,0:T(8,128)(4,1)S(1)} fusion(s32[4]{0:T(128)S(1)} %get-tuple-element.73, s32[4]{0:T(128)S(1)} %get-tuple-element.74, s32[4,8]{1,0:T(4,128)} %param.4), kind=kLoop, calls=%fused_computation.141 | loop fusion | flops 384 | bytes 288 | tf_op jit(solution)/shard_map/and | solution.py:100
  9.1 3.0 %select_reduce_fusion = (f32[4,128]{1,0:T(4,128)S(1)}, f32[4,128,4,128]{3,1,2,0:T(8,128)S(1)}) fusion(f32[4,8,128,128]{3,2,1,0:T(8,128)} %param.3, pred[4,8,4]{2,1,0:T(8,128)(4,1)S(1)} %compare_and_fusion), kind=kLoop, calls=%fused_computation.1 | loop fusion | flops 6028800 | bytes 3147904 | tf_op jit(solution)/shard_map/reduce_sum | solution.py:107
  12.1 0.1 copy_bitcast_fusion
  12.2 0.1 broadcast_bitcast_fusion
  12.3 0.1 fusion.32
  12.4 0.6 gather_fusion
  13.1 0.1 bitcast_select_fusion
  13.3 0.3 copy.7
  13.7 1.6 %collective-permute-start.4 = (s32[2,128]{1,0:T(2,128)S(1)}, s32[2,128]{1,0:T(2,128)S(1)}, u32[]{:S(2)}, u32[]{:S(2)}) collective-permute-start(s32[2,128]{1,0:T(2,128)S(1)} %pad_add_fusion.2), channel_id=1, source_target_pairs={{0,2},{1,3},{2,0},{3,1},{4,6},{5,7},{6,4},{7,5},{8,10},{9,11},{10,... | collective-permute-start | bytes 3080 | tf_op jit(solution)/shard_map/ppermute | solution.py:37
  15.2 1.0 %fusion.5 = f32[4,128,128]{2,1,0:T(8,128)S(1)} fusion(f32[4,128,512]{2,1,0:T(8,128)S(1)} %bitcast.238, s32[512]{0:T(512)S(1)} %get-tuple-element.61), kind=kOutput, calls=%fused_computation.22 | convolution fusion | flops 402784256 | bytes 1312768 | tf_op jit(solution)/shard_map/dot_general | solution.py:121
  16.3 1.0 %collective-permute-done.4 = s32[2,128]{1,0:T(2,128)S(1)} collective-permute-done((s32[2,128]{1,0:T(2,128)S(1)}, s32[2,128]{1,0:T(2,128)S(1)}, u32[]{:S(2)}, u32[]{:S(2)}) %collective-permute-start.4) | collective-permute-done | bytes 1056 | tf_op jit(solution)/shard_map/ppermute | solution.py:37
  17.3 0.1 fusion.8
  17.4 0.2 fusion.29
  17.7 0.1 collective-permute-start.5
  17.7 1.6 %collective-permute-start.6 = (f32[131,128]{1,0:T(8,128)S(1)}, f32[131,128]{1,0:T(8,128)S(1)}, u32[]{:S(2)}, u32[]{:S(2)}) collective-permute-start(f32[131,128]{1,0:T(8,128)S(1)} %get-tuple-element.69), channel_id=1, source_target_pairs={{0,2},{1,3},{2,0},{3,1},{4,6},{5,7},{6,4},{7,5},{8,10},{9,11},{10,... | collective-permute-start | bytes 201224 | tf_op jit(solution)/shard_map/ppermute | solution.py:59
  19.3 1.4 %collective-permute-start.7 = (f32[131,128]{1,0:T(8,128)S(1)}, f32[131,128]{1,0:T(8,128)S(1)}, u32[]{:S(2)}, u32[]{:S(2)}) collective-permute-start(f32[131,128]{1,0:T(8,128)S(1)} %get-tuple-element.70), channel_id=1, source_target_pairs={{0,3},{1,0},{2,1},{3,2},{4,7},{5,4},{6,5},{7,6},{8,11},{9,8},{10,9... | collective-permute-start | bytes 201224 | tf_op jit(solution)/shard_map/ppermute | solution.py:59
  20.7 0.9 %collective-permute-done.5 = f32[131,128]{1,0:T(8,128)S(1)} collective-permute-done((f32[131,128]{1,0:T(8,128)S(1)}, f32[131,128]{1,0:T(8,128)S(1)}, u32[]{:S(2)}, u32[]{:S(2)}) %collective-permute-start.5) | collective-permute-done | bytes 67104 | tf_op jit(solution)/shard_map/ppermute | solution.py:59
  21.6 1.0 %collective-permute-done.6 = f32[131,128]{1,0:T(8,128)S(1)} collective-permute-done((f32[131,128]{1,0:T(8,128)S(1)}, f32[131,128]{1,0:T(8,128)S(1)}, u32[]{:S(2)}, u32[]{:S(2)}) %collective-permute-start.6) | collective-permute-done | bytes 67104 | tf_op jit(solution)/shard_map/ppermute | solution.py:59
  22.5 0.2 collective-permute-done.7
  22.7 0.1 fusion.88
  22.8 0.1 fusion.34
  22.9 0.9 %collective-permute-start.11 = (f32[128,128]{1,0:T(8,128)S(1)}, f32[128,128]{1,0:T(8,128)S(1)}, u32[]{:S(2)}, u32[]{:S(2)}) collective-permute-start(f32[128,128]{1,0:T(8,128)S(1)} %fusion.34), channel_id=1, source_target_pairs={{0,1},{1,0},{2,3},{3,2},{4,5},{5,4},{6,7},{7,6},{8,9},{9,8},{10,11... | collective-permute-start | bytes 196616 | tf_op jit(solution)/shard_map/ppermute | solution.py:35
  23.8 0.7 %collective-permute-start.8 = (f32[130,128]{1,0:T(8,128)S(1)}, f32[130,128]{1,0:T(8,128)S(1)}, u32[]{:S(2)}, u32[]{:S(2)}) collective-permute-start(f32[130,128]{1,0:T(8,128)S(1)} %get-tuple-element.58), channel_id=1, source_target_pairs={{0,4},{4,8},{8,12},{12,0},{1,5},{5,9},{9,13},{13,1},{2,6},{6,10},{... | collective-permute-start | bytes 199688 | tf_op jit(solution)/shard_map/ppermute | solution.py:41
  24.6 0.3 collective-permute-start.9
  24.9 2.8 %collective-permute-start.10 = (f32[130,128]{1,0:T(8,128)S(1)}, f32[130,128]{1,0:T(8,128)S(1)}, u32[]{:S(2)}, u32[]{:S(2)}) collective-permute-start(f32[130,128]{1,0:T(8,128)S(1)} %get-tuple-element.58), channel_id=1, source_target_pairs={{0,12},{4,0},{8,4},{12,8},{1,13},{5,1},{9,5},{13,9},{2,14},{6,2},{... | collective-permute-start | bytes 199688 | tf_op jit(solution)/shard_map/ppermute | solution.py:41
  27.7 1.6 %collective-permute-start.12 = (f32[2,128,128]{2,1,0:T(8,128)S(1)}, f32[2,128,128]{2,1,0:T(8,128)S(1)}, u32[]{:S(2)}, u32[]{:S(2)}) collective-permute-start(f32[2,128,128]{2,1,0:T(8,128)S(1)} %pad_maximum_fusion.7), channel_id=1, source_target_pairs={{0,2},{1,3},{2,0},{3,1},{4,6},{5,7},{6,4},{7,5},{8,10},{9,11},{10,... | collective-permute-start | bytes 393224 | tf_op jit(solution)/shard_map/ppermute | solution.py:37
  29.3 1.5 %collective-permute-done.8 = f32[130,128]{1,0:T(8,128)S(1)} collective-permute-done((f32[130,128]{1,0:T(8,128)S(1)}, f32[130,128]{1,0:T(8,128)S(1)}, u32[]{:S(2)}, u32[]{:S(2)}) %collective-permute-start.8) | collective-permute-done | bytes 66592 | tf_op jit(solution)/shard_map/ppermute | solution.py:41
  30.8 2.1 %collective-permute-done.9 = f32[130,128]{1,0:T(8,128)S(1)} collective-permute-done((f32[130,128]{1,0:T(8,128)S(1)}, f32[130,128]{1,0:T(8,128)S(1)}, u32[]{:S(2)}, u32[]{:S(2)}) %collective-permute-start.9) | collective-permute-done | bytes 66592 | tf_op jit(solution)/shard_map/ppermute | solution.py:41
  33.0 0.1 multiply_reduce_fusion.3
  33.1 0.2 multiply_subtract_fusion.1
  33.3 1.0 %fusion.81 = f32[4,128,128]{2,1,0:T(8,128)S(1)} fusion(f32[4,128,512]{2,1,0:T(8,128)S(1)} %bitcast.239, f32[512,128,1]{1,0,2:T(8,128)S(1)} %bitcast.245), kind=kOutput, calls=%fused_computation.215 | convolution fusion | flops 402653184 | bytes 1572864 | tf_op jit(solution)/shard_map/dot_general | solution.py:121
  34.4 1.5 %collective-permute-start.14 = (f32[132,128]{1,0:T(8,128)S(1)}, f32[132,128]{1,0:T(8,128)S(1)}, u32[]{:S(2)}, u32[]{:S(2)}) collective-permute-start(f32[132,128]{1,0:T(8,128)S(1)} %concatenate.65), channel_id=1, source_target_pairs={{0,2},{1,3},{2,0},{3,1},{4,6},{5,7},{6,4},{7,5},{8,10},{9,11},{10,... | collective-permute-start | bytes 202760 | tf_op jit(solution)/shard_map/ppermute | solution.py:59
  36.1 0.5 collective-permute-start.13
  36.6 2.2 %collective-permute-done.14 = f32[132,128]{1,0:T(8,128)S(1)} collective-permute-done((f32[132,128]{1,0:T(8,128)S(1)}, f32[132,128]{1,0:T(8,128)S(1)}, u32[]{:S(2)}, u32[]{:S(2)}) %collective-permute-start.14) | collective-permute-done | bytes 67616 | tf_op jit(solution)/shard_map/ppermute | solution.py:59
  38.8 0.5 collective-permute-done.15
  39.3 1.0 %collective-permute-done.13 = f32[132,128]{1,0:T(8,128)S(1)} collective-permute-done((f32[132,128]{1,0:T(8,128)S(1)}, f32[132,128]{1,0:T(8,128)S(1)}, u32[]{:S(2)}, u32[]{:S(2)}) %collective-permute-start.13) | collective-permute-done | bytes 67616 | tf_op jit(solution)/shard_map/ppermute | solution.py:59
  40.3 0.1 multiply_subtract_fusion.3
  40.4 0.1 collective-permute-start.19
  40.5 1.5 %collective-permute-start.16 = (f32[132,128]{1,0:T(8,128)S(1)}, f32[132,128]{1,0:T(8,128)S(1)}, u32[]{:S(2)}, u32[]{:S(2)}) collective-permute-start(f32[132,128]{1,0:T(8,128)S(1)} %get-tuple-element.56), channel_id=1, source_target_pairs={{0,4},{4,8},{8,12},{12,0},{1,5},{5,9},{9,13},{13,1},{2,6},{6,10},{... | collective-permute-start | bytes 202760 | tf_op jit(solution)/shard_map/ppermute | solution.py:41
  42.0 0.9 %collective-permute-start.17 = (f32[132,128]{1,0:T(8,128)S(1)}, f32[132,128]{1,0:T(8,128)S(1)}, u32[]{:S(2)}, u32[]{:S(2)}) collective-permute-start(f32[132,128]{1,0:T(8,128)S(1)} %get-tuple-element.56), channel_id=1, source_target_pairs={{0,8},{4,12},{8,0},{12,4},{1,9},{5,13},{9,1},{13,5},{2,10},{6,14},... | collective-permute-start | bytes 202760 | tf_op jit(solution)/shard_map/ppermute | solution.py:41
  43.0 2.2 %collective-permute-start.18 = (f32[132,128]{1,0:T(8,128)S(1)}, f32[132,128]{1,0:T(8,128)S(1)}, u32[]{:S(2)}, u32[]{:S(2)}) collective-permute-start(f32[132,128]{1,0:T(8,128)S(1)} %get-tuple-element.56), channel_id=1, source_target_pairs={{0,12},{4,0},{8,4},{12,8},{1,13},{5,1},{9,5},{13,9},{2,14},{6,2},{... | collective-permute-start | bytes 202760 | tf_op jit(solution)/shard_map/ppermute | solution.py:41
  45.2 1.4 %collective-permute-start.20 = (f32[2,128,128]{2,1,0:T(8,128)S(1)}, f32[2,128,128]{2,1,0:T(8,128)S(1)}, u32[]{:S(2)}, u32[]{:S(2)}) collective-permute-start(f32[2,128,128]{2,1,0:T(8,128)S(1)} %pad_maximum_fusion.8), channel_id=1, source_target_pairs={{0,2},{1,3},{2,0},{3,1},{4,6},{5,7},{6,4},{7,5},{8,10},{9,11},{10,... | collective-permute-start | bytes 393224 | tf_op jit(solution)/shard_map/ppermute | solution.py:37
  46.6 0.9 %collective-permute-done.16 = f32[132,128]{1,0:T(8,128)S(1)} collective-permute-done((f32[132,128]{1,0:T(8,128)S(1)}, f32[132,128]{1,0:T(8,128)S(1)}, u32[]{:S(2)}, u32[]{:S(2)}) %collective-permute-start.16) | collective-permute-done | bytes 67616 | tf_op jit(solution)/shard_map/ppermute | solution.py:41
  47.5 2.5 %collective-permute-done.17 = f32[132,128]{1,0:T(8,128)S(1)} collective-permute-done((f32[132,128]{1,0:T(8,128)S(1)}, f32[132,128]{1,0:T(8,128)S(1)}, u32[]{:S(2)}, u32[]{:S(2)}) %collective-permute-start.17) | collective-permute-done | bytes 67616 | tf_op jit(solution)/shard_map/ppermute | solution.py:41
  50.1 0.1 multiply_reduce_fusion.2
  50.2 0.1 collective-permute-done.20
  50.4 0.2 fusion.2
  50.6 1.0 %fusion.82 = f32[4,128,128]{2,1,0:T(8,128)S(1)} fusion(f32[4,128,512]{2,1,0:T(8,128)S(1)} %bitcast.240, f32[512,128,1]{1,0,2:T(8,128)S(1)} %bitcast.244), kind=kOutput, calls=%fused_computation.216 | convolution fusion | flops 402653184 | bytes 1572864 | tf_op jit(solution)/shard_map/dot_general | solution.py:121
  51.7 0.1 collective-permute-start.21
  51.8 1.3 %collective-permute-start.22 = (f32[132,128]{1,0:T(8,128)S(1)}, f32[132,128]{1,0:T(8,128)S(1)}, u32[]{:S(2)}, u32[]{:S(2)}) collective-permute-start(f32[132,128]{1,0:T(8,128)S(1)} %concatenate.70), channel_id=1, source_target_pairs={{0,2},{1,3},{2,0},{3,1},{4,6},{5,7},{6,4},{7,5},{8,10},{9,11},{10,... | collective-permute-start | bytes 202760 | tf_op jit(solution)/shard_map/ppermute | solution.py:59
  53.1 1.5 %collective-permute-start.23 = (f32[132,128]{1,0:T(8,128)S(1)}, f32[132,128]{1,0:T(8,128)S(1)}, u32[]{:S(2)}, u32[]{:S(2)}) collective-permute-start(f32[132,128]{1,0:T(8,128)S(1)} %concatenate.71), channel_id=1, source_target_pairs={{0,3},{1,0},{2,1},{3,2},{4,7},{5,4},{6,5},{7,6},{8,11},{9,8},{10,9... | collective-permute-start | bytes 202760 | tf_op jit(solution)/shard_map/ppermute | solution.py:59
  54.6 1.0 %collective-permute-done.21 = f32[132,128]{1,0:T(8,128)S(1)} collective-permute-done((f32[132,128]{1,0:T(8,128)S(1)}, f32[132,128]{1,0:T(8,128)S(1)}, u32[]{:S(2)}, u32[]{:S(2)}) %collective-permute-start.21) | collective-permute-done | bytes 67616 | tf_op jit(solution)/shard_map/ppermute | solution.py:59
  55.6 1.1 %collective-permute-done.22 = f32[132,128]{1,0:T(8,128)S(1)} collective-permute-done((f32[132,128]{1,0:T(8,128)S(1)}, f32[132,128]{1,0:T(8,128)S(1)}, u32[]{:S(2)}, u32[]{:S(2)}) %collective-permute-start.22) | collective-permute-done | bytes 67616 | tf_op jit(solution)/shard_map/ppermute | solution.py:59
  56.7 2.1 %collective-permute-start.24 = (f32[4,128]{1,0:T(4,128)S(1)}, f32[4,128]{1,0:T(4,128)S(1)}, u32[]{:S(2)}, u32[]{:S(2)}) collective-permute-start(f32[4,128]{1,0:T(4,128)S(1)} %select_add_fusion.1), channel_id=1, source_target_pairs={{0,4},{4,8},{8,12},{12,0},{1,5},{5,9},{9,13},{13,1},{2,6},{6,10},{... | collective-permute-start | bytes 6152 | tf_op jit(solution)/shard_map/ppermute | solution.py:41
  58.8 1.1 %collective-permute-start.25 = (f32[4,128]{1,0:T(4,128)S(1)}, f32[4,128]{1,0:T(4,128)S(1)}, u32[]{:S(2)}, u32[]{:S(2)}) collective-permute-start(f32[4,128]{1,0:T(4,128)S(1)} %select_add_fusion.1), channel_id=1, source_target_pairs={{0,8},{4,12},{8,0},{12,4},{1,9},{5,13},{9,1},{13,5},{2,10},{6,14},... | collective-permute-start | bytes 6152 | tf_op jit(solution)/shard_map/ppermute | solution.py:41
  59.9 1.4 %collective-permute-start.26 = (f32[4,128]{1,0:T(4,128)S(1)}, f32[4,128]{1,0:T(4,128)S(1)}, u32[]{:S(2)}, u32[]{:S(2)}) collective-permute-start(f32[4,128]{1,0:T(4,128)S(1)} %select_add_fusion.1), channel_id=1, source_target_pairs={{0,12},{4,0},{8,4},{12,8},{1,13},{5,1},{9,5},{13,9},{2,14},{6,2},{... | collective-permute-start | bytes 6152 | tf_op jit(solution)/shard_map/ppermute | solution.py:41
  61.3 0.9 %collective-permute-done.24 = f32[4,128]{1,0:T(4,128)S(1)} collective-permute-done((f32[4,128]{1,0:T(4,128)S(1)}, f32[4,128]{1,0:T(4,128)S(1)}, u32[]{:S(2)}, u32[]{:S(2)}) %collective-permute-start.24) | collective-permute-done | bytes 2080 | tf_op jit(solution)/shard_map/ppermute | solution.py:41
  62.2 1.1 %collective-permute-done.25 = f32[4,128]{1,0:T(4,128)S(1)} collective-permute-done((f32[4,128]{1,0:T(4,128)S(1)}, f32[4,128]{1,0:T(4,128)S(1)}, u32[]{:S(2)}, u32[]{:S(2)}) %collective-permute-start.25) | collective-permute-done | bytes 2080 | tf_op jit(solution)/shard_map/ppermute | solution.py:41
  63.3 0.1 collective-permute-done.26
  63.5 0.8 %fusion.27 = (f32[128,128]{1,0:T(8,128)}, f32[128,128]{1,0:T(8,128)}) fusion(f32[132,128]{1,0:T(8,128)S(1)} %collective-permute-done.23, f32[132,128]{1,0:T(8,128)S(1)} %collective-permute-done.22, f32[132,128]{1,0:T(8,128)S(1)} %collective-permute-done.21, f32[128,128]{1,0:T(8,128)S(1)} %get-tuple-element.36, f32[4,128,128]{2,1,0:T(8,128)S(1)} %fusion.82, ...), kind=kLoop, calls=%fused_computation.79 | loop fusion | flops 425984 | bytes 527876 | tf_op jit(solution)/shard_map/sub | solution.py:175
  (54 shorter events, 0.8 us)
Async XLA Ops:
  0.6 14.6 %collective-permute-start = (s32[128]{0:T(128)}, s32[128]{0:T(128)S(1)}, u32[]{:S(2)}, u32[]{:S(2)}) collective-permute-start(s32[128]{0:T(128)} %bitcast.266), channel_id=1, source_target_pairs={{0,4},{4,8},{8,12},{12,0},{1,5},{5,9},{9,13},{13,1},{2,6},{6,10},{... | collective-permute-start | bytes 1544 | tf_op jit(solution)/shard_map/ppermute | solution.py:41
  3.7 11.5 %collective-permute-start.1 = (s32[128]{0:T(128)}, s32[128]{0:T(128)S(1)}, u32[]{:S(2)}, u32[]{:S(2)}) collective-permute-start(s32[128]{0:T(128)} %bitcast.267), channel_id=1, source_target_pairs={{0,8},{4,12},{8,0},{12,4},{1,9},{5,13},{9,1},{13,5},{2,10},{6,14},... | collective-permute-start | bytes 1544 | tf_op jit(solution)/shard_map/ppermute | solution.py:41
  6.3 8.9 %collective-permute-start.2 = (s32[128]{0:T(128)}, s32[128]{0:T(128)S(1)}, u32[]{:S(2)}, u32[]{:S(2)}) collective-permute-start(s32[128]{0:T(128)} %bitcast.268), channel_id=1, source_target_pairs={{0,12},{4,0},{8,4},{12,8},{1,13},{5,1},{9,5},{13,9},{2,14},{6,2},{... | collective-permute-start | bytes 1544 | tf_op jit(solution)/shard_map/ppermute | solution.py:41
  7.6 6.0 %collective-permute-start.3 = (s32[128]{0:T(128)}, s32[128]{0:T(128)S(1)}, u32[]{:S(2)}, u32[]{:S(2)}) collective-permute-start(s32[128]{0:T(128)} %bitcast.269), channel_id=1, source_target_pairs={{0,1},{1,0},{2,3},{3,2},{4,5},{5,4},{6,7},{7,6},{8,9},{9,8},{10,11... | collective-permute-start | bytes 1544 | tf_op jit(solution)/shard_map/ppermute | solution.py:35
  9.1 3.2 %copy-start = (s32[128,1]{0,1:T(1,128)S(1)}, s32[128,1]{0,1:T(1,128)}, u32[]{:S(2)}) copy-start(s32[128,1]{0,1:T(1,128)} %param.5) | copy-start | bytes 1540
  13.7 3.6 %collective-permute-start.4 = (s32[2,128]{1,0:T(2,128)S(1)}, s32[2,128]{1,0:T(2,128)S(1)}, u32[]{:S(2)}, u32[]{:S(2)}) collective-permute-start(s32[2,128]{1,0:T(2,128)S(1)} %pad_add_fusion.2), channel_id=1, source_target_pairs={{0,2},{1,3},{2,0},{3,1},{4,6},{5,7},{6,4},{7,5},{8,10},{9,11},{10,... | collective-permute-start | bytes 3080 | tf_op jit(solution)/shard_map/ppermute | solution.py:37
  17.7 3.9 %collective-permute-start.5 = (f32[131,128]{1,0:T(8,128)S(1)}, f32[131,128]{1,0:T(8,128)S(1)}, u32[]{:S(2)}, u32[]{:S(2)}) collective-permute-start(f32[131,128]{1,0:T(8,128)S(1)} %get-tuple-element.68), channel_id=1, source_target_pairs={{0,1},{1,2},{2,3},{3,0},{4,5},{5,6},{6,7},{7,4},{8,9},{9,10},{10,1... | collective-permute-start | bytes 201224 | tf_op jit(solution)/shard_map/ppermute | solution.py:59
  17.7 4.8 %collective-permute-start.6 = (f32[131,128]{1,0:T(8,128)S(1)}, f32[131,128]{1,0:T(8,128)S(1)}, u32[]{:S(2)}, u32[]{:S(2)}) collective-permute-start(f32[131,128]{1,0:T(8,128)S(1)} %get-tuple-element.69), channel_id=1, source_target_pairs={{0,2},{1,3},{2,0},{3,1},{4,6},{5,7},{6,4},{7,5},{8,10},{9,11},{10,... | collective-permute-start | bytes 201224 | tf_op jit(solution)/shard_map/ppermute | solution.py:59
  19.3 3.4 %collective-permute-start.7 = (f32[131,128]{1,0:T(8,128)S(1)}, f32[131,128]{1,0:T(8,128)S(1)}, u32[]{:S(2)}, u32[]{:S(2)}) collective-permute-start(f32[131,128]{1,0:T(8,128)S(1)} %get-tuple-element.70), channel_id=1, source_target_pairs={{0,3},{1,0},{2,1},{3,2},{4,7},{5,4},{6,5},{7,6},{8,11},{9,8},{10,9... | collective-permute-start | bytes 201224 | tf_op jit(solution)/shard_map/ppermute | solution.py:59
  22.9 4.8 %collective-permute-start.11 = (f32[128,128]{1,0:T(8,128)S(1)}, f32[128,128]{1,0:T(8,128)S(1)}, u32[]{:S(2)}, u32[]{:S(2)}) collective-permute-start(f32[128,128]{1,0:T(8,128)S(1)} %fusion.34), channel_id=1, source_target_pairs={{0,1},{1,0},{2,3},{3,2},{4,5},{5,4},{6,7},{7,6},{8,9},{9,8},{10,11... | collective-permute-start | bytes 196616 | tf_op jit(solution)/shard_map/ppermute | solution.py:35
  23.8 7.0 %collective-permute-start.8 = (f32[130,128]{1,0:T(8,128)S(1)}, f32[130,128]{1,0:T(8,128)S(1)}, u32[]{:S(2)}, u32[]{:S(2)}) collective-permute-start(f32[130,128]{1,0:T(8,128)S(1)} %get-tuple-element.58), channel_id=1, source_target_pairs={{0,4},{4,8},{8,12},{12,0},{1,5},{5,9},{9,13},{13,1},{2,6},{6,10},{... | collective-permute-start | bytes 199688 | tf_op jit(solution)/shard_map/ppermute | solution.py:41
  24.6 8.3 %collective-permute-start.9 = (f32[130,128]{1,0:T(8,128)S(1)}, f32[130,128]{1,0:T(8,128)S(1)}, u32[]{:S(2)}, u32[]{:S(2)}) collective-permute-start(f32[130,128]{1,0:T(8,128)S(1)} %get-tuple-element.58), channel_id=1, source_target_pairs={{0,8},{4,12},{8,0},{12,4},{1,9},{5,13},{9,1},{13,5},{2,10},{6,14},... | collective-permute-start | bytes 199688 | tf_op jit(solution)/shard_map/ppermute | solution.py:41
  24.9 8.0 %collective-permute-start.10 = (f32[130,128]{1,0:T(8,128)S(1)}, f32[130,128]{1,0:T(8,128)S(1)}, u32[]{:S(2)}, u32[]{:S(2)}) collective-permute-start(f32[130,128]{1,0:T(8,128)S(1)} %get-tuple-element.58), channel_id=1, source_target_pairs={{0,12},{4,0},{8,4},{12,8},{1,13},{5,1},{9,5},{13,9},{2,14},{6,2},{... | collective-permute-start | bytes 199688 | tf_op jit(solution)/shard_map/ppermute | solution.py:41
  27.7 5.3 %collective-permute-start.12 = (f32[2,128,128]{2,1,0:T(8,128)S(1)}, f32[2,128,128]{2,1,0:T(8,128)S(1)}, u32[]{:S(2)}, u32[]{:S(2)}) collective-permute-start(f32[2,128,128]{2,1,0:T(8,128)S(1)} %pad_maximum_fusion.7), channel_id=1, source_target_pairs={{0,2},{1,3},{2,0},{3,1},{4,6},{5,7},{6,4},{7,5},{8,10},{9,11},{10,... | collective-permute-start | bytes 393224 | tf_op jit(solution)/shard_map/ppermute | solution.py:37
  34.4 4.4 %collective-permute-start.14 = (f32[132,128]{1,0:T(8,128)S(1)}, f32[132,128]{1,0:T(8,128)S(1)}, u32[]{:S(2)}, u32[]{:S(2)}) collective-permute-start(f32[132,128]{1,0:T(8,128)S(1)} %concatenate.65), channel_id=1, source_target_pairs={{0,2},{1,3},{2,0},{3,1},{4,6},{5,7},{6,4},{7,5},{8,10},{9,11},{10,... | collective-permute-start | bytes 202760 | tf_op jit(solution)/shard_map/ppermute | solution.py:59
  36.0 3.3 %collective-permute-start.15 = (f32[132,128]{1,0:T(8,128)S(1)}, f32[132,128]{1,0:T(8,128)S(1)}, u32[]{:S(2)}, u32[]{:S(2)}) collective-permute-start(f32[132,128]{1,0:T(8,128)S(1)} %concatenate.66), channel_id=1, source_target_pairs={{0,3},{1,0},{2,1},{3,2},{4,7},{5,4},{6,5},{7,6},{8,11},{9,8},{10,9... | collective-permute-start | bytes 202760 | tf_op jit(solution)/shard_map/ppermute | solution.py:59
  36.1 4.2 %collective-permute-start.13 = (f32[132,128]{1,0:T(8,128)S(1)}, f32[132,128]{1,0:T(8,128)S(1)}, u32[]{:S(2)}, u32[]{:S(2)}) collective-permute-start(f32[132,128]{1,0:T(8,128)S(1)} %concatenate.64), channel_id=1, source_target_pairs={{0,1},{1,2},{2,3},{3,0},{4,5},{5,6},{6,7},{7,4},{8,9},{9,10},{10,1... | collective-permute-start | bytes 202760 | tf_op jit(solution)/shard_map/ppermute | solution.py:59
  40.4 4.8 %collective-permute-start.19 = (f32[128,128]{1,0:T(8,128)S(1)}, f32[128,128]{1,0:T(8,128)S(1)}, u32[]{:S(2)}, u32[]{:S(2)}) collective-permute-start(f32[128,128]{1,0:T(8,128)S(1)} %multiply_subtract_fusion.3), channel_id=1, source_target_pairs={{0,1},{1,0},{2,3},{3,2},{4,5},{5,4},{6,7},{7,6},{8,9},{9,8},{10,11... | collective-permute-start | bytes 196616 | tf_op jit(solution)/shard_map/ppermute | solution.py:35
  40.5 6.9 %collective-permute-start.16 = (f32[132,128]{1,0:T(8,128)S(1)}, f32[132,128]{1,0:T(8,128)S(1)}, u32[]{:S(2)}, u32[]{:S(2)}) collective-permute-start(f32[132,128]{1,0:T(8,128)S(1)} %get-tuple-element.56), channel_id=1, source_target_pairs={{0,4},{4,8},{8,12},{12,0},{1,5},{5,9},{9,13},{13,1},{2,6},{6,10},{... | collective-permute-start | bytes 202760 | tf_op jit(solution)/shard_map/ppermute | solution.py:41
  42.0 8.0 %collective-permute-start.17 = (f32[132,128]{1,0:T(8,128)S(1)}, f32[132,128]{1,0:T(8,128)S(1)}, u32[]{:S(2)}, u32[]{:S(2)}) collective-permute-start(f32[132,128]{1,0:T(8,128)S(1)} %get-tuple-element.56), channel_id=1, source_target_pairs={{0,8},{4,12},{8,0},{12,4},{1,9},{5,13},{9,1},{13,5},{2,10},{6,14},... | collective-permute-start | bytes 202760 | tf_op jit(solution)/shard_map/ppermute | solution.py:41
  43.0 7.0 %collective-permute-start.18 = (f32[132,128]{1,0:T(8,128)S(1)}, f32[132,128]{1,0:T(8,128)S(1)}, u32[]{:S(2)}, u32[]{:S(2)}) collective-permute-start(f32[132,128]{1,0:T(8,128)S(1)} %get-tuple-element.56), channel_id=1, source_target_pairs={{0,12},{4,0},{8,4},{12,8},{1,13},{5,1},{9,5},{13,9},{2,14},{6,2},{... | collective-permute-start | bytes 202760 | tf_op jit(solution)/shard_map/ppermute | solution.py:41
  45.2 5.1 %collective-permute-start.20 = (f32[2,128,128]{2,1,0:T(8,128)S(1)}, f32[2,128,128]{2,1,0:T(8,128)S(1)}, u32[]{:S(2)}, u32[]{:S(2)}) collective-permute-start(f32[2,128,128]{2,1,0:T(8,128)S(1)} %pad_maximum_fusion.8), channel_id=1, source_target_pairs={{0,2},{1,3},{2,0},{3,1},{4,6},{5,7},{6,4},{7,5},{8,10},{9,11},{10,... | collective-permute-start | bytes 393224 | tf_op jit(solution)/shard_map/ppermute | solution.py:37
  51.7 3.9 %collective-permute-start.21 = (f32[132,128]{1,0:T(8,128)S(1)}, f32[132,128]{1,0:T(8,128)S(1)}, u32[]{:S(2)}, u32[]{:S(2)}) collective-permute-start(f32[132,128]{1,0:T(8,128)S(1)} %concatenate.69), channel_id=1, source_target_pairs={{0,1},{1,2},{2,3},{3,0},{4,5},{5,6},{6,7},{7,4},{8,9},{9,10},{10,1... | collective-permute-start | bytes 202760 | tf_op jit(solution)/shard_map/ppermute | solution.py:59
  51.8 4.9 %collective-permute-start.22 = (f32[132,128]{1,0:T(8,128)S(1)}, f32[132,128]{1,0:T(8,128)S(1)}, u32[]{:S(2)}, u32[]{:S(2)}) collective-permute-start(f32[132,128]{1,0:T(8,128)S(1)} %concatenate.70), channel_id=1, source_target_pairs={{0,2},{1,3},{2,0},{3,1},{4,6},{5,7},{6,4},{7,5},{8,10},{9,11},{10,... | collective-permute-start | bytes 202760 | tf_op jit(solution)/shard_map/ppermute | solution.py:59
  53.1 3.6 %collective-permute-start.23 = (f32[132,128]{1,0:T(8,128)S(1)}, f32[132,128]{1,0:T(8,128)S(1)}, u32[]{:S(2)}, u32[]{:S(2)}) collective-permute-start(f32[132,128]{1,0:T(8,128)S(1)} %concatenate.71), channel_id=1, source_target_pairs={{0,3},{1,0},{2,1},{3,2},{4,7},{5,4},{6,5},{7,6},{8,11},{9,8},{10,9... | collective-permute-start | bytes 202760 | tf_op jit(solution)/shard_map/ppermute | solution.py:59
  56.7 5.4 %collective-permute-start.24 = (f32[4,128]{1,0:T(4,128)S(1)}, f32[4,128]{1,0:T(4,128)S(1)}, u32[]{:S(2)}, u32[]{:S(2)}) collective-permute-start(f32[4,128]{1,0:T(4,128)S(1)} %select_add_fusion.1), channel_id=1, source_target_pairs={{0,4},{4,8},{8,12},{12,0},{1,5},{5,9},{9,13},{13,1},{2,6},{6,10},{... | collective-permute-start | bytes 6152 | tf_op jit(solution)/shard_map/ppermute | solution.py:41
  58.8 4.5 %collective-permute-start.25 = (f32[4,128]{1,0:T(4,128)S(1)}, f32[4,128]{1,0:T(4,128)S(1)}, u32[]{:S(2)}, u32[]{:S(2)}) collective-permute-start(f32[4,128]{1,0:T(4,128)S(1)} %select_add_fusion.1), channel_id=1, source_target_pairs={{0,8},{4,12},{8,0},{12,4},{1,9},{5,13},{9,1},{13,5},{2,10},{6,14},... | collective-permute-start | bytes 6152 | tf_op jit(solution)/shard_map/ppermute | solution.py:41
  59.9 3.6 %collective-permute-start.26 = (f32[4,128]{1,0:T(4,128)S(1)}, f32[4,128]{1,0:T(4,128)S(1)}, u32[]{:S(2)}, u32[]{:S(2)}) collective-permute-start(f32[4,128]{1,0:T(4,128)S(1)} %select_add_fusion.1), channel_id=1, source_target_pairs={{0,12},{4,0},{8,4},{12,8},{1,13},{5,1},{9,5},{13,9},{2,14},{6,2},{... | collective-permute-start | bytes 6152 | tf_op jit(solution)/shard_map/ppermute | solution.py:41

commit v15 on v9

--- a/solution.py
+++ b/solution.py
@@ -95,14 +95,15 @@
     width = SEED_CLASSES
     column_blocks = n_narrow * br_local
     local_column = pattern // groups * br_local + pattern % br_local
-    pick = local_column[:, :, None] == jnp.arange(column_blocks, dtype=local_column.dtype)
-    dense = jnp.sum(
-        jnp.where(pick[:, :, None, :, None], tiles[:, :, :, None, :], 0.0), axis=1
-    )
-    column_sums = jnp.sum(dense, axis=(0, 1)).reshape(n_narrow, own_rows)
+    combined = (
+        jnp.zeros((groups, column_blocks, tile, tile), tiles.dtype)
+        .at[jnp.arange(groups)[:, None], local_column]
+        .add(tiles)
+    )
+    column_sums = jnp.sum(combined, axis=(0, 2)).reshape(n_narrow, own_rows)
     order = source("wide", n_wide, jnp.arange(n_wide))
-    dense = jnp.take(dense.reshape(n_wide, own_rows, column_blocks * tile), order, axis=0)
-    transposed = dense.reshape(groups * tile, column_blocks * tile).T
+    combined = jnp.take(combined.reshape(n_wide, br_local, column_blocks, tile, tile), order, axis=0)
+    transposed = combined.transpose(2, 4, 0, 1, 3).reshape(column_blocks * tile, groups * tile)
 
     labels = seed_label[:, 0]
     seeded = (labels < SEED_CLASSES).astype(jnp.float32)

time: 64.5 us -> 71.9 us (1.11)
  other arithmetic: 7.31 us -> 10.2 us
  waiting for transfers between devices: 18.2 us -> 21 us
  matrix products: 3.02 us -> 5.51 us
  starting transfers between devices: 33.5 us -> 32.6 us
    scatter-add x0 -> x1, other arithmetic: none -> 5.17 us  [local(): combined = jnp.zeros((groups, column_blocks, tile, tile), tiles.dtype).at...]
    reduce_sum x1, other arithmetic: 2.97 us -> 0.09 us  [local(): column_sums = jnp.sum(combined, axis=(0, 2)).reshape(n_narrow, own_rows)]
    dot_general x3, matrix products: 3.02 us -> 5.51 us  [product(): jnp.dot(transposed, row_values.reshape(groups * tile, width), precision=l...]
    ppermute x9, waiting for transfers between devices: 7.81 us -> 9.23 us  [scatter_with(): got = lax.ppermute(jnp.concatenate([sent, extra], axis=0), axis, pairs)]
    ppermute x3, waiting for transfers between devices: 1.12 us -> 2.23 us  [gather_blocks(): lax.ppermute(both, axis, [(i, i ^ 2) for i in range(count)])]
    ppermute x12, starting transfers between devices: 20.1 us -> 19.1 us  [gather_blocks(): parts.append(lax.ppermute(values, axis, pairs))]
    select_n x3 -> x1, other arithmetic: 0.84 us -> 0.01 us  [local(): jnp.take(combined.reshape(n_wide, br_local, column_blocks, tile, tile), o...]
  transfers between devices with their start and end apart: 27 -> 27, of which waited for: 17 -> 18; matrix products, arithmetic and copies ran while one was open for 12% -> 15% of each run, Pallas kernels for 0% -> 0%
where the time goes in v15:
time: 71.9 us; the launch traced here: 71.7 us
  starting transfers between devices  32.6 us (45%)
  waiting for transfers between devices  21 us (29%)
  other arithmetic  10.2 us (14%)
  matrix products  5.51 us (8%)
  local copies, waits for them, and re-layouts  1.38 us (2%)
  between operations  0.99 us (1%)
    ppermute x12, starting transfers between devices, gather_blocks(): parts.append(lax.ppermute(values, axis, pairs))  19.1 us
    ppermute x12, waiting for transfers between devices, gather_blocks(): parts.append(lax.ppermute(values, axis, pairs))  9.49 us
    ppermute x9, waiting for transfers between devices, scatter_with(): got = lax.ppermute(jnp.concatenate([sent, extra], axis=0), axis, pairs)  9.23 us
    ppermute x9, starting transfers between devices, scatter_with(): got = lax.ppermute(jnp.concatenate([sent, extra], axis=0), axis, pairs)  7.9 us
    dot_general x3, matrix products, product(): jnp.dot(transposed, row_values.reshape(groups * tile, width), precision=l...  5.51 us
    scatter-add x1, other arithmetic, local(): combined = jnp.zeros((groups, column_blocks, tile, tile), tiles.dtype).at...  5.17 us
    ppermute x3, starting transfers between devices, gather_blocks(): lax.ppermute(both, axis, [(i, i ^ 2) for i in range(count)])  4.18 us
    ppermute x3, waiting for transfers between devices, gather_blocks(): lax.ppermute(both, axis, [(i, i ^ 2) for i in range(count)])  2.23 us
  transfers between devices with their start and end apart: 27, of which 18 were waited for; matrix products, arithmetic and copies ran while one was open for 15% of the time, Pallas kernels for 0%

profile of v15, /device:TPU:0, one launch (start us, length us, event | category | flops | bytes accessed | tf_op | source)
XLA Modules:
  0.0 71.7 jit_solution(2890409464796995520)
XLA Ops:
  0.6 0.5 collective-permute-start.3
  1.1 4.7 %collective-permute-start.2 = (s32[128]{0:T(128)}, s32[128]{0:T(128)S(1)}, u32[]{:S(2)}, u32[]{:S(2)}) collective-permute-start(s32[128]{0:T(128)} %bitcast.270), channel_id=1, source_target_pairs={{0,12},{4,0},{8,4},{12,8},{1,13},{5,1},{9,5},{13,9},{2,14},{6,2},{... | collective-permute-start | bytes 1544 | tf_op jit(solution)/shard_map/ppermute | solution.py:41
  5.8 1.0 %collective-permute-start = (s32[128]{0:T(128)}, s32[128]{0:T(128)S(1)}, u32[]{:S(2)}, u32[]{:S(2)}) collective-permute-start(s32[128]{0:T(128)} %bitcast.272), channel_id=1, source_target_pairs={{0,4},{4,8},{8,12},{12,0},{1,5},{5,9},{9,13},{13,1},{2,6},{6,10},{... | collective-permute-start | bytes 1544 | tf_op jit(solution)/shard_map/ppermute | solution.py:41
  6.8 0.7 fusion.85
  7.6 0.8 %fusion.33 = (f32[128]{0:T(128)S(1)}, f32[128]{0:T(128)S(1)}) fusion(s32[128]{0:T(128)} %bitcast.273, f32[128]{0:T(128)S(1)} %fusion.85), kind=kLoop, calls=%fused_computation.83 | loop fusion | flops 114432 | bytes 2048 | tf_op jit(solution)/shard_map/reduce_sum | solution.py:157
  8.3 0.7 fusion.59
  9.0 0.1 reshape.377
  9.1 0.1 broadcast_in_dim.19
  9.2 5.2 %scatter_fusion = f32[4,4,128,128]{3,2,1,0:T(8,128)S(1)} fusion(f32[4,4,128,128]{3,2,1,0:T(8,128)S(1)} %broadcast_in_dim.19, s32[32]{0:T(128)S(1)} %reshape.377, f32[32,128,128]{2,1,0:T(8,128)} %bitcast.244), kind=kCustom, calls=%fused_computation.1 | custom fusion | flops 524288 | bytes 6291712 | tf_op jit(solution)/shard_map/scatter-add | solution.py:101
  14.4 0.1 reduce_sum.243
  14.5 0.6 gather_fusion
  15.1 0.2 fusion
  15.3 0.1 copy.5
  15.5 0.3 copy-done
  15.8 1.5 %collective-permute-start.4 = (s32[2,128]{1,0:T(2,128)S(1)}, s32[2,128]{1,0:T(2,128)S(1)}, u32[]{:S(2)}, u32[]{:S(2)}) collective-permute-start(s32[2,128]{1,0:T(2,128)S(1)} %pad_add_fusion.2), channel_id=1, source_target_pairs={{0,2},{1,3},{2,0},{3,1},{4,6},{5,7},{6,4},{7,5},{8,10},{9,11},{10,... | collective-permute-start | bytes 3080 | tf_op jit(solution)/shard_map/ppermute | solution.py:37
  17.3 1.9 %fusion.6 = f32[4,128,128]{2,1,0:T(8,128)S(1)} fusion(f32[4,128,512]{1,2,0:T(8,128)S(1)} %bitcast.241, s32[512]{0:T(512)S(1)} %get-tuple-element.59), kind=kOutput, calls=%fused_computation.21 | convolution fusion | flops 402784256 | bytes 1312768 | tf_op jit(solution)/shard_map/dot_general | solution.py:117
  19.3 0.1 collective-permute-done.4
  19.4 0.1 fusion.9
  19.5 0.2 fusion.30
  19.8 1.6 %collective-permute-start.6 = (f32[131,128]{1,0:T(8,128)S(1)}, f32[131,128]{1,0:T(8,128)S(1)}, u32[]{:S(2)}, u32[]{:S(2)}) collective-permute-start(f32[131,128]{1,0:T(8,128)S(1)} %get-tuple-element.67), channel_id=1, source_target_pairs={{0,2},{1,3},{2,0},{3,1},{4,6},{5,7},{6,4},{7,5},{8,10},{9,11},{10,... | collective-permute-start | bytes 201224 | tf_op jit(solution)/shard_map/ppermute | solution.py:59
  21.4 1.4 %collective-permute-start.7 = (f32[131,128]{1,0:T(8,128)S(1)}, f32[131,128]{1,0:T(8,128)S(1)}, u32[]{:S(2)}, u32[]{:S(2)}) collective-permute-start(f32[131,128]{1,0:T(8,128)S(1)} %get-tuple-element.68), channel_id=1, source_target_pairs={{0,3},{1,0},{2,1},{3,2},{4,7},{5,4},{6,5},{7,6},{8,11},{9,8},{10,9... | collective-permute-start | bytes 201224 | tf_op jit(solution)/shard_map/ppermute | solution.py:59
  22.7 0.9 %collective-permute-done.5 = f32[131,128]{1,0:T(8,128)S(1)} collective-permute-done((f32[131,128]{1,0:T(8,128)S(1)}, f32[131,128]{1,0:T(8,128)S(1)}, u32[]{:S(2)}, u32[]{:S(2)}) %collective-permute-start.5) | collective-permute-done | bytes 67104 | tf_op jit(solution)/shard_map/ppermute | solution.py:59
  23.7 0.9 %collective-permute-done.6 = f32[131,128]{1,0:T(8,128)S(1)} collective-permute-done((f32[131,128]{1,0:T(8,128)S(1)}, f32[131,128]{1,0:T(8,128)S(1)}, u32[]{:S(2)}, u32[]{:S(2)}) %collective-permute-start.6) | collective-permute-done | bytes 67104 | tf_op jit(solution)/shard_map/ppermute | solution.py:59
  24.6 0.2 collective-permute-done.7
  24.8 0.1 fusion.96
  24.9 0.1 fusion.35
  25.0 0.9 %collective-permute-start.11 = (f32[128,128]{1,0:T(8,128)S(1)}, f32[128,128]{1,0:T(8,128)S(1)}, u32[]{:S(2)}, u32[]{:S(2)}) collective-permute-start(f32[128,128]{1,0:T(8,128)S(1)} %fusion.35), channel_id=1, source_target_pairs={{0,1},{1,0},{2,3},{3,2},{4,5},{5,4},{6,7},{7,6},{8,9},{9,8},{10,11... | collective-permute-start | bytes 196616 | tf_op jit(solution)/shard_map/ppermute | solution.py:35
  25.9 2.0 %collective-permute-start.9 = (f32[130,128]{1,0:T(8,128)S(1)}, f32[130,128]{1,0:T(8,128)S(1)}, u32[]{:S(2)}, u32[]{:S(2)}) collective-permute-start(f32[130,128]{1,0:T(8,128)S(1)} %get-tuple-element.56), channel_id=1, source_target_pairs={{0,8},{4,12},{8,0},{12,4},{1,9},{5,13},{9,1},{13,5},{2,10},{6,14},... | collective-permute-start | bytes 199688 | tf_op jit(solution)/shard_map/ppermute | solution.py:41
  27.9 1.4 %collective-permute-start.8 = (f32[130,128]{1,0:T(8,128)S(1)}, f32[130,128]{1,0:T(8,128)S(1)}, u32[]{:S(2)}, u32[]{:S(2)}) collective-permute-start(f32[130,128]{1,0:T(8,128)S(1)} %get-tuple-element.56), channel_id=1, source_target_pairs={{0,4},{4,8},{8,12},{12,0},{1,5},{5,9},{9,13},{13,1},{2,6},{6,10},{... | collective-permute-start | bytes 199688 | tf_op jit(solution)/shard_map/ppermute | solution.py:41
  29.4 2.4 %collective-permute-start.10 = (f32[130,128]{1,0:T(8,128)S(1)}, f32[130,128]{1,0:T(8,128)S(1)}, u32[]{:S(2)}, u32[]{:S(2)}) collective-permute-start(f32[130,128]{1,0:T(8,128)S(1)} %get-tuple-element.56), channel_id=1, source_target_pairs={{0,12},{4,0},{8,4},{12,8},{1,13},{5,1},{9,5},{13,9},{2,14},{6,2},{... | collective-permute-start | bytes 199688 | tf_op jit(solution)/shard_map/ppermute | solution.py:41
  31.8 1.6 %collective-permute-start.12 = (f32[2,128,128]{2,1,0:T(8,128)S(1)}, f32[2,128,128]{2,1,0:T(8,128)S(1)}, u32[]{:S(2)}, u32[]{:S(2)}) collective-permute-start(f32[2,128,128]{2,1,0:T(8,128)S(1)} %pad_maximum_fusion.7), channel_id=1, source_target_pairs={{0,2},{1,3},{2,0},{3,1},{4,6},{5,7},{6,4},{7,5},{8,10},{9,11},{10,... | collective-permute-start | bytes 393224 | tf_op jit(solution)/shard_map/ppermute | solution.py:37
  33.3 1.9 %collective-permute-done.8 = f32[130,128]{1,0:T(8,128)S(1)} collective-permute-done((f32[130,128]{1,0:T(8,128)S(1)}, f32[130,128]{1,0:T(8,128)S(1)}, u32[]{:S(2)}, u32[]{:S(2)}) %collective-permute-start.8) | collective-permute-done | bytes 66592 | tf_op jit(solution)/shard_map/ppermute | solution.py:41
  35.2 0.1 multiply_reduce_fusion.3
  35.4 1.4 %collective-permute-done.12 = f32[2,128,128]{2,1,0:T(8,128)S(1)} collective-permute-done((f32[2,128,128]{2,1,0:T(8,128)S(1)}, f32[2,128,128]{2,1,0:T(8,128)S(1)}, u32[]{:S(2)}, u32[]{:S(2)}) %collective-permute-start.12) | collective-permute-done | bytes 131104 | tf_op jit(solution)/shard_map/ppermute | solution.py:37
  36.8 0.2 multiply_subtract_fusion.1
  37.0 1.8 %fusion.89 = f32[4,128,128]{2,1,0:T(8,128)S(1)} fusion(f32[4,128,512]{1,2,0:T(8,128)S(1)} %bitcast.242, f32[512,128,1]{1,0,2:T(8,128)S(1)} %bitcast.248), kind=kOutput, calls=%fused_computation.227 | convolution fusion | flops 402653184 | bytes 1572864 | tf_op jit(solution)/shard_map/dot_general | solution.py:117
  39.1 1.7 %collective-permute-start.15 = (f32[132,128]{1,0:T(8,128)S(1)}, f32[132,128]{1,0:T(8,128)S(1)}, u32[]{:S(2)}, u32[]{:S(2)}) collective-permute-start(f32[132,128]{1,0:T(8,128)S(1)} %concatenate.70), channel_id=1, source_target_pairs={{0,3},{1,0},{2,1},{3,2},{4,7},{5,4},{6,5},{7,6},{8,11},{9,8},{10,9... | collective-permute-start | bytes 202760 | tf_op jit(solution)/shard_map/ppermute | solution.py:59
  40.8 1.5 %collective-permute-start.14 = (f32[132,128]{1,0:T(8,128)S(1)}, f32[132,128]{1,0:T(8,128)S(1)}, u32[]{:S(2)}, u32[]{:S(2)}) collective-permute-start(f32[132,128]{1,0:T(8,128)S(1)} %concatenate.69), channel_id=1, source_target_pairs={{0,2},{1,3},{2,0},{3,1},{4,6},{5,7},{6,4},{7,5},{8,10},{9,11},{10,... | collective-permute-start | bytes 202760 | tf_op jit(solution)/shard_map/ppermute | solution.py:59
  42.3 0.5 collective-permute-done.13
  42.8 0.5 collective-permute-done.15
  43.3 2.2 %collective-permute-done.14 = f32[132,128]{1,0:T(8,128)S(1)} collective-permute-done((f32[132,128]{1,0:T(8,128)S(1)}, f32[132,128]{1,0:T(8,128)S(1)}, u32[]{:S(2)}, u32[]{:S(2)}) %collective-permute-start.14) | collective-permute-done | bytes 67616 | tf_op jit(solution)/shard_map/ppermute | solution.py:59
  45.5 0.1 multiply_subtract_fusion.3
  45.8 0.8 %collective-permute-start.17 = (f32[132,128]{1,0:T(8,128)S(1)}, f32[132,128]{1,0:T(8,128)S(1)}, u32[]{:S(2)}, u32[]{:S(2)}) collective-permute-start(f32[132,128]{1,0:T(8,128)S(1)} %get-tuple-element.54), channel_id=1, source_target_pairs={{0,8},{4,12},{8,0},{12,4},{1,9},{5,13},{9,1},{13,5},{2,10},{6,14},... | collective-permute-start | bytes 202760 | tf_op jit(solution)/shard_map/ppermute | solution.py:41
  46.6 1.1 %collective-permute-start.16 = (f32[132,128]{1,0:T(8,128)S(1)}, f32[132,128]{1,0:T(8,128)S(1)}, u32[]{:S(2)}, u32[]{:S(2)}) collective-permute-start(f32[132,128]{1,0:T(8,128)S(1)} %get-tuple-element.54), channel_id=1, source_target_pairs={{0,4},{4,8},{8,12},{12,0},{1,5},{5,9},{9,13},{13,1},{2,6},{6,10},{... | collective-permute-start | bytes 202760 | tf_op jit(solution)/shard_map/ppermute | solution.py:41
  47.8 2.7 %collective-permute-start.18 = (f32[132,128]{1,0:T(8,128)S(1)}, f32[132,128]{1,0:T(8,128)S(1)}, u32[]{:S(2)}, u32[]{:S(2)}) collective-permute-start(f32[132,128]{1,0:T(8,128)S(1)} %get-tuple-element.54), channel_id=1, source_target_pairs={{0,12},{4,0},{8,4},{12,8},{1,13},{5,1},{9,5},{13,9},{2,14},{6,2},{... | collective-permute-start | bytes 202760 | tf_op jit(solution)/shard_map/ppermute | solution.py:41
  50.5 1.1 %collective-permute-start.20 = (f32[2,128,128]{2,1,0:T(8,128)S(1)}, f32[2,128,128]{2,1,0:T(8,128)S(1)}, u32[]{:S(2)}, u32[]{:S(2)}) collective-permute-start(f32[2,128,128]{2,1,0:T(8,128)S(1)} %pad_maximum_fusion.8), channel_id=1, source_target_pairs={{0,2},{1,3},{2,0},{3,1},{4,6},{5,7},{6,4},{7,5},{8,10},{9,11},{10,... | collective-permute-start | bytes 393224 | tf_op jit(solution)/shard_map/ppermute | solution.py:37
  51.6 2.1 %collective-permute-done.17 = f32[132,128]{1,0:T(8,128)S(1)} collective-permute-done((f32[132,128]{1,0:T(8,128)S(1)}, f32[132,128]{1,0:T(8,128)S(1)}, u32[]{:S(2)}, u32[]{:S(2)}) %collective-permute-start.17) | collective-permute-done | bytes 67616 | tf_op jit(solution)/shard_map/ppermute | solution.py:41
  53.7 1.0 %collective-permute-done.18 = f32[132,128]{1,0:T(8,128)S(1)} collective-permute-done((f32[132,128]{1,0:T(8,128)S(1)}, f32[132,128]{1,0:T(8,128)S(1)}, u32[]{:S(2)}, u32[]{:S(2)}) %collective-permute-start.18) | collective-permute-done | bytes 67616 | tf_op jit(solution)/shard_map/ppermute | solution.py:41
  54.7 0.1 multiply_reduce_fusion.2
  54.9 0.7 collective-permute-done.20
  55.6 0.2 fusion.3
  55.8 1.8 %fusion.90 = f32[4,128,128]{2,1,0:T(8,128)S(1)} fusion(f32[4,128,512]{1,2,0:T(8,128)S(1)} %bitcast.243, f32[512,128,1]{1,0,2:T(8,128)S(1)} %bitcast.247), kind=kOutput, calls=%fused_computation.228 | convolution fusion | flops 402653184 | bytes 1572864 | tf_op jit(solution)/shard_map/dot_general | solution.py:117
  57.9 0.5 collective-permute-start.21
  58.4 1.1 %collective-permute-start.22 = (f32[132,128]{1,0:T(8,128)S(1)}, f32[132,128]{1,0:T(8,128)S(1)}, u32[]{:S(2)}, u32[]{:S(2)}) collective-permute-start(f32[132,128]{1,0:T(8,128)S(1)} %concatenate.74), channel_id=1, source_target_pairs={{0,2},{1,3},{2,0},{3,1},{4,6},{5,7},{6,4},{7,5},{8,10},{9,11},{10,... | collective-permute-start | bytes 202760 | tf_op jit(solution)/shard_map/ppermute | solution.py:59
  59.4 0.5 collective-permute-done.23
  59.9 2.1 %collective-permute-done.21 = f32[132,128]{1,0:T(8,128)S(1)} collective-permute-done((f32[132,128]{1,0:T(8,128)S(1)}, f32[132,128]{1,0:T(8,128)S(1)}, u32[]{:S(2)}, u32[]{:S(2)}) %collective-permute-start.21) | collective-permute-done | bytes 67616 | tf_op jit(solution)/shard_map/ppermute | solution.py:59
  62.0 1.4 %collective-permute-done.22 = f32[132,128]{1,0:T(8,128)S(1)} collective-permute-done((f32[132,128]{1,0:T(8,128)S(1)}, f32[132,128]{1,0:T(8,128)S(1)}, u32[]{:S(2)}, u32[]{:S(2)}) %collective-permute-start.22) | collective-permute-done | bytes 67616 | tf_op jit(solution)/shard_map/ppermute | solution.py:59
  63.4 1.3 %collective-permute-start.26 = (f32[4,128]{1,0:T(4,128)S(1)}, f32[4,128]{1,0:T(4,128)S(1)}, u32[]{:S(2)}, u32[]{:S(2)}) collective-permute-start(f32[4,128]{1,0:T(4,128)S(1)} %select_add_fusion.1), channel_id=1, source_target_pairs={{0,12},{4,0},{8,4},{12,8},{1,13},{5,1},{9,5},{13,9},{2,14},{6,2},{... | collective-permute-start | bytes 6152 | tf_op jit(solution)/shard_map/ppermute | solution.py:41
  64.7 0.7 %collective-permute-start.25 = (f32[4,128]{1,0:T(4,128)S(1)}, f32[4,128]{1,0:T(4,128)S(1)}, u32[]{:S(2)}, u32[]{:S(2)}) collective-permute-start(f32[4,128]{1,0:T(4,128)S(1)} %select_add_fusion.1), channel_id=1, source_target_pairs={{0,8},{4,12},{8,0},{12,4},{1,9},{5,13},{9,1},{13,5},{2,10},{6,14},... | collective-permute-start | bytes 6152 | tf_op jit(solution)/shard_map/ppermute | solution.py:41
  65.5 0.9 %collective-permute-start.24 = (f32[4,128]{1,0:T(4,128)S(1)}, f32[4,128]{1,0:T(4,128)S(1)}, u32[]{:S(2)}, u32[]{:S(2)}) collective-permute-start(f32[4,128]{1,0:T(4,128)S(1)} %select_add_fusion.1), channel_id=1, source_target_pairs={{0,4},{4,8},{8,12},{12,0},{1,5},{5,9},{9,13},{13,1},{2,6},{6,10},{... | collective-permute-start | bytes 6152 | tf_op jit(solution)/shard_map/ppermute | solution.py:41
  66.3 0.7 %collective-permute-done.26 = f32[4,128]{1,0:T(4,128)S(1)} collective-permute-done((f32[4,128]{1,0:T(4,128)S(1)}, f32[4,128]{1,0:T(4,128)S(1)}, u32[]{:S(2)}, u32[]{:S(2)}) %collective-permute-start.26) | collective-permute-done | bytes 2080 | tf_op jit(solution)/shard_map/ppermute | solution.py:41
  67.1 2.1 %collective-permute-done.25 = f32[4,128]{1,0:T(4,128)S(1)} collective-permute-done((f32[4,128]{1,0:T(4,128)S(1)}, f32[4,128]{1,0:T(4,128)S(1)}, u32[]{:S(2)}, u32[]{:S(2)}) %collective-permute-start.25) | collective-permute-done | bytes 2080 | tf_op jit(solution)/shard_map/ppermute | solution.py:41
  69.2 1.6 %collective-permute-done.24 = f32[4,128]{1,0:T(4,128)S(1)} collective-permute-done((f32[4,128]{1,0:T(4,128)S(1)}, f32[4,128]{1,0:T(4,128)S(1)}, u32[]{:S(2)}, u32[]{:S(2)}) %collective-permute-start.24) | collective-permute-done | bytes 2080 | tf_op jit(solution)/shard_map/ppermute | solution.py:41
  70.9 0.8 %fusion.28 = (f32[128,128]{1,0:T(8,128)}, f32[128,128]{1,0:T(8,128)}) fusion(f32[132,128]{1,0:T(8,128)S(1)} %collective-permute-done.23, f32[132,128]{1,0:T(8,128)S(1)} %collective-permute-done.22, f32[132,128]{1,0:T(8,128)S(1)} %collective-permute-done.21, f32[128,128]{1,0:T(8,128)S(1)} %get-tuple-element.34, f32[4,128,128]{2,1,0:T(8,128)S(1)} %fusion.90, ...), kind=kLoop, calls=%fused_computation.78 | loop fusion | flops 425984 | bytes 527876 | tf_op jit(solution)/shard_map/sub | solution.py:171
  (54 shorter events, 1.0 us)
Async XLA Ops:
  0.6 14.8 %collective-permute-start.3 = (s32[128]{0:T(128)}, s32[128]{0:T(128)S(1)}, u32[]{:S(2)}, u32[]{:S(2)}) collective-permute-start(s32[128]{0:T(128)} %bitcast.269), channel_id=1, source_target_pairs={{0,1},{1,0},{2,3},{3,2},{4,5},{5,4},{6,7},{7,6},{8,9},{9,8},{10,11... | collective-permute-start | bytes 1544 | tf_op jit(solution)/shard_map/ppermute | solution.py:35
  1.1 16.1 %collective-permute-start.2 = (s32[128]{0:T(128)}, s32[128]{0:T(128)S(1)}, u32[]{:S(2)}, u32[]{:S(2)}) collective-permute-start(s32[128]{0:T(128)} %bitcast.270), channel_id=1, source_target_pairs={{0,12},{4,0},{8,4},{12,8},{1,13},{5,1},{9,5},{13,9},{2,14},{6,2},{... | collective-permute-start | bytes 1544 | tf_op jit(solution)/shard_map/ppermute | solution.py:41
  5.8 11.5 %collective-permute-start.1 = (s32[128]{0:T(128)}, s32[128]{0:T(128)S(1)}, u32[]{:S(2)}, u32[]{:S(2)}) collective-permute-start(s32[128]{0:T(128)} %bitcast.271), channel_id=1, source_target_pairs={{0,8},{4,12},{8,0},{12,4},{1,9},{5,13},{9,1},{13,5},{2,10},{6,14},... | collective-permute-start | bytes 1544 | tf_op jit(solution)/shard_map/ppermute | solution.py:41
  5.8 11.5 %collective-permute-start = (s32[128]{0:T(128)}, s32[128]{0:T(128)S(1)}, u32[]{:S(2)}, u32[]{:S(2)}) collective-permute-start(s32[128]{0:T(128)} %bitcast.272), channel_id=1, source_target_pairs={{0,4},{4,8},{8,12},{12,0},{1,5},{5,9},{9,13},{13,1},{2,6},{6,10},{... | collective-permute-start | bytes 1544 | tf_op jit(solution)/shard_map/ppermute | solution.py:41
  15.1 0.7 copy-start
  15.8 3.6 %collective-permute-start.4 = (s32[2,128]{1,0:T(2,128)S(1)}, s32[2,128]{1,0:T(2,128)S(1)}, u32[]{:S(2)}, u32[]{:S(2)}) collective-permute-start(s32[2,128]{1,0:T(2,128)S(1)} %pad_add_fusion.2), channel_id=1, source_target_pairs={{0,2},{1,3},{2,0},{3,1},{4,6},{5,7},{6,4},{7,5},{8,10},{9,11},{10,... | collective-permute-start | bytes 3080 | tf_op jit(solution)/shard_map/ppermute | solution.py:37
  19.7 3.9 %collective-permute-start.5 = (f32[131,128]{1,0:T(8,128)S(1)}, f32[131,128]{1,0:T(8,128)S(1)}, u32[]{:S(2)}, u32[]{:S(2)}) collective-permute-start(f32[131,128]{1,0:T(8,128)S(1)} %get-tuple-element.66), channel_id=1, source_target_pairs={{0,1},{1,2},{2,3},{3,0},{4,5},{5,6},{6,7},{7,4},{8,9},{9,10},{10,1... | collective-permute-start | bytes 201224 | tf_op jit(solution)/shard_map/ppermute | solution.py:59
  19.8 4.8 %collective-permute-start.6 = (f32[131,128]{1,0:T(8,128)S(1)}, f32[131,128]{1,0:T(8,128)S(1)}, u32[]{:S(2)}, u32[]{:S(2)}) collective-permute-start(f32[131,128]{1,0:T(8,128)S(1)} %get-tuple-element.67), channel_id=1, source_target_pairs={{0,2},{1,3},{2,0},{3,1},{4,6},{5,7},{6,4},{7,5},{8,10},{9,11},{10,... | collective-permute-start | bytes 201224 | tf_op jit(solution)/shard_map/ppermute | solution.py:59
  21.4 3.4 %collective-permute-start.7 = (f32[131,128]{1,0:T(8,128)S(1)}, f32[131,128]{1,0:T(8,128)S(1)}, u32[]{:S(2)}, u32[]{:S(2)}) collective-permute-start(f32[131,128]{1,0:T(8,128)S(1)} %get-tuple-element.68), channel_id=1, source_target_pairs={{0,3},{1,0},{2,1},{3,2},{4,7},{5,4},{6,5},{7,6},{8,11},{9,8},{10,9... | collective-permute-start | bytes 201224 | tf_op jit(solution)/shard_map/ppermute | solution.py:59
  25.0 6.8 %collective-permute-start.11 = (f32[128,128]{1,0:T(8,128)S(1)}, f32[128,128]{1,0:T(8,128)S(1)}, u32[]{:S(2)}, u32[]{:S(2)}) collective-permute-start(f32[128,128]{1,0:T(8,128)S(1)} %fusion.35), channel_id=1, source_target_pairs={{0,1},{1,0},{2,3},{3,2},{4,5},{5,4},{6,7},{7,6},{8,9},{9,8},{10,11... | collective-permute-start | bytes 196616 | tf_op jit(solution)/shard_map/ppermute | solution.py:35
  25.9 7.4 %collective-permute-start.9 = (f32[130,128]{1,0:T(8,128)S(1)}, f32[130,128]{1,0:T(8,128)S(1)}, u32[]{:S(2)}, u32[]{:S(2)}) collective-permute-start(f32[130,128]{1,0:T(8,128)S(1)} %get-tuple-element.56), channel_id=1, source_target_pairs={{0,8},{4,12},{8,0},{12,4},{1,9},{5,13},{9,1},{13,5},{2,10},{6,14},... | collective-permute-start | bytes 199688 | tf_op jit(solution)/shard_map/ppermute | solution.py:41
  27.9 7.3 %collective-permute-start.8 = (f32[130,128]{1,0:T(8,128)S(1)}, f32[130,128]{1,0:T(8,128)S(1)}, u32[]{:S(2)}, u32[]{:S(2)}) collective-permute-start(f32[130,128]{1,0:T(8,128)S(1)} %get-tuple-element.56), channel_id=1, source_target_pairs={{0,4},{4,8},{8,12},{12,0},{1,5},{5,9},{9,13},{13,1},{2,6},{6,10},{... | collective-permute-start | bytes 199688 | tf_op jit(solution)/shard_map/ppermute | solution.py:41
  29.4 5.8 %collective-permute-start.10 = (f32[130,128]{1,0:T(8,128)S(1)}, f32[130,128]{1,0:T(8,128)S(1)}, u32[]{:S(2)}, u32[]{:S(2)}) collective-permute-start(f32[130,128]{1,0:T(8,128)S(1)} %get-tuple-element.56), channel_id=1, source_target_pairs={{0,12},{4,0},{8,4},{12,8},{1,13},{5,1},{9,5},{13,9},{2,14},{6,2},{... | collective-permute-start | bytes 199688 | tf_op jit(solution)/shard_map/ppermute | solution.py:41
  31.8 5.0 %collective-permute-start.12 = (f32[2,128,128]{2,1,0:T(8,128)S(1)}, f32[2,128,128]{2,1,0:T(8,128)S(1)}, u32[]{:S(2)}, u32[]{:S(2)}) collective-permute-start(f32[2,128,128]{2,1,0:T(8,128)S(1)} %pad_maximum_fusion.7), channel_id=1, source_target_pairs={{0,2},{1,3},{2,0},{3,1},{4,6},{5,7},{6,4},{7,5},{8,10},{9,11},{10,... | collective-permute-start | bytes 393224 | tf_op jit(solution)/shard_map/ppermute | solution.py:37
  39.0 3.8 %collective-permute-start.13 = (f32[132,128]{1,0:T(8,128)S(1)}, f32[132,128]{1,0:T(8,128)S(1)}, u32[]{:S(2)}, u32[]{:S(2)}) collective-permute-start(f32[132,128]{1,0:T(8,128)S(1)} %concatenate.68), channel_id=1, source_target_pairs={{0,1},{1,2},{2,3},{3,0},{4,5},{5,6},{6,7},{7,4},{8,9},{9,10},{10,1... | collective-permute-start | bytes 202760 | tf_op jit(solution)/shard_map/ppermute | solution.py:59
  39.1 4.2 %collective-permute-start.15 = (f32[132,128]{1,0:T(8,128)S(1)}, f32[132,128]{1,0:T(8,128)S(1)}, u32[]{:S(2)}, u32[]{:S(2)}) collective-permute-start(f32[132,128]{1,0:T(8,128)S(1)} %concatenate.70), channel_id=1, source_target_pairs={{0,3},{1,0},{2,1},{3,2},{4,7},{5,4},{6,5},{7,6},{8,11},{9,8},{10,9... | collective-permute-start | bytes 202760 | tf_op jit(solution)/shard_map/ppermute | solution.py:59
  40.8 4.7 %collective-permute-start.14 = (f32[132,128]{1,0:T(8,128)S(1)}, f32[132,128]{1,0:T(8,128)S(1)}, u32[]{:S(2)}, u32[]{:S(2)}) collective-permute-start(f32[132,128]{1,0:T(8,128)S(1)} %concatenate.69), channel_id=1, source_target_pairs={{0,2},{1,3},{2,0},{3,1},{4,6},{5,7},{6,4},{7,5},{8,10},{9,11},{10,... | collective-permute-start | bytes 202760 | tf_op jit(solution)/shard_map/ppermute | solution.py:59
  45.7 4.8 %collective-permute-start.19 = (f32[128,128]{1,0:T(8,128)S(1)}, f32[128,128]{1,0:T(8,128)S(1)}, u32[]{:S(2)}, u32[]{:S(2)}) collective-permute-start(f32[128,128]{1,0:T(8,128)S(1)} %multiply_subtract_fusion.3), channel_id=1, source_target_pairs={{0,1},{1,0},{2,3},{3,2},{4,5},{5,4},{6,7},{7,6},{8,9},{9,8},{10,11... | collective-permute-start | bytes 196616 | tf_op jit(solution)/shard_map/ppermute | solution.py:35
  45.8 7.9 %collective-permute-start.17 = (f32[132,128]{1,0:T(8,128)S(1)}, f32[132,128]{1,0:T(8,128)S(1)}, u32[]{:S(2)}, u32[]{:S(2)}) collective-permute-start(f32[132,128]{1,0:T(8,128)S(1)} %get-tuple-element.54), channel_id=1, source_target_pairs={{0,8},{4,12},{8,0},{12,4},{1,9},{5,13},{9,1},{13,5},{2,10},{6,14},... | collective-permute-start | bytes 202760 | tf_op jit(solution)/shard_map/ppermute | solution.py:41
  46.6 7.1 %collective-permute-start.16 = (f32[132,128]{1,0:T(8,128)S(1)}, f32[132,128]{1,0:T(8,128)S(1)}, u32[]{:S(2)}, u32[]{:S(2)}) collective-permute-start(f32[132,128]{1,0:T(8,128)S(1)} %get-tuple-element.54), channel_id=1, source_target_pairs={{0,4},{4,8},{8,12},{12,0},{1,5},{5,9},{9,13},{13,1},{2,6},{6,10},{... | collective-permute-start | bytes 202760 | tf_op jit(solution)/shard_map/ppermute | solution.py:41
  47.8 7.0 %collective-permute-start.18 = (f32[132,128]{1,0:T(8,128)S(1)}, f32[132,128]{1,0:T(8,128)S(1)}, u32[]{:S(2)}, u32[]{:S(2)}) collective-permute-start(f32[132,128]{1,0:T(8,128)S(1)} %get-tuple-element.54), channel_id=1, source_target_pairs={{0,12},{4,0},{8,4},{12,8},{1,13},{5,1},{9,5},{13,9},{2,14},{6,2},{... | collective-permute-start | bytes 202760 | tf_op jit(solution)/shard_map/ppermute | solution.py:41
  50.5 5.1 %collective-permute-start.20 = (f32[2,128,128]{2,1,0:T(8,128)S(1)}, f32[2,128,128]{2,1,0:T(8,128)S(1)}, u32[]{:S(2)}, u32[]{:S(2)}) collective-permute-start(f32[2,128,128]{2,1,0:T(8,128)S(1)} %pad_maximum_fusion.8), channel_id=1, source_target_pairs={{0,2},{1,3},{2,0},{3,1},{4,6},{5,7},{6,4},{7,5},{8,10},{9,11},{10,... | collective-permute-start | bytes 393224 | tf_op jit(solution)/shard_map/ppermute | solution.py:37
  57.8 2.1 %collective-permute-start.23 = (f32[132,128]{1,0:T(8,128)S(1)}, f32[132,128]{1,0:T(8,128)S(1)}, u32[]{:S(2)}, u32[]{:S(2)}) collective-permute-start(f32[132,128]{1,0:T(8,128)S(1)} %concatenate.75), channel_id=1, source_target_pairs={{0,3},{1,0},{2,1},{3,2},{4,7},{5,4},{6,5},{7,6},{8,11},{9,8},{10,9... | collective-permute-start | bytes 202760 | tf_op jit(solution)/shard_map/ppermute | solution.py:59
  57.9 4.1 %collective-permute-start.21 = (f32[132,128]{1,0:T(8,128)S(1)}, f32[132,128]{1,0:T(8,128)S(1)}, u32[]{:S(2)}, u32[]{:S(2)}) collective-permute-start(f32[132,128]{1,0:T(8,128)S(1)} %concatenate.73), channel_id=1, source_target_pairs={{0,1},{1,2},{2,3},{3,0},{4,5},{5,6},{6,7},{7,4},{8,9},{9,10},{10,1... | collective-permute-start | bytes 202760 | tf_op jit(solution)/shard_map/ppermute | solution.py:59
  58.4 5.1 %collective-permute-start.22 = (f32[132,128]{1,0:T(8,128)S(1)}, f32[132,128]{1,0:T(8,128)S(1)}, u32[]{:S(2)}, u32[]{:S(2)}) collective-permute-start(f32[132,128]{1,0:T(8,128)S(1)} %concatenate.74), channel_id=1, source_target_pairs={{0,2},{1,3},{2,0},{3,1},{4,6},{5,7},{6,4},{7,5},{8,10},{9,11},{10,... | collective-permute-start | bytes 202760 | tf_op jit(solution)/shard_map/ppermute | solution.py:59
  63.4 3.6 %collective-permute-start.26 = (f32[4,128]{1,0:T(4,128)S(1)}, f32[4,128]{1,0:T(4,128)S(1)}, u32[]{:S(2)}, u32[]{:S(2)}) collective-permute-start(f32[4,128]{1,0:T(4,128)S(1)} %select_add_fusion.1), channel_id=1, source_target_pairs={{0,12},{4,0},{8,4},{12,8},{1,13},{5,1},{9,5},{13,9},{2,14},{6,2},{... | collective-permute-start | bytes 6152 | tf_op jit(solution)/shard_map/ppermute | solution.py:41
  64.7 4.5 %collective-permute-start.25 = (f32[4,128]{1,0:T(4,128)S(1)}, f32[4,128]{1,0:T(4,128)S(1)}, u32[]{:S(2)}, u32[]{:S(2)}) collective-permute-start(f32[4,128]{1,0:T(4,128)S(1)} %select_add_fusion.1), channel_id=1, source_target_pairs={{0,8},{4,12},{8,0},{12,4},{1,9},{5,13},{9,1},{13,5},{2,10},{6,14},... | collective-permute-start | bytes 6152 | tf_op jit(solution)/shard_map/ppermute | solution.py:41
  65.5 5.4 %collective-permute-start.24 = (f32[4,128]{1,0:T(4,128)S(1)}, f32[4,128]{1,0:T(4,128)S(1)}, u32[]{:S(2)}, u32[]{:S(2)}) collective-permute-start(f32[4,128]{1,0:T(4,128)S(1)} %select_add_fusion.1), channel_id=1, source_target_pairs={{0,4},{4,8},{8,12},{12,0},{1,5},{5,9},{9,13},{13,1},{2,6},{6,10},{... | collective-permute-start | bytes 6152 | tf_op jit(solution)/shard_map/ppermute | solution.py:41

commit v16 on v14

--- a/solution.py
+++ b/solution.py
@@ -135,7 +135,7 @@
 
     def wide_step(applied, narrow_sums, last):
         if last:
-            sums = canonical_sum(gather_blocks(narrow_sums, "wide", n_wide), "wide", n_wide)
+            sums = jnp.sum(lax.all_gather(narrow_sums, "wide", axis=0, tiled=False), axis=0)
             return None, None, sums
         got = gather_blocks(jnp.concatenate([applied, narrow_sums], axis=0), "wide", n_wide)
         sums = canonical_sum(got[:, own_rows:], "wide", n_wide)

time: 64.5 us -> 69.6 us (1.079)
  blocking collectives: 0 us -> 11.9 us
  starting transfers between devices: 33.5 us -> 28.9 us
  waiting for transfers between devices: 18.2 us -> 16 us
    all_gather x0 -> x1, blocking collectives: none -> 11.9 us  [wide_step(): lax.all_gather(narrow_sums, 'wide', axis=0, tiled=False)]
    ppermute x12 -> x9, starting transfers between devices: 20.1 us -> 15.6 us  [gather_blocks(): parts.append(lax.ppermute(values, axis, pairs))]
    ppermute x12 -> x9, waiting for transfers between devices: 9.23 us -> 7.04 us  [gather_blocks(): parts.append(lax.ppermute(values, axis, pairs))]
  transfers between devices with their start and end apart: 27 -> 24, of which waited for: 17 -> 14; matrix products, arithmetic and copies ran while one was open for 12% -> 11% of each run, Pallas kernels for 0% -> 0%
where the time goes in v16:
time: 69.6 us; the launch traced here: 69.4 us
  starting transfers between devices  28.9 us (42%)
  waiting for transfers between devices  16 us (23%)
  blocking collectives  11.9 us (17%)
  other arithmetic  7.3 us (10%)
  matrix products  3.02 us (4%)
  local copies, waits for them, and re-layouts  1.34 us (2%)
  between operations  1 us (1%)
    ppermute x9, starting transfers between devices, gather_blocks(): parts.append(lax.ppermute(values, axis, pairs))  15.6 us
    all_gather x1, blocking collectives, wide_step(): lax.all_gather(narrow_sums, 'wide', axis=0, tiled=False)  11.9 us
    ppermute x9, starting transfers between devices, scatter_with(): got = lax.ppermute(jnp.concatenate([sent, extra], axis=0), axis, pairs)  7.95 us
    ppermute x9, waiting for transfers between devices, scatter_with(): got = lax.ppermute(jnp.concatenate([sent, extra], axis=0), axis, pairs)  7.81 us
    ppermute x9, waiting for transfers between devices, gather_blocks(): parts.append(lax.ppermute(values, axis, pairs))  7.04 us
    ppermute x3, starting transfers between devices, gather_blocks(): lax.ppermute(both, axis, [(i, i ^ 2) for i in range(count)])  4.47 us
    dot_general x3, matrix products, product(): jnp.dot(transposed, row_values.reshape(groups * tile, width), precision=l...  3.02 us
    reduce_sum x1, other arithmetic, local(): column_sums = jnp.sum(dense, axis=(0, 1)).reshape(n_narrow, own_rows)  2.97 us
  transfers between devices with their start and end apart: 24, of which 14 were waited for; matrix products, arithmetic and copies ran while one was open for 11% of the time, Pallas kernels for 0%

profile of v16, /device:TPU:0, one launch (start us, length us, event | category | flops | bytes accessed | tf_op | source)
XLA Modules:
  0.0 69.4 jit_solution(13781452735980364219)
XLA Ops:
  0.6 3.1 %collective-permute-start = (s32[128]{0:T(128)}, s32[128]{0:T(128)S(1)}, u32[]{:S(2)}, u32[]{:S(2)}) collective-permute-start(s32[128]{0:T(128)} %bitcast.268), channel_id=1, source_target_pairs={{0,4},{4,8},{8,12},{12,0},{1,5},{5,9},{9,13},{13,1},{2,6},{6,10},{... | collective-permute-start | bytes 1544 | tf_op jit(solution)/shard_map/ppermute | solution.py:41
  3.7 2.6 %collective-permute-start.1 = (s32[128]{0:T(128)}, s32[128]{0:T(128)S(1)}, u32[]{:S(2)}, u32[]{:S(2)}) collective-permute-start(s32[128]{0:T(128)} %bitcast.269), channel_id=1, source_target_pairs={{0,8},{4,12},{8,0},{12,4},{1,9},{5,13},{9,1},{13,5},{2,10},{6,14},... | collective-permute-start | bytes 1544 | tf_op jit(solution)/shard_map/ppermute | solution.py:41
  6.3 1.3 %collective-permute-start.2 = (s32[128]{0:T(128)}, s32[128]{0:T(128)S(1)}, u32[]{:S(2)}, u32[]{:S(2)}) collective-permute-start(s32[128]{0:T(128)} %bitcast.270), channel_id=1, source_target_pairs={{0,12},{4,0},{8,4},{12,8},{1,13},{5,1},{9,5},{13,9},{2,14},{6,2},{... | collective-permute-start | bytes 1544 | tf_op jit(solution)/shard_map/ppermute | solution.py:41
  7.6 0.0 collective-permute-start.3
  7.7 0.7 fusion.77
  8.4 0.8 %compare_and_fusion = pred[4,8,4]{2,1,0:T(8,128)(4,1)S(1)} fusion(s32[4]{0:T(128)S(1)} %get-tuple-element.73, s32[4]{0:T(128)S(1)} %get-tuple-element.74, s32[4,8]{1,0:T(4,128)} %param.4), kind=kLoop, calls=%fused_computation.141 | loop fusion | flops 384 | bytes 288 | tf_op jit(solution)/shard_map/and | solution.py:100
  9.1 3.0 %select_reduce_fusion = (f32[4,128]{1,0:T(4,128)S(1)}, f32[4,128,4,128]{3,1,2,0:T(8,128)S(1)}) fusion(f32[4,8,128,128]{3,2,1,0:T(8,128)} %param.3, pred[4,8,4]{2,1,0:T(8,128)(4,1)S(1)} %compare_and_fusion), kind=kLoop, calls=%fused_computation.1 | loop fusion | flops 6028800 | bytes 3147904 | tf_op jit(solution)/shard_map/reduce_sum | solution.py:107
  12.1 0.1 copy_bitcast_fusion
  12.2 0.1 broadcast_bitcast_fusion
  12.3 0.1 fusion.32
  12.4 0.6 gather_fusion
  13.1 0.1 bitcast_select_fusion
  13.3 0.3 copy.8
  13.7 1.6 %collective-permute-start.4 = (s32[2,128]{1,0:T(2,128)S(1)}, s32[2,128]{1,0:T(2,128)S(1)}, u32[]{:S(2)}, u32[]{:S(2)}) collective-permute-start(s32[2,128]{1,0:T(2,128)S(1)} %pad_add_fusion.2), channel_id=1, source_target_pairs={{0,2},{1,3},{2,0},{3,1},{4,6},{5,7},{6,4},{7,5},{8,10},{9,11},{10,... | collective-permute-start | bytes 3080 | tf_op jit(solution)/shard_map/ppermute | solution.py:37
  15.2 1.0 %fusion.5 = f32[4,128,128]{2,1,0:T(8,128)S(1)} fusion(f32[4,128,512]{2,1,0:T(8,128)S(1)} %bitcast.240, s32[512]{0:T(512)S(1)} %get-tuple-element.61), kind=kOutput, calls=%fused_computation.22 | convolution fusion | flops 402784256 | bytes 1312768 | tf_op jit(solution)/shard_map/dot_general | solution.py:121
  16.3 1.0 %collective-permute-done.4 = s32[2,128]{1,0:T(2,128)S(1)} collective-permute-done((s32[2,128]{1,0:T(2,128)S(1)}, s32[2,128]{1,0:T(2,128)S(1)}, u32[]{:S(2)}, u32[]{:S(2)}) %collective-permute-start.4) | collective-permute-done | bytes 1056 | tf_op jit(solution)/shard_map/ppermute | solution.py:37
  17.3 0.1 fusion.8
  17.4 0.2 fusion.29
  17.7 0.1 collective-permute-start.5
  17.7 1.6 %collective-permute-start.6 = (f32[131,128]{1,0:T(8,128)S(1)}, f32[131,128]{1,0:T(8,128)S(1)}, u32[]{:S(2)}, u32[]{:S(2)}) collective-permute-start(f32[131,128]{1,0:T(8,128)S(1)} %get-tuple-element.69), channel_id=1, source_target_pairs={{0,2},{1,3},{2,0},{3,1},{4,6},{5,7},{6,4},{7,5},{8,10},{9,11},{10,... | collective-permute-start | bytes 201224 | tf_op jit(solution)/shard_map/ppermute | solution.py:59
  19.3 1.4 %collective-permute-start.7 = (f32[131,128]{1,0:T(8,128)S(1)}, f32[131,128]{1,0:T(8,128)S(1)}, u32[]{:S(2)}, u32[]{:S(2)}) collective-permute-start(f32[131,128]{1,0:T(8,128)S(1)} %get-tuple-element.70), channel_id=1, source_target_pairs={{0,3},{1,0},{2,1},{3,2},{4,7},{5,4},{6,5},{7,6},{8,11},{9,8},{10,9... | collective-permute-start | bytes 201224 | tf_op jit(solution)/shard_map/ppermute | solution.py:59
  20.7 0.9 %collective-permute-done.5 = f32[131,128]{1,0:T(8,128)S(1)} collective-permute-done((f32[131,128]{1,0:T(8,128)S(1)}, f32[131,128]{1,0:T(8,128)S(1)}, u32[]{:S(2)}, u32[]{:S(2)}) %collective-permute-start.5) | collective-permute-done | bytes 67104 | tf_op jit(solution)/shard_map/ppermute | solution.py:59
  21.6 1.0 %collective-permute-done.6 = f32[131,128]{1,0:T(8,128)S(1)} collective-permute-done((f32[131,128]{1,0:T(8,128)S(1)}, f32[131,128]{1,0:T(8,128)S(1)}, u32[]{:S(2)}, u32[]{:S(2)}) %collective-permute-start.6) | collective-permute-done | bytes 67104 | tf_op jit(solution)/shard_map/ppermute | solution.py:59
  22.5 0.2 collective-permute-done.7
  22.7 0.1 fusion.88
  22.8 0.1 fusion.34
  22.9 0.9 %collective-permute-start.11 = (f32[128,128]{1,0:T(8,128)S(1)}, f32[128,128]{1,0:T(8,128)S(1)}, u32[]{:S(2)}, u32[]{:S(2)}) collective-permute-start(f32[128,128]{1,0:T(8,128)S(1)} %fusion.34), channel_id=1, source_target_pairs={{0,1},{1,0},{2,3},{3,2},{4,5},{5,4},{6,7},{7,6},{8,9},{9,8},{10,11... | collective-permute-start | bytes 196616 | tf_op jit(solution)/shard_map/ppermute | solution.py:35
  23.8 0.7 %collective-permute-start.8 = (f32[130,128]{1,0:T(8,128)S(1)}, f32[130,128]{1,0:T(8,128)S(1)}, u32[]{:S(2)}, u32[]{:S(2)}) collective-permute-start(f32[130,128]{1,0:T(8,128)S(1)} %get-tuple-element.58), channel_id=1, source_target_pairs={{0,4},{4,8},{8,12},{12,0},{1,5},{5,9},{9,13},{13,1},{2,6},{6,10},{... | collective-permute-start | bytes 199688 | tf_op jit(solution)/shard_map/ppermute | solution.py:41
  24.6 0.3 collective-permute-start.9
  24.9 2.8 %collective-permute-start.10 = (f32[130,128]{1,0:T(8,128)S(1)}, f32[130,128]{1,0:T(8,128)S(1)}, u32[]{:S(2)}, u32[]{:S(2)}) collective-permute-start(f32[130,128]{1,0:T(8,128)S(1)} %get-tuple-element.58), channel_id=1, source_target_pairs={{0,12},{4,0},{8,4},{12,8},{1,13},{5,1},{9,5},{13,9},{2,14},{6,2},{... | collective-permute-start | bytes 199688 | tf_op jit(solution)/shard_map/ppermute | solution.py:41
  27.7 0.0 collective-permute-done.11
  27.7 1.6 %collective-permute-start.12 = (f32[2,128,128]{2,1,0:T(8,128)S(1)}, f32[2,128,128]{2,1,0:T(8,128)S(1)}, u32[]{:S(2)}, u32[]{:S(2)}) collective-permute-start(f32[2,128,128]{2,1,0:T(8,128)S(1)} %pad_maximum_fusion.7), channel_id=1, source_target_pairs={{0,2},{1,3},{2,0},{3,1},{4,6},{5,7},{6,4},{7,5},{8,10},{9,11},{10,... | collective-permute-start | bytes 393224 | tf_op jit(solution)/shard_map/ppermute | solution.py:37
  29.3 1.5 %collective-permute-done.8 = f32[130,128]{1,0:T(8,128)S(1)} collective-permute-done((f32[130,128]{1,0:T(8,128)S(1)}, f32[130,128]{1,0:T(8,128)S(1)}, u32[]{:S(2)}, u32[]{:S(2)}) %collective-permute-start.8) | collective-permute-done | bytes 66592 | tf_op jit(solution)/shard_map/ppermute | solution.py:41
  30.8 2.1 %collective-permute-done.9 = f32[130,128]{1,0:T(8,128)S(1)} collective-permute-done((f32[130,128]{1,0:T(8,128)S(1)}, f32[130,128]{1,0:T(8,128)S(1)}, u32[]{:S(2)}, u32[]{:S(2)}) %collective-permute-start.9) | collective-permute-done | bytes 66592 | tf_op jit(solution)/shard_map/ppermute | solution.py:41
  32.9 0.0 collective-permute-done.10
  33.0 0.1 multiply_reduce_fusion.3
  33.1 0.0 collective-permute-done.12
  33.1 0.2 multiply_subtract_fusion.1
  33.3 1.0 %fusion.81 = f32[4,128,128]{2,1,0:T(8,128)S(1)} fusion(f32[4,128,512]{2,1,0:T(8,128)S(1)} %bitcast.241, f32[512,128,1]{1,0,2:T(8,128)S(1)} %bitcast.247), kind=kOutput, calls=%fused_computation.214 | convolution fusion | flops 402653184 | bytes 1572864 | tf_op jit(solution)/shard_map/dot_general | solution.py:121
  34.4 1.5 %collective-permute-start.14 = (f32[132,128]{1,0:T(8,128)S(1)}, f32[132,128]{1,0:T(8,128)S(1)}, u32[]{:S(2)}, u32[]{:S(2)}) collective-permute-start(f32[132,128]{1,0:T(8,128)S(1)} %concatenate.65), channel_id=1, source_target_pairs={{0,2},{1,3},{2,0},{3,1},{4,6},{5,7},{6,4},{7,5},{8,10},{9,11},{10,... | collective-permute-start | bytes 202760 | tf_op jit(solution)/shard_map/ppermute | solution.py:59
  36.0 0.0 collective-permute-start.15
  36.1 0.5 collective-permute-start.13
  36.6 2.2 %collective-permute-done.14 = f32[132,128]{1,0:T(8,128)S(1)} collective-permute-done((f32[132,128]{1,0:T(8,128)S(1)}, f32[132,128]{1,0:T(8,128)S(1)}, u32[]{:S(2)}, u32[]{:S(2)}) %collective-permute-start.14) | collective-permute-done | bytes 67616 | tf_op jit(solution)/shard_map/ppermute | solution.py:59
  38.8 0.5 collective-permute-done.15
  39.3 1.0 %collective-permute-done.13 = f32[132,128]{1,0:T(8,128)S(1)} collective-permute-done((f32[132,128]{1,0:T(8,128)S(1)}, f32[132,128]{1,0:T(8,128)S(1)}, u32[]{:S(2)}, u32[]{:S(2)}) %collective-permute-start.13) | collective-permute-done | bytes 67616 | tf_op jit(solution)/shard_map/ppermute | solution.py:59
  40.3 0.1 multiply_subtract_fusion.3
  40.4 0.1 collective-permute-start.19
  40.5 1.5 %collective-permute-start.16 = (f32[132,128]{1,0:T(8,128)S(1)}, f32[132,128]{1,0:T(8,128)S(1)}, u32[]{:S(2)}, u32[]{:S(2)}) collective-permute-start(f32[132,128]{1,0:T(8,128)S(1)} %get-tuple-element.56), channel_id=1, source_target_pairs={{0,4},{4,8},{8,12},{12,0},{1,5},{5,9},{9,13},{13,1},{2,6},{6,10},{... | collective-permute-start | bytes 202760 | tf_op jit(solution)/shard_map/ppermute | solution.py:41
  42.0 0.9 %collective-permute-start.17 = (f32[132,128]{1,0:T(8,128)S(1)}, f32[132,128]{1,0:T(8,128)S(1)}, u32[]{:S(2)}, u32[]{:S(2)}) collective-permute-start(f32[132,128]{1,0:T(8,128)S(1)} %get-tuple-element.56), channel_id=1, source_target_pairs={{0,8},{4,12},{8,0},{12,4},{1,9},{5,13},{9,1},{13,5},{2,10},{6,14},... | collective-permute-start | bytes 202760 | tf_op jit(solution)/shard_map/ppermute | solution.py:41
  43.0 2.2 %collective-permute-start.18 = (f32[132,128]{1,0:T(8,128)S(1)}, f32[132,128]{1,0:T(8,128)S(1)}, u32[]{:S(2)}, u32[]{:S(2)}) collective-permute-start(f32[132,128]{1,0:T(8,128)S(1)} %get-tuple-element.56), channel_id=1, source_target_pairs={{0,12},{4,0},{8,4},{12,8},{1,13},{5,1},{9,5},{13,9},{2,14},{6,2},{... | collective-permute-start | bytes 202760 | tf_op jit(solution)/shard_map/ppermute | solution.py:41
  45.2 1.4 %collective-permute-start.20 = (f32[2,128,128]{2,1,0:T(8,128)S(1)}, f32[2,128,128]{2,1,0:T(8,128)S(1)}, u32[]{:S(2)}, u32[]{:S(2)}) collective-permute-start(f32[2,128,128]{2,1,0:T(8,128)S(1)} %pad_maximum_fusion.8), channel_id=1, source_target_pairs={{0,2},{1,3},{2,0},{3,1},{4,6},{5,7},{6,4},{7,5},{8,10},{9,11},{10,... | collective-permute-start | bytes 393224 | tf_op jit(solution)/shard_map/ppermute | solution.py:37
  46.6 0.9 %collective-permute-done.16 = f32[132,128]{1,0:T(8,128)S(1)} collective-permute-done((f32[132,128]{1,0:T(8,128)S(1)}, f32[132,128]{1,0:T(8,128)S(1)}, u32[]{:S(2)}, u32[]{:S(2)}) %collective-permute-start.16) | collective-permute-done | bytes 67616 | tf_op jit(solution)/shard_map/ppermute | solution.py:41
  47.5 2.5 %collective-permute-done.17 = f32[132,128]{1,0:T(8,128)S(1)} collective-permute-done((f32[132,128]{1,0:T(8,128)S(1)}, f32[132,128]{1,0:T(8,128)S(1)}, u32[]{:S(2)}, u32[]{:S(2)}) %collective-permute-start.17) | collective-permute-done | bytes 67616 | tf_op jit(solution)/shard_map/ppermute | solution.py:41
  50.1 0.1 multiply_reduce_fusion.2
  50.2 0.1 collective-permute-done.20
  50.4 0.2 fusion.2
  50.6 1.0 %fusion.82 = f32[4,128,128]{2,1,0:T(8,128)S(1)} fusion(f32[4,128,512]{2,1,0:T(8,128)S(1)} %bitcast.242, f32[512,128,1]{1,0,2:T(8,128)S(1)} %bitcast.246), kind=kOutput, calls=%fused_computation.215 | convolution fusion | flops 402653184 | bytes 1572864 | tf_op jit(solution)/shard_map/dot_general | solution.py:121
  51.7 0.1 collective-permute-start.21
  51.8 1.3 %collective-permute-start.22 = (f32[132,128]{1,0:T(8,128)S(1)}, f32[132,128]{1,0:T(8,128)S(1)}, u32[]{:S(2)}, u32[]{:S(2)}) collective-permute-start(f32[132,128]{1,0:T(8,128)S(1)} %concatenate.70), channel_id=1, source_target_pairs={{0,2},{1,3},{2,0},{3,1},{4,6},{5,7},{6,4},{7,5},{8,10},{9,11},{10,... | collective-permute-start | bytes 202760 | tf_op jit(solution)/shard_map/ppermute | solution.py:59
  53.1 1.5 %collective-permute-start.23 = (f32[132,128]{1,0:T(8,128)S(1)}, f32[132,128]{1,0:T(8,128)S(1)}, u32[]{:S(2)}, u32[]{:S(2)}) collective-permute-start(f32[132,128]{1,0:T(8,128)S(1)} %concatenate.71), channel_id=1, source_target_pairs={{0,3},{1,0},{2,1},{3,2},{4,7},{5,4},{6,5},{7,6},{8,11},{9,8},{10,9... | collective-permute-start | bytes 202760 | tf_op jit(solution)/shard_map/ppermute | solution.py:59
  54.6 1.0 %collective-permute-done.21 = f32[132,128]{1,0:T(8,128)S(1)} collective-permute-done((f32[132,128]{1,0:T(8,128)S(1)}, f32[132,128]{1,0:T(8,128)S(1)}, u32[]{:S(2)}, u32[]{:S(2)}) %collective-permute-start.21) | collective-permute-done | bytes 67616 | tf_op jit(solution)/shard_map/ppermute | solution.py:59
  55.6 1.1 %collective-permute-done.22 = f32[132,128]{1,0:T(8,128)S(1)} collective-permute-done((f32[132,128]{1,0:T(8,128)S(1)}, f32[132,128]{1,0:T(8,128)S(1)}, u32[]{:S(2)}, u32[]{:S(2)}) %collective-permute-start.22) | collective-permute-done | bytes 67616 | tf_op jit(solution)/shard_map/ppermute | solution.py:59
  56.7 11.9 %all-gather.1 = f32[4,4,128]{2,1,0:T(4,128)S(1)} all-gather(f32[1,4,128]{2,1,0:T(4,128)S(1)} %add_bitcast_fusion), channel_id=2, replica_groups=mesh['vol'=2,'wide'=4,'narrow'=4] {'wide'}, dimensions={0}, use_global_device_ids=true | all-gather | bytes 10240 | tf_op jit(solution)/shard_map/all_gather | solution.py:138
  68.6 0.8 %fusion.27 = (f32[128,128]{1,0:T(8,128)}, f32[128,128]{1,0:T(8,128)}) fusion(f32[132,128]{1,0:T(8,128)S(1)} %collective-permute-done.23, f32[132,128]{1,0:T(8,128)S(1)} %collective-permute-done.22, f32[132,128]{1,0:T(8,128)S(1)} %collective-permute-done.21, f32[128,128]{1,0:T(8,128)S(1)} %get-tuple-element.36, f32[4,128,128]{2,1,0:T(8,128)S(1)} %fusion.82, ...), kind=kLoop, calls=%fused_computation.79 | loop fusion | flops 425984 | bytes 527876 | tf_op jit(solution)/shard_map/sub | solution.py:175
  (49 shorter events, 0.8 us)
Async XLA Ops:
  0.6 14.6 %collective-permute-start = (s32[128]{0:T(128)}, s32[128]{0:T(128)S(1)}, u32[]{:S(2)}, u32[]{:S(2)}) collective-permute-start(s32[128]{0:T(128)} %bitcast.268), channel_id=1, source_target_pairs={{0,4},{4,8},{8,12},{12,0},{1,5},{5,9},{9,13},{13,1},{2,6},{6,10},{... | collective-permute-start | bytes 1544 | tf_op jit(solution)/shard_map/ppermute | solution.py:41
  3.7 11.5 %collective-permute-start.1 = (s32[128]{0:T(128)}, s32[128]{0:T(128)S(1)}, u32[]{:S(2)}, u32[]{:S(2)}) collective-permute-start(s32[128]{0:T(128)} %bitcast.269), channel_id=1, source_target_pairs={{0,8},{4,12},{8,0},{12,4},{1,9},{5,13},{9,1},{13,5},{2,10},{6,14},... | collective-permute-start | bytes 1544 | tf_op jit(solution)/shard_map/ppermute | solution.py:41
  6.3 8.9 %collective-permute-start.2 = (s32[128]{0:T(128)}, s32[128]{0:T(128)S(1)}, u32[]{:S(2)}, u32[]{:S(2)}) collective-permute-start(s32[128]{0:T(128)} %bitcast.270), channel_id=1, source_target_pairs={{0,12},{4,0},{8,4},{12,8},{1,13},{5,1},{9,5},{13,9},{2,14},{6,2},{... | collective-permute-start | bytes 1544 | tf_op jit(solution)/shard_map/ppermute | solution.py:41
  7.6 6.0 %collective-permute-start.3 = (s32[128]{0:T(128)}, s32[128]{0:T(128)S(1)}, u32[]{:S(2)}, u32[]{:S(2)}) collective-permute-start(s32[128]{0:T(128)} %bitcast.271), channel_id=1, source_target_pairs={{0,1},{1,0},{2,3},{3,2},{4,5},{5,4},{6,7},{7,6},{8,9},{9,8},{10,11... | collective-permute-start | bytes 1544 | tf_op jit(solution)/shard_map/ppermute | solution.py:35
  9.1 3.2 %copy-start = (s32[128,1]{0,1:T(1,128)S(1)}, s32[128,1]{0,1:T(1,128)}, u32[]{:S(2)}) copy-start(s32[128,1]{0,1:T(1,128)} %param.5) | copy-start | bytes 1540
  13.7 3.6 %collective-permute-start.4 = (s32[2,128]{1,0:T(2,128)S(1)}, s32[2,128]{1,0:T(2,128)S(1)}, u32[]{:S(2)}, u32[]{:S(2)}) collective-permute-start(s32[2,128]{1,0:T(2,128)S(1)} %pad_add_fusion.2), channel_id=1, source_target_pairs={{0,2},{1,3},{2,0},{3,1},{4,6},{5,7},{6,4},{7,5},{8,10},{9,11},{10,... | collective-permute-start | bytes 3080 | tf_op jit(solution)/shard_map/ppermute | solution.py:37
  17.7 3.9 %collective-permute-start.5 = (f32[131,128]{1,0:T(8,128)S(1)}, f32[131,128]{1,0:T(8,128)S(1)}, u32[]{:S(2)}, u32[]{:S(2)}) collective-permute-start(f32[131,128]{1,0:T(8,128)S(1)} %get-tuple-element.68), channel_id=1, source_target_pairs={{0,1},{1,2},{2,3},{3,0},{4,5},{5,6},{6,7},{7,4},{8,9},{9,10},{10,1... | collective-permute-start | bytes 201224 | tf_op jit(solution)/shard_map/ppermute | solution.py:59
  17.7 4.8 %collective-permute-start.6 = (f32[131,128]{1,0:T(8,128)S(1)}, f32[131,128]{1,0:T(8,128)S(1)}, u32[]{:S(2)}, u32[]{:S(2)}) collective-permute-start(f32[131,128]{1,0:T(8,128)S(1)} %get-tuple-element.69), channel_id=1, source_target_pairs={{0,2},{1,3},{2,0},{3,1},{4,6},{5,7},{6,4},{7,5},{8,10},{9,11},{10,... | collective-permute-start | bytes 201224 | tf_op jit(solution)/shard_map/ppermute | solution.py:59
  19.3 3.4 %collective-permute-start.7 = (f32[131,128]{1,0:T(8,128)S(1)}, f32[131,128]{1,0:T(8,128)S(1)}, u32[]{:S(2)}, u32[]{:S(2)}) collective-permute-start(f32[131,128]{1,0:T(8,128)S(1)} %get-tuple-element.70), channel_id=1, source_target_pairs={{0,3},{1,0},{2,1},{3,2},{4,7},{5,4},{6,5},{7,6},{8,11},{9,8},{10,9... | collective-permute-start | bytes 201224 | tf_op jit(solution)/shard_map/ppermute | solution.py:59
  22.9 4.8 %collective-permute-start.11 = (f32[128,128]{1,0:T(8,128)S(1)}, f32[128,128]{1,0:T(8,128)S(1)}, u32[]{:S(2)}, u32[]{:S(2)}) collective-permute-start(f32[128,128]{1,0:T(8,128)S(1)} %fusion.34), channel_id=1, source_target_pairs={{0,1},{1,0},{2,3},{3,2},{4,5},{5,4},{6,7},{7,6},{8,9},{9,8},{10,11... | collective-permute-start | bytes 196616 | tf_op jit(solution)/shard_map/ppermute | solution.py:35
  23.8 7.0 %collective-permute-start.8 = (f32[130,128]{1,0:T(8,128)S(1)}, f32[130,128]{1,0:T(8,128)S(1)}, u32[]{:S(2)}, u32[]{:S(2)}) collective-permute-start(f32[130,128]{1,0:T(8,128)S(1)} %get-tuple-element.58), channel_id=1, source_target_pairs={{0,4},{4,8},{8,12},{12,0},{1,5},{5,9},{9,13},{13,1},{2,6},{6,10},{... | collective-permute-start | bytes 199688 | tf_op jit(solution)/shard_map/ppermute | solution.py:41
  24.6 8.3 %collective-permute-start.9 = (f32[130,128]{1,0:T(8,128)S(1)}, f32[130,128]{1,0:T(8,128)S(1)}, u32[]{:S(2)}, u32[]{:S(2)}) collective-permute-start(f32[130,128]{1,0:T(8,128)S(1)} %get-tuple-element.58), channel_id=1, source_target_pairs={{0,8},{4,12},{8,0},{12,4},{1,9},{5,13},{9,1},{13,5},{2,10},{6,14},... | collective-permute-start | bytes 199688 | tf_op jit(solution)/shard_map/ppermute | solution.py:41
  24.9 8.0 %collective-permute-start.10 = (f32[130,128]{1,0:T(8,128)S(1)}, f32[130,128]{1,0:T(8,128)S(1)}, u32[]{:S(2)}, u32[]{:S(2)}) collective-permute-start(f32[130,128]{1,0:T(8,128)S(1)} %get-tuple-element.58), channel_id=1, source_target_pairs={{0,12},{4,0},{8,4},{12,8},{1,13},{5,1},{9,5},{13,9},{2,14},{6,2},{... | collective-permute-start | bytes 199688 | tf_op jit(solution)/shard_map/ppermute | solution.py:41
  27.7 5.3 %collective-permute-start.12 = (f32[2,128,128]{2,1,0:T(8,128)S(1)}, f32[2,128,128]{2,1,0:T(8,128)S(1)}, u32[]{:S(2)}, u32[]{:S(2)}) collective-permute-start(f32[2,128,128]{2,1,0:T(8,128)S(1)} %pad_maximum_fusion.7), channel_id=1, source_target_pairs={{0,2},{1,3},{2,0},{3,1},{4,6},{5,7},{6,4},{7,5},{8,10},{9,11},{10,... | collective-permute-start | bytes 393224 | tf_op jit(solution)/shard_map/ppermute | solution.py:37
  34.4 4.4 %collective-permute-start.14 = (f32[132,128]{1,0:T(8,128)S(1)}, f32[132,128]{1,0:T(8,128)S(1)}, u32[]{:S(2)}, u32[]{:S(2)}) collective-permute-start(f32[132,128]{1,0:T(8,128)S(1)} %concatenate.65), channel_id=1, source_target_pairs={{0,2},{1,3},{2,0},{3,1},{4,6},{5,7},{6,4},{7,5},{8,10},{9,11},{10,... | collective-permute-start | bytes 202760 | tf_op jit(solution)/shard_map/ppermute | solution.py:59
  36.0 3.3 %collective-permute-start.15 = (f32[132,128]{1,0:T(8,128)S(1)}, f32[132,128]{1,0:T(8,128)S(1)}, u32[]{:S(2)}, u32[]{:S(2)}) collective-permute-start(f32[132,128]{1,0:T(8,128)S(1)} %concatenate.66), channel_id=1, source_target_pairs={{0,3},{1,0},{2,1},{3,2},{4,7},{5,4},{6,5},{7,6},{8,11},{9,8},{10,9... | collective-permute-start | bytes 202760 | tf_op jit(solution)/shard_map/ppermute | solution.py:59
  36.1 4.2 %collective-permute-start.13 = (f32[132,128]{1,0:T(8,128)S(1)}, f32[132,128]{1,0:T(8,128)S(1)}, u32[]{:S(2)}, u32[]{:S(2)}) collective-permute-start(f32[132,128]{1,0:T(8,128)S(1)} %concatenate.64), channel_id=1, source_target_pairs={{0,1},{1,2},{2,3},{3,0},{4,5},{5,6},{6,7},{7,4},{8,9},{9,10},{10,1... | collective-permute-start | bytes 202760 | tf_op jit(solution)/shard_map/ppermute | solution.py:59
  40.4 4.8 %collective-permute-start.19 = (f32[128,128]{1,0:T(8,128)S(1)}, f32[128,128]{1,0:T(8,128)S(1)}, u32[]{:S(2)}, u32[]{:S(2)}) collective-permute-start(f32[128,128]{1,0:T(8,128)S(1)} %multiply_subtract_fusion.3), channel_id=1, source_target_pairs={{0,1},{1,0},{2,3},{3,2},{4,5},{5,4},{6,7},{7,6},{8,9},{9,8},{10,11... | collective-permute-start | bytes 196616 | tf_op jit(solution)/shard_map/ppermute | solution.py:35
  40.5 6.9 %collective-permute-start.16 = (f32[132,128]{1,0:T(8,128)S(1)}, f32[132,128]{1,0:T(8,128)S(1)}, u32[]{:S(2)}, u32[]{:S(2)}) collective-permute-start(f32[132,128]{1,0:T(8,128)S(1)} %get-tuple-element.56), channel_id=1, source_target_pairs={{0,4},{4,8},{8,12},{12,0},{1,5},{5,9},{9,13},{13,1},{2,6},{6,10},{... | collective-permute-start | bytes 202760 | tf_op jit(solution)/shard_map/ppermute | solution.py:41
  42.0 8.0 %collective-permute-start.17 = (f32[132,128]{1,0:T(8,128)S(1)}, f32[132,128]{1,0:T(8,128)S(1)}, u32[]{:S(2)}, u32[]{:S(2)}) collective-permute-start(f32[132,128]{1,0:T(8,128)S(1)} %get-tuple-element.56), channel_id=1, source_target_pairs={{0,8},{4,12},{8,0},{12,4},{1,9},{5,13},{9,1},{13,5},{2,10},{6,14},... | collective-permute-start | bytes 202760 | tf_op jit(solution)/shard_map/ppermute | solution.py:41
  43.0 7.0 %collective-permute-start.18 = (f32[132,128]{1,0:T(8,128)S(1)}, f32[132,128]{1,0:T(8,128)S(1)}, u32[]{:S(2)}, u32[]{:S(2)}) collective-permute-start(f32[132,128]{1,0:T(8,128)S(1)} %get-tuple-element.56), channel_id=1, source_target_pairs={{0,12},{4,0},{8,4},{12,8},{1,13},{5,1},{9,5},{13,9},{2,14},{6,2},{... | collective-permute-start | bytes 202760 | tf_op jit(solution)/shard_map/ppermute | solution.py:41
  45.2 5.1 %collective-permute-start.20 = (f32[2,128,128]{2,1,0:T(8,128)S(1)}, f32[2,128,128]{2,1,0:T(8,128)S(1)}, u32[]{:S(2)}, u32[]{:S(2)}) collective-permute-start(f32[2,128,128]{2,1,0:T(8,128)S(1)} %pad_maximum_fusion.8), channel_id=1, source_target_pairs={{0,2},{1,3},{2,0},{3,1},{4,6},{5,7},{6,4},{7,5},{8,10},{9,11},{10,... | collective-permute-start | bytes 393224 | tf_op jit(solution)/shard_map/ppermute | solution.py:37
  51.7 3.9 %collective-permute-start.21 = (f32[132,128]{1,0:T(8,128)S(1)}, f32[132,128]{1,0:T(8,128)S(1)}, u32[]{:S(2)}, u32[]{:S(2)}) collective-permute-start(f32[132,128]{1,0:T(8,128)S(1)} %concatenate.69), channel_id=1, source_target_pairs={{0,1},{1,2},{2,3},{3,0},{4,5},{5,6},{6,7},{7,4},{8,9},{9,10},{10,1... | collective-permute-start | bytes 202760 | tf_op jit(solution)/shard_map/ppermute | solution.py:59
  51.8 4.9 %collective-permute-start.22 = (f32[132,128]{1,0:T(8,128)S(1)}, f32[132,128]{1,0:T(8,128)S(1)}, u32[]{:S(2)}, u32[]{:S(2)}) collective-permute-start(f32[132,128]{1,0:T(8,128)S(1)} %concatenate.70), channel_id=1, source_target_pairs={{0,2},{1,3},{2,0},{3,1},{4,6},{5,7},{6,4},{7,5},{8,10},{9,11},{10,... | collective-permute-start | bytes 202760 | tf_op jit(solution)/shard_map/ppermute | solution.py:59
  53.1 3.6 %collective-permute-start.23 = (f32[132,128]{1,0:T(8,128)S(1)}, f32[132,128]{1,0:T(8,128)S(1)}, u32[]{:S(2)}, u32[]{:S(2)}) collective-permute-start(f32[132,128]{1,0:T(8,128)S(1)} %concatenate.71), channel_id=1, source_target_pairs={{0,3},{1,0},{2,1},{3,2},{4,7},{5,4},{6,5},{7,6},{8,11},{9,8},{10,9... | collective-permute-start | bytes 202760 | tf_op jit(solution)/shard_map/ppermute | solution.py:59

commit v17 on v10

--- a/solution.py
+++ b/solution.py
@@ -31,10 +31,15 @@
 def gather_blocks(values, axis, count):
     if count > 4:
         return lax.all_gather(values, axis, axis=0, tiled=False)
-    if count == 4:
+    if axis == "narrow" and count == 4:
         partner = lax.ppermute(values, axis, [(i, i ^ 1) for i in range(count)])
         both = jnp.stack([values, partner])
         return jnp.concatenate([both, lax.ppermute(both, axis, [(i, i ^ 2) for i in range(count)])])
+    if axis == "wide" and count == 4:
+        parts = [values]
+        for mask in range(1, count):
+            parts.append(lax.ppermute(values, axis, [(i, i ^ mask) for i in range(count)]))
+        return jnp.stack(parts)
     parts = [values]
     for shift in range(1, count):
         pairs = [(i, (i + shift) % count) for i in range(count)]
@@ -94,8 +99,13 @@
     n_all = n_wide * n_narrow
     width = SEED_CLASSES
     column_blocks = n_narrow * br_local
-    local_column = pattern // groups * br_local + pattern % br_local
-    pick = local_column[:, :, None] == jnp.arange(column_blocks, dtype=local_column.dtype)
+    blocks_of = jnp.arange(column_blocks, dtype=pattern.dtype)
+    if br_local == 1:
+        low = pattern[:, :, None] >= blocks_of * groups
+        pick = low & (pattern[:, :, None] < (blocks_of + 1) * groups)
+    else:
+        local_column = pattern // groups * br_local + pattern % br_local
+        pick = local_column[:, :, None] == blocks_of
     dense = jnp.sum(
         jnp.where(pick[:, :, None, :, None], tiles[:, :, :, None, :], 0.0), axis=1
     )

time: 72.6 us -> 66.8 us (0.920)
  waiting for transfers between devices: 36.2 us -> 21.2 us
  starting transfers between devices: 22.8 us -> 32.8 us
    ppermute x0 -> x12, starting transfers between devices: none -> 19 us  [gather_blocks(): lax.ppermute(values, axis, [(i, i ^ mask) for i in range(count)])]
    ppermute x7 -> x3, waiting for transfers between devices: 16 us -> 0.74 us  [gather_blocks(): lax.ppermute(both, axis, [(i, i ^ 2) for i in range(count)])]
    ppermute x0 -> x12, waiting for transfers between devices: none -> 12.5 us  [gather_blocks(): lax.ppermute(values, axis, [(i, i ^ mask) for i in range(count)])]
    ppermute x7 -> x3, waiting for transfers between devices: 10.8 us -> 0.01 us  [gather_blocks(): partner = lax.ppermute(values, axis, [(i, i ^ 1) for i in range(count)])]
    ppermute x7 -> x3, starting transfers between devices: 10.6 us -> 4.9 us  [gather_blocks(): lax.ppermute(both, axis, [(i, i ^ 2) for i in range(count)])]
    ppermute x7 -> x3, starting transfers between devices: 5.2 us -> 0.72 us  [gather_blocks(): partner = lax.ppermute(values, axis, [(i, i ^ 1) for i in range(count)])]
    ppermute x9, waiting for transfers between devices: 9.38 us -> 7.96 us  [scatter_with(): got = lax.ppermute(jnp.concatenate([sent, extra], axis=0), axis, pairs)]
    ppermute x9, starting transfers between devices: 6.97 us -> 8.1 us  [scatter_with(): got = lax.ppermute(jnp.concatenate([sent, extra], axis=0), axis, pairs)]
  transfers between devices with their start and end apart: 23 -> 27, of which waited for: 13 -> 14; matrix products, arithmetic and copies ran while one was open for 9% -> 11% of each run, Pallas kernels for 0% -> 0%
where the time goes in v17:
time: 66.8 us; the launch traced here: 66.6 us
  starting transfers between devices  32.8 us (49%)
  waiting for transfers between devices  21.2 us (32%)
  other arithmetic  7.28 us (11%)
  matrix products  3.02 us (5%)
  local copies, waits for them, and re-layouts  1.34 us (2%)
  between operations  1.03 us (2%)
    ppermute x12, starting transfers between devices, gather_blocks(): lax.ppermute(values, axis, [(i, i ^ mask) for i in range(count)])  19 us
    ppermute x12, waiting for transfers between devices, gather_blocks(): lax.ppermute(values, axis, [(i, i ^ mask) for i in range(count)])  12.5 us
    ppermute x9, starting transfers between devices, scatter_with(): got = lax.ppermute(jnp.concatenate([sent, extra], axis=0), axis, pairs)  8.1 us
    ppermute x9, waiting for transfers between devices, scatter_with(): got = lax.ppermute(jnp.concatenate([sent, extra], axis=0), axis, pairs)  7.96 us
    ppermute x3, starting transfers between devices, gather_blocks(): lax.ppermute(both, axis, [(i, i ^ 2) for i in range(count)])  4.9 us
    dot_general x3, matrix products, product(): jnp.dot(transposed, row_values.reshape(groups * tile, width), precision=l...  3.02 us
    reduce_sum x1, other arithmetic, local(): column_sums = jnp.sum(dense, axis=(0, 1)).reshape(n_narrow, own_rows)  2.97 us
  transfers between devices with their start and end apart: 27, of which 14 were waited for; matrix products, arithmetic and copies ran while one was open for 11% of the time, Pallas kernels for 0%

profile of v17, /device:TPU:0, one launch (start us, length us, event | category | flops | bytes accessed | tf_op | source)
XLA Modules:
  0.0 66.6 jit_solution(4049594217403933714)
XLA Ops:
  0.6 3.1 %collective-permute-start = (s32[128]{0:T(128)}, s32[128]{0:T(128)S(1)}, u32[]{:S(2)}, u32[]{:S(2)}) collective-permute-start(s32[128]{0:T(128)} %bitcast.266), channel_id=1, source_target_pairs={{0,4},{4,0},{8,12},{12,8},{1,5},{5,1},{9,13},{13,9},{2,6},{6,2},{1... | collective-permute-start | bytes 1544 | tf_op jit(solution)/shard_map/ppermute | solution.py:41
  3.7 2.6 %collective-permute-start.1 = (s32[128]{0:T(128)}, s32[128]{0:T(128)S(1)}, u32[]{:S(2)}, u32[]{:S(2)}) collective-permute-start(s32[128]{0:T(128)} %bitcast.267), channel_id=1, source_target_pairs={{0,8},{4,12},{8,0},{12,4},{1,9},{5,13},{9,1},{13,5},{2,10},{6,14},... | collective-permute-start | bytes 1544 | tf_op jit(solution)/shard_map/ppermute | solution.py:41
  6.4 0.7 %fusion.75 = f32[128]{0:T(128)S(1)} fusion(s32[128,1]{0,1:T(1,128)} %param.5), kind=kLoop, calls=%fused_computation.203 | loop fusion | flops 384 | bytes 1024 | tf_op jit(solution)/shard_map/mul | solution.py:167
  7.0 0.8 %compare_and_fusion = pred[4,8,4]{2,1,0:T(8,128)(4,1)S(1)} fusion(s32[4]{0:T(128)S(1)} %get-tuple-element.73, s32[4]{0:T(128)S(1)} %get-tuple-element.74, s32[4,8]{1,0:T(4,128)} %param.4), kind=kLoop, calls=%fused_computation.141 | loop fusion | flops 384 | bytes 288 | tf_op jit(solution)/shard_map/and | solution.py:105
  7.8 3.0 %select_reduce_fusion = (f32[4,128]{1,0:T(4,128)S(1)}, f32[4,128,4,128]{3,1,2,0:T(8,128)S(1)}) fusion(f32[4,8,128,128]{3,2,1,0:T(8,128)} %param.3, pred[4,8,4]{2,1,0:T(8,128)(4,1)S(1)} %compare_and_fusion), kind=kLoop, calls=%fused_computation.1 | loop fusion | flops 6028800 | bytes 3147904 | tf_op jit(solution)/shard_map/reduce_sum | solution.py:112
  10.8 0.1 copy_bitcast_fusion
  10.9 0.1 broadcast_bitcast_fusion
  11.0 0.1 fusion.32
  11.1 0.6 gather_fusion
  11.7 0.1 bitcast_select_fusion
  11.9 0.3 copy.7
  12.3 0.0 collective-permute-done.3
  12.3 1.8 %collective-permute-start.4 = (s32[2,128]{1,0:T(2,128)S(1)}, s32[2,128]{1,0:T(2,128)S(1)}, u32[]{:S(2)}, u32[]{:S(2)}) collective-permute-start(s32[2,128]{1,0:T(2,128)S(1)} %pad_add_fusion.2), channel_id=1, source_target_pairs={{0,2},{1,3},{2,0},{3,1},{4,6},{5,7},{6,4},{7,5},{8,10},{9,11},{10,... | collective-permute-start | bytes 3080 | tf_op jit(solution)/shard_map/ppermute | solution.py:37
  14.1 0.0 collective-permute-done
  14.1 0.0 collective-permute-done.1
  14.1 0.0 collective-permute-done.2
  14.1 1.0 %fusion.5 = f32[4,128,128]{2,1,0:T(8,128)S(1)} fusion(f32[4,128,512]{2,1,0:T(8,128)S(1)} %bitcast.238, s32[512]{0:T(512)S(1)} %get-tuple-element.61), kind=kOutput, calls=%fused_computation.22 | convolution fusion | flops 402784256 | bytes 1312768 | tf_op jit(solution)/shard_map/dot_general | solution.py:126
  15.2 0.7 %collective-permute-done.4 = s32[2,128]{1,0:T(2,128)S(1)} collective-permute-done((s32[2,128]{1,0:T(2,128)S(1)}, s32[2,128]{1,0:T(2,128)S(1)}, u32[]{:S(2)}, u32[]{:S(2)}) %collective-permute-start.4) | collective-permute-done | bytes 1056 | tf_op jit(solution)/shard_map/ppermute | solution.py:37
  16.0 0.1 fusion.8
  16.1 0.2 fusion.29
  16.3 0.1 collective-permute-start.5
  16.4 1.8 %collective-permute-start.6 = (f32[131,128]{1,0:T(8,128)S(1)}, f32[131,128]{1,0:T(8,128)S(1)}, u32[]{:S(2)}, u32[]{:S(2)}) collective-permute-start(f32[131,128]{1,0:T(8,128)S(1)} %get-tuple-element.69), channel_id=1, source_target_pairs={{0,2},{1,3},{2,0},{3,1},{4,6},{5,7},{6,4},{7,5},{8,10},{9,11},{10,... | collective-permute-start | bytes 201224 | tf_op jit(solution)/shard_map/ppermute | solution.py:64
  18.2 1.4 %collective-permute-start.7 = (f32[131,128]{1,0:T(8,128)S(1)}, f32[131,128]{1,0:T(8,128)S(1)}, u32[]{:S(2)}, u32[]{:S(2)}) collective-permute-start(f32[131,128]{1,0:T(8,128)S(1)} %get-tuple-element.70), channel_id=1, source_target_pairs={{0,3},{1,0},{2,1},{3,2},{4,7},{5,4},{6,5},{7,6},{8,11},{9,8},{10,9... | collective-permute-start | bytes 201224 | tf_op jit(solution)/shard_map/ppermute | solution.py:64
  19.6 0.7 %collective-permute-done.5 = f32[131,128]{1,0:T(8,128)S(1)} collective-permute-done((f32[131,128]{1,0:T(8,128)S(1)}, f32[131,128]{1,0:T(8,128)S(1)}, u32[]{:S(2)}, u32[]{:S(2)}) %collective-permute-start.5) | collective-permute-done | bytes 67104 | tf_op jit(solution)/shard_map/ppermute | solution.py:64
  20.2 0.7 %collective-permute-done.6 = f32[131,128]{1,0:T(8,128)S(1)} collective-permute-done((f32[131,128]{1,0:T(8,128)S(1)}, f32[131,128]{1,0:T(8,128)S(1)}, u32[]{:S(2)}, u32[]{:S(2)}) %collective-permute-start.6) | collective-permute-done | bytes 67104 | tf_op jit(solution)/shard_map/ppermute | solution.py:64
  20.9 0.6 collective-permute-done.7
  21.6 0.1 fusion.86
  21.7 0.1 fusion.34
  21.8 0.7 collective-permute-start.11
  22.5 1.0 %collective-permute-start.8 = (f32[130,128]{1,0:T(8,128)S(1)}, f32[130,128]{1,0:T(8,128)S(1)}, u32[]{:S(2)}, u32[]{:S(2)}) collective-permute-start(f32[130,128]{1,0:T(8,128)S(1)} %get-tuple-element.58), channel_id=1, source_target_pairs={{0,4},{4,0},{8,12},{12,8},{1,5},{5,1},{9,13},{13,9},{2,6},{6,2},{1... | collective-permute-start | bytes 199688 | tf_op jit(solution)/shard_map/ppermute | solution.py:41
  23.5 3.5 %collective-permute-start.9 = (f32[130,128]{1,0:T(8,128)S(1)}, f32[130,128]{1,0:T(8,128)S(1)}, u32[]{:S(2)}, u32[]{:S(2)}) collective-permute-start(f32[130,128]{1,0:T(8,128)S(1)} %get-tuple-element.58), channel_id=1, source_target_pairs={{0,8},{4,12},{8,0},{12,4},{1,9},{5,13},{9,1},{13,5},{2,10},{6,14},... | collective-permute-start | bytes 199688 | tf_op jit(solution)/shard_map/ppermute | solution.py:41
  27.0 1.8 %collective-permute-start.12 = (f32[2,128,128]{2,1,0:T(8,128)S(1)}, f32[2,128,128]{2,1,0:T(8,128)S(1)}, u32[]{:S(2)}, u32[]{:S(2)}) collective-permute-start(f32[2,128,128]{2,1,0:T(8,128)S(1)} %pad_maximum_fusion.7), channel_id=1, source_target_pairs={{0,2},{1,3},{2,0},{3,1},{4,6},{5,7},{6,4},{7,5},{8,10},{9,11},{10,... | collective-permute-start | bytes 393224 | tf_op jit(solution)/shard_map/ppermute | solution.py:37
  28.8 3.1 %collective-permute-done.9 = f32[130,128]{1,0:T(8,128)S(1)} collective-permute-done((f32[130,128]{1,0:T(8,128)S(1)}, f32[130,128]{1,0:T(8,128)S(1)}, u32[]{:S(2)}, u32[]{:S(2)}) %collective-permute-start.9) | collective-permute-done | bytes 66592 | tf_op jit(solution)/shard_map/ppermute | solution.py:41
  31.9 1.3 %collective-permute-done.10 = f32[130,128]{1,0:T(8,128)S(1)} collective-permute-done((f32[130,128]{1,0:T(8,128)S(1)}, f32[130,128]{1,0:T(8,128)S(1)}, u32[]{:S(2)}, u32[]{:S(2)}) %collective-permute-start.10) | collective-permute-done | bytes 66592 | tf_op jit(solution)/shard_map/ppermute | solution.py:41
  33.2 0.1 multiply_reduce_fusion.3
  33.4 0.2 multiply_subtract_fusion.1
  33.6 1.0 %fusion.79 = f32[4,128,128]{2,1,0:T(8,128)S(1)} fusion(f32[4,128,512]{2,1,0:T(8,128)S(1)} %bitcast.239, f32[512,128,1]{1,0,2:T(8,128)S(1)} %bitcast.245), kind=kOutput, calls=%fused_computation.207 | convolution fusion | flops 402653184 | bytes 1572864 | tf_op jit(solution)/shard_map/dot_general | solution.py:126
  34.7 1.5 %collective-permute-start.14 = (f32[132,128]{1,0:T(8,128)S(1)}, f32[132,128]{1,0:T(8,128)S(1)}, u32[]{:S(2)}, u32[]{:S(2)}) collective-permute-start(f32[132,128]{1,0:T(8,128)S(1)} %concatenate.65), channel_id=1, source_target_pairs={{0,2},{1,3},{2,0},{3,1},{4,6},{5,7},{6,4},{7,5},{8,10},{9,11},{10,... | collective-permute-start | bytes 202760 | tf_op jit(solution)/shard_map/ppermute | solution.py:64
  36.3 0.0 collective-permute-start.15
  36.4 0.5 collective-permute-start.13
  36.9 2.2 %collective-permute-done.14 = f32[132,128]{1,0:T(8,128)S(1)} collective-permute-done((f32[132,128]{1,0:T(8,128)S(1)}, f32[132,128]{1,0:T(8,128)S(1)}, u32[]{:S(2)}, u32[]{:S(2)}) %collective-permute-start.14) | collective-permute-done | bytes 67616 | tf_op jit(solution)/shard_map/ppermute | solution.py:64
  39.1 0.5 collective-permute-done.15
  39.6 1.0 %collective-permute-done.13 = f32[132,128]{1,0:T(8,128)S(1)} collective-permute-done((f32[132,128]{1,0:T(8,128)S(1)}, f32[132,128]{1,0:T(8,128)S(1)}, u32[]{:S(2)}, u32[]{:S(2)}) %collective-permute-start.13) | collective-permute-done | bytes 67616 | tf_op jit(solution)/shard_map/ppermute | solution.py:64
  40.6 0.1 multiply_subtract_fusion.3
  40.7 0.1 collective-permute-start.19
  40.8 1.0 %collective-permute-start.16 = (f32[132,128]{1,0:T(8,128)S(1)}, f32[132,128]{1,0:T(8,128)S(1)}, u32[]{:S(2)}, u32[]{:S(2)}) collective-permute-start(f32[132,128]{1,0:T(8,128)S(1)} %get-tuple-element.56), channel_id=1, source_target_pairs={{0,4},{4,0},{8,12},{12,8},{1,5},{5,1},{9,13},{13,9},{2,6},{6,2},{1... | collective-permute-start | bytes 202760 | tf_op jit(solution)/shard_map/ppermute | solution.py:41
  41.8 2.1 %collective-permute-start.17 = (f32[132,128]{1,0:T(8,128)S(1)}, f32[132,128]{1,0:T(8,128)S(1)}, u32[]{:S(2)}, u32[]{:S(2)}) collective-permute-start(f32[132,128]{1,0:T(8,128)S(1)} %get-tuple-element.56), channel_id=1, source_target_pairs={{0,8},{4,12},{8,0},{12,4},{1,9},{5,13},{9,1},{13,5},{2,10},{6,14},... | collective-permute-start | bytes 202760 | tf_op jit(solution)/shard_map/ppermute | solution.py:41
  43.9 1.3 %collective-permute-start.18 = (f32[132,128]{1,0:T(8,128)S(1)}, f32[132,128]{1,0:T(8,128)S(1)}, u32[]{:S(2)}, u32[]{:S(2)}) collective-permute-start(f32[132,128]{1,0:T(8,128)S(1)} %get-tuple-element.56), channel_id=1, source_target_pairs={{0,12},{4,8},{8,4},{12,0},{1,13},{5,9},{9,5},{13,1},{2,14},{6,10},... | collective-permute-start | bytes 202760 | tf_op jit(solution)/shard_map/ppermute | solution.py:41
  45.3 1.4 %collective-permute-start.20 = (f32[2,128,128]{2,1,0:T(8,128)S(1)}, f32[2,128,128]{2,1,0:T(8,128)S(1)}, u32[]{:S(2)}, u32[]{:S(2)}) collective-permute-start(f32[2,128,128]{2,1,0:T(8,128)S(1)} %pad_maximum_fusion.8), channel_id=1, source_target_pairs={{0,2},{1,3},{2,0},{3,1},{4,6},{5,7},{6,4},{7,5},{8,10},{9,11},{10,... | collective-permute-start | bytes 393224 | tf_op jit(solution)/shard_map/ppermute | solution.py:37
  46.6 3.8 %collective-permute-done.17 = f32[132,128]{1,0:T(8,128)S(1)} collective-permute-done((f32[132,128]{1,0:T(8,128)S(1)}, f32[132,128]{1,0:T(8,128)S(1)}, u32[]{:S(2)}, u32[]{:S(2)}) %collective-permute-start.17) | collective-permute-done | bytes 67616 | tf_op jit(solution)/shard_map/ppermute | solution.py:41
  50.5 0.1 multiply_reduce_fusion.2
  50.7 0.2 fusion.2
  50.9 1.0 %fusion.80 = f32[4,128,128]{2,1,0:T(8,128)S(1)} fusion(f32[4,128,512]{2,1,0:T(8,128)S(1)} %bitcast.240, f32[512,128,1]{1,0,2:T(8,128)S(1)} %bitcast.244), kind=kOutput, calls=%fused_computation.208 | convolution fusion | flops 402653184 | bytes 1572864 | tf_op jit(solution)/shard_map/dot_general | solution.py:126
  52.0 0.1 collective-permute-start.21
  52.1 1.2 %collective-permute-start.22 = (f32[132,128]{1,0:T(8,128)S(1)}, f32[132,128]{1,0:T(8,128)S(1)}, u32[]{:S(2)}, u32[]{:S(2)}) collective-permute-start(f32[132,128]{1,0:T(8,128)S(1)} %concatenate.70), channel_id=1, source_target_pairs={{0,2},{1,3},{2,0},{3,1},{4,6},{5,7},{6,4},{7,5},{8,10},{9,11},{10,... | collective-permute-start | bytes 202760 | tf_op jit(solution)/shard_map/ppermute | solution.py:64
  53.4 1.5 %collective-permute-start.23 = (f32[132,128]{1,0:T(8,128)S(1)}, f32[132,128]{1,0:T(8,128)S(1)}, u32[]{:S(2)}, u32[]{:S(2)}) collective-permute-start(f32[132,128]{1,0:T(8,128)S(1)} %concatenate.71), channel_id=1, source_target_pairs={{0,3},{1,0},{2,1},{3,2},{4,7},{5,4},{6,5},{7,6},{8,11},{9,8},{10,9... | collective-permute-start | bytes 202760 | tf_op jit(solution)/shard_map/ppermute | solution.py:64
  54.8 1.1 %collective-permute-done.21 = f32[132,128]{1,0:T(8,128)S(1)} collective-permute-done((f32[132,128]{1,0:T(8,128)S(1)}, f32[132,128]{1,0:T(8,128)S(1)}, u32[]{:S(2)}, u32[]{:S(2)}) %collective-permute-start.21) | collective-permute-done | bytes 67616 | tf_op jit(solution)/shard_map/ppermute | solution.py:64
  55.9 1.2 %collective-permute-done.22 = f32[132,128]{1,0:T(8,128)S(1)} collective-permute-done((f32[132,128]{1,0:T(8,128)S(1)}, f32[132,128]{1,0:T(8,128)S(1)}, u32[]{:S(2)}, u32[]{:S(2)}) %collective-permute-start.22) | collective-permute-done | bytes 67616 | tf_op jit(solution)/shard_map/ppermute | solution.py:64
  57.1 1.7 %collective-permute-start.24 = (f32[4,128]{1,0:T(4,128)S(1)}, f32[4,128]{1,0:T(4,128)S(1)}, u32[]{:S(2)}, u32[]{:S(2)}) collective-permute-start(f32[4,128]{1,0:T(4,128)S(1)} %select_add_fusion.1), channel_id=1, source_target_pairs={{0,4},{4,0},{8,12},{12,8},{1,5},{5,1},{9,13},{13,9},{2,6},{6,2},{1... | collective-permute-start | bytes 6152 | tf_op jit(solution)/shard_map/ppermute | solution.py:41
  58.9 1.6 %collective-permute-start.25 = (f32[4,128]{1,0:T(4,128)S(1)}, f32[4,128]{1,0:T(4,128)S(1)}, u32[]{:S(2)}, u32[]{:S(2)}) collective-permute-start(f32[4,128]{1,0:T(4,128)S(1)} %select_add_fusion.1), channel_id=1, source_target_pairs={{0,8},{4,12},{8,0},{12,4},{1,9},{5,13},{9,1},{13,5},{2,10},{6,14},... | collective-permute-start | bytes 6152 | tf_op jit(solution)/shard_map/ppermute | solution.py:41
  60.4 1.2 %collective-permute-start.26 = (f32[4,128]{1,0:T(4,128)S(1)}, f32[4,128]{1,0:T(4,128)S(1)}, u32[]{:S(2)}, u32[]{:S(2)}) collective-permute-start(f32[4,128]{1,0:T(4,128)S(1)} %select_add_fusion.1), channel_id=1, source_target_pairs={{0,12},{4,8},{8,4},{12,0},{1,13},{5,9},{9,5},{13,1},{2,14},{6,10},... | collective-permute-start | bytes 6152 | tf_op jit(solution)/shard_map/ppermute | solution.py:41
  61.6 1.8 %collective-permute-done.25 = f32[4,128]{1,0:T(4,128)S(1)} collective-permute-done((f32[4,128]{1,0:T(4,128)S(1)}, f32[4,128]{1,0:T(4,128)S(1)}, u32[]{:S(2)}, u32[]{:S(2)}) %collective-permute-start.25) | collective-permute-done | bytes 2080 | tf_op jit(solution)/shard_map/ppermute | solution.py:41
  63.3 2.5 %collective-permute-done.26 = f32[4,128]{1,0:T(4,128)S(1)} collective-permute-done((f32[4,128]{1,0:T(4,128)S(1)}, f32[4,128]{1,0:T(4,128)S(1)}, u32[]{:S(2)}, u32[]{:S(2)}) %collective-permute-start.26) | collective-permute-done | bytes 2080 | tf_op jit(solution)/shard_map/ppermute | solution.py:41
  65.8 0.8 %fusion.27 = (f32[128,128]{1,0:T(8,128)}, f32[128,128]{1,0:T(8,128)}) fusion(f32[132,128]{1,0:T(8,128)S(1)} %collective-permute-done.23, f32[132,128]{1,0:T(8,128)S(1)} %collective-permute-done.22, f32[132,128]{1,0:T(8,128)S(1)} %collective-permute-done.21, f32[128,128]{1,0:T(8,128)S(1)} %get-tuple-element.36, f32[4,128,128]{2,1,0:T(8,128)S(1)} %fusion.80, ...), kind=kLoop, calls=%fused_computation.79 | loop fusion | flops 425984 | bytes 527876 | tf_op jit(solution)/shard_map/sub | solution.py:180
  (54 shorter events, 0.8 us)
Async XLA Ops:
  0.6 13.5 %collective-permute-start = (s32[128]{0:T(128)}, s32[128]{0:T(128)S(1)}, u32[]{:S(2)}, u32[]{:S(2)}) collective-permute-start(s32[128]{0:T(128)} %bitcast.266), channel_id=1, source_target_pairs={{0,4},{4,0},{8,12},{12,8},{1,5},{5,1},{9,13},{13,9},{2,6},{6,2},{1... | collective-permute-start | bytes 1544 | tf_op jit(solution)/shard_map/ppermute | solution.py:41
  3.7 10.4 %collective-permute-start.1 = (s32[128]{0:T(128)}, s32[128]{0:T(128)S(1)}, u32[]{:S(2)}, u32[]{:S(2)}) collective-permute-start(s32[128]{0:T(128)} %bitcast.267), channel_id=1, source_target_pairs={{0,8},{4,12},{8,0},{12,4},{1,9},{5,13},{9,1},{13,5},{2,10},{6,14},... | collective-permute-start | bytes 1544 | tf_op jit(solution)/shard_map/ppermute | solution.py:41
  6.3 7.8 %collective-permute-start.2 = (s32[128]{0:T(128)}, s32[128]{0:T(128)S(1)}, u32[]{:S(2)}, u32[]{:S(2)}) collective-permute-start(s32[128]{0:T(128)} %bitcast.268), channel_id=1, source_target_pairs={{0,12},{4,8},{8,4},{12,0},{1,13},{5,9},{9,5},{13,1},{2,14},{6,10},... | collective-permute-start | bytes 1544 | tf_op jit(solution)/shard_map/ppermute | solution.py:41
  6.3 6.0 %collective-permute-start.3 = (s32[128]{0:T(128)}, s32[128]{0:T(128)S(1)}, u32[]{:S(2)}, u32[]{:S(2)}) collective-permute-start(s32[128]{0:T(128)} %bitcast.269), channel_id=1, source_target_pairs={{0,1},{1,0},{2,3},{3,2},{4,5},{5,4},{6,7},{7,6},{8,9},{9,8},{10,11... | collective-permute-start | bytes 1544 | tf_op jit(solution)/shard_map/ppermute | solution.py:35
  7.8 3.2 %copy-start = (s32[128,1]{0,1:T(1,128)S(1)}, s32[128,1]{0,1:T(1,128)}, u32[]{:S(2)}) copy-start(s32[128,1]{0,1:T(1,128)} %param.5) | copy-start | bytes 1540
  12.3 3.6 %collective-permute-start.4 = (s32[2,128]{1,0:T(2,128)S(1)}, s32[2,128]{1,0:T(2,128)S(1)}, u32[]{:S(2)}, u32[]{:S(2)}) collective-permute-start(s32[2,128]{1,0:T(2,128)S(1)} %pad_add_fusion.2), channel_id=1, source_target_pairs={{0,2},{1,3},{2,0},{3,1},{4,6},{5,7},{6,4},{7,5},{8,10},{9,11},{10,... | collective-permute-start | bytes 3080 | tf_op jit(solution)/shard_map/ppermute | solution.py:37
  16.3 3.9 %collective-permute-start.5 = (f32[131,128]{1,0:T(8,128)S(1)}, f32[131,128]{1,0:T(8,128)S(1)}, u32[]{:S(2)}, u32[]{:S(2)}) collective-permute-start(f32[131,128]{1,0:T(8,128)S(1)} %get-tuple-element.68), channel_id=1, source_target_pairs={{0,1},{1,2},{2,3},{3,0},{4,5},{5,6},{6,7},{7,4},{8,9},{9,10},{10,1... | collective-permute-start | bytes 201224 | tf_op jit(solution)/shard_map/ppermute | solution.py:64
  16.4 4.6 %collective-permute-start.6 = (f32[131,128]{1,0:T(8,128)S(1)}, f32[131,128]{1,0:T(8,128)S(1)}, u32[]{:S(2)}, u32[]{:S(2)}) collective-permute-start(f32[131,128]{1,0:T(8,128)S(1)} %get-tuple-element.69), channel_id=1, source_target_pairs={{0,2},{1,3},{2,0},{3,1},{4,6},{5,7},{6,4},{7,5},{8,10},{9,11},{10,... | collective-permute-start | bytes 201224 | tf_op jit(solution)/shard_map/ppermute | solution.py:64
  18.2 3.4 %collective-permute-start.7 = (f32[131,128]{1,0:T(8,128)S(1)}, f32[131,128]{1,0:T(8,128)S(1)}, u32[]{:S(2)}, u32[]{:S(2)}) collective-permute-start(f32[131,128]{1,0:T(8,128)S(1)} %get-tuple-element.70), channel_id=1, source_target_pairs={{0,3},{1,0},{2,1},{3,2},{4,7},{5,4},{6,5},{7,6},{8,11},{9,8},{10,9... | collective-permute-start | bytes 201224 | tf_op jit(solution)/shard_map/ppermute | solution.py:64
  21.8 5.2 %collective-permute-start.11 = (f32[128,128]{1,0:T(8,128)S(1)}, f32[128,128]{1,0:T(8,128)S(1)}, u32[]{:S(2)}, u32[]{:S(2)}) collective-permute-start(f32[128,128]{1,0:T(8,128)S(1)} %fusion.34), channel_id=1, source_target_pairs={{0,1},{1,0},{2,3},{3,2},{4,5},{5,4},{6,7},{7,6},{8,9},{9,8},{10,11... | collective-permute-start | bytes 196616 | tf_op jit(solution)/shard_map/ppermute | solution.py:35
  22.5 6.3 %collective-permute-start.8 = (f32[130,128]{1,0:T(8,128)S(1)}, f32[130,128]{1,0:T(8,128)S(1)}, u32[]{:S(2)}, u32[]{:S(2)}) collective-permute-start(f32[130,128]{1,0:T(8,128)S(1)} %get-tuple-element.58), channel_id=1, source_target_pairs={{0,4},{4,0},{8,12},{12,8},{1,5},{5,1},{9,13},{13,9},{2,6},{6,2},{1... | collective-permute-start | bytes 199688 | tf_op jit(solution)/shard_map/ppermute | solution.py:41
  23.5 8.4 %collective-permute-start.9 = (f32[130,128]{1,0:T(8,128)S(1)}, f32[130,128]{1,0:T(8,128)S(1)}, u32[]{:S(2)}, u32[]{:S(2)}) collective-permute-start(f32[130,128]{1,0:T(8,128)S(1)} %get-tuple-element.58), channel_id=1, source_target_pairs={{0,8},{4,12},{8,0},{12,4},{1,9},{5,13},{9,1},{13,5},{2,10},{6,14},... | collective-permute-start | bytes 199688 | tf_op jit(solution)/shard_map/ppermute | solution.py:41
  27.0 6.2 %collective-permute-start.10 = (f32[130,128]{1,0:T(8,128)S(1)}, f32[130,128]{1,0:T(8,128)S(1)}, u32[]{:S(2)}, u32[]{:S(2)}) collective-permute-start(f32[130,128]{1,0:T(8,128)S(1)} %get-tuple-element.58), channel_id=1, source_target_pairs={{0,12},{4,8},{8,4},{12,0},{1,13},{5,9},{9,5},{13,1},{2,14},{6,10},... | collective-permute-start | bytes 199688 | tf_op jit(solution)/shard_map/ppermute | solution.py:41
  27.0 6.4 %collective-permute-start.12 = (f32[2,128,128]{2,1,0:T(8,128)S(1)}, f32[2,128,128]{2,1,0:T(8,128)S(1)}, u32[]{:S(2)}, u32[]{:S(2)}) collective-permute-start(f32[2,128,128]{2,1,0:T(8,128)S(1)} %pad_maximum_fusion.7), channel_id=1, source_target_pairs={{0,2},{1,3},{2,0},{3,1},{4,6},{5,7},{6,4},{7,5},{8,10},{9,11},{10,... | collective-permute-start | bytes 393224 | tf_op jit(solution)/shard_map/ppermute | solution.py:37
  34.7 4.4 %collective-permute-start.14 = (f32[132,128]{1,0:T(8,128)S(1)}, f32[132,128]{1,0:T(8,128)S(1)}, u32[]{:S(2)}, u32[]{:S(2)}) collective-permute-start(f32[132,128]{1,0:T(8,128)S(1)} %concatenate.65), channel_id=1, source_target_pairs={{0,2},{1,3},{2,0},{3,1},{4,6},{5,7},{6,4},{7,5},{8,10},{9,11},{10,... | collective-permute-start | bytes 202760 | tf_op jit(solution)/shard_map/ppermute | solution.py:64
  36.3 3.3 %collective-permute-start.15 = (f32[132,128]{1,0:T(8,128)S(1)}, f32[132,128]{1,0:T(8,128)S(1)}, u32[]{:S(2)}, u32[]{:S(2)}) collective-permute-start(f32[132,128]{1,0:T(8,128)S(1)} %concatenate.66), channel_id=1, source_target_pairs={{0,3},{1,0},{2,1},{3,2},{4,7},{5,4},{6,5},{7,6},{8,11},{9,8},{10,9... | collective-permute-start | bytes 202760 | tf_op jit(solution)/shard_map/ppermute | solution.py:64
  36.4 4.2 %collective-permute-start.13 = (f32[132,128]{1,0:T(8,128)S(1)}, f32[132,128]{1,0:T(8,128)S(1)}, u32[]{:S(2)}, u32[]{:S(2)}) collective-permute-start(f32[132,128]{1,0:T(8,128)S(1)} %concatenate.64), channel_id=1, source_target_pairs={{0,1},{1,2},{2,3},{3,0},{4,5},{5,6},{6,7},{7,4},{8,9},{9,10},{10,1... | collective-permute-start | bytes 202760 | tf_op jit(solution)/shard_map/ppermute | solution.py:64
  40.7 4.6 %collective-permute-start.19 = (f32[128,128]{1,0:T(8,128)S(1)}, f32[128,128]{1,0:T(8,128)S(1)}, u32[]{:S(2)}, u32[]{:S(2)}) collective-permute-start(f32[128,128]{1,0:T(8,128)S(1)} %multiply_subtract_fusion.3), channel_id=1, source_target_pairs={{0,1},{1,0},{2,3},{3,2},{4,5},{5,4},{6,7},{7,6},{8,9},{9,8},{10,11... | collective-permute-start | bytes 196616 | tf_op jit(solution)/shard_map/ppermute | solution.py:35
  40.8 5.8 %collective-permute-start.16 = (f32[132,128]{1,0:T(8,128)S(1)}, f32[132,128]{1,0:T(8,128)S(1)}, u32[]{:S(2)}, u32[]{:S(2)}) collective-permute-start(f32[132,128]{1,0:T(8,128)S(1)} %get-tuple-element.56), channel_id=1, source_target_pairs={{0,4},{4,0},{8,12},{12,8},{1,5},{5,1},{9,13},{13,9},{2,6},{6,2},{1... | collective-permute-start | bytes 202760 | tf_op jit(solution)/shard_map/ppermute | solution.py:41
  41.8 8.7 %collective-permute-start.17 = (f32[132,128]{1,0:T(8,128)S(1)}, f32[132,128]{1,0:T(8,128)S(1)}, u32[]{:S(2)}, u32[]{:S(2)}) collective-permute-start(f32[132,128]{1,0:T(8,128)S(1)} %get-tuple-element.56), channel_id=1, source_target_pairs={{0,8},{4,12},{8,0},{12,4},{1,9},{5,13},{9,1},{13,5},{2,10},{6,14},... | collective-permute-start | bytes 202760 | tf_op jit(solution)/shard_map/ppermute | solution.py:41
  43.9 6.6 %collective-permute-start.18 = (f32[132,128]{1,0:T(8,128)S(1)}, f32[132,128]{1,0:T(8,128)S(1)}, u32[]{:S(2)}, u32[]{:S(2)}) collective-permute-start(f32[132,128]{1,0:T(8,128)S(1)} %get-tuple-element.56), channel_id=1, source_target_pairs={{0,12},{4,8},{8,4},{12,0},{1,13},{5,9},{9,5},{13,1},{2,14},{6,10},... | collective-permute-start | bytes 202760 | tf_op jit(solution)/shard_map/ppermute | solution.py:41
  45.3 5.4 %collective-permute-start.20 = (f32[2,128,128]{2,1,0:T(8,128)S(1)}, f32[2,128,128]{2,1,0:T(8,128)S(1)}, u32[]{:S(2)}, u32[]{:S(2)}) collective-permute-start(f32[2,128,128]{2,1,0:T(8,128)S(1)} %pad_maximum_fusion.8), channel_id=1, source_target_pairs={{0,2},{1,3},{2,0},{3,1},{4,6},{5,7},{6,4},{7,5},{8,10},{9,11},{10,... | collective-permute-start | bytes 393224 | tf_op jit(solution)/shard_map/ppermute | solution.py:37
  52.0 3.9 %collective-permute-start.21 = (f32[132,128]{1,0:T(8,128)S(1)}, f32[132,128]{1,0:T(8,128)S(1)}, u32[]{:S(2)}, u32[]{:S(2)}) collective-permute-start(f32[132,128]{1,0:T(8,128)S(1)} %concatenate.69), channel_id=1, source_target_pairs={{0,1},{1,2},{2,3},{3,0},{4,5},{5,6},{6,7},{7,4},{8,9},{9,10},{10,1... | collective-permute-start | bytes 202760 | tf_op jit(solution)/shard_map/ppermute | solution.py:64
  52.1 5.0 %collective-permute-start.22 = (f32[132,128]{1,0:T(8,128)S(1)}, f32[132,128]{1,0:T(8,128)S(1)}, u32[]{:S(2)}, u32[]{:S(2)}) collective-permute-start(f32[132,128]{1,0:T(8,128)S(1)} %concatenate.70), channel_id=1, source_target_pairs={{0,2},{1,3},{2,0},{3,1},{4,6},{5,7},{6,4},{7,5},{8,10},{9,11},{10,... | collective-permute-start | bytes 202760 | tf_op jit(solution)/shard_map/ppermute | solution.py:64
  53.4 3.8 %collective-permute-start.23 = (f32[132,128]{1,0:T(8,128)S(1)}, f32[132,128]{1,0:T(8,128)S(1)}, u32[]{:S(2)}, u32[]{:S(2)}) collective-permute-start(f32[132,128]{1,0:T(8,128)S(1)} %concatenate.71), channel_id=1, source_target_pairs={{0,3},{1,0},{2,1},{3,2},{4,7},{5,4},{6,5},{7,6},{8,11},{9,8},{10,9... | collective-permute-start | bytes 202760 | tf_op jit(solution)/shard_map/ppermute | solution.py:64
  57.1 4.5 %collective-permute-start.24 = (f32[4,128]{1,0:T(4,128)S(1)}, f32[4,128]{1,0:T(4,128)S(1)}, u32[]{:S(2)}, u32[]{:S(2)}) collective-permute-start(f32[4,128]{1,0:T(4,128)S(1)} %select_add_fusion.1), channel_id=1, source_target_pairs={{0,4},{4,0},{8,12},{12,8},{1,5},{5,1},{9,13},{13,9},{2,6},{6,2},{1... | collective-permute-start | bytes 6152 | tf_op jit(solution)/shard_map/ppermute | solution.py:41
  58.9 4.5 %collective-permute-start.25 = (f32[4,128]{1,0:T(4,128)S(1)}, f32[4,128]{1,0:T(4,128)S(1)}, u32[]{:S(2)}, u32[]{:S(2)}) collective-permute-start(f32[4,128]{1,0:T(4,128)S(1)} %select_add_fusion.1), channel_id=1, source_target_pairs={{0,8},{4,12},{8,0},{12,4},{1,9},{5,13},{9,1},{13,5},{2,10},{6,14},... | collective-permute-start | bytes 6152 | tf_op jit(solution)/shard_map/ppermute | solution.py:41
  60.4 5.4 %collective-permute-start.26 = (f32[4,128]{1,0:T(4,128)S(1)}, f32[4,128]{1,0:T(4,128)S(1)}, u32[]{:S(2)}, u32[]{:S(2)}) collective-permute-start(f32[4,128]{1,0:T(4,128)S(1)} %select_add_fusion.1), channel_id=1, source_target_pairs={{0,12},{4,8},{8,4},{12,0},{1,13},{5,9},{9,5},{13,1},{2,14},{6,10},... | collective-permute-start | bytes 6152 | tf_op jit(solution)/shard_map/ppermute | solution.py:41

commit v18 on v14

--- a/solution.py
+++ b/solution.py
@@ -32,9 +32,9 @@
     if count > 4:
         return lax.all_gather(values, axis, axis=0, tiled=False)
     if axis == "narrow" and count == 4:
-        partner = lax.ppermute(values, axis, [(i, i ^ 1) for i in range(count)])
+        partner = lax.ppermute(values, axis, [(i, i ^ 2) for i in range(count)])
         both = jnp.stack([values, partner])
-        return jnp.concatenate([both, lax.ppermute(both, axis, [(i, i ^ 2) for i in range(count)])])
+        return jnp.concatenate([both, lax.ppermute(both, axis, [(i, i ^ 1) for i in range(count)])])
     parts = [values]
     for shift in range(1, count):
         pairs = [(i, (i + shift) % count) for i in range(count)]
@@ -80,7 +80,7 @@
     if count > 4:
         return entry
     if axis == "narrow" and count == 4:
-        return lax.axis_index(axis) ^ entry
+        return lax.axis_index(axis) ^ (entry % 2 * 2 + entry // 2)
     return (lax.axis_index(axis) - entry) % count
 
 

time: 64.5 us -> 64.3 us (level)
  starting transfers between devices: 33.5 us -> 29.2 us
  waiting for transfers between devices: 18.2 us -> 22.2 us
    ppermute x12, waiting for transfers between devices: 9.23 us -> 12.6 us  [gather_blocks(): parts.append(lax.ppermute(values, axis, pairs))]
    ppermute x6, starting transfers between devices: 5.42 us -> 3.28 us  [the longest x3 3.07 us: gather_blocks(): partner = lax.ppermute(values, axis, [(i, i ^ 2) for i in range(count)])]
    ppermute x9, waiting for transfers between devices: 7.81 us -> 9.54 us  [scatter_with(): got = lax.ppermute(jnp.concatenate([sent, extra], axis=0), axis, pairs)]
    ppermute x9, starting transfers between devices: 7.95 us -> 6.6 us  [scatter_with(): got = lax.ppermute(jnp.concatenate([sent, extra], axis=0), axis, pairs)]
    ppermute x6, waiting for transfers between devices: 1.12 us -> 0.02 us  [the longest x3 0.01 us: gather_blocks(): partner = lax.ppermute(values, axis, [(i, i ^ 2) for i in range(count)])]
    ppermute x12, starting transfers between devices: 20.1 us -> 19.3 us  [gather_blocks(): parts.append(lax.ppermute(values, axis, pairs))]
  transfers between devices with their start and end apart: 27 -> 27, of which waited for: 17 -> 14; matrix products, arithmetic and copies ran while one was open for 12% -> 12% of each run, Pallas kernels for 0% -> 0%
where the time goes in v18:
time: 64.3 us; the launch traced here: 64.1 us
  starting transfers between devices  29.2 us (45%)
  waiting for transfers between devices  22.2 us (35%)
  other arithmetic  7.3 us (11%)
  matrix products  3.03 us (5%)
  local copies, waits for them, and re-layouts  1.34 us (2%)
  between operations  1.05 us (2%)
    ppermute x12, starting transfers between devices, gather_blocks(): parts.append(lax.ppermute(values, axis, pairs))  19.3 us
    ppermute x12, waiting for transfers between devices, gather_blocks(): parts.append(lax.ppermute(values, axis, pairs))  12.6 us
    ppermute x9, waiting for transfers between devices, scatter_with(): got = lax.ppermute(jnp.concatenate([sent, extra], axis=0), axis, pairs)  9.54 us
    ppermute x9, starting transfers between devices, scatter_with(): got = lax.ppermute(jnp.concatenate([sent, extra], axis=0), axis, pairs)  6.6 us
    ppermute x3, starting transfers between devices, gather_blocks(): partner = lax.ppermute(values, axis, [(i, i ^ 2) for i in range(count)])  3.07 us
    dot_general x3, matrix products, product(): jnp.dot(transposed, row_values.reshape(groups * tile, width), precision=l...  3.03 us
    reduce_sum x1, other arithmetic, local(): column_sums = jnp.sum(dense, axis=(0, 1)).reshape(n_narrow, own_rows)  2.97 us
  transfers between devices with their start and end apart: 27, of which 14 were waited for; matrix products, arithmetic and copies ran while one was open for 12% of the time, Pallas kernels for 0%

profile of v18, /device:TPU:0, one launch (start us, length us, event | category | flops | bytes accessed | tf_op | source)
XLA Modules:
  0.0 64.1 jit_solution(10957770193142029854)
XLA Ops:
  0.6 3.1 %collective-permute-start = (s32[128]{0:T(128)}, s32[128]{0:T(128)S(1)}, u32[]{:S(2)}, u32[]{:S(2)}) collective-permute-start(s32[128]{0:T(128)} %bitcast.266), channel_id=1, source_target_pairs={{0,4},{4,8},{8,12},{12,0},{1,5},{5,9},{9,13},{13,1},{2,6},{6,10},{... | collective-permute-start | bytes 1544 | tf_op jit(solution)/shard_map/ppermute | solution.py:41
  3.7 2.6 %collective-permute-start.1 = (s32[128]{0:T(128)}, s32[128]{0:T(128)S(1)}, u32[]{:S(2)}, u32[]{:S(2)}) collective-permute-start(s32[128]{0:T(128)} %bitcast.267), channel_id=1, source_target_pairs={{0,8},{4,12},{8,0},{12,4},{1,9},{5,13},{9,1},{13,5},{2,10},{6,14},... | collective-permute-start | bytes 1544 | tf_op jit(solution)/shard_map/ppermute | solution.py:41
  6.3 1.3 %collective-permute-start.2 = (s32[128]{0:T(128)}, s32[128]{0:T(128)S(1)}, u32[]{:S(2)}, u32[]{:S(2)}) collective-permute-start(s32[128]{0:T(128)} %bitcast.268), channel_id=1, source_target_pairs={{0,12},{4,0},{8,4},{12,8},{1,13},{5,1},{9,5},{13,9},{2,14},{6,2},{... | collective-permute-start | bytes 1544 | tf_op jit(solution)/shard_map/ppermute | solution.py:41
  7.6 1.5 %collective-permute-start.3 = (s32[128]{0:T(128)}, s32[128]{0:T(128)S(1)}, u32[]{:S(2)}, u32[]{:S(2)}) collective-permute-start(s32[128]{0:T(128)} %bitcast.269), channel_id=1, source_target_pairs={{0,2},{1,3},{2,0},{3,1},{4,6},{5,7},{6,4},{7,5},{8,10},{9,11},{10,... | collective-permute-start | bytes 1544 | tf_op jit(solution)/shard_map/ppermute | solution.py:35
  9.2 0.7 %fusion.77 = f32[128]{0:T(128)S(1)} fusion(s32[128,1]{0,1:T(1,128)} %param.5), kind=kLoop, calls=%fused_computation.211 | loop fusion | flops 384 | bytes 1024 | tf_op jit(solution)/shard_map/mul | solution.py:162
  9.9 0.8 %compare_and_fusion = pred[4,8,4]{2,1,0:T(8,128)(4,1)S(1)} fusion(s32[4]{0:T(128)S(1)} %get-tuple-element.73, s32[4]{0:T(128)S(1)} %get-tuple-element.74, s32[4,8]{1,0:T(4,128)} %param.4), kind=kLoop, calls=%fused_computation.141 | loop fusion | flops 384 | bytes 288 | tf_op jit(solution)/shard_map/and | solution.py:100
  10.6 3.0 %select_reduce_fusion = (f32[4,128]{1,0:T(4,128)S(1)}, f32[4,128,4,128]{3,1,2,0:T(8,128)S(1)}) fusion(f32[4,8,128,128]{3,2,1,0:T(8,128)} %param.3, pred[4,8,4]{2,1,0:T(8,128)(4,1)S(1)} %compare_and_fusion), kind=kLoop, calls=%fused_computation.1 | loop fusion | flops 6028800 | bytes 3147904 | tf_op jit(solution)/shard_map/reduce_sum | solution.py:107
  13.6 0.1 copy_bitcast_fusion
  13.7 0.1 broadcast_bitcast_fusion
  13.8 0.1 fusion.32
  13.9 0.6 gather_fusion
  14.6 0.1 bitcast_select_fusion
  14.8 0.3 copy.7
  15.1 0.0 collective-permute-done.3
  15.1 0.1 collective-permute-start.4
  15.3 1.1 %fusion.5 = f32[4,128,128]{2,1,0:T(8,128)S(1)} fusion(f32[4,128,512]{2,1,0:T(8,128)S(1)} %bitcast.238, s32[512]{0:T(512)S(1)} %get-tuple-element.61), kind=kOutput, calls=%fused_computation.22 | convolution fusion | flops 402784256 | bytes 1312768 | tf_op jit(solution)/shard_map/dot_general | solution.py:121
  16.4 0.1 fusion.8
  16.5 0.2 fusion.29
  16.7 0.5 collective-permute-start.5
  17.3 0.5 collective-permute-start.6
  17.8 1.0 %collective-permute-start.7 = (f32[131,128]{1,0:T(8,128)S(1)}, f32[131,128]{1,0:T(8,128)S(1)}, u32[]{:S(2)}, u32[]{:S(2)}) collective-permute-start(f32[131,128]{1,0:T(8,128)S(1)} %get-tuple-element.70), channel_id=1, source_target_pairs={{0,3},{1,0},{2,1},{3,2},{4,7},{5,4},{6,5},{7,6},{8,11},{9,8},{10,9... | collective-permute-start | bytes 201224 | tf_op jit(solution)/shard_map/ppermute | solution.py:59
  18.8 1.7 %collective-permute-done.5 = f32[131,128]{1,0:T(8,128)S(1)} collective-permute-done((f32[131,128]{1,0:T(8,128)S(1)}, f32[131,128]{1,0:T(8,128)S(1)}, u32[]{:S(2)}, u32[]{:S(2)}) %collective-permute-start.5) | collective-permute-done | bytes 67104 | tf_op jit(solution)/shard_map/ppermute | solution.py:59
  20.5 1.5 %collective-permute-done.6 = f32[131,128]{1,0:T(8,128)S(1)} collective-permute-done((f32[131,128]{1,0:T(8,128)S(1)}, f32[131,128]{1,0:T(8,128)S(1)}, u32[]{:S(2)}, u32[]{:S(2)}) %collective-permute-start.6) | collective-permute-done | bytes 67104 | tf_op jit(solution)/shard_map/ppermute | solution.py:59
  22.1 0.1 fusion.88
  22.2 0.1 fusion.34
  22.3 0.7 %collective-permute-start.11 = (f32[128,128]{1,0:T(8,128)S(1)}, f32[128,128]{1,0:T(8,128)S(1)}, u32[]{:S(2)}, u32[]{:S(2)}) collective-permute-start(f32[128,128]{1,0:T(8,128)S(1)} %fusion.34), channel_id=1, source_target_pairs={{0,2},{1,3},{2,0},{3,1},{4,6},{5,7},{6,4},{7,5},{8,10},{9,11},{10,... | collective-permute-start | bytes 196616 | tf_op jit(solution)/shard_map/ppermute | solution.py:35
  23.0 0.7 %collective-permute-start.8 = (f32[130,128]{1,0:T(8,128)S(1)}, f32[130,128]{1,0:T(8,128)S(1)}, u32[]{:S(2)}, u32[]{:S(2)}) collective-permute-start(f32[130,128]{1,0:T(8,128)S(1)} %get-tuple-element.58), channel_id=1, source_target_pairs={{0,4},{4,8},{8,12},{12,0},{1,5},{5,9},{9,13},{13,1},{2,6},{6,10},{... | collective-permute-start | bytes 199688 | tf_op jit(solution)/shard_map/ppermute | solution.py:41
  23.8 0.3 collective-permute-start.9
  24.1 2.8 %collective-permute-start.10 = (f32[130,128]{1,0:T(8,128)S(1)}, f32[130,128]{1,0:T(8,128)S(1)}, u32[]{:S(2)}, u32[]{:S(2)}) collective-permute-start(f32[130,128]{1,0:T(8,128)S(1)} %get-tuple-element.58), channel_id=1, source_target_pairs={{0,12},{4,0},{8,4},{12,8},{1,13},{5,1},{9,5},{13,9},{2,14},{6,2},{... | collective-permute-start | bytes 199688 | tf_op jit(solution)/shard_map/ppermute | solution.py:41
  26.9 0.1 collective-permute-start.12
  27.0 3.0 %collective-permute-done.8 = f32[130,128]{1,0:T(8,128)S(1)} collective-permute-done((f32[130,128]{1,0:T(8,128)S(1)}, f32[130,128]{1,0:T(8,128)S(1)}, u32[]{:S(2)}, u32[]{:S(2)}) %collective-permute-start.8) | collective-permute-done | bytes 66592 | tf_op jit(solution)/shard_map/ppermute | solution.py:41
  30.0 2.5 %collective-permute-done.9 = f32[130,128]{1,0:T(8,128)S(1)} collective-permute-done((f32[130,128]{1,0:T(8,128)S(1)}, f32[130,128]{1,0:T(8,128)S(1)}, u32[]{:S(2)}, u32[]{:S(2)}) %collective-permute-start.9) | collective-permute-done | bytes 66592 | tf_op jit(solution)/shard_map/ppermute | solution.py:41
  32.5 0.1 multiply_reduce_fusion.3
  32.7 0.2 multiply_subtract_fusion.1
  32.9 1.0 %fusion.81 = f32[4,128,128]{2,1,0:T(8,128)S(1)} fusion(f32[4,128,512]{2,1,0:T(8,128)S(1)} %bitcast.239, f32[512,128,1]{1,0,2:T(8,128)S(1)} %bitcast.245), kind=kOutput, calls=%fused_computation.215 | convolution fusion | flops 402653184 | bytes 1572864 | tf_op jit(solution)/shard_map/dot_general | solution.py:121
  34.0 1.3 %collective-permute-start.14 = (f32[132,128]{1,0:T(8,128)S(1)}, f32[132,128]{1,0:T(8,128)S(1)}, u32[]{:S(2)}, u32[]{:S(2)}) collective-permute-start(f32[132,128]{1,0:T(8,128)S(1)} %concatenate.65), channel_id=1, source_target_pairs={{0,2},{1,3},{2,0},{3,1},{4,6},{5,7},{6,4},{7,5},{8,10},{9,11},{10,... | collective-permute-start | bytes 202760 | tf_op jit(solution)/shard_map/ppermute | solution.py:59
  35.3 0.0 collective-permute-start.15
  35.4 0.5 collective-permute-start.13
  35.9 2.4 %collective-permute-done.14 = f32[132,128]{1,0:T(8,128)S(1)} collective-permute-done((f32[132,128]{1,0:T(8,128)S(1)}, f32[132,128]{1,0:T(8,128)S(1)}, u32[]{:S(2)}, u32[]{:S(2)}) %collective-permute-start.14) | collective-permute-done | bytes 67616 | tf_op jit(solution)/shard_map/ppermute | solution.py:59
  38.4 0.2 collective-permute-done.15
  38.6 1.3 %collective-permute-done.13 = f32[132,128]{1,0:T(8,128)S(1)} collective-permute-done((f32[132,128]{1,0:T(8,128)S(1)}, f32[132,128]{1,0:T(8,128)S(1)}, u32[]{:S(2)}, u32[]{:S(2)}) %collective-permute-start.13) | collective-permute-done | bytes 67616 | tf_op jit(solution)/shard_map/ppermute | solution.py:59
  39.9 0.1 multiply_subtract_fusion.3
  40.0 0.8 %collective-permute-start.19 = (f32[128,128]{1,0:T(8,128)S(1)}, f32[128,128]{1,0:T(8,128)S(1)}, u32[]{:S(2)}, u32[]{:S(2)}) collective-permute-start(f32[128,128]{1,0:T(8,128)S(1)} %multiply_subtract_fusion.3), channel_id=1, source_target_pairs={{0,2},{1,3},{2,0},{3,1},{4,6},{5,7},{6,4},{7,5},{8,10},{9,11},{10,... | collective-permute-start | bytes 196616 | tf_op jit(solution)/shard_map/ppermute | solution.py:35
  40.9 1.6 %collective-permute-start.16 = (f32[132,128]{1,0:T(8,128)S(1)}, f32[132,128]{1,0:T(8,128)S(1)}, u32[]{:S(2)}, u32[]{:S(2)}) collective-permute-start(f32[132,128]{1,0:T(8,128)S(1)} %get-tuple-element.56), channel_id=1, source_target_pairs={{0,4},{4,8},{8,12},{12,0},{1,5},{5,9},{9,13},{13,1},{2,6},{6,10},{... | collective-permute-start | bytes 202760 | tf_op jit(solution)/shard_map/ppermute | solution.py:41
  42.4 1.5 %collective-permute-start.17 = (f32[132,128]{1,0:T(8,128)S(1)}, f32[132,128]{1,0:T(8,128)S(1)}, u32[]{:S(2)}, u32[]{:S(2)}) collective-permute-start(f32[132,128]{1,0:T(8,128)S(1)} %get-tuple-element.56), channel_id=1, source_target_pairs={{0,8},{4,12},{8,0},{12,4},{1,9},{5,13},{9,1},{13,5},{2,10},{6,14},... | collective-permute-start | bytes 202760 | tf_op jit(solution)/shard_map/ppermute | solution.py:41
  43.9 0.9 %collective-permute-start.18 = (f32[132,128]{1,0:T(8,128)S(1)}, f32[132,128]{1,0:T(8,128)S(1)}, u32[]{:S(2)}, u32[]{:S(2)}) collective-permute-start(f32[132,128]{1,0:T(8,128)S(1)} %get-tuple-element.56), channel_id=1, source_target_pairs={{0,12},{4,0},{8,4},{12,8},{1,13},{5,1},{9,5},{13,9},{2,14},{6,2},{... | collective-permute-start | bytes 202760 | tf_op jit(solution)/shard_map/ppermute | solution.py:41
  44.9 0.1 collective-permute-start.20
  45.0 2.9 %collective-permute-done.16 = f32[132,128]{1,0:T(8,128)S(1)} collective-permute-done((f32[132,128]{1,0:T(8,128)S(1)}, f32[132,128]{1,0:T(8,128)S(1)}, u32[]{:S(2)}, u32[]{:S(2)}) %collective-permute-start.16) | collective-permute-done | bytes 67616 | tf_op jit(solution)/shard_map/ppermute | solution.py:41
  47.8 2.0 %collective-permute-done.17 = f32[132,128]{1,0:T(8,128)S(1)} collective-permute-done((f32[132,128]{1,0:T(8,128)S(1)}, f32[132,128]{1,0:T(8,128)S(1)}, u32[]{:S(2)}, u32[]{:S(2)}) %collective-permute-start.17) | collective-permute-done | bytes 67616 | tf_op jit(solution)/shard_map/ppermute | solution.py:41
  49.9 0.1 multiply_reduce_fusion.2
  50.1 0.2 fusion.2
  50.3 1.0 %fusion.82 = f32[4,128,128]{2,1,0:T(8,128)S(1)} fusion(f32[4,128,512]{2,1,0:T(8,128)S(1)} %bitcast.240, f32[512,128,1]{1,0,2:T(8,128)S(1)} %bitcast.244), kind=kOutput, calls=%fused_computation.216 | convolution fusion | flops 402653184 | bytes 1572864 | tf_op jit(solution)/shard_map/dot_general | solution.py:121
  51.4 0.1 collective-permute-start.21
  51.5 1.2 %collective-permute-start.22 = (f32[132,128]{1,0:T(8,128)S(1)}, f32[132,128]{1,0:T(8,128)S(1)}, u32[]{:S(2)}, u32[]{:S(2)}) collective-permute-start(f32[132,128]{1,0:T(8,128)S(1)} %concatenate.70), channel_id=1, source_target_pairs={{0,2},{1,3},{2,0},{3,1},{4,6},{5,7},{6,4},{7,5},{8,10},{9,11},{10,... | collective-permute-start | bytes 202760 | tf_op jit(solution)/shard_map/ppermute | solution.py:59
  52.7 1.5 %collective-permute-start.23 = (f32[132,128]{1,0:T(8,128)S(1)}, f32[132,128]{1,0:T(8,128)S(1)}, u32[]{:S(2)}, u32[]{:S(2)}) collective-permute-start(f32[132,128]{1,0:T(8,128)S(1)} %concatenate.71), channel_id=1, source_target_pairs={{0,3},{1,0},{2,1},{3,2},{4,7},{5,4},{6,5},{7,6},{8,11},{9,8},{10,9... | collective-permute-start | bytes 202760 | tf_op jit(solution)/shard_map/ppermute | solution.py:59
  54.2 1.1 %collective-permute-done.21 = f32[132,128]{1,0:T(8,128)S(1)} collective-permute-done((f32[132,128]{1,0:T(8,128)S(1)}, f32[132,128]{1,0:T(8,128)S(1)}, u32[]{:S(2)}, u32[]{:S(2)}) %collective-permute-start.21) | collective-permute-done | bytes 67616 | tf_op jit(solution)/shard_map/ppermute | solution.py:59
  55.3 1.2 %collective-permute-done.22 = f32[132,128]{1,0:T(8,128)S(1)} collective-permute-done((f32[132,128]{1,0:T(8,128)S(1)}, f32[132,128]{1,0:T(8,128)S(1)}, u32[]{:S(2)}, u32[]{:S(2)}) %collective-permute-start.22) | collective-permute-done | bytes 67616 | tf_op jit(solution)/shard_map/ppermute | solution.py:59
  56.6 2.0 %collective-permute-start.24 = (f32[4,128]{1,0:T(4,128)S(1)}, f32[4,128]{1,0:T(4,128)S(1)}, u32[]{:S(2)}, u32[]{:S(2)}) collective-permute-start(f32[4,128]{1,0:T(4,128)S(1)} %select_add_fusion.1), channel_id=1, source_target_pairs={{0,4},{4,8},{8,12},{12,0},{1,5},{5,9},{9,13},{13,1},{2,6},{6,10},{... | collective-permute-start | bytes 6152 | tf_op jit(solution)/shard_map/ppermute | solution.py:41
  58.6 1.1 %collective-permute-start.25 = (f32[4,128]{1,0:T(4,128)S(1)}, f32[4,128]{1,0:T(4,128)S(1)}, u32[]{:S(2)}, u32[]{:S(2)}) collective-permute-start(f32[4,128]{1,0:T(4,128)S(1)} %select_add_fusion.1), channel_id=1, source_target_pairs={{0,8},{4,12},{8,0},{12,4},{1,9},{5,13},{9,1},{13,5},{2,10},{6,14},... | collective-permute-start | bytes 6152 | tf_op jit(solution)/shard_map/ppermute | solution.py:41
  59.7 1.3 %collective-permute-start.26 = (f32[4,128]{1,0:T(4,128)S(1)}, f32[4,128]{1,0:T(4,128)S(1)}, u32[]{:S(2)}, u32[]{:S(2)}) collective-permute-start(f32[4,128]{1,0:T(4,128)S(1)} %select_add_fusion.1), channel_id=1, source_target_pairs={{0,12},{4,0},{8,4},{12,8},{1,13},{5,1},{9,5},{13,9},{2,14},{6,2},{... | collective-permute-start | bytes 6152 | tf_op jit(solution)/shard_map/ppermute | solution.py:41
  61.0 1.0 %collective-permute-done.24 = f32[4,128]{1,0:T(4,128)S(1)} collective-permute-done((f32[4,128]{1,0:T(4,128)S(1)}, f32[4,128]{1,0:T(4,128)S(1)}, u32[]{:S(2)}, u32[]{:S(2)}) %collective-permute-start.24) | collective-permute-done | bytes 2080 | tf_op jit(solution)/shard_map/ppermute | solution.py:41
  62.0 1.1 %collective-permute-done.25 = f32[4,128]{1,0:T(4,128)S(1)} collective-permute-done((f32[4,128]{1,0:T(4,128)S(1)}, f32[4,128]{1,0:T(4,128)S(1)}, u32[]{:S(2)}, u32[]{:S(2)}) %collective-permute-start.25) | collective-permute-done | bytes 2080 | tf_op jit(solution)/shard_map/ppermute | solution.py:41
  63.1 0.2 collective-permute-done.26
  63.3 0.8 %fusion.27 = (f32[128,128]{1,0:T(8,128)}, f32[128,128]{1,0:T(8,128)}) fusion(f32[132,128]{1,0:T(8,128)S(1)} %collective-permute-done.23, f32[132,128]{1,0:T(8,128)S(1)} %collective-permute-done.22, f32[132,128]{1,0:T(8,128)S(1)} %collective-permute-done.21, f32[128,128]{1,0:T(8,128)S(1)} %get-tuple-element.36, f32[4,128,128]{2,1,0:T(8,128)S(1)} %fusion.82, ...), kind=kLoop, calls=%fused_computation.79 | loop fusion | flops 425984 | bytes 527876 | tf_op jit(solution)/shard_map/sub | solution.py:175
  (54 shorter events, 0.8 us)
Async XLA Ops:
  0.6 14.6 %collective-permute-start = (s32[128]{0:T(128)}, s32[128]{0:T(128)S(1)}, u32[]{:S(2)}, u32[]{:S(2)}) collective-permute-start(s32[128]{0:T(128)} %bitcast.266), channel_id=1, source_target_pairs={{0,4},{4,8},{8,12},{12,0},{1,5},{5,9},{9,13},{13,1},{2,6},{6,10},{... | collective-permute-start | bytes 1544 | tf_op jit(solution)/shard_map/ppermute | solution.py:41
  3.7 11.5 %collective-permute-start.1 = (s32[128]{0:T(128)}, s32[128]{0:T(128)S(1)}, u32[]{:S(2)}, u32[]{:S(2)}) collective-permute-start(s32[128]{0:T(128)} %bitcast.267), channel_id=1, source_target_pairs={{0,8},{4,12},{8,0},{12,4},{1,9},{5,13},{9,1},{13,5},{2,10},{6,14},... | collective-permute-start | bytes 1544 | tf_op jit(solution)/shard_map/ppermute | solution.py:41
  6.3 9.0 %collective-permute-start.2 = (s32[128]{0:T(128)}, s32[128]{0:T(128)S(1)}, u32[]{:S(2)}, u32[]{:S(2)}) collective-permute-start(s32[128]{0:T(128)} %bitcast.268), channel_id=1, source_target_pairs={{0,12},{4,0},{8,4},{12,8},{1,13},{5,1},{9,5},{13,9},{2,14},{6,2},{... | collective-permute-start | bytes 1544 | tf_op jit(solution)/shard_map/ppermute | solution.py:41
  7.6 7.5 %collective-permute-start.3 = (s32[128]{0:T(128)}, s32[128]{0:T(128)S(1)}, u32[]{:S(2)}, u32[]{:S(2)}) collective-permute-start(s32[128]{0:T(128)} %bitcast.269), channel_id=1, source_target_pairs={{0,2},{1,3},{2,0},{3,1},{4,6},{5,7},{6,4},{7,5},{8,10},{9,11},{10,... | collective-permute-start | bytes 1544 | tf_op jit(solution)/shard_map/ppermute | solution.py:35
  10.6 3.2 %copy-start = (s32[128,1]{0,1:T(1,128)S(1)}, s32[128,1]{0,1:T(1,128)}, u32[]{:S(2)}) copy-start(s32[128,1]{0,1:T(1,128)} %param.5) | copy-start | bytes 1540
  15.1 1.2 %collective-permute-start.4 = (s32[2,128]{1,0:T(2,128)S(1)}, s32[2,128]{1,0:T(2,128)S(1)}, u32[]{:S(2)}, u32[]{:S(2)}) collective-permute-start(s32[2,128]{1,0:T(2,128)S(1)} %pad_add_fusion.2), channel_id=1, source_target_pairs={{0,1},{1,0},{2,3},{3,2},{4,5},{5,4},{6,7},{7,6},{8,9},{9,8},{10,11... | collective-permute-start | bytes 3080 | tf_op jit(solution)/shard_map/ppermute | solution.py:37
  16.7 3.8 %collective-permute-start.5 = (f32[131,128]{1,0:T(8,128)S(1)}, f32[131,128]{1,0:T(8,128)S(1)}, u32[]{:S(2)}, u32[]{:S(2)}) collective-permute-start(f32[131,128]{1,0:T(8,128)S(1)} %get-tuple-element.68), channel_id=1, source_target_pairs={{0,1},{1,2},{2,3},{3,0},{4,5},{5,6},{6,7},{7,4},{8,9},{9,10},{10,1... | collective-permute-start | bytes 201224 | tf_op jit(solution)/shard_map/ppermute | solution.py:59
  17.3 4.8 %collective-permute-start.6 = (f32[131,128]{1,0:T(8,128)S(1)}, f32[131,128]{1,0:T(8,128)S(1)}, u32[]{:S(2)}, u32[]{:S(2)}) collective-permute-start(f32[131,128]{1,0:T(8,128)S(1)} %get-tuple-element.69), channel_id=1, source_target_pairs={{0,2},{1,3},{2,0},{3,1},{4,6},{5,7},{6,4},{7,5},{8,10},{9,11},{10,... | collective-permute-start | bytes 201224 | tf_op jit(solution)/shard_map/ppermute | solution.py:59
  17.8 4.2 %collective-permute-start.7 = (f32[131,128]{1,0:T(8,128)S(1)}, f32[131,128]{1,0:T(8,128)S(1)}, u32[]{:S(2)}, u32[]{:S(2)}) collective-permute-start(f32[131,128]{1,0:T(8,128)S(1)} %get-tuple-element.70), channel_id=1, source_target_pairs={{0,3},{1,0},{2,1},{3,2},{4,7},{5,4},{6,5},{7,6},{8,11},{9,8},{10,9... | collective-permute-start | bytes 201224 | tf_op jit(solution)/shard_map/ppermute | solution.py:59
  22.3 4.7 %collective-permute-start.11 = (f32[128,128]{1,0:T(8,128)S(1)}, f32[128,128]{1,0:T(8,128)S(1)}, u32[]{:S(2)}, u32[]{:S(2)}) collective-permute-start(f32[128,128]{1,0:T(8,128)S(1)} %fusion.34), channel_id=1, source_target_pairs={{0,2},{1,3},{2,0},{3,1},{4,6},{5,7},{6,4},{7,5},{8,10},{9,11},{10,... | collective-permute-start | bytes 196616 | tf_op jit(solution)/shard_map/ppermute | solution.py:35
  23.0 6.9 %collective-permute-start.8 = (f32[130,128]{1,0:T(8,128)S(1)}, f32[130,128]{1,0:T(8,128)S(1)}, u32[]{:S(2)}, u32[]{:S(2)}) collective-permute-start(f32[130,128]{1,0:T(8,128)S(1)} %get-tuple-element.58), channel_id=1, source_target_pairs={{0,4},{4,8},{8,12},{12,0},{1,5},{5,9},{9,13},{13,1},{2,6},{6,10},{... | collective-permute-start | bytes 199688 | tf_op jit(solution)/shard_map/ppermute | solution.py:41
  23.8 8.7 %collective-permute-start.9 = (f32[130,128]{1,0:T(8,128)S(1)}, f32[130,128]{1,0:T(8,128)S(1)}, u32[]{:S(2)}, u32[]{:S(2)}) collective-permute-start(f32[130,128]{1,0:T(8,128)S(1)} %get-tuple-element.58), channel_id=1, source_target_pairs={{0,8},{4,12},{8,0},{12,4},{1,9},{5,13},{9,1},{13,5},{2,10},{6,14},... | collective-permute-start | bytes 199688 | tf_op jit(solution)/shard_map/ppermute | solution.py:41
  24.1 8.4 %collective-permute-start.10 = (f32[130,128]{1,0:T(8,128)S(1)}, f32[130,128]{1,0:T(8,128)S(1)}, u32[]{:S(2)}, u32[]{:S(2)}) collective-permute-start(f32[130,128]{1,0:T(8,128)S(1)} %get-tuple-element.58), channel_id=1, source_target_pairs={{0,12},{4,0},{8,4},{12,8},{1,13},{5,1},{9,5},{13,9},{2,14},{6,2},{... | collective-permute-start | bytes 199688 | tf_op jit(solution)/shard_map/ppermute | solution.py:41
  26.9 5.7 %collective-permute-start.12 = (f32[2,128,128]{2,1,0:T(8,128)S(1)}, f32[2,128,128]{2,1,0:T(8,128)S(1)}, u32[]{:S(2)}, u32[]{:S(2)}) collective-permute-start(f32[2,128,128]{2,1,0:T(8,128)S(1)} %pad_maximum_fusion.7), channel_id=1, source_target_pairs={{0,1},{1,0},{2,3},{3,2},{4,5},{5,4},{6,7},{7,6},{8,9},{9,8},{10,11... | collective-permute-start | bytes 393224 | tf_op jit(solution)/shard_map/ppermute | solution.py:37
  34.0 4.4 %collective-permute-start.14 = (f32[132,128]{1,0:T(8,128)S(1)}, f32[132,128]{1,0:T(8,128)S(1)}, u32[]{:S(2)}, u32[]{:S(2)}) collective-permute-start(f32[132,128]{1,0:T(8,128)S(1)} %concatenate.65), channel_id=1, source_target_pairs={{0,2},{1,3},{2,0},{3,1},{4,6},{5,7},{6,4},{7,5},{8,10},{9,11},{10,... | collective-permute-start | bytes 202760 | tf_op jit(solution)/shard_map/ppermute | solution.py:59
  35.3 3.3 %collective-permute-start.15 = (f32[132,128]{1,0:T(8,128)S(1)}, f32[132,128]{1,0:T(8,128)S(1)}, u32[]{:S(2)}, u32[]{:S(2)}) collective-permute-start(f32[132,128]{1,0:T(8,128)S(1)} %concatenate.66), channel_id=1, source_target_pairs={{0,3},{1,0},{2,1},{3,2},{4,7},{5,4},{6,5},{7,6},{8,11},{9,8},{10,9... | collective-permute-start | bytes 202760 | tf_op jit(solution)/shard_map/ppermute | solution.py:59
  35.4 4.5 %collective-permute-start.13 = (f32[132,128]{1,0:T(8,128)S(1)}, f32[132,128]{1,0:T(8,128)S(1)}, u32[]{:S(2)}, u32[]{:S(2)}) collective-permute-start(f32[132,128]{1,0:T(8,128)S(1)} %concatenate.64), channel_id=1, source_target_pairs={{0,1},{1,2},{2,3},{3,0},{4,5},{5,6},{6,7},{7,4},{8,9},{9,10},{10,1... | collective-permute-start | bytes 202760 | tf_op jit(solution)/shard_map/ppermute | solution.py:59
  40.0 4.9 %collective-permute-start.19 = (f32[128,128]{1,0:T(8,128)S(1)}, f32[128,128]{1,0:T(8,128)S(1)}, u32[]{:S(2)}, u32[]{:S(2)}) collective-permute-start(f32[128,128]{1,0:T(8,128)S(1)} %multiply_subtract_fusion.3), channel_id=1, source_target_pairs={{0,2},{1,3},{2,0},{3,1},{4,6},{5,7},{6,4},{7,5},{8,10},{9,11},{10,... | collective-permute-start | bytes 196616 | tf_op jit(solution)/shard_map/ppermute | solution.py:35
  40.9 7.0 %collective-permute-start.16 = (f32[132,128]{1,0:T(8,128)S(1)}, f32[132,128]{1,0:T(8,128)S(1)}, u32[]{:S(2)}, u32[]{:S(2)}) collective-permute-start(f32[132,128]{1,0:T(8,128)S(1)} %get-tuple-element.56), channel_id=1, source_target_pairs={{0,4},{4,8},{8,12},{12,0},{1,5},{5,9},{9,13},{13,1},{2,6},{6,10},{... | collective-permute-start | bytes 202760 | tf_op jit(solution)/shard_map/ppermute | solution.py:41
  42.4 7.4 %collective-permute-start.17 = (f32[132,128]{1,0:T(8,128)S(1)}, f32[132,128]{1,0:T(8,128)S(1)}, u32[]{:S(2)}, u32[]{:S(2)}) collective-permute-start(f32[132,128]{1,0:T(8,128)S(1)} %get-tuple-element.56), channel_id=1, source_target_pairs={{0,8},{4,12},{8,0},{12,4},{1,9},{5,13},{9,1},{13,5},{2,10},{6,14},... | collective-permute-start | bytes 202760 | tf_op jit(solution)/shard_map/ppermute | solution.py:41
  43.9 5.9 %collective-permute-start.18 = (f32[132,128]{1,0:T(8,128)S(1)}, f32[132,128]{1,0:T(8,128)S(1)}, u32[]{:S(2)}, u32[]{:S(2)}) collective-permute-start(f32[132,128]{1,0:T(8,128)S(1)} %get-tuple-element.56), channel_id=1, source_target_pairs={{0,12},{4,0},{8,4},{12,8},{1,13},{5,1},{9,5},{13,9},{2,14},{6,2},{... | collective-permute-start | bytes 202760 | tf_op jit(solution)/shard_map/ppermute | solution.py:41
  44.9 5.2 %collective-permute-start.20 = (f32[2,128,128]{2,1,0:T(8,128)S(1)}, f32[2,128,128]{2,1,0:T(8,128)S(1)}, u32[]{:S(2)}, u32[]{:S(2)}) collective-permute-start(f32[2,128,128]{2,1,0:T(8,128)S(1)} %pad_maximum_fusion.8), channel_id=1, source_target_pairs={{0,1},{1,0},{2,3},{3,2},{4,5},{5,4},{6,7},{7,6},{8,9},{9,8},{10,11... | collective-permute-start | bytes 393224 | tf_op jit(solution)/shard_map/ppermute | solution.py:37
  51.4 3.9 %collective-permute-start.21 = (f32[132,128]{1,0:T(8,128)S(1)}, f32[132,128]{1,0:T(8,128)S(1)}, u32[]{:S(2)}, u32[]{:S(2)}) collective-permute-start(f32[132,128]{1,0:T(8,128)S(1)} %concatenate.69), channel_id=1, source_target_pairs={{0,1},{1,2},{2,3},{3,0},{4,5},{5,6},{6,7},{7,4},{8,9},{9,10},{10,1... | collective-permute-start | bytes 202760 | tf_op jit(solution)/shard_map/ppermute | solution.py:59
  51.5 5.0 %collective-permute-start.22 = (f32[132,128]{1,0:T(8,128)S(1)}, f32[132,128]{1,0:T(8,128)S(1)}, u32[]{:S(2)}, u32[]{:S(2)}) collective-permute-start(f32[132,128]{1,0:T(8,128)S(1)} %concatenate.70), channel_id=1, source_target_pairs={{0,2},{1,3},{2,0},{3,1},{4,6},{5,7},{6,4},{7,5},{8,10},{9,11},{10,... | collective-permute-start | bytes 202760 | tf_op jit(solution)/shard_map/ppermute | solution.py:59
  52.7 3.9 %collective-permute-start.23 = (f32[132,128]{1,0:T(8,128)S(1)}, f32[132,128]{1,0:T(8,128)S(1)}, u32[]{:S(2)}, u32[]{:S(2)}) collective-permute-start(f32[132,128]{1,0:T(8,128)S(1)} %concatenate.71), channel_id=1, source_target_pairs={{0,3},{1,0},{2,1},{3,2},{4,7},{5,4},{6,5},{7,6},{8,11},{9,8},{10,9... | collective-permute-start | bytes 202760 | tf_op jit(solution)/shard_map/ppermute | solution.py:59
  56.6 5.4 %collective-permute-start.24 = (f32[4,128]{1,0:T(4,128)S(1)}, f32[4,128]{1,0:T(4,128)S(1)}, u32[]{:S(2)}, u32[]{:S(2)}) collective-permute-start(f32[4,128]{1,0:T(4,128)S(1)} %select_add_fusion.1), channel_id=1, source_target_pairs={{0,4},{4,8},{8,12},{12,0},{1,5},{5,9},{9,13},{13,1},{2,6},{6,10},{... | collective-permute-start | bytes 6152 | tf_op jit(solution)/shard_map/ppermute | solution.py:41
  58.6 4.5 %collective-permute-start.25 = (f32[4,128]{1,0:T(4,128)S(1)}, f32[4,128]{1,0:T(4,128)S(1)}, u32[]{:S(2)}, u32[]{:S(2)}) collective-permute-start(f32[4,128]{1,0:T(4,128)S(1)} %select_add_fusion.1), channel_id=1, source_target_pairs={{0,8},{4,12},{8,0},{12,4},{1,9},{5,13},{9,1},{13,5},{2,10},{6,14},... | collective-permute-start | bytes 6152 | tf_op jit(solution)/shard_map/ppermute | solution.py:41
  59.7 3.6 %collective-permute-start.26 = (f32[4,128]{1,0:T(4,128)S(1)}, f32[4,128]{1,0:T(4,128)S(1)}, u32[]{:S(2)}, u32[]{:S(2)}) collective-permute-start(f32[4,128]{1,0:T(4,128)S(1)} %select_add_fusion.1), channel_id=1, source_target_pairs={{0,12},{4,0},{8,4},{12,8},{1,13},{5,1},{9,5},{13,9},{2,14},{6,2},{... | collective-permute-start | bytes 6152 | tf_op jit(solution)/shard_map/ppermute | solution.py:41

commit v19 on v14

--- a/solution.py
+++ b/solution.py
@@ -54,21 +54,25 @@
     total = lax.dynamic_index_in_dim(blocks, me, 0, keepdims=False)
     extras = [extra]
     for shift in range(1, count):
-        sent = lax.dynamic_index_in_dim(blocks, (me + shift) % count, 0, keepdims=False)
-        pairs = [(i, (i + shift) % count) for i in range(count)]
+        target = me ^ shift if count == 4 else (me + shift) % count
+        sent = lax.dynamic_index_in_dim(blocks, target, 0, keepdims=False)
+        if count == 4:
+            pairs = [(i, i ^ shift) for i in range(count)]
+        else:
+            pairs = [(i, (i + shift) % count) for i in range(count)]
         got = lax.ppermute(jnp.concatenate([sent, extra], axis=0), axis, pairs)
         total = total + got[:rows]
         extras.append(got[rows:])
     return total, jnp.stack(extras)
 
 
-def canonical_sum(extras, axis, count):
+def canonical_sum(extras, axis, count, paired=False):
     if count > 4:
         return jnp.sum(extras, axis=0)
     me = lax.axis_index(axis)
     total = None
     for device in range(count):
-        wanted = (me - device) % count
+        wanted = me ^ device if paired and count == 4 else (me - device) % count
         term = extras[count - 1]
         for entry in range(count - 2, -1, -1):
             term = jnp.where(wanted == entry, extras[entry], term)
@@ -131,7 +135,7 @@
 
     def narrow_step(partial, partial_sums):
         weighted, extras = scatter_with(partial, partial_sums, "narrow", n_narrow)
-        return weighted, canonical_sum(extras, "narrow", n_narrow)
+        return weighted, canonical_sum(extras, "narrow", n_narrow, paired=True)
 
     def wide_step(applied, narrow_sums, last):
         if last:

time: 64.5 us -> 67.5 us (1.047)
  waiting for transfers between devices: 18.2 us -> 23.5 us
  starting transfers between devices: 33.5 us -> 31.2 us
    ppermute x9, waiting for transfers between devices: 7.81 us -> 11.6 us  [scatter_with(): got = lax.ppermute(jnp.concatenate([sent, extra], axis=0), axis, pairs)]
    ppermute x9, starting transfers between devices: 7.95 us -> 6.55 us  [scatter_with(): got = lax.ppermute(jnp.concatenate([sent, extra], axis=0), axis, pairs)]
    ppermute x3, waiting for transfers between devices: 0.01 us -> 1.15 us  [gather_blocks(): partner = lax.ppermute(values, axis, [(i, i ^ 1) for i in range(count)])]
    ppermute x3, waiting for transfers between devices: 1.11 us -> 1.83 us  [gather_blocks(): lax.ppermute(both, axis, [(i, i ^ 2) for i in range(count)])]
    ppermute x12, starting transfers between devices: 20.1 us -> 19.4 us  [gather_blocks(): parts.append(lax.ppermute(values, axis, pairs))]
  transfers between devices with their start and end apart: 27 -> 27, of which waited for: 17 -> 14; matrix products, arithmetic and copies ran while one was open for 12% -> 11% of each run, Pallas kernels for 0% -> 0%
where the time goes in v19:
time: 67.5 us; the launch traced here: 67.3 us
  starting transfers between devices  31.2 us (46%)
  waiting for transfers between devices  23.5 us (35%)
  other arithmetic  7.24 us (11%)
  matrix products  3.01 us (4%)
  local copies, waits for them, and re-layouts  1.33 us (2%)
  between operations  0.96 us (1%)
    ppermute x12, starting transfers between devices, gather_blocks(): parts.append(lax.ppermute(values, axis, pairs))  19.4 us
    ppermute x9, waiting for transfers between devices, scatter_with(): got = lax.ppermute(jnp.concatenate([sent, extra], axis=0), axis, pairs)  11.6 us
    ppermute x12, waiting for transfers between devices, gather_blocks(): parts.append(lax.ppermute(values, axis, pairs))  8.94 us
    ppermute x9, starting transfers between devices, scatter_with(): got = lax.ppermute(jnp.concatenate([sent, extra], axis=0), axis, pairs)  6.55 us
    ppermute x3, starting transfers between devices, gather_blocks(): lax.ppermute(both, axis, [(i, i ^ 2) for i in range(count)])  4.66 us
    dot_general x3, matrix products, product(): jnp.dot(transposed, row_values.reshape(groups * tile, width), precision=l...  3.01 us
    reduce_sum x1, other arithmetic, local(): column_sums = jnp.sum(dense, axis=(0, 1)).reshape(n_narrow, own_rows)  2.97 us
    ppermute x3, waiting for transfers between devices, gather_blocks(): lax.ppermute(both, axis, [(i, i ^ 2) for i in range(count)])  1.83 us
  transfers between devices with their start and end apart: 27, of which 14 were waited for; matrix products, arithmetic and copies ran while one was open for 11% of the time, Pallas kernels for 0%

profile of v19, /device:TPU:0, one launch (start us, length us, event | category | flops | bytes accessed | tf_op | source)
XLA Modules:
  0.0 67.3 jit_solution(671836550187371233)
XLA Ops:
  0.6 0.5 collective-permute-start.3
  1.1 4.7 %collective-permute-start.2 = (s32[128]{0:T(128)}, s32[128]{0:T(128)S(1)}, u32[]{:S(2)}, u32[]{:S(2)}) collective-permute-start(s32[128]{0:T(128)} %bitcast.309), channel_id=1, source_target_pairs={{0,12},{4,0},{8,4},{12,8},{1,13},{5,1},{9,5},{13,9},{2,14},{6,2},{... | collective-permute-start | bytes 1544 | tf_op jit(solution)/shard_map/ppermute | solution.py:41
  5.8 0.0 collective-permute-start.1
  5.8 1.0 %collective-permute-start = (s32[128]{0:T(128)}, s32[128]{0:T(128)S(1)}, u32[]{:S(2)}, u32[]{:S(2)}) collective-permute-start(s32[128]{0:T(128)} %bitcast.311), channel_id=1, source_target_pairs={{0,4},{4,8},{8,12},{12,0},{1,5},{5,9},{9,13},{13,1},{2,6},{6,10},{... | collective-permute-start | bytes 1544 | tf_op jit(solution)/shard_map/ppermute | solution.py:41
  6.9 0.7 %fusion.83 = f32[128]{0:T(128)S(1)} fusion(s32[128,1]{0,1:T(1,128)} %param.5), kind=kLoop, calls=%fused_computation.217 | loop fusion | flops 384 | bytes 1024 | tf_op jit(solution)/shard_map/mul | solution.py:166
  7.6 0.8 %compare_and_fusion = pred[4,8,4]{2,1,0:T(8,128)(4,1)S(1)} fusion(s32[4]{0:T(128)S(1)} %get-tuple-element.69, s32[4]{0:T(128)S(1)} %get-tuple-element.70, s32[4,8]{1,0:T(4,128)} %param.4), kind=kLoop, calls=%fused_computation.147 | loop fusion | flops 384 | bytes 288 | tf_op jit(solution)/shard_map/and | solution.py:104
  8.3 3.0 %select_reduce_fusion = (f32[4,128]{1,0:T(4,128)S(1)}, f32[4,128,4,128]{3,1,2,0:T(8,128)S(1)}) fusion(f32[4,8,128,128]{3,2,1,0:T(8,128)} %param.3, pred[4,8,4]{2,1,0:T(8,128)(4,1)S(1)} %compare_and_fusion), kind=kLoop, calls=%fused_computation.1 | loop fusion | flops 6028800 | bytes 3147904 | tf_op jit(solution)/shard_map/reduce_sum | solution.py:111
  11.3 0.1 copy_bitcast_fusion
  11.4 0.1 broadcast_bitcast_fusion
  11.5 0.1 fusion.32
  11.6 0.6 gather_fusion
  12.3 0.1 bitcast_select_fusion
  12.4 0.3 copy.7
  12.8 1.6 %collective-permute-start.4 = (s32[2,128]{1,0:T(2,128)S(1)}, s32[2,128]{1,0:T(2,128)S(1)}, u32[]{:S(2)}, u32[]{:S(2)}) collective-permute-start(s32[2,128]{1,0:T(2,128)S(1)} %pad_add_fusion.2), channel_id=1, source_target_pairs={{0,2},{1,3},{2,0},{3,1},{4,6},{5,7},{6,4},{7,5},{8,10},{9,11},{10,... | collective-permute-start | bytes 3080 | tf_op jit(solution)/shard_map/ppermute | solution.py:37
  14.4 1.0 %fusion.5 = f32[4,128,128]{2,1,0:T(8,128)S(1)} fusion(f32[4,128,512]{2,1,0:T(8,128)S(1)} %bitcast.280, s32[512]{0:T(512)S(1)} %get-tuple-element.57), kind=kOutput, calls=%fused_computation.22 | convolution fusion | flops 402784256 | bytes 1312768 | tf_op jit(solution)/shard_map/dot_general | solution.py:125
  15.5 1.0 %collective-permute-done.4 = s32[2,128]{1,0:T(2,128)S(1)} collective-permute-done((s32[2,128]{1,0:T(2,128)S(1)}, s32[2,128]{1,0:T(2,128)S(1)}, u32[]{:S(2)}, u32[]{:S(2)}) %collective-permute-start.4) | collective-permute-done | bytes 1056 | tf_op jit(solution)/shard_map/ppermute | solution.py:37
  16.4 0.1 fusion.8
  16.6 0.2 fusion.29
  16.8 0.1 collective-permute-start.5
  16.9 1.6 %collective-permute-start.7 = (f32[131,128]{1,0:T(8,128)S(1)}, f32[131,128]{1,0:T(8,128)S(1)}, u32[]{:S(2)}, u32[]{:S(2)}) collective-permute-start(f32[131,128]{1,0:T(8,128)S(1)} %get-tuple-element.66), channel_id=1, source_target_pairs={{0,3},{1,2},{2,1},{3,0},{4,7},{5,6},{6,5},{7,4},{8,11},{9,10},{10,... | collective-permute-start | bytes 201224 | tf_op jit(solution)/shard_map/ppermute | solution.py:63
  18.5 0.5 collective-permute-start.6
  19.0 2.0 %collective-permute-done.7 = f32[131,128]{1,0:T(8,128)S(1)} collective-permute-done((f32[131,128]{1,0:T(8,128)S(1)}, f32[131,128]{1,0:T(8,128)S(1)}, u32[]{:S(2)}, u32[]{:S(2)}) %collective-permute-start.7) | collective-permute-done | bytes 67104 | tf_op jit(solution)/shard_map/ppermute | solution.py:63
  21.0 1.9 %collective-permute-done.6 = f32[131,128]{1,0:T(8,128)S(1)} collective-permute-done((f32[131,128]{1,0:T(8,128)S(1)}, f32[131,128]{1,0:T(8,128)S(1)}, u32[]{:S(2)}, u32[]{:S(2)}) %collective-permute-start.6) | collective-permute-done | bytes 67104 | tf_op jit(solution)/shard_map/ppermute | solution.py:63
  23.0 0.1 fusion.34
  23.1 2.5 %collective-permute-start.8 = (f32[130,128]{1,0:T(8,128)S(1)}, f32[130,128]{1,0:T(8,128)S(1)}, u32[]{:S(2)}, u32[]{:S(2)}) collective-permute-start(f32[130,128]{1,0:T(8,128)S(1)} %get-tuple-element.54), channel_id=1, source_target_pairs={{0,4},{4,8},{8,12},{12,0},{1,5},{5,9},{9,13},{13,1},{2,6},{6,10},{... | collective-permute-start | bytes 199688 | tf_op jit(solution)/shard_map/ppermute | solution.py:41
  25.6 1.3 %collective-permute-start.10 = (f32[130,128]{1,0:T(8,128)S(1)}, f32[130,128]{1,0:T(8,128)S(1)}, u32[]{:S(2)}, u32[]{:S(2)}) collective-permute-start(f32[130,128]{1,0:T(8,128)S(1)} %get-tuple-element.54), channel_id=1, source_target_pairs={{0,12},{4,0},{8,4},{12,8},{1,13},{5,1},{9,5},{13,9},{2,14},{6,2},{... | collective-permute-start | bytes 199688 | tf_op jit(solution)/shard_map/ppermute | solution.py:41
  27.0 0.2 collective-permute-start.9
  27.2 0.0 collective-permute-start.11
  27.2 0.1 fusion.94
  27.3 1.1 %collective-permute-done.11 = f32[128,128]{1,0:T(8,128)S(1)} collective-permute-done((f32[128,128]{1,0:T(8,128)S(1)}, f32[128,128]{1,0:T(8,128)S(1)}, u32[]{:S(2)}, u32[]{:S(2)}) %collective-permute-start.11) | collective-permute-done | bytes 65568 | tf_op jit(solution)/shard_map/ppermute | solution.py:35
  28.4 1.6 %collective-permute-start.12 = (f32[2,128,128]{2,1,0:T(8,128)S(1)}, f32[2,128,128]{2,1,0:T(8,128)S(1)}, u32[]{:S(2)}, u32[]{:S(2)}) collective-permute-start(f32[2,128,128]{2,1,0:T(8,128)S(1)} %pad_maximum_fusion.7), channel_id=1, source_target_pairs={{0,2},{1,3},{2,0},{3,1},{4,6},{5,7},{6,4},{7,5},{8,10},{9,11},{10,... | collective-permute-start | bytes 393224 | tf_op jit(solution)/shard_map/ppermute | solution.py:37
  30.0 0.0 collective-permute-done.8
  30.0 0.4 collective-permute-done.10
  30.3 2.7 %collective-permute-done.9 = f32[130,128]{1,0:T(8,128)S(1)} collective-permute-done((f32[130,128]{1,0:T(8,128)S(1)}, f32[130,128]{1,0:T(8,128)S(1)}, u32[]{:S(2)}, u32[]{:S(2)}) %collective-permute-start.9) | collective-permute-done | bytes 66592 | tf_op jit(solution)/shard_map/ppermute | solution.py:41
  33.1 0.1 multiply_reduce_fusion.3
  33.2 0.9 %collective-permute-done.12 = f32[2,128,128]{2,1,0:T(8,128)S(1)} collective-permute-done((f32[2,128,128]{2,1,0:T(8,128)S(1)}, f32[2,128,128]{2,1,0:T(8,128)S(1)}, u32[]{:S(2)}, u32[]{:S(2)}) %collective-permute-start.12) | collective-permute-done | bytes 131104 | tf_op jit(solution)/shard_map/ppermute | solution.py:37
  34.1 0.2 multiply_subtract_fusion.1
  34.3 1.0 %fusion.87 = f32[4,128,128]{2,1,0:T(8,128)S(1)} fusion(f32[4,128,512]{2,1,0:T(8,128)S(1)} %bitcast.281, f32[512,128,1]{1,0,2:T(8,128)S(1)} %bitcast.287), kind=kOutput, calls=%fused_computation.221 | convolution fusion | flops 402653184 | bytes 1572864 | tf_op jit(solution)/shard_map/dot_general | solution.py:125
  35.3 0.1 fusion.52
  35.4 0.1 collective-permute-start.13
  35.5 1.7 %collective-permute-start.15 = (f32[132,128]{1,0:T(8,128)S(1)}, f32[132,128]{1,0:T(8,128)S(1)}, u32[]{:S(2)}, u32[]{:S(2)}) collective-permute-start(f32[132,128]{1,0:T(8,128)S(1)} %concatenate.66), channel_id=1, source_target_pairs={{0,3},{1,2},{2,1},{3,0},{4,7},{5,6},{6,5},{7,4},{8,11},{9,10},{10,... | collective-permute-start | bytes 202760 | tf_op jit(solution)/shard_map/ppermute | solution.py:63
  37.1 0.6 collective-permute-start.14
  37.7 1.9 %collective-permute-done.15 = f32[132,128]{1,0:T(8,128)S(1)} collective-permute-done((f32[132,128]{1,0:T(8,128)S(1)}, f32[132,128]{1,0:T(8,128)S(1)}, u32[]{:S(2)}, u32[]{:S(2)}) %collective-permute-start.15) | collective-permute-done | bytes 67616 | tf_op jit(solution)/shard_map/ppermute | solution.py:63
  39.6 1.9 %collective-permute-done.14 = f32[132,128]{1,0:T(8,128)S(1)} collective-permute-done((f32[132,128]{1,0:T(8,128)S(1)}, f32[132,128]{1,0:T(8,128)S(1)}, u32[]{:S(2)}, u32[]{:S(2)}) %collective-permute-start.14) | collective-permute-done | bytes 67616 | tf_op jit(solution)/shard_map/ppermute | solution.py:63
  41.5 0.1 multiply_subtract_fusion.3
  41.6 0.1 collective-permute-start.19
  41.7 2.9 %collective-permute-start.18 = (f32[132,128]{1,0:T(8,128)S(1)}, f32[132,128]{1,0:T(8,128)S(1)}, u32[]{:S(2)}, u32[]{:S(2)}) collective-permute-start(f32[132,128]{1,0:T(8,128)S(1)} %get-tuple-element.52), channel_id=1, source_target_pairs={{0,12},{4,0},{8,4},{12,8},{1,13},{5,1},{9,5},{13,9},{2,14},{6,2},{... | collective-permute-start | bytes 202760 | tf_op jit(solution)/shard_map/ppermute | solution.py:41
  44.7 1.9 %collective-permute-start.16 = (f32[132,128]{1,0:T(8,128)S(1)}, f32[132,128]{1,0:T(8,128)S(1)}, u32[]{:S(2)}, u32[]{:S(2)}) collective-permute-start(f32[132,128]{1,0:T(8,128)S(1)} %get-tuple-element.52), channel_id=1, source_target_pairs={{0,4},{4,8},{8,12},{12,0},{1,5},{5,9},{9,13},{13,1},{2,6},{6,10},{... | collective-permute-start | bytes 202760 | tf_op jit(solution)/shard_map/ppermute | solution.py:41
  46.6 1.5 %collective-permute-start.20 = (f32[2,128,128]{2,1,0:T(8,128)S(1)}, f32[2,128,128]{2,1,0:T(8,128)S(1)}, u32[]{:S(2)}, u32[]{:S(2)}) collective-permute-start(f32[2,128,128]{2,1,0:T(8,128)S(1)} %pad_maximum_fusion.8), channel_id=1, source_target_pairs={{0,2},{1,3},{2,0},{3,1},{4,6},{5,7},{6,4},{7,5},{8,10},{9,11},{10,... | collective-permute-start | bytes 393224 | tf_op jit(solution)/shard_map/ppermute | solution.py:37
  48.1 4.6 %collective-permute-done.17 = f32[132,128]{1,0:T(8,128)S(1)} collective-permute-done((f32[132,128]{1,0:T(8,128)S(1)}, f32[132,128]{1,0:T(8,128)S(1)}, u32[]{:S(2)}, u32[]{:S(2)}) %collective-permute-start.17) | collective-permute-done | bytes 67616 | tf_op jit(solution)/shard_map/ppermute | solution.py:41
  52.8 0.1 multiply_reduce_fusion.2
  52.9 0.2 fusion.2
  53.2 1.0 %fusion.88 = f32[4,128,128]{2,1,0:T(8,128)S(1)} fusion(f32[4,128,512]{2,1,0:T(8,128)S(1)} %bitcast.282, f32[512,128,1]{1,0,2:T(8,128)S(1)} %bitcast.286), kind=kOutput, calls=%fused_computation.222 | convolution fusion | flops 402653184 | bytes 1572864 | tf_op jit(solution)/shard_map/dot_general | solution.py:125
  54.3 0.9 %collective-permute-start.23 = (f32[132,128]{1,0:T(8,128)S(1)}, f32[132,128]{1,0:T(8,128)S(1)}, u32[]{:S(2)}, u32[]{:S(2)}) collective-permute-start(f32[132,128]{1,0:T(8,128)S(1)} %concatenate.71), channel_id=1, source_target_pairs={{0,3},{1,2},{2,1},{3,0},{4,7},{5,6},{6,5},{7,4},{8,11},{9,10},{10,... | collective-permute-start | bytes 202760 | tf_op jit(solution)/shard_map/ppermute | solution.py:63
  55.2 0.7 %collective-permute-start.22 = (f32[132,128]{1,0:T(8,128)S(1)}, f32[132,128]{1,0:T(8,128)S(1)}, u32[]{:S(2)}, u32[]{:S(2)}) collective-permute-start(f32[132,128]{1,0:T(8,128)S(1)} %concatenate.70), channel_id=1, source_target_pairs={{0,2},{1,3},{2,0},{3,1},{4,6},{5,7},{6,4},{7,5},{8,10},{9,11},{10,... | collective-permute-start | bytes 202760 | tf_op jit(solution)/shard_map/ppermute | solution.py:63
  55.9 0.4 collective-permute-start.21
  56.3 2.4 %collective-permute-done.23 = f32[132,128]{1,0:T(8,128)S(1)} collective-permute-done((f32[132,128]{1,0:T(8,128)S(1)}, f32[132,128]{1,0:T(8,128)S(1)}, u32[]{:S(2)}, u32[]{:S(2)}) %collective-permute-start.23) | collective-permute-done | bytes 67616 | tf_op jit(solution)/shard_map/ppermute | solution.py:63
  58.7 1.5 %collective-permute-done.22 = f32[132,128]{1,0:T(8,128)S(1)} collective-permute-done((f32[132,128]{1,0:T(8,128)S(1)}, f32[132,128]{1,0:T(8,128)S(1)}, u32[]{:S(2)}, u32[]{:S(2)}) %collective-permute-start.22) | collective-permute-done | bytes 67616 | tf_op jit(solution)/shard_map/ppermute | solution.py:63
  60.3 0.4 collective-permute-start.24
  60.7 1.6 %collective-permute-start.25 = (f32[4,128]{1,0:T(4,128)S(1)}, f32[4,128]{1,0:T(4,128)S(1)}, u32[]{:S(2)}, u32[]{:S(2)}) collective-permute-start(f32[4,128]{1,0:T(4,128)S(1)} %select_add_fusion.1), channel_id=1, source_target_pairs={{0,8},{4,12},{8,0},{12,4},{1,9},{5,13},{9,1},{13,5},{2,10},{6,14},... | collective-permute-start | bytes 6152 | tf_op jit(solution)/shard_map/ppermute | solution.py:41
  62.3 2.8 %collective-permute-start.26 = (f32[4,128]{1,0:T(4,128)S(1)}, f32[4,128]{1,0:T(4,128)S(1)}, u32[]{:S(2)}, u32[]{:S(2)}) collective-permute-start(f32[4,128]{1,0:T(4,128)S(1)} %select_add_fusion.1), channel_id=1, source_target_pairs={{0,12},{4,0},{8,4},{12,8},{1,13},{5,1},{9,5},{13,9},{2,14},{6,2},{... | collective-permute-start | bytes 6152 | tf_op jit(solution)/shard_map/ppermute | solution.py:41
  65.2 0.6 collective-permute-done.24
  65.7 0.7 %collective-permute-done.26 = f32[4,128]{1,0:T(4,128)S(1)} collective-permute-done((f32[4,128]{1,0:T(4,128)S(1)}, f32[4,128]{1,0:T(4,128)S(1)}, u32[]{:S(2)}, u32[]{:S(2)}) %collective-permute-start.26) | collective-permute-done | bytes 2080 | tf_op jit(solution)/shard_map/ppermute | solution.py:41
  66.5 0.8 %fusion.27 = (f32[128,128]{1,0:T(8,128)}, f32[128,128]{1,0:T(8,128)}) fusion(f32[132,128]{1,0:T(8,128)S(1)} %collective-permute-done.23, f32[132,128]{1,0:T(8,128)S(1)} %collective-permute-done.22, f32[132,128]{1,0:T(8,128)S(1)} %collective-permute-done.21, f32[128,128]{1,0:T(8,128)S(1)} %get-tuple-element.41, f32[4,128,128]{2,1,0:T(8,128)S(1)} %fusion.88, ...), kind=kLoop, calls=%fused_computation.79 | loop fusion | flops 425984 | bytes 527876 | tf_op jit(solution)/shard_map/sub | solution.py:179
  (52 shorter events, 0.6 us)
Async XLA Ops:
  0.6 12.2 %collective-permute-start.3 = (s32[128]{0:T(128)}, s32[128]{0:T(128)S(1)}, u32[]{:S(2)}, u32[]{:S(2)}) collective-permute-start(s32[128]{0:T(128)} %bitcast.308), channel_id=1, source_target_pairs={{0,1},{1,0},{2,3},{3,2},{4,5},{5,4},{6,7},{7,6},{8,9},{9,8},{10,11... | collective-permute-start | bytes 1544 | tf_op jit(solution)/shard_map/ppermute | solution.py:35
  1.1 13.2 %collective-permute-start.2 = (s32[128]{0:T(128)}, s32[128]{0:T(128)S(1)}, u32[]{:S(2)}, u32[]{:S(2)}) collective-permute-start(s32[128]{0:T(128)} %bitcast.309), channel_id=1, source_target_pairs={{0,12},{4,0},{8,4},{12,8},{1,13},{5,1},{9,5},{13,9},{2,14},{6,2},{... | collective-permute-start | bytes 1544 | tf_op jit(solution)/shard_map/ppermute | solution.py:41
  5.8 8.6 %collective-permute-start.1 = (s32[128]{0:T(128)}, s32[128]{0:T(128)S(1)}, u32[]{:S(2)}, u32[]{:S(2)}) collective-permute-start(s32[128]{0:T(128)} %bitcast.310), channel_id=1, source_target_pairs={{0,8},{4,12},{8,0},{12,4},{1,9},{5,13},{9,1},{13,5},{2,10},{6,14},... | collective-permute-start | bytes 1544 | tf_op jit(solution)/shard_map/ppermute | solution.py:41
  5.8 8.6 %collective-permute-start = (s32[128]{0:T(128)}, s32[128]{0:T(128)S(1)}, u32[]{:S(2)}, u32[]{:S(2)}) collective-permute-start(s32[128]{0:T(128)} %bitcast.311), channel_id=1, source_target_pairs={{0,4},{4,8},{8,12},{12,0},{1,5},{5,9},{9,13},{13,1},{2,6},{6,10},{... | collective-permute-start | bytes 1544 | tf_op jit(solution)/shard_map/ppermute | solution.py:41
  8.3 3.2 %copy-start = (s32[128,1]{0,1:T(1,128)S(1)}, s32[128,1]{0,1:T(1,128)}, u32[]{:S(2)}) copy-start(s32[128,1]{0,1:T(1,128)} %param.5) | copy-start | bytes 1540
  12.8 3.6 %collective-permute-start.4 = (s32[2,128]{1,0:T(2,128)S(1)}, s32[2,128]{1,0:T(2,128)S(1)}, u32[]{:S(2)}, u32[]{:S(2)}) collective-permute-start(s32[2,128]{1,0:T(2,128)S(1)} %pad_add_fusion.2), channel_id=1, source_target_pairs={{0,2},{1,3},{2,0},{3,1},{4,6},{5,7},{6,4},{7,5},{8,10},{9,11},{10,... | collective-permute-start | bytes 3080 | tf_op jit(solution)/shard_map/ppermute | solution.py:37
  16.8 2.2 %collective-permute-start.5 = (f32[131,128]{1,0:T(8,128)S(1)}, f32[131,128]{1,0:T(8,128)S(1)}, u32[]{:S(2)}, u32[]{:S(2)}) collective-permute-start(f32[131,128]{1,0:T(8,128)S(1)} %get-tuple-element.64), channel_id=1, source_target_pairs={{0,1},{1,0},{2,3},{3,2},{4,5},{5,4},{6,7},{7,6},{8,9},{9,8},{10,11... | collective-permute-start | bytes 201224 | tf_op jit(solution)/shard_map/ppermute | solution.py:63
  16.9 4.1 %collective-permute-start.7 = (f32[131,128]{1,0:T(8,128)S(1)}, f32[131,128]{1,0:T(8,128)S(1)}, u32[]{:S(2)}, u32[]{:S(2)}) collective-permute-start(f32[131,128]{1,0:T(8,128)S(1)} %get-tuple-element.66), channel_id=1, source_target_pairs={{0,3},{1,2},{2,1},{3,0},{4,7},{5,6},{6,5},{7,4},{8,11},{9,10},{10,... | collective-permute-start | bytes 201224 | tf_op jit(solution)/shard_map/ppermute | solution.py:63
  18.5 4.4 %collective-permute-start.6 = (f32[131,128]{1,0:T(8,128)S(1)}, f32[131,128]{1,0:T(8,128)S(1)}, u32[]{:S(2)}, u32[]{:S(2)}) collective-permute-start(f32[131,128]{1,0:T(8,128)S(1)} %get-tuple-element.65), channel_id=1, source_target_pairs={{0,2},{1,3},{2,0},{3,1},{4,6},{5,7},{6,4},{7,5},{8,10},{9,11},{10,... | collective-permute-start | bytes 201224 | tf_op jit(solution)/shard_map/ppermute | solution.py:63
  23.1 6.9 %collective-permute-start.8 = (f32[130,128]{1,0:T(8,128)S(1)}, f32[130,128]{1,0:T(8,128)S(1)}, u32[]{:S(2)}, u32[]{:S(2)}) collective-permute-start(f32[130,128]{1,0:T(8,128)S(1)} %get-tuple-element.54), channel_id=1, source_target_pairs={{0,4},{4,8},{8,12},{12,0},{1,5},{5,9},{9,13},{13,1},{2,6},{6,10},{... | collective-permute-start | bytes 199688 | tf_op jit(solution)/shard_map/ppermute | solution.py:41
  25.6 4.7 %collective-permute-start.10 = (f32[130,128]{1,0:T(8,128)S(1)}, f32[130,128]{1,0:T(8,128)S(1)}, u32[]{:S(2)}, u32[]{:S(2)}) collective-permute-start(f32[130,128]{1,0:T(8,128)S(1)} %get-tuple-element.54), channel_id=1, source_target_pairs={{0,12},{4,0},{8,4},{12,8},{1,13},{5,1},{9,5},{13,9},{2,14},{6,2},{... | collective-permute-start | bytes 199688 | tf_op jit(solution)/shard_map/ppermute | solution.py:41
  27.0 6.0 %collective-permute-start.9 = (f32[130,128]{1,0:T(8,128)S(1)}, f32[130,128]{1,0:T(8,128)S(1)}, u32[]{:S(2)}, u32[]{:S(2)}) collective-permute-start(f32[130,128]{1,0:T(8,128)S(1)} %get-tuple-element.54), channel_id=1, source_target_pairs={{0,8},{4,12},{8,0},{12,4},{1,9},{5,13},{9,1},{13,5},{2,10},{6,14},... | collective-permute-start | bytes 199688 | tf_op jit(solution)/shard_map/ppermute | solution.py:41
  27.2 1.3 %collective-permute-start.11 = (f32[128,128]{1,0:T(8,128)S(1)}, f32[128,128]{1,0:T(8,128)S(1)}, u32[]{:S(2)}, u32[]{:S(2)}) collective-permute-start(f32[128,128]{1,0:T(8,128)S(1)} %fusion.34), channel_id=1, source_target_pairs={{0,1},{1,0},{2,3},{3,2},{4,5},{5,4},{6,7},{7,6},{8,9},{9,8},{10,11... | collective-permute-start | bytes 196616 | tf_op jit(solution)/shard_map/ppermute | solution.py:35
  28.4 5.6 %collective-permute-start.12 = (f32[2,128,128]{2,1,0:T(8,128)S(1)}, f32[2,128,128]{2,1,0:T(8,128)S(1)}, u32[]{:S(2)}, u32[]{:S(2)}) collective-permute-start(f32[2,128,128]{2,1,0:T(8,128)S(1)} %pad_maximum_fusion.7), channel_id=1, source_target_pairs={{0,2},{1,3},{2,0},{3,1},{4,6},{5,7},{6,4},{7,5},{8,10},{9,11},{10,... | collective-permute-start | bytes 393224 | tf_op jit(solution)/shard_map/ppermute | solution.py:37
  35.4 2.4 %collective-permute-start.13 = (f32[132,128]{1,0:T(8,128)S(1)}, f32[132,128]{1,0:T(8,128)S(1)}, u32[]{:S(2)}, u32[]{:S(2)}) collective-permute-start(f32[132,128]{1,0:T(8,128)S(1)} %concatenate.64), channel_id=1, source_target_pairs={{0,1},{1,0},{2,3},{3,2},{4,5},{5,4},{6,7},{7,6},{8,9},{9,8},{10,11... | collective-permute-start | bytes 202760 | tf_op jit(solution)/shard_map/ppermute | solution.py:63
  35.5 4.2 %collective-permute-start.15 = (f32[132,128]{1,0:T(8,128)S(1)}, f32[132,128]{1,0:T(8,128)S(1)}, u32[]{:S(2)}, u32[]{:S(2)}) collective-permute-start(f32[132,128]{1,0:T(8,128)S(1)} %concatenate.66), channel_id=1, source_target_pairs={{0,3},{1,2},{2,1},{3,0},{4,7},{5,6},{6,5},{7,4},{8,11},{9,10},{10,... | collective-permute-start | bytes 202760 | tf_op jit(solution)/shard_map/ppermute | solution.py:63
  37.1 4.4 %collective-permute-start.14 = (f32[132,128]{1,0:T(8,128)S(1)}, f32[132,128]{1,0:T(8,128)S(1)}, u32[]{:S(2)}, u32[]{:S(2)}) collective-permute-start(f32[132,128]{1,0:T(8,128)S(1)} %concatenate.65), channel_id=1, source_target_pairs={{0,2},{1,3},{2,0},{3,1},{4,6},{5,7},{6,4},{7,5},{8,10},{9,11},{10,... | collective-permute-start | bytes 202760 | tf_op jit(solution)/shard_map/ppermute | solution.py:63
  41.6 5.0 %collective-permute-start.19 = (f32[128,128]{1,0:T(8,128)S(1)}, f32[128,128]{1,0:T(8,128)S(1)}, u32[]{:S(2)}, u32[]{:S(2)}) collective-permute-start(f32[128,128]{1,0:T(8,128)S(1)} %multiply_subtract_fusion.3), channel_id=1, source_target_pairs={{0,1},{1,0},{2,3},{3,2},{4,5},{5,4},{6,7},{7,6},{8,9},{9,8},{10,11... | collective-permute-start | bytes 196616 | tf_op jit(solution)/shard_map/ppermute | solution.py:35
  41.7 6.4 %collective-permute-start.18 = (f32[132,128]{1,0:T(8,128)S(1)}, f32[132,128]{1,0:T(8,128)S(1)}, u32[]{:S(2)}, u32[]{:S(2)}) collective-permute-start(f32[132,128]{1,0:T(8,128)S(1)} %get-tuple-element.52), channel_id=1, source_target_pairs={{0,12},{4,0},{8,4},{12,8},{1,13},{5,1},{9,5},{13,9},{2,14},{6,2},{... | collective-permute-start | bytes 202760 | tf_op jit(solution)/shard_map/ppermute | solution.py:41
  44.7 8.1 %collective-permute-start.17 = (f32[132,128]{1,0:T(8,128)S(1)}, f32[132,128]{1,0:T(8,128)S(1)}, u32[]{:S(2)}, u32[]{:S(2)}) collective-permute-start(f32[132,128]{1,0:T(8,128)S(1)} %get-tuple-element.52), channel_id=1, source_target_pairs={{0,8},{4,12},{8,0},{12,4},{1,9},{5,13},{9,1},{13,5},{2,10},{6,14},... | collective-permute-start | bytes 202760 | tf_op jit(solution)/shard_map/ppermute | solution.py:41
  44.7 8.1 %collective-permute-start.16 = (f32[132,128]{1,0:T(8,128)S(1)}, f32[132,128]{1,0:T(8,128)S(1)}, u32[]{:S(2)}, u32[]{:S(2)}) collective-permute-start(f32[132,128]{1,0:T(8,128)S(1)} %get-tuple-element.52), channel_id=1, source_target_pairs={{0,4},{4,8},{8,12},{12,0},{1,5},{5,9},{9,13},{13,1},{2,6},{6,10},{... | collective-permute-start | bytes 202760 | tf_op jit(solution)/shard_map/ppermute | solution.py:41
  46.6 6.3 %collective-permute-start.20 = (f32[2,128,128]{2,1,0:T(8,128)S(1)}, f32[2,128,128]{2,1,0:T(8,128)S(1)}, u32[]{:S(2)}, u32[]{:S(2)}) collective-permute-start(f32[2,128,128]{2,1,0:T(8,128)S(1)} %pad_maximum_fusion.8), channel_id=1, source_target_pairs={{0,2},{1,3},{2,0},{3,1},{4,6},{5,7},{6,4},{7,5},{8,10},{9,11},{10,... | collective-permute-start | bytes 393224 | tf_op jit(solution)/shard_map/ppermute | solution.py:37
  54.3 4.5 %collective-permute-start.23 = (f32[132,128]{1,0:T(8,128)S(1)}, f32[132,128]{1,0:T(8,128)S(1)}, u32[]{:S(2)}, u32[]{:S(2)}) collective-permute-start(f32[132,128]{1,0:T(8,128)S(1)} %concatenate.71), channel_id=1, source_target_pairs={{0,3},{1,2},{2,1},{3,0},{4,7},{5,6},{6,5},{7,4},{8,11},{9,10},{10,... | collective-permute-start | bytes 202760 | tf_op jit(solution)/shard_map/ppermute | solution.py:63
  55.2 5.1 %collective-permute-start.22 = (f32[132,128]{1,0:T(8,128)S(1)}, f32[132,128]{1,0:T(8,128)S(1)}, u32[]{:S(2)}, u32[]{:S(2)}) collective-permute-start(f32[132,128]{1,0:T(8,128)S(1)} %concatenate.70), channel_id=1, source_target_pairs={{0,2},{1,3},{2,0},{3,1},{4,6},{5,7},{6,4},{7,5},{8,10},{9,11},{10,... | collective-permute-start | bytes 202760 | tf_op jit(solution)/shard_map/ppermute | solution.py:63
  55.9 4.4 %collective-permute-start.21 = (f32[132,128]{1,0:T(8,128)S(1)}, f32[132,128]{1,0:T(8,128)S(1)}, u32[]{:S(2)}, u32[]{:S(2)}) collective-permute-start(f32[132,128]{1,0:T(8,128)S(1)} %concatenate.69), channel_id=1, source_target_pairs={{0,1},{1,0},{2,3},{3,2},{4,5},{5,4},{6,7},{7,6},{8,9},{9,8},{10,11... | collective-permute-start | bytes 202760 | tf_op jit(solution)/shard_map/ppermute | solution.py:63
  60.3 5.4 %collective-permute-start.24 = (f32[4,128]{1,0:T(4,128)S(1)}, f32[4,128]{1,0:T(4,128)S(1)}, u32[]{:S(2)}, u32[]{:S(2)}) collective-permute-start(f32[4,128]{1,0:T(4,128)S(1)} %select_add_fusion.1), channel_id=1, source_target_pairs={{0,4},{4,8},{8,12},{12,0},{1,5},{5,9},{9,13},{13,1},{2,6},{6,10},{... | collective-permute-start | bytes 6152 | tf_op jit(solution)/shard_map/ppermute | solution.py:41
  60.7 5.0 %collective-permute-start.25 = (f32[4,128]{1,0:T(4,128)S(1)}, f32[4,128]{1,0:T(4,128)S(1)}, u32[]{:S(2)}, u32[]{:S(2)}) collective-permute-start(f32[4,128]{1,0:T(4,128)S(1)} %select_add_fusion.1), channel_id=1, source_target_pairs={{0,8},{4,12},{8,0},{12,4},{1,9},{5,13},{9,1},{13,5},{2,10},{6,14},... | collective-permute-start | bytes 6152 | tf_op jit(solution)/shard_map/ppermute | solution.py:41
  62.3 4.2 %collective-permute-start.26 = (f32[4,128]{1,0:T(4,128)S(1)}, f32[4,128]{1,0:T(4,128)S(1)}, u32[]{:S(2)}, u32[]{:S(2)}) collective-permute-start(f32[4,128]{1,0:T(4,128)S(1)} %select_add_fusion.1), channel_id=1, source_target_pairs={{0,12},{4,0},{8,4},{12,8},{1,13},{5,1},{9,5},{13,9},{2,14},{6,2},{... | collective-permute-start | bytes 6152 | tf_op jit(solution)/shard_map/ppermute | solution.py:41
